TPU v7x, 256 devices: a whole 4x4x8 slice. The times are simulated.
256 devices in a mesh: row: 16 (over z, y_lo), col: 16 (over y_hi, x, core).
Axes of the slice: x: 4, y: 4 (y_hi: 2, y_lo: 2; y = y_hi * 2 + y_lo), z: 8, core: 2. Of those that a mesh axis runs over, the one named last changes fastest.
Arguments:
- points: float32 [32, 65536], P(None, ('row', 'col')), may hold values from -6 to 6
- candidates: float32 [32, 16384], P(None, ('row', 'col')), may hold values from -6 to 6
- length_scales: float32 [32], replicated, may hold values from 1.5 to 4
- signal_var: float32 [1], replicated, may hold values from 0.5 to 2
- noise_var: float32 [1], replicated, may hold values from 0.1 to 1
- cand_prior: float32 [16384], P(('row', 'col')), may hold values from -6 to 6
- weights: float32 [16, 65536], P(None, ('row', 'col')), may hold values from -6 to 6
- residual: float32 [16, 65536], P(None, ('row', 'col')), may hold values from -300 to 300, as said below
- direction: float32 [16, 65536], P(None, ('row', 'col')), may hold values from -300 to 300, as said below
Outputs:
- weights_new: float32 [16, 65536], P(None, ('row', 'col'))
- residual_new: float32 [16, 65536], P(None, ('row', 'col'))
- direction_new: float32 [16, 65536], P(None, ('row', 'col'))
- cand_fit: float32 [16, 16384], P(None, ('row', 'col'))
Inputs may be any that keep to these rules, and one draw needn't show every extreme that they name: `residual`: real values. `direction`: real values.
All inputs are finite; a program needn't handle non-finite values.
Results may differ from a plain program's by a relative error of at most 0.011.
Values may be sent and summed in bfloat16 or wider, within the bound.
No kernel may reach another device: no remote copies, remote signals or barrier semaphores. Data moves between devices by JAX's collectives and lax.ppermute only.
A program may use at most 64 MiB of HBM per device.

v0:
```python
import math

import jax
import jax.numpy as jnp
from jax import lax
from jax.sharding import PartitionSpec as P

root_five = math.sqrt(5.0)
contract_first = (((0,), (0,)), ((), ()))
contract_last = (((1,), (1,)), ((), ()))


def square_norms(scaled):
    return jnp.sum(jnp.square(scaled.astype(jnp.float32)), axis=0)


def matern_block(row_pts, row_sq, col_pts, col_sq, signal_scalar):
    inner_prod = lax.dot_general(
        row_pts, col_pts, contract_first, preferred_element_type=jnp.float32
    )
    dist_sq = jnp.maximum(row_sq[:, None] + col_sq[None, :] - 2.0 * inner_prod, 0.0)
    distance = jnp.sqrt(dist_sq)
    kern_vals = (
        signal_scalar
        * (1.0 + root_five * distance + 5.0 / 3.0 * dist_sq)
        * jnp.exp(-root_five * distance)
    )
    return kern_vals.astype(jnp.bfloat16)


def kernel_apply(running, row_pts, row_sq, col_pts, col_sq, vectors, signal_scalar):
    row_count = row_pts.shape[1]
    width_all = col_pts.shape[1]
    block_len = math.gcd(width_all, max(256, 1048576 // row_count))
    num_blocks = width_all // block_len

    def one_block(total, pieces):
        pts_blk, sq_blk, vec_blk = pieces
        kern_vals = matern_block(row_pts, row_sq, pts_blk, sq_blk, signal_scalar)
        return (
            total
            + lax.dot_general(
                vec_blk, kern_vals, contract_last, preferred_element_type=jnp.float32
            ),
            None,
        )

    feature_count = col_pts.shape[0]
    pts_blocks = col_pts.reshape(feature_count, num_blocks, block_len).transpose(1, 0, 2)
    sq_blocks = col_sq.reshape(num_blocks, block_len)
    vec_blocks = vectors.reshape(vectors.shape[0], num_blocks, block_len).transpose(1, 0, 2)
    result, ignored = lax.scan(one_block, running, (pts_blocks, sq_blocks, vec_blocks))
    return result


def per_device(
    points,
    candidates,
    length_scales,
    signal_var,
    noise_var,
    cand_prior,
    weights,
    residual,
    direction,
):
    scaled = (points / length_scales[:, None]).astype(jnp.bfloat16)
    cand_scaled = (candidates / length_scales[:, None]).astype(jnp.bfloat16)
    signal_scalar = signal_var[0]
    dir_low = direction.astype(jnp.bfloat16)
    col_total = direction.shape[0]
    norm_now = lax.psum(jnp.sum(residual * residual, axis=1), ("row", "col"))
    row_pts, row_cands = (
        lax.all_gather(scaled, "col", axis=1, tiled=True),
        lax.all_gather(cand_scaled, "col", axis=1, tiled=True),
    )
    col_pts = lax.all_gather(scaled, "row", axis=1, tiled=True)
    row_sq = square_norms(row_pts)
    col_sq = square_norms(col_pts)
    cand_sq = square_norms(row_cands)
    start_rows = jnp.zeros((col_total, row_pts.shape[1]), jnp.float32)
    pts_piece = col_pts
    sq_piece = col_sq
    partial_rows = kernel_apply(
        start_rows,
        row_pts,
        row_sq,
        pts_piece,
        sq_piece,
        lax.all_gather(dir_low, "row", axis=1, tiled=True),
        signal_scalar,
    )
    kernel_out = lax.psum_scatter(partial_rows, "col", scatter_dimension=1, tiled=True)
    image_vec = kernel_out + noise_var[0] * direction
    curvature = lax.psum(jnp.sum(direction * image_vec, axis=1), ("row", "col"))
    step_len = norm_now / curvature
    weights_new = weights + step_len[:, None] * direction
    residual_new = residual - step_len[:, None] * image_vec
    norm_next = lax.psum(jnp.sum(residual_new * residual_new, axis=1), ("row", "col"))
    direction_new = residual_new + (norm_next / norm_now)[:, None] * direction
    w_low = weights_new.astype(jnp.bfloat16)
    start_cands = jnp.zeros((col_total, row_cands.shape[1]), jnp.float32)
    pts_piece = col_pts
    sq_piece = col_sq
    partial_fit = kernel_apply(
        start_cands,
        row_cands,
        cand_sq,
        pts_piece,
        sq_piece,
        lax.all_gather(w_low, "row", axis=1, tiled=True),
        signal_scalar,
    )
    fitted = lax.psum_scatter(partial_fit, "col", scatter_dimension=1, tiled=True)
    cand_fit = cand_prior[None, :] + fitted
    return (weights_new, residual_new, direction_new, cand_fit)


def solution(mesh):
    placed = (
        P(None, ("row", "col")),
        P(None, ("row", "col")),
        P(),
        P(),
        P(),
        P(("row", "col")),
        P(None, ("row", "col")),
        P(None, ("row", "col")),
        P(None, ("row", "col")),
    )
    return jax.shard_map(
        per_device,
        mesh=mesh,
        in_specs=placed,
        out_specs=(
            P(None, ("row", "col")),
            P(None, ("row", "col")),
            P(None, ("row", "col")),
            P(None, ("row", "col")),
        ),
        check_vma=False,
    )
```

profile of v0, /device:TPU:2, one launch (start us, length us, event | category | flops | bytes accessed | tf_op | source)
XLA Modules:
  0.0 508.7 jit_solution(10705769252974074291)
XLA Ops:
  7.2 0.0 reduce-scatter.5.cloned.1.call-start
  7.2 0.8 divide_convert_fusion
  8.1 37.8 %all_gather.17 = bf16[32,4096]{1,0:T(8,128)(2,1)S(1)} all-gather(bf16[32,256]{1,0:T(8,128)(2,1)S(1)} %divide_convert_fusion), channel_id=1, replica_groups=mesh['row'=16,'col'=16] {'row'}, dimensions={1}, use_global_device_ids=true | all-gather | bytes 278528 | tf_op jit(solution)/shard_map/all_gather | solution.py:77
  45.9 20.4 %all_gather.16 = bf16[32,4096]{1,0:T(8,128)(2,1)S(1)} all-gather(bf16[32,256]{1,0:T(8,128)(2,1)S(1)} %divide_convert_fusion), channel_id=1, replica_groups=mesh['row'=16,'col'=16] {'col'}, dimensions={1}, use_global_device_ids=true | all-gather | bytes 278528 | tf_op jit(solution)/shard_map/all_gather | solution.py:74
  66.3 0.1 multiply_reduce_fusion
  66.4 0.1 multiply_reduce_fusion.1
  66.5 0.5 copy-done.1
  67.0 30.2 %all_gather.15 = bf16[16,4096]{1,0:T(8,128)(2,1)S(1)} all-gather(bf16[16,256]{1,0:T(8,128)(2,1)S(1)} %convert_element_type.27), channel_id=1, replica_groups=mesh['row'=16,'col'=16] {'row'}, dimensions={1}, use_global_device_ids=true | all-gather | bytes 139264 | tf_op jit(solution)/shard_map/all_gather | solution.py:90
  97.2 62.3 %while.22 = (s32[]{:T(128)}, f32[16,4096]{1,0:T(8,128)S(1)}, bf16[16,16,256]{2,1,0:T(8,128)(2,1)S(1)}, f32[]{:T(128)}, f32[4096]{0:T(1024)S(1)}, /*index=5*/f32[...) while((s32[]{:T(128)}, f32[16,4096]{1,0:T(8,128)S(1)}, ...), condition=%wide.region_5.6_spmd.clone, body=%wide.region_4.0_spmd.clone.sunk | while | flops 113377280 | bytes 832115 | solution.py:52
  97.3 3.9 convolution_add_fusion.2
  101.2 3.9 convolution_add_fusion.2
  105.1 3.8 convolution_add_fusion.2
  109.0 3.8 convolution_add_fusion.2
  112.8 3.8 convolution_add_fusion.2
  116.7 3.8 convolution_add_fusion.2
  120.6 3.8 convolution_add_fusion.2
  124.5 3.8 convolution_add_fusion.2
  128.4 3.8 convolution_add_fusion.2
  132.3 3.8 convolution_add_fusion.2
  136.2 3.8 convolution_add_fusion.2
  140.1 3.8 convolution_add_fusion.2
  144.0 3.8 convolution_add_fusion.2
  147.9 3.8 convolution_add_fusion.2
  151.8 3.8 convolution_add_fusion.2
  155.6 3.8 convolution_add_fusion.2
  159.5 0.0 copy-start
  159.5 0.0 copy-start.5
  159.5 0.0 copy-start.7
  159.5 0.7 copy-done
  160.2 0.0 reduce-scatter.5.cloned.1.call-update
  160.2 0.0 reduce-scatter.7.cloned.1.call-start
  160.3 0.0 copy-start.3
  160.3 0.2 reshape.37
  161.1 0.0 copy-done.5
  161.2 0.0 copy-done.7
  161.2 0.1 fusion.34
  161.2 24.1 %all-gather = bf16[16,64,32]{1,2,0:T(8,128)(2,1)S(1)} all-gather(bf16[1,64,32]{1,2,0:T(8,128)(2,1)S(1)} %fusion.34), channel_id=1, replica_groups=mesh['row'=16,'col'=16] {'col'}, dimensions={0}, use_global_device_ids=true | all-gather | bytes 69632 | tf_op jit(solution)/shard_map/all_gather | solution.py:75
  185.3 0.1 copy.28
  185.4 0.1 reshape.39
  185.5 0.0 copy-done.3
  185.5 0.1 multiply_reduce_fusion.5
  185.7 46.0 %reduce-scatter.5.cloned.1.call-done = f32[16,256]{1,0:T(8,128)} async-done(((f32[16,4096]{1,0:T(8,128)}), f32[16,256]{1,0:T(8,128)}) %reduce-scatter.5.cloned.1.call-update) | async-done | bytes 16400 | tf_op jit(solution)/shard_map/reduce_scatter | solution.py:93
  231.7 0.9 multiply_reduce_fusion.4
  232.6 0.1 copy.29
  232.6 73.9 %all-reduce = (f32[16]{0:T(128)S(1)}, f32[16]{0:T(128)S(1)}) all-reduce(f32[16]{0:T(128)S(1)} %multiply_reduce_fusion.5, f32[16]{0:T(128)S(1)} %multiply_reduce_fusion.4), channel_id=1, replica_groups=mesh['row'=16,'col'=16] {'row','col'}, use_global_device_ids=true, to_apply=%region_1.0 | all-reduce | flops 32 | bytes 256 | tf_op jit(solution)/shard_map/psum | solution.py:72
  306.6 0.0 copy-done.6
  306.6 0.0 copy-done.4
  306.6 0.8 multiply_reduce_fusion.3
  307.4 74.3 %psum.23 = f32[16]{0:T(128)S(1)} all-reduce(f32[16]{0:T(128)S(1)} %get-tuple-element.228), channel_id=1, replica_groups=mesh['row'=16,'col'=16] {'row','col'}, use_global_device_ids=true, to_apply=%region_10.11 | all-reduce | flops 16 | bytes 128 | tf_op jit(solution)/shard_map/psum | solution.py:99
  381.7 30.4 %all_gather.18 = bf16[16,4096]{1,0:T(8,128)(2,1)S(1)} all-gather(bf16[16,256]{1,0:T(8,128)(2,1)S(1)} %get-tuple-element.230), channel_id=1, replica_groups=mesh['row'=16,'col'=16] {'row'}, dimensions={1}, use_global_device_ids=true | all-gather | bytes 139264 | tf_op jit(solution)/shard_map/all_gather | solution.py:111
  412.1 15.4 %while.23 = (s32[]{:T(128)}, f32[16,1024]{1,0:T(8,128)S(1)}, bf16[4,16,1024]{2,1,0:T(8,128)(2,1)S(1)}, f32[]{:T(128)}, f32[1024]{0:T(1024)S(1)}, /*index=5*/f32[...) while((s32[]{:T(128)}, f32[16,1024]{1,0:T(8,128)S(1)}, ...), condition=%wide.region_13.14_spmd.clone, body=%wide.region_12.13_spmd.clone.sunk | while | flops 113278976 | bytes 312947 | solution.py:52
  412.1 3.8 fusion.51
  416.0 3.8 fusion.51
  419.8 3.8 fusion.51
  423.7 3.8 fusion.51
  427.5 0.0 copy-start.8
  427.5 1.0 copy.30
  428.5 0.0 reduce-scatter.7.cloned.1.call-update
  428.5 0.0 copy-done.2
  428.6 0.7 multiply_add_fusion
  429.2 71.2 %reduce-scatter.7.cloned.1.call-done = f32[64,16]{1,0:T(8,128)} async-done(((f32[1024,16]{1,0:T(8,128)}), f32[64,16]{1,0:T(8,128)}) %reduce-scatter.7.cloned.1.call-update) | async-done | bytes 4112
  500.4 0.8 copy.31
  501.2 0.0 copy-done.8
  501.2 0.6 broadcast_add_fusion
  (36 shorter events, 0.3 us)
Async XLA Ops:
  7.2 224.5 %reduce-scatter.5.cloned.1.call-start = ((), (), s32[]{:S(2)}) async-start(), calls=%async_computation.2 | async-start | bytes 278528 | tf_op jit(solution)/shard_map/reduce_scatter | solution.py:93
  66.3 0.7 copy-start.1
  159.5 0.7 copy-start
  159.5 1.6 copy-start.5
  159.5 1.6 copy-start.7
  160.2 340.2 %reduce-scatter.7.cloned.1.call-start = ((), (), s32[]{:S(2)}) async-start(), calls=%async_computation.3 | async-start | bytes 557056
  160.3 25.2 %copy-start.3 = (f32[16,256]{1,0:T(8,128)S(1)}, f32[16,256]{1,0:T(8,128)}, u32[]{:S(2)}) copy-start(f32[16,256]{1,0:T(8,128)} %param.20) | copy-start | bytes 49156
  185.3 121.3 %copy-start.6 = (f32[16,256]{1,0:T(8,128)S(1)}, f32[16,256]{1,0:T(8,128)}, u32[]{:S(2)}) copy-start(f32[16,256]{1,0:T(8,128)} %param.19) | copy-start | bytes 49156
  231.7 74.9 %copy-start.4 = (f32[16,256]{1,0:T(8,128)S(1)}, f32[16,256]{1,0:T(8,128)}, u32[]{:S(2)}) copy-start(f32[16,256]{1,0:T(8,128)} %reduce-scatter.5.cloned.1.call-done) | copy-start | bytes 49156
  307.4 121.2 %copy-start.2 = (f32[16,256]{1,0:T(8,128)}, f32[16,256]{1,0:T(8,128)S(1)}, u32[]{:S(2)}) copy-start(f32[16,256]{1,0:T(8,128)S(1)} %get-tuple-element.229) | copy-start | bytes 49156
  427.5 73.7 %copy-start.8 = (f32[64]{0:T(128)S(1)}, f32[64]{0:T(128)}, u32[]{:S(2)}) copy-start(f32[64]{0:T(128)} %param.18) | copy-start | bytes 772
Sparse Core Ops, SparseCore 0:
  160.3 71.2 reduce-scatter.4
  428.7 71.7 reduce-scatter.6
where the time goes:
time: 509 us
  blocking collectives  291 us (57%)
  waiting for transfers between devices  117 us (23%)
  matrix products  76.8 us (15%)
  between operations  14.9 us (3%)
    dot_general x20, matrix products, one_block(): lax.dot_general(vec_blk, kern_vals, contract_last, preferred_element_type...  76.8 us
    psum x1, blocking collectives, per_device(): lax.psum(jnp.sum(residual_new * residual_new, axis=1), ('row', 'col'))  74.3 us
    psum x1, blocking collectives, per_device(): norm_now = lax.psum(jnp.sum(residual * residual, axis=1), ('row', 'col'))  73.9 us
    unnamed x3, waiting for transfers between devices  71.2 us
    reduce_scatter x1, waiting for transfers between devices, per_device(): lax.psum_scatter(partial_rows, 'col', scatter_dimension=1, tiled=True)  46 us
    all_gather x1, blocking collectives, per_device(): col_pts = lax.all_gather(scaled, 'row', axis=1, tiled=True)  37.8 us
    all_gather x1, blocking collectives, per_device(): lax.all_gather(w_low, 'row', axis=1, tiled=True)  30.4 us
    all_gather x1, blocking collectives, per_device(): lax.all_gather(dir_low, 'row', axis=1, tiled=True)  30.2 us
  transfers between devices with their start and end apart: 2, of which 2 were waited for; matrix products, arithmetic and copies ran while one was open for 0% of the time, Pallas kernels for 0%

commit v1 on v0

v1 whole, which is shorter than its diff:
```python
import math

import jax
import jax.numpy as jnp
from jax import lax
from jax.sharding import PartitionSpec as P

root_five = math.sqrt(5.0)
contract_first = (((0,), (0,)), ((), ()))
contract_last = (((1,), (1,)), ((), ()))


def square_norms(scaled):
    return jnp.sum(jnp.square(scaled.astype(jnp.float32)), axis=0)


def matern_block(row_pts, row_sq, col_pts, col_sq, signal_scalar):
    inner_prod = lax.dot_general(
        row_pts, col_pts, contract_first, preferred_element_type=jnp.float32
    )
    dist_sq = jnp.maximum(row_sq[:, None] + col_sq[None, :] - 2.0 * inner_prod, 0.0)
    distance = jnp.sqrt(dist_sq)
    kern_vals = (
        signal_scalar
        * (1.0 + root_five * distance + 5.0 / 3.0 * dist_sq)
        * jnp.exp(-root_five * distance)
    )
    return kern_vals.astype(jnp.bfloat16)


def kernel_apply(row_pts, row_sq, col_pts, col_sq, vectors, signal_scalar, block_len):
    feature_count = col_pts.shape[0]
    num_blocks = col_pts.shape[1] // block_len
    pts_blocks = col_pts.reshape(feature_count, num_blocks, block_len).transpose(1, 0, 2)
    sq_blocks = col_sq.reshape(num_blocks, block_len)
    vec_blocks = vectors.reshape(vectors.shape[0], num_blocks, block_len).transpose(1, 0, 2)

    def one_block(total, pieces):
        pts_blk, sq_blk, vec_blk = pieces
        kern_vals = matern_block(row_pts, row_sq, pts_blk, sq_blk, signal_scalar)
        return (
            total
            + lax.dot_general(
                vec_blk, kern_vals, contract_last, preferred_element_type=jnp.float32
            ),
            None,
        )

    start = jnp.zeros((vectors.shape[0], row_pts.shape[1]), jnp.float32)
    result, ignored = lax.scan(one_block, start, (pts_blocks, sq_blocks, vec_blocks))
    return result


def xor_perm(size, bit):
    return [(i, i ^ (1 << bit)) for i in range(size)]


def gather_last(x, axis_name, size):
    me = lax.axis_index(axis_name)
    buf = x
    for bit in range(size.bit_length() - 1):
        recv = lax.ppermute(buf, axis_name, xor_perm(size, bit))
        low = ((me >> bit) & 1) == 0
        buf = jnp.where(
            low, jnp.concatenate([buf, recv], -1), jnp.concatenate([recv, buf], -1)
        )
    return buf


def reduce_scatter_last(x, axis_name, size):
    me = lax.axis_index(axis_name)
    buf = x
    for bit in reversed(range(size.bit_length() - 1)):
        half = buf.shape[-1] // 2
        lower, upper = buf[..., :half], buf[..., half:]
        low = ((me >> bit) & 1) == 0
        keep = jnp.where(low, lower, upper)
        send = jnp.where(low, upper, lower)
        buf = keep + lax.ppermute(send, axis_name, xor_perm(size, bit))
    return buf


def all_sum(x, axis_name, size):
    for bit in range(size.bit_length() - 1):
        x = x + lax.ppermute(x, axis_name, xor_perm(size, bit))
    return x


def per_device(
    points,
    candidates,
    length_scales,
    signal_var,
    noise_var,
    cand_prior,
    weights,
    residual,
    direction,
    n_row,
    n_col,
):
    scaled = (points / length_scales[:, None]).astype(jnp.bfloat16)
    cand_scaled = (candidates / length_scales[:, None]).astype(jnp.bfloat16)
    signal_scalar = signal_var[0]
    dir_low = direction.astype(jnp.bfloat16)
    cols, own = direction.shape
    own_cand = cand_scaled.shape[1]
    feats = scaled.shape[0]

    row_pack = gather_last(jnp.concatenate([scaled, cand_scaled], 1), "col", n_col)
    row_pack = row_pack.reshape(feats, n_col, own + own_cand)
    row_pts = row_pack[:, :, :own].reshape(feats, n_col * own)
    row_cands = row_pack[:, :, own:].reshape(feats, n_col * own_cand)
    col_pack = gather_last(jnp.concatenate([scaled, dir_low], 0), "row", n_row)
    col_pts = col_pack[:feats]
    col_dir = col_pack[feats:]
    row_state = gather_last(jnp.concatenate([residual, direction], 0), "col", n_col)
    res_row, dir_row = row_state[:cols], row_state[cols:]
    col_state = gather_last(jnp.concatenate([weights, direction], 0), "row", n_row)
    w_col, d_col = col_state[:cols], col_state[cols:]

    row_sq = square_norms(row_pts)
    col_sq = square_norms(col_pts)
    cand_sq = square_norms(row_cands)

    partial_rows = kernel_apply(
        row_pts, row_sq, col_pts, col_sq, col_dir, signal_scalar, 256
    )
    kernel_row = all_sum(partial_rows, "col", n_col)
    image_row = kernel_row + noise_var[0] * dir_row
    sums = all_sum(
        jnp.concatenate(
            [jnp.sum(res_row * res_row, axis=1), jnp.sum(dir_row * image_row, axis=1)]
        ),
        "row",
        n_row,
    )
    norm_now, curvature = sums[:cols], sums[cols:]
    step_len = norm_now / curvature
    residual_new_row = res_row - step_len[:, None] * image_row
    norm_next = all_sum(jnp.sum(residual_new_row * residual_new_row, axis=1), "row", n_row)

    me_col = lax.axis_index("col")
    image_vec = lax.dynamic_slice_in_dim(image_row, me_col * own, own, axis=1)
    weights_new = weights + step_len[:, None] * direction
    residual_new = residual - step_len[:, None] * image_vec
    direction_new = residual_new + (norm_next / norm_now)[:, None] * direction

    w_low_col = (w_col + step_len[:, None] * d_col).astype(jnp.bfloat16)
    partial_fit = kernel_apply(
        row_cands, cand_sq, col_pts, col_sq, w_low_col, signal_scalar, 1024
    )
    fitted = reduce_scatter_last(partial_fit, "col", n_col)
    cand_fit = cand_prior[None, :] + fitted
    return (weights_new, residual_new, direction_new, cand_fit)


def solution(mesh):
    placed = (
        P(None, ("row", "col")),
        P(None, ("row", "col")),
        P(),
        P(),
        P(),
        P(("row", "col")),
        P(None, ("row", "col")),
        P(None, ("row", "col")),
        P(None, ("row", "col")),
    )
    n_row, n_col = mesh.shape["row"], mesh.shape["col"]

    def body(*args):
        return per_device(*args, n_row=n_row, n_col=n_col)

    return jax.shard_map(
        body,
        mesh=mesh,
        in_specs=placed,
        out_specs=(
            P(None, ("row", "col")),
            P(None, ("row", "col")),
            P(None, ("row", "col")),
            P(None, ("row", "col")),
        ),
        check_vma=False,
    )
```

time: 509 us -> 229 us (0.45)
  blocking collectives: 291 us -> 0 us
  starting transfers between devices: 0.08 us -> 65.5 us
  waiting for transfers between devices: 117 us -> 73 us
  between operations: 14.9 us -> 1.67 us
    psum x2 -> x0, blocking collectives: 148 us -> none  [the longest x1 74.3 us: per_device(): lax.psum(jnp.sum(residual_new * residual_new, axis=1), ('row', 'col'))]
    all_gather x5 -> x0, blocking collectives: 143 us -> none  [the longest x1 37.8 us: per_device(): col_pts = lax.all_gather(scaled, 'row', axis=1, tiled=True)]
    ppermute x0 -> x32, waiting for transfers between devices: none -> 73 us  [the longest x16 32.9 us: gather_last(): recv = lax.ppermute(buf, axis_name, xor_perm(size, bit))]
    unnamed x3 -> x0, waiting for transfers between devices: 71.2 us -> none
    ppermute x0 -> x32, starting transfers between devices: none -> 65.5 us  [the longest x16 35.2 us: gather_last(): recv = lax.ppermute(buf, axis_name, xor_perm(size, bit))]
    reduce_scatter x1 -> x0, waiting for transfers between devices: 46 us -> none  [per_device(): lax.psum_scatter(partial_rows, 'col', scatter_dimension=1, tiled=True)]
  transfers between devices with their start and end apart: 2 -> 32, of which waited for: 2 -> 27; matrix products, arithmetic and copies ran while one was open for 0% -> 2% of each run, Pallas kernels for 0% -> 0%
where the time goes in v1:
time: 229 us; the launch traced here: 226 us
  matrix products  76.8 us (34%)
  waiting for transfers between devices  73 us (32%)
  starting transfers between devices  65.5 us (29%)
  other arithmetic  5.99 us (3%)
  local copies, waits for them, and re-layouts  2.38 us (1%)
    dot_general x20, matrix products, one_block(): lax.dot_general(vec_blk, kern_vals, contract_last, preferred_element_type...  76.8 us
    ppermute x16, starting transfers between devices, gather_last(): recv = lax.ppermute(buf, axis_name, xor_perm(size, bit))  35.2 us
    ppermute x16, waiting for transfers between devices, gather_last(): recv = lax.ppermute(buf, axis_name, xor_perm(size, bit))  32.9 us
    ppermute x12, waiting for transfers between devices, all_sum(): x = x + lax.ppermute(x, axis_name, xor_perm(size, bit))  28.4 us
    ppermute x12, starting transfers between devices, all_sum(): x = x + lax.ppermute(x, axis_name, xor_perm(size, bit))  26.2 us
    ppermute x4, waiting for transfers between devices, reduce_scatter_last(): buf = keep + lax.ppermute(send, axis_name, xor_perm(size, bit))  11.7 us
  transfers between devices with their start and end apart: 32, of which 27 were waited for; matrix products, arithmetic and copies ran while one was open for 2% of the time, Pallas kernels for 0%

profile of v1, /device:TPU:2, one launch (start us, length us, event | category | flops | bytes accessed | tf_op | source)
XLA Modules:
  0.0 225.9 jit_solution(5813205564933078130)
XLA Ops:
  3.9 1.6 collective-permute-start.4
  6.5 1.2 collective-permute-done.4
  7.8 2.0 collective-permute-start.5
  9.8 2.2 collective-permute-start.10
  12.4 3.4 %collective-permute-start.6 = (bf16[48,1024]{1,0:T(8,128)(2,1)S(1)}, bf16[48,1024]{1,0:T(8,128)(2,1)S(1)}, u32[]{:S(2)}, u32[]{:S(2)}) collective-permute-start(bf16[48,1024]{1,0:T(8,128)(2,1)S(1)} %maximum_select_fusion.11), channel_id=1, source_target_pairs={{0,64},{16,80},{32,96},{48,112},{64,0},{80,16},{96,32},{112,48},{1... | collective-permute-start | bytes 294920 | tf_op jit(solution)/shard_map/ppermute | solution.py:62
  15.9 3.3 %collective-permute-start.11 = (bf16[32,2560]{1,0:T(8,128)(2,1)S(1)}, bf16[32,2560]{1,0:T(8,128)(2,1)S(1)}, u32[]{:S(2)}, u32[]{:S(2)}) collective-permute-start(bf16[32,2560]{1,0:T(8,128)(2,1)S(1)} %maximum_select_fusion.8), channel_id=1, source_target_pairs={{0,8},{1,9},{2,10},{3,11},{4,12},{5,13},{6,14},{7,15},{8,0},{9,1},... | collective-permute-start | bytes 491528 | tf_op jit(solution)/shard_map/ppermute | solution.py:62
  19.9 6.6 %collective-permute-start.7 = (bf16[48,2048]{1,0:T(8,128)(2,1)S(1)}, bf16[48,2048]{1,0:T(8,128)(2,1)S(1)}, u32[]{:S(2)}, u32[]{:S(2)}) collective-permute-start(bf16[48,2048]{1,0:T(8,128)(2,1)S(1)} %maximum_select_fusion.6), channel_id=1, source_target_pairs={{0,128},{16,144},{32,160},{48,176},{64,192},{80,208},{96,224},{112... | collective-permute-start | bytes 589832 | tf_op jit(solution)/shard_map/ppermute | solution.py:62
  27.1 5.5 %collective-permute-done.7 = bf16[48,2048]{1,0:T(8,128)(2,1)S(1)} collective-permute-done((bf16[48,2048]{1,0:T(8,128)(2,1)S(1)}, bf16[48,2048]{1,0:T(8,128)(2,1)S(1)}, u32[]{:S(2)}, u32[]{:S(2)}) %collective-permute-start.7) | collective-permute-done | bytes 196640 | tf_op jit(solution)/shard_map/ppermute | solution.py:62
  33.1 62.2 %while.22 = (s32[]{:T(128)}, f32[16,4096]{1,0:T(8,128)S(1)}, bf16[16,16,256]{2,1,0:T(8,128)(2,1)S(1)}, f32[]{:T(128)}, f32[4096]{0:T(1024)S(1)}, /*index=5*/f32[...) while((s32[]{:T(128)}, f32[16,4096]{1,0:T(8,128)S(1)}, ...), condition=%wide.region_4.5_spmd.clone, body=%wide.region_3.4_spmd.clone.sunk | while | flops 113377280 | bytes 832126 | solution.py:50
  33.1 3.8 %convolution_add_fusion.2 = f32[16,4096]{1,0:T(8,128)S(1)} fusion(bf16[32,4096]{1,0:T(8,128)(2,1)S(1)} %get-tuple-element.326, f32[256]{0:T(256)S(1)} %bitcast.92, f32[4096]{0:T(1024)S(1)} %get-tuple-element.323, f32[]{:T(128)} %get-tuple-element.322, f32[16,4096]{1,0:T(8,128)S(1)} %get-tuple-element.310, pred[]{:T(512)S(6)} %compare.6, ...), kind=kOutput, calls=%fused_computation.4.clone.1 | convolution fusion | flops 113377280 | bytes 829956 | tf_op jit(solution)/shard_map/while/body/eval_jaxpr/dot_general | solution.py:43
  37.0 3.8 %convolution_add_fusion.2 = f32[16,4096]{1,0:T(8,128)S(1)} fusion(bf16[32,4096]{1,0:T(8,128)(2,1)S(1)} %get-tuple-element.326, f32[256]{0:T(256)S(1)} %bitcast.92, f32[4096]{0:T(1024)S(1)} %get-tuple-element.323, f32[]{:T(128)} %get-tuple-element.322, f32[16,4096]{1,0:T(8,128)S(1)} %get-tuple-element.310, pred[]{:T(512)S(6)} %compare.6, ...), kind=kOutput, calls=%fused_computation.4.clone.1 | convolution fusion | flops 113377280 | bytes 829956 | tf_op jit(solution)/shard_map/while/body/eval_jaxpr/dot_general | solution.py:43
  40.9 3.8 %convolution_add_fusion.2 = f32[16,4096]{1,0:T(8,128)S(1)} fusion(bf16[32,4096]{1,0:T(8,128)(2,1)S(1)} %get-tuple-element.326, f32[256]{0:T(256)S(1)} %bitcast.92, f32[4096]{0:T(1024)S(1)} %get-tuple-element.323, f32[]{:T(128)} %get-tuple-element.322, f32[16,4096]{1,0:T(8,128)S(1)} %get-tuple-element.310, pred[]{:T(512)S(6)} %compare.6, ...), kind=kOutput, calls=%fused_computation.4.clone.1 | convolution fusion | flops 113377280 | bytes 829956 | tf_op jit(solution)/shard_map/while/body/eval_jaxpr/dot_general | solution.py:43
  44.8 3.8 %convolution_add_fusion.2 = f32[16,4096]{1,0:T(8,128)S(1)} fusion(bf16[32,4096]{1,0:T(8,128)(2,1)S(1)} %get-tuple-element.326, f32[256]{0:T(256)S(1)} %bitcast.92, f32[4096]{0:T(1024)S(1)} %get-tuple-element.323, f32[]{:T(128)} %get-tuple-element.322, f32[16,4096]{1,0:T(8,128)S(1)} %get-tuple-element.310, pred[]{:T(512)S(6)} %compare.6, ...), kind=kOutput, calls=%fused_computation.4.clone.1 | convolution fusion | flops 113377280 | bytes 829956 | tf_op jit(solution)/shard_map/while/body/eval_jaxpr/dot_general | solution.py:43
  48.6 3.8 %convolution_add_fusion.2 = f32[16,4096]{1,0:T(8,128)S(1)} fusion(bf16[32,4096]{1,0:T(8,128)(2,1)S(1)} %get-tuple-element.326, f32[256]{0:T(256)S(1)} %bitcast.92, f32[4096]{0:T(1024)S(1)} %get-tuple-element.323, f32[]{:T(128)} %get-tuple-element.322, f32[16,4096]{1,0:T(8,128)S(1)} %get-tuple-element.310, pred[]{:T(512)S(6)} %compare.6, ...), kind=kOutput, calls=%fused_computation.4.clone.1 | convolution fusion | flops 113377280 | bytes 829956 | tf_op jit(solution)/shard_map/while/body/eval_jaxpr/dot_general | solution.py:43
  52.5 3.8 %convolution_add_fusion.2 = f32[16,4096]{1,0:T(8,128)S(1)} fusion(bf16[32,4096]{1,0:T(8,128)(2,1)S(1)} %get-tuple-element.326, f32[256]{0:T(256)S(1)} %bitcast.92, f32[4096]{0:T(1024)S(1)} %get-tuple-element.323, f32[]{:T(128)} %get-tuple-element.322, f32[16,4096]{1,0:T(8,128)S(1)} %get-tuple-element.310, pred[]{:T(512)S(6)} %compare.6, ...), kind=kOutput, calls=%fused_computation.4.clone.1 | convolution fusion | flops 113377280 | bytes 829956 | tf_op jit(solution)/shard_map/while/body/eval_jaxpr/dot_general | solution.py:43
  56.4 3.8 %convolution_add_fusion.2 = f32[16,4096]{1,0:T(8,128)S(1)} fusion(bf16[32,4096]{1,0:T(8,128)(2,1)S(1)} %get-tuple-element.326, f32[256]{0:T(256)S(1)} %bitcast.92, f32[4096]{0:T(1024)S(1)} %get-tuple-element.323, f32[]{:T(128)} %get-tuple-element.322, f32[16,4096]{1,0:T(8,128)S(1)} %get-tuple-element.310, pred[]{:T(512)S(6)} %compare.6, ...), kind=kOutput, calls=%fused_computation.4.clone.1 | convolution fusion | flops 113377280 | bytes 829956 | tf_op jit(solution)/shard_map/while/body/eval_jaxpr/dot_general | solution.py:43
  60.3 3.8 %convolution_add_fusion.2 = f32[16,4096]{1,0:T(8,128)S(1)} fusion(bf16[32,4096]{1,0:T(8,128)(2,1)S(1)} %get-tuple-element.326, f32[256]{0:T(256)S(1)} %bitcast.92, f32[4096]{0:T(1024)S(1)} %get-tuple-element.323, f32[]{:T(128)} %get-tuple-element.322, f32[16,4096]{1,0:T(8,128)S(1)} %get-tuple-element.310, pred[]{:T(512)S(6)} %compare.6, ...), kind=kOutput, calls=%fused_computation.4.clone.1 | convolution fusion | flops 113377280 | bytes 829956 | tf_op jit(solution)/shard_map/while/body/eval_jaxpr/dot_general | solution.py:43
  64.2 3.8 %convolution_add_fusion.2 = f32[16,4096]{1,0:T(8,128)S(1)} fusion(bf16[32,4096]{1,0:T(8,128)(2,1)S(1)} %get-tuple-element.326, f32[256]{0:T(256)S(1)} %bitcast.92, f32[4096]{0:T(1024)S(1)} %get-tuple-element.323, f32[]{:T(128)} %get-tuple-element.322, f32[16,4096]{1,0:T(8,128)S(1)} %get-tuple-element.310, pred[]{:T(512)S(6)} %compare.6, ...), kind=kOutput, calls=%fused_computation.4.clone.1 | convolution fusion | flops 113377280 | bytes 829956 | tf_op jit(solution)/shard_map/while/body/eval_jaxpr/dot_general | solution.py:43
  68.1 3.8 %convolution_add_fusion.2 = f32[16,4096]{1,0:T(8,128)S(1)} fusion(bf16[32,4096]{1,0:T(8,128)(2,1)S(1)} %get-tuple-element.326, f32[256]{0:T(256)S(1)} %bitcast.92, f32[4096]{0:T(1024)S(1)} %get-tuple-element.323, f32[]{:T(128)} %get-tuple-element.322, f32[16,4096]{1,0:T(8,128)S(1)} %get-tuple-element.310, pred[]{:T(512)S(6)} %compare.6, ...), kind=kOutput, calls=%fused_computation.4.clone.1 | convolution fusion | flops 113377280 | bytes 829956 | tf_op jit(solution)/shard_map/while/body/eval_jaxpr/dot_general | solution.py:43
  72.0 3.8 %convolution_add_fusion.2 = f32[16,4096]{1,0:T(8,128)S(1)} fusion(bf16[32,4096]{1,0:T(8,128)(2,1)S(1)} %get-tuple-element.326, f32[256]{0:T(256)S(1)} %bitcast.92, f32[4096]{0:T(1024)S(1)} %get-tuple-element.323, f32[]{:T(128)} %get-tuple-element.322, f32[16,4096]{1,0:T(8,128)S(1)} %get-tuple-element.310, pred[]{:T(512)S(6)} %compare.6, ...), kind=kOutput, calls=%fused_computation.4.clone.1 | convolution fusion | flops 113377280 | bytes 829956 | tf_op jit(solution)/shard_map/while/body/eval_jaxpr/dot_general | solution.py:43
  75.8 3.8 %convolution_add_fusion.2 = f32[16,4096]{1,0:T(8,128)S(1)} fusion(bf16[32,4096]{1,0:T(8,128)(2,1)S(1)} %get-tuple-element.326, f32[256]{0:T(256)S(1)} %bitcast.92, f32[4096]{0:T(1024)S(1)} %get-tuple-element.323, f32[]{:T(128)} %get-tuple-element.322, f32[16,4096]{1,0:T(8,128)S(1)} %get-tuple-element.310, pred[]{:T(512)S(6)} %compare.6, ...), kind=kOutput, calls=%fused_computation.4.clone.1 | convolution fusion | flops 113377280 | bytes 829956 | tf_op jit(solution)/shard_map/while/body/eval_jaxpr/dot_general | solution.py:43
  79.7 3.8 %convolution_add_fusion.2 = f32[16,4096]{1,0:T(8,128)S(1)} fusion(bf16[32,4096]{1,0:T(8,128)(2,1)S(1)} %get-tuple-element.326, f32[256]{0:T(256)S(1)} %bitcast.92, f32[4096]{0:T(1024)S(1)} %get-tuple-element.323, f32[]{:T(128)} %get-tuple-element.322, f32[16,4096]{1,0:T(8,128)S(1)} %get-tuple-element.310, pred[]{:T(512)S(6)} %compare.6, ...), kind=kOutput, calls=%fused_computation.4.clone.1 | convolution fusion | flops 113377280 | bytes 829956 | tf_op jit(solution)/shard_map/while/body/eval_jaxpr/dot_general | solution.py:43
  83.6 3.8 %convolution_add_fusion.2 = f32[16,4096]{1,0:T(8,128)S(1)} fusion(bf16[32,4096]{1,0:T(8,128)(2,1)S(1)} %get-tuple-element.326, f32[256]{0:T(256)S(1)} %bitcast.92, f32[4096]{0:T(1024)S(1)} %get-tuple-element.323, f32[]{:T(128)} %get-tuple-element.322, f32[16,4096]{1,0:T(8,128)S(1)} %get-tuple-element.310, pred[]{:T(512)S(6)} %compare.6, ...), kind=kOutput, calls=%fused_computation.4.clone.1 | convolution fusion | flops 113377280 | bytes 829956 | tf_op jit(solution)/shard_map/while/body/eval_jaxpr/dot_general | solution.py:43
  87.5 3.8 %convolution_add_fusion.2 = f32[16,4096]{1,0:T(8,128)S(1)} fusion(bf16[32,4096]{1,0:T(8,128)(2,1)S(1)} %get-tuple-element.326, f32[256]{0:T(256)S(1)} %bitcast.92, f32[4096]{0:T(1024)S(1)} %get-tuple-element.323, f32[]{:T(128)} %get-tuple-element.322, f32[16,4096]{1,0:T(8,128)S(1)} %get-tuple-element.310, pred[]{:T(512)S(6)} %compare.6, ...), kind=kOutput, calls=%fused_computation.4.clone.1 | convolution fusion | flops 113377280 | bytes 829956 | tf_op jit(solution)/shard_map/while/body/eval_jaxpr/dot_general | solution.py:43
  91.4 3.8 %convolution_add_fusion.2 = f32[16,4096]{1,0:T(8,128)S(1)} fusion(bf16[32,4096]{1,0:T(8,128)(2,1)S(1)} %get-tuple-element.326, f32[256]{0:T(256)S(1)} %bitcast.92, f32[4096]{0:T(1024)S(1)} %get-tuple-element.323, f32[]{:T(128)} %get-tuple-element.322, f32[16,4096]{1,0:T(8,128)S(1)} %get-tuple-element.310, pred[]{:T(512)S(6)} %compare.6, ...), kind=kOutput, calls=%fused_computation.4.clone.1 | convolution fusion | flops 113377280 | bytes 829956 | tf_op jit(solution)/shard_map/while/body/eval_jaxpr/dot_general | solution.py:43
  99.2 2.8 %collective-permute-done.1 = f32[32,512]{1,0:T(8,128)S(1)} collective-permute-done((f32[32,512]{1,0:T(8,128)S(1)}, f32[32,512]{1,0:T(8,128)S(1)}, u32[]{:S(2)}, u32[]{:S(2)}) %collective-permute-start.1) | collective-permute-done | bytes 65568 | tf_op jit(solution)/shard_map/ppermute | solution.py:62
  101.9 2.4 %collective-permute-start.2 = (f32[32,1024]{1,0:T(8,128)S(1)}, f32[32,1024]{1,0:T(8,128)S(1)}, u32[]{:S(2)}, u32[]{:S(2)}) collective-permute-start(f32[32,1024]{1,0:T(8,128)S(1)} %maximum_select_fusion.9), channel_id=1, source_target_pairs={{0,4},{1,5},{2,6},{3,7},{4,0},{5,1},{6,2},{7,3},{8,12},{9,13},{10,... | collective-permute-start | bytes 393224 | tf_op jit(solution)/shard_map/ppermute | solution.py:62
  104.4 3.2 %collective-permute-done.13 = f32[16,4096]{1,0:T(8,128)S(1)} collective-permute-done((f32[16,4096]{1,0:T(8,128)S(1)}, f32[16,4096]{1,0:T(8,128)S(1)}, u32[]{:S(2)}, u32[]{:S(2)}) %collective-permute-start.13) | collective-permute-done | bytes 262176 | tf_op jit(solution)/shard_map/ppermute | solution.py:85
  107.6 2.3 %collective-permute-start.14 = (f32[16,4096]{1,0:T(8,128)S(1)}, f32[16,4096]{1,0:T(8,128)S(1)}, u32[]{:S(2)}, u32[]{:S(2)}) collective-permute-start(f32[16,4096]{1,0:T(8,128)S(1)} %add.126), channel_id=1, source_target_pairs={{0,4},{1,5},{2,6},{3,7},{4,0},{5,1},{6,2},{7,3},{8,12},{9,13},{10,... | collective-permute-start | bytes 786440 | tf_op jit(solution)/shard_map/ppermute | solution.py:85
  110.7 1.9 collective-permute-start.3
  113.2 3.0 %collective-permute-done.14 = f32[16,4096]{1,0:T(8,128)S(1)} collective-permute-done((f32[16,4096]{1,0:T(8,128)S(1)}, f32[16,4096]{1,0:T(8,128)S(1)}, u32[]{:S(2)}, u32[]{:S(2)}) %collective-permute-start.14) | collective-permute-done | bytes 262176 | tf_op jit(solution)/shard_map/ppermute | solution.py:85
  116.3 2.1 collective-permute-start.15
  118.4 3.0 %collective-permute-done.3 = f32[32,2048]{1,0:T(8,128)S(1)} collective-permute-done((f32[32,2048]{1,0:T(8,128)S(1)}, f32[32,2048]{1,0:T(8,128)S(1)}, u32[]{:S(2)}, u32[]{:S(2)}) %collective-permute-start.3) | collective-permute-done | bytes 262176 | tf_op jit(solution)/shard_map/ppermute | solution.py:62
  121.5 4.1 %collective-permute-done.15 = f32[16,4096]{1,0:T(8,128)S(1)} collective-permute-done((f32[16,4096]{1,0:T(8,128)S(1)}, f32[16,4096]{1,0:T(8,128)S(1)}, u32[]{:S(2)}, u32[]{:S(2)}) %collective-permute-start.15) | collective-permute-done | bytes 262176 | tf_op jit(solution)/shard_map/ppermute | solution.py:85
  126.5 2.9 %collective-permute-done.16 = f32[32]{0:T(128)S(1)} collective-permute-done((f32[32]{0:T(128)S(1)}, f32[32]{0:T(128)S(1)}, u32[]{:S(2)}, u32[]{:S(2)}) %collective-permute-start.16) | collective-permute-done | bytes 160 | tf_op jit(solution)/shard_map/ppermute | solution.py:85
  129.8 3.3 %collective-permute-done.17 = f32[32]{0:T(128)S(1)} collective-permute-done((f32[32]{0:T(128)S(1)}, f32[32]{0:T(128)S(1)}, u32[]{:S(2)}, u32[]{:S(2)}) %collective-permute-start.17) | collective-permute-done | bytes 160 | tf_op jit(solution)/shard_map/ppermute | solution.py:85
  133.1 3.0 %collective-permute-start.18 = (f32[32]{0:T(128)S(1)}, f32[32]{0:T(128)S(1)}, u32[]{:S(2)}, u32[]{:S(2)}) collective-permute-start(f32[32]{0:T(128)S(1)} %add.131), channel_id=1, source_target_pairs={{0,64},{16,80},{32,96},{48,112},{64,0},{80,16},{96,32},{112,48},{1... | collective-permute-start | bytes 392 | tf_op jit(solution)/shard_map/ppermute | solution.py:85
  136.1 1.5 collective-permute-done.18
  137.7 6.3 %collective-permute-start.19 = (f32[32]{0:T(128)S(1)}, f32[32]{0:T(128)S(1)}, u32[]{:S(2)}, u32[]{:S(2)}) collective-permute-start(f32[32]{0:T(128)S(1)} %add.132), channel_id=1, source_target_pairs={{0,128},{16,144},{32,160},{48,176},{64,192},{80,208},{96,224},{112... | collective-permute-start | bytes 392 | tf_op jit(solution)/shard_map/ppermute | solution.py:85
  144.0 1.5 collective-permute-done.19
  146.6 2.9 %collective-permute-done.20 = f32[16]{0:T(128)S(1)} collective-permute-done((f32[16]{0:T(128)S(1)}, f32[16]{0:T(128)S(1)}, u32[]{:S(2)}, u32[]{:S(2)}) %collective-permute-start.20) | collective-permute-done | bytes 96 | tf_op jit(solution)/shard_map/ppermute | solution.py:85
  149.5 1.2 collective-permute-start.21
  150.7 2.4 %collective-permute-done.21 = f32[16]{0:T(128)S(1)} collective-permute-done((f32[16]{0:T(128)S(1)}, f32[16]{0:T(128)S(1)}, u32[]{:S(2)}, u32[]{:S(2)}) %collective-permute-start.21) | collective-permute-done | bytes 96 | tf_op jit(solution)/shard_map/ppermute | solution.py:85
  153.1 2.6 %collective-permute-start.22 = (f32[16]{0:T(128)S(1)}, f32[16]{0:T(128)S(1)}, u32[]{:S(2)}, u32[]{:S(2)}) collective-permute-start(f32[16]{0:T(128)S(1)} %add.137), channel_id=1, source_target_pairs={{0,64},{16,80},{32,96},{48,112},{64,0},{80,16},{96,32},{112,48},{1... | collective-permute-start | bytes 200 | tf_op jit(solution)/shard_map/ppermute | solution.py:85
  155.6 1.9 collective-permute-done.22
  157.5 5.9 %collective-permute-start.23 = (f32[16]{0:T(128)S(1)}, f32[16]{0:T(128)S(1)}, u32[]{:S(2)}, u32[]{:S(2)}) collective-permute-start(f32[16]{0:T(128)S(1)} %add.138), channel_id=1, source_target_pairs={{0,128},{16,144},{32,160},{48,176},{64,192},{80,208},{96,224},{112... | collective-permute-start | bytes 200 | tf_op jit(solution)/shard_map/ppermute | solution.py:85
  163.5 1.5 collective-permute-done.23
  166.4 3.3 %collective-permute-done.24 = f32[32,256]{1,0:T(8,128)S(1)} collective-permute-done((f32[32,256]{1,0:T(8,128)S(1)}, f32[32,256]{1,0:T(8,128)S(1)}, u32[]{:S(2)}, u32[]{:S(2)}) %collective-permute-start.24) | collective-permute-done | bytes 32800 | tf_op jit(solution)/shard_map/ppermute | solution.py:62
  169.7 1.3 collective-permute-start.25
  170.9 3.7 %collective-permute-done.25 = f32[32,512]{1,0:T(8,128)S(1)} collective-permute-done((f32[32,512]{1,0:T(8,128)S(1)}, f32[32,512]{1,0:T(8,128)S(1)}, u32[]{:S(2)}, u32[]{:S(2)}) %collective-permute-start.25) | collective-permute-done | bytes 65568 | tf_op jit(solution)/shard_map/ppermute | solution.py:62
  174.7 3.4 %collective-permute-start.26 = (f32[32,1024]{1,0:T(8,128)S(1)}, f32[32,1024]{1,0:T(8,128)S(1)}, u32[]{:S(2)}, u32[]{:S(2)}) collective-permute-start(f32[32,1024]{1,0:T(8,128)S(1)} %maximum_select_fusion.10), channel_id=1, source_target_pairs={{0,64},{16,80},{32,96},{48,112},{64,0},{80,16},{96,32},{112,48},{1... | collective-permute-start | bytes 393224 | tf_op jit(solution)/shard_map/ppermute | solution.py:62
  178.1 4.9 %collective-permute-done.26 = f32[32,1024]{1,0:T(8,128)S(1)} collective-permute-done((f32[32,1024]{1,0:T(8,128)S(1)}, f32[32,1024]{1,0:T(8,128)S(1)}, u32[]{:S(2)}, u32[]{:S(2)}) %collective-permute-start.26) | collective-permute-done | bytes 131104 | tf_op jit(solution)/shard_map/ppermute | solution.py:62
  183.0 4.0 %collective-permute-start.27 = (f32[32,2048]{1,0:T(8,128)S(1)}, f32[32,2048]{1,0:T(8,128)S(1)}, u32[]{:S(2)}, u32[]{:S(2)}) collective-permute-start(f32[32,2048]{1,0:T(8,128)S(1)} %maximum_select_fusion.5), channel_id=1, source_target_pairs={{0,128},{16,144},{32,160},{48,176},{64,192},{80,208},{96,224},{112... | collective-permute-start | bytes 786440 | tf_op jit(solution)/shard_map/ppermute | solution.py:62
  187.6 6.1 %collective-permute-done.27 = f32[32,2048]{1,0:T(8,128)S(1)} collective-permute-done((f32[32,2048]{1,0:T(8,128)S(1)}, f32[32,2048]{1,0:T(8,128)S(1)}, u32[]{:S(2)}, u32[]{:S(2)}) %collective-permute-start.27) | collective-permute-done | bytes 262176 | tf_op jit(solution)/shard_map/ppermute | solution.py:62
  193.9 15.5 %while.23 = (s32[]{:T(128)}, f32[16,1024]{1,0:T(8,128)S(1)}, bf16[4,16,1024]{2,1,0:T(8,128)(2,1)S(1)}, f32[]{:T(128)}, f32[1024]{0:T(1024)S(1)}, /*index=5*/f32[...) while((s32[]{:T(128)}, f32[16,1024]{1,0:T(8,128)S(1)}, ...), condition=%wide.region_9.10_spmd.clone, body=%wide.region_8.9_spmd.clone.sunk | while | flops 113278976 | bytes 312958 | solution.py:50
  193.9 3.8 %fusion.53 = f32[16,1024]{1,0:T(8,128)S(1)} fusion(bf16[32,1024]{1,0:T(8,128)(2,1)S(1)} %get-tuple-element.356, f32[1024]{0:T(1024)S(1)} %bitcast.90, f32[1024]{0:T(1024)S(1)} %get-tuple-element.353, f32[]{:T(128)} %get-tuple-element.352, f32[16,1024]{1,0:T(8,128)S(1)} %get-tuple-element.340, bf16[4,32,1024]{2,1,0:T(8,128)(2,1)S(1)} %get-tuple-element.355, ...), kind=kOutput, calls=%fused_computation.22.clone.1 | convolution fusion | flops 113278976 | bytes 304644 | tf_op jit(solution)/shard_map/while/body/eval_jaxpr/dot_general | solution.py:43
  197.8 3.8 %fusion.53 = f32[16,1024]{1,0:T(8,128)S(1)} fusion(bf16[32,1024]{1,0:T(8,128)(2,1)S(1)} %get-tuple-element.356, f32[1024]{0:T(1024)S(1)} %bitcast.90, f32[1024]{0:T(1024)S(1)} %get-tuple-element.353, f32[]{:T(128)} %get-tuple-element.352, f32[16,1024]{1,0:T(8,128)S(1)} %get-tuple-element.340, bf16[4,32,1024]{2,1,0:T(8,128)(2,1)S(1)} %get-tuple-element.355, ...), kind=kOutput, calls=%fused_computation.22.clone.1 | convolution fusion | flops 113278976 | bytes 304644 | tf_op jit(solution)/shard_map/while/body/eval_jaxpr/dot_general | solution.py:43
  201.7 3.8 %fusion.53 = f32[16,1024]{1,0:T(8,128)S(1)} fusion(bf16[32,1024]{1,0:T(8,128)(2,1)S(1)} %get-tuple-element.356, f32[1024]{0:T(1024)S(1)} %bitcast.90, f32[1024]{0:T(1024)S(1)} %get-tuple-element.353, f32[]{:T(128)} %get-tuple-element.352, f32[16,1024]{1,0:T(8,128)S(1)} %get-tuple-element.340, bf16[4,32,1024]{2,1,0:T(8,128)(2,1)S(1)} %get-tuple-element.355, ...), kind=kOutput, calls=%fused_computation.22.clone.1 | convolution fusion | flops 113278976 | bytes 304644 | tf_op jit(solution)/shard_map/while/body/eval_jaxpr/dot_general | solution.py:43
  205.5 3.8 %fusion.53 = f32[16,1024]{1,0:T(8,128)S(1)} fusion(bf16[32,1024]{1,0:T(8,128)(2,1)S(1)} %get-tuple-element.356, f32[1024]{0:T(1024)S(1)} %bitcast.90, f32[1024]{0:T(1024)S(1)} %get-tuple-element.353, f32[]{:T(128)} %get-tuple-element.352, f32[16,1024]{1,0:T(8,128)S(1)} %get-tuple-element.340, bf16[4,32,1024]{2,1,0:T(8,128)(2,1)S(1)} %get-tuple-element.355, ...), kind=kOutput, calls=%fused_computation.22.clone.1 | convolution fusion | flops 113278976 | bytes 304644 | tf_op jit(solution)/shard_map/while/body/eval_jaxpr/dot_general | solution.py:43
  210.4 4.5 %collective-permute-done.28 = f32[16,512]{1,0:T(8,128)S(1)} collective-permute-done((f32[16,512]{1,0:T(8,128)S(1)}, f32[16,512]{1,0:T(8,128)S(1)}, u32[]{:S(2)}, u32[]{:S(2)}) %collective-permute-start.28) | collective-permute-done | bytes 32800 | tf_op jit(solution)/shard_map/ppermute | solution.py:79
  214.9 1.6 collective-permute-start.29
  216.5 3.7 %collective-permute-done.29 = f32[16,256]{1,0:T(8,128)S(1)} collective-permute-done((f32[16,256]{1,0:T(8,128)S(1)}, f32[16,256]{1,0:T(8,128)S(1)}, u32[]{:S(2)}, u32[]{:S(2)}) %collective-permute-start.29) | collective-permute-done | bytes 16416 | tf_op jit(solution)/shard_map/ppermute | solution.py:79
  220.2 1.3 collective-permute-start.30
  221.6 2.4 %collective-permute-done.30 = f32[16,128]{1,0:T(8,128)S(1)} collective-permute-done((f32[16,128]{1,0:T(8,128)S(1)}, f32[16,128]{1,0:T(8,128)S(1)}, u32[]{:S(2)}, u32[]{:S(2)}) %collective-permute-start.30) | collective-permute-done | bytes 8224 | tf_op jit(solution)/shard_map/ppermute | solution.py:79
  (126 shorter events, 19.1 us)
Async XLA Ops:
  2.3 3.2 %collective-permute-start.8 = (bf16[32,320]{1,0:T(8,128)(2,1)S(1)}, bf16[32,320]{1,0:T(8,128)(2,1)S(1)}, u32[]{:S(2)}, u32[]{:S(2)}) collective-permute-start(bf16[32,320]{1,0:T(8,128)(2,1)S(1)} %pad_maximum_fusion.1), channel_id=1, source_target_pairs={{0,1},{1,0},{2,3},{3,2},{4,5},{5,4},{6,7},{7,6},{8,9},{9,8},{10,11... | collective-permute-start | bytes 61448 | tf_op jit(solution)/shard_map/ppermute | solution.py:62
  3.9 3.8 %collective-permute-start.4 = (bf16[48,256]{1,0:T(8,128)(2,1)S(1)}, bf16[48,256]{1,0:T(8,128)(2,1)S(1)}, u32[]{:S(2)}, u32[]{:S(2)}) collective-permute-start(bf16[48,256]{1,0:T(8,128)(2,1)S(1)} %pad_maximum_fusion), channel_id=1, source_target_pairs={{0,16},{16,0},{32,48},{48,32},{64,80},{80,64},{96,112},{112,96},{1... | collective-permute-start | bytes 73736 | tf_op jit(solution)/shard_map/ppermute | solution.py:62
  5.7 4.1 %collective-permute-start.9 = (bf16[32,640]{1,0:T(8,128)(2,1)S(1)}, bf16[32,640]{1,0:T(8,128)(2,1)S(1)}, u32[]{:S(2)}, u32[]{:S(2)}) collective-permute-start(bf16[32,640]{1,0:T(8,128)(2,1)S(1)} %maximum_select_fusion.17), channel_id=1, source_target_pairs={{0,2},{1,3},{2,0},{3,1},{4,6},{5,7},{6,4},{7,5},{8,10},{9,11},{10,... | collective-permute-start | bytes 122888 | tf_op jit(solution)/shard_map/ppermute | solution.py:62
  7.8 4.6 %collective-permute-start.5 = (bf16[48,512]{1,0:T(8,128)(2,1)S(1)}, bf16[48,512]{1,0:T(8,128)(2,1)S(1)}, u32[]{:S(2)}, u32[]{:S(2)}) collective-permute-start(bf16[48,512]{1,0:T(8,128)(2,1)S(1)} %maximum_select_fusion.16), channel_id=1, source_target_pairs={{0,32},{16,48},{32,0},{48,16},{64,96},{80,112},{96,64},{112,80},{1... | collective-permute-start | bytes 147464 | tf_op jit(solution)/shard_map/ppermute | solution.py:62
  9.8 6.0 %collective-permute-start.10 = (bf16[32,1280]{1,0:T(8,128)(2,1)S(1)}, bf16[32,1280]{1,0:T(8,128)(2,1)S(1)}, u32[]{:S(2)}, u32[]{:S(2)}) collective-permute-start(bf16[32,1280]{1,0:T(8,128)(2,1)S(1)} %maximum_select_fusion.13), channel_id=1, source_target_pairs={{0,4},{1,5},{2,6},{3,7},{4,0},{5,1},{6,2},{7,3},{8,12},{9,13},{10,... | collective-permute-start | bytes 245768 | tf_op jit(solution)/shard_map/ppermute | solution.py:62
  12.4 7.5 %collective-permute-start.6 = (bf16[48,1024]{1,0:T(8,128)(2,1)S(1)}, bf16[48,1024]{1,0:T(8,128)(2,1)S(1)}, u32[]{:S(2)}, u32[]{:S(2)}) collective-permute-start(bf16[48,1024]{1,0:T(8,128)(2,1)S(1)} %maximum_select_fusion.11), channel_id=1, source_target_pairs={{0,64},{16,80},{32,96},{48,112},{64,0},{80,16},{96,32},{112,48},{1... | collective-permute-start | bytes 294920 | tf_op jit(solution)/shard_map/ppermute | solution.py:62
  15.9 10.7 %collective-permute-start.11 = (bf16[32,2560]{1,0:T(8,128)(2,1)S(1)}, bf16[32,2560]{1,0:T(8,128)(2,1)S(1)}, u32[]{:S(2)}, u32[]{:S(2)}) collective-permute-start(bf16[32,2560]{1,0:T(8,128)(2,1)S(1)} %maximum_select_fusion.8), channel_id=1, source_target_pairs={{0,8},{1,9},{2,10},{3,11},{4,12},{5,13},{6,14},{7,15},{8,0},{9,1},... | collective-permute-start | bytes 491528 | tf_op jit(solution)/shard_map/ppermute | solution.py:62
  19.9 12.7 %collective-permute-start.7 = (bf16[48,2048]{1,0:T(8,128)(2,1)S(1)}, bf16[48,2048]{1,0:T(8,128)(2,1)S(1)}, u32[]{:S(2)}, u32[]{:S(2)}) collective-permute-start(bf16[48,2048]{1,0:T(8,128)(2,1)S(1)} %maximum_select_fusion.6), channel_id=1, source_target_pairs={{0,128},{16,144},{32,160},{48,176},{64,192},{80,208},{96,224},{112... | collective-permute-start | bytes 589832 | tf_op jit(solution)/shard_map/ppermute | solution.py:62
  95.2 2.8 %collective-permute-start.12 = (f32[16,4096]{1,0:T(8,128)S(1)}, f32[16,4096]{1,0:T(8,128)S(1)}, u32[]{:S(2)}, u32[]{:S(2)}) collective-permute-start(f32[16,4096]{1,0:T(8,128)S(1)} %get-tuple-element.88), channel_id=1, source_target_pairs={{0,1},{1,0},{2,3},{3,2},{4,5},{5,4},{6,7},{7,6},{8,9},{9,8},{10,11... | collective-permute-start | bytes 786440 | tf_op jit(solution)/shard_map/ppermute | solution.py:85
  95.3 1.6 collective-permute-start
  96.9 5.0 %collective-permute-start.1 = (f32[32,512]{1,0:T(8,128)S(1)}, f32[32,512]{1,0:T(8,128)S(1)}, u32[]{:S(2)}, u32[]{:S(2)}) collective-permute-start(f32[32,512]{1,0:T(8,128)S(1)} %maximum_select_fusion.14), channel_id=1, source_target_pairs={{0,2},{1,3},{2,0},{3,1},{4,6},{5,7},{6,4},{7,5},{8,10},{9,11},{10,... | collective-permute-start | bytes 196616 | tf_op jit(solution)/shard_map/ppermute | solution.py:62
  98.1 9.5 %collective-permute-start.13 = (f32[16,4096]{1,0:T(8,128)S(1)}, f32[16,4096]{1,0:T(8,128)S(1)}, u32[]{:S(2)}, u32[]{:S(2)}) collective-permute-start(f32[16,4096]{1,0:T(8,128)S(1)} %add.125), channel_id=1, source_target_pairs={{0,2},{1,3},{2,0},{3,1},{4,6},{5,7},{6,4},{7,5},{8,10},{9,11},{10,... | collective-permute-start | bytes 786440 | tf_op jit(solution)/shard_map/ppermute | solution.py:85
  101.9 8.8 %collective-permute-start.2 = (f32[32,1024]{1,0:T(8,128)S(1)}, f32[32,1024]{1,0:T(8,128)S(1)}, u32[]{:S(2)}, u32[]{:S(2)}) collective-permute-start(f32[32,1024]{1,0:T(8,128)S(1)} %maximum_select_fusion.9), channel_id=1, source_target_pairs={{0,4},{1,5},{2,6},{3,7},{4,0},{5,1},{6,2},{7,3},{8,12},{9,13},{10,... | collective-permute-start | bytes 393224 | tf_op jit(solution)/shard_map/ppermute | solution.py:62
  107.6 8.7 %collective-permute-start.14 = (f32[16,4096]{1,0:T(8,128)S(1)}, f32[16,4096]{1,0:T(8,128)S(1)}, u32[]{:S(2)}, u32[]{:S(2)}) collective-permute-start(f32[16,4096]{1,0:T(8,128)S(1)} %add.126), channel_id=1, source_target_pairs={{0,4},{1,5},{2,6},{3,7},{4,0},{5,1},{6,2},{7,3},{8,12},{9,13},{10,... | collective-permute-start | bytes 786440 | tf_op jit(solution)/shard_map/ppermute | solution.py:85
  110.7 10.7 %collective-permute-start.3 = (f32[32,2048]{1,0:T(8,128)S(1)}, f32[32,2048]{1,0:T(8,128)S(1)}, u32[]{:S(2)}, u32[]{:S(2)}) collective-permute-start(f32[32,2048]{1,0:T(8,128)S(1)} %maximum_select_fusion.4), channel_id=1, source_target_pairs={{0,8},{1,9},{2,10},{3,11},{4,12},{5,13},{6,14},{7,15},{8,0},{9,1},... | collective-permute-start | bytes 786440 | tf_op jit(solution)/shard_map/ppermute | solution.py:62
  116.3 9.3 %collective-permute-start.15 = (f32[16,4096]{1,0:T(8,128)S(1)}, f32[16,4096]{1,0:T(8,128)S(1)}, u32[]{:S(2)}, u32[]{:S(2)}) collective-permute-start(f32[16,4096]{1,0:T(8,128)S(1)} %add.127), channel_id=1, source_target_pairs={{0,8},{1,9},{2,10},{3,11},{4,12},{5,13},{6,14},{7,15},{8,0},{9,1},... | collective-permute-start | bytes 786440 | tf_op jit(solution)/shard_map/ppermute | solution.py:85
  125.8 39.2 %copy-start = (f32[16,256]{1,0:T(8,128)S(1)}, f32[16,256]{1,0:T(8,128)}, u32[]{:S(2)}) copy-start(f32[16,256]{1,0:T(8,128)} %param.21) | copy-start | bytes 49156
  125.8 39.2 %copy-start.1 = (f32[16,256]{1,0:T(8,128)S(1)}, f32[16,256]{1,0:T(8,128)}, u32[]{:S(2)}) copy-start(f32[16,256]{1,0:T(8,128)} %param.20) | copy-start | bytes 49156
  125.8 39.2 %copy-start.2 = (f32[16,256]{1,0:T(8,128)S(1)}, f32[16,256]{1,0:T(8,128)}, u32[]{:S(2)}) copy-start(f32[16,256]{1,0:T(8,128)} %param.19) | copy-start | bytes 49156
  125.9 3.6 %collective-permute-start.16 = (f32[32]{0:T(128)S(1)}, f32[32]{0:T(128)S(1)}, u32[]{:S(2)}, u32[]{:S(2)}) collective-permute-start(f32[32]{0:T(128)S(1)} %pad_maximum_fusion.2), channel_id=1, source_target_pairs={{0,16},{16,0},{32,48},{48,32},{64,80},{80,64},{96,112},{112,96},{1... | collective-permute-start | bytes 392 | tf_op jit(solution)/shard_map/ppermute | solution.py:85
  129.5 3.6 %collective-permute-start.17 = (f32[32]{0:T(128)S(1)}, f32[32]{0:T(128)S(1)}, u32[]{:S(2)}, u32[]{:S(2)}) collective-permute-start(f32[32]{0:T(128)S(1)} %fusion.39), channel_id=1, source_target_pairs={{0,32},{16,48},{32,0},{48,16},{64,96},{80,112},{96,64},{112,80},{1... | collective-permute-start | bytes 392 | tf_op jit(solution)/shard_map/ppermute | solution.py:85
  133.1 4.5 %collective-permute-start.18 = (f32[32]{0:T(128)S(1)}, f32[32]{0:T(128)S(1)}, u32[]{:S(2)}, u32[]{:S(2)}) collective-permute-start(f32[32]{0:T(128)S(1)} %add.131), channel_id=1, source_target_pairs={{0,64},{16,80},{32,96},{48,112},{64,0},{80,16},{96,32},{112,48},{1... | collective-permute-start | bytes 392 | tf_op jit(solution)/shard_map/ppermute | solution.py:85
  137.7 7.8 %collective-permute-start.19 = (f32[32]{0:T(128)S(1)}, f32[32]{0:T(128)S(1)}, u32[]{:S(2)}, u32[]{:S(2)}) collective-permute-start(f32[32]{0:T(128)S(1)} %add.132), channel_id=1, source_target_pairs={{0,128},{16,144},{32,160},{48,176},{64,192},{80,208},{96,224},{112... | collective-permute-start | bytes 392 | tf_op jit(solution)/shard_map/ppermute | solution.py:85
  145.8 3.7 %collective-permute-start.20 = (f32[16]{0:T(128)S(1)}, f32[16]{0:T(128)S(1)}, u32[]{:S(2)}, u32[]{:S(2)}) collective-permute-start(f32[16]{0:T(128)S(1)} %multiply_reduce_fusion.3), channel_id=1, source_target_pairs={{0,16},{16,0},{32,48},{48,32},{64,80},{80,64},{96,112},{112,96},{1... | collective-permute-start | bytes 200 | tf_op jit(solution)/shard_map/ppermute | solution.py:85
  149.5 3.6 %collective-permute-start.21 = (f32[16]{0:T(128)S(1)}, f32[16]{0:T(128)S(1)}, u32[]{:S(2)}, u32[]{:S(2)}) collective-permute-start(f32[16]{0:T(128)S(1)} %add.136), channel_id=1, source_target_pairs={{0,32},{16,48},{32,0},{48,16},{64,96},{80,112},{96,64},{112,80},{1... | collective-permute-start | bytes 200 | tf_op jit(solution)/shard_map/ppermute | solution.py:85
  153.1 4.5 %collective-permute-start.22 = (f32[16]{0:T(128)S(1)}, f32[16]{0:T(128)S(1)}, u32[]{:S(2)}, u32[]{:S(2)}) collective-permute-start(f32[16]{0:T(128)S(1)} %add.137), channel_id=1, source_target_pairs={{0,64},{16,80},{32,96},{48,112},{64,0},{80,16},{96,32},{112,48},{1... | collective-permute-start | bytes 200 | tf_op jit(solution)/shard_map/ppermute | solution.py:85
  157.5 7.5 %collective-permute-start.23 = (f32[16]{0:T(128)S(1)}, f32[16]{0:T(128)S(1)}, u32[]{:S(2)}, u32[]{:S(2)}) collective-permute-start(f32[16]{0:T(128)S(1)} %add.138), channel_id=1, source_target_pairs={{0,128},{16,144},{32,160},{48,176},{64,192},{80,208},{96,224},{112... | collective-permute-start | bytes 200 | tf_op jit(solution)/shard_map/ppermute | solution.py:85
  165.7 3.9 %collective-permute-start.24 = (f32[32,256]{1,0:T(8,128)S(1)}, f32[32,256]{1,0:T(8,128)S(1)}, u32[]{:S(2)}, u32[]{:S(2)}) collective-permute-start(f32[32,256]{1,0:T(8,128)S(1)} %constant_dynamic-update-slice_fusion.2), channel_id=1, source_target_pairs={{0,16},{16,0},{32,48},{48,32},{64,80},{80,64},{96,112},{112,96},{1... | collective-permute-start | bytes 98312 | tf_op jit(solution)/shard_map/ppermute | solution.py:62
  169.7 5.0 %collective-permute-start.25 = (f32[32,512]{1,0:T(8,128)S(1)}, f32[32,512]{1,0:T(8,128)S(1)}, u32[]{:S(2)}, u32[]{:S(2)}) collective-permute-start(f32[32,512]{1,0:T(8,128)S(1)} %maximum_select_fusion.15), channel_id=1, source_target_pairs={{0,32},{16,48},{32,0},{48,16},{64,96},{80,112},{96,64},{112,80},{1... | collective-permute-start | bytes 196616 | tf_op jit(solution)/shard_map/ppermute | solution.py:62
  174.7 8.3 %collective-permute-start.26 = (f32[32,1024]{1,0:T(8,128)S(1)}, f32[32,1024]{1,0:T(8,128)S(1)}, u32[]{:S(2)}, u32[]{:S(2)}) collective-permute-start(f32[32,1024]{1,0:T(8,128)S(1)} %maximum_select_fusion.10), channel_id=1, source_target_pairs={{0,64},{16,80},{32,96},{48,112},{64,0},{80,16},{96,32},{112,48},{1... | collective-permute-start | bytes 393224 | tf_op jit(solution)/shard_map/ppermute | solution.py:62
  183.0 10.7 %collective-permute-start.27 = (f32[32,2048]{1,0:T(8,128)S(1)}, f32[32,2048]{1,0:T(8,128)S(1)}, u32[]{:S(2)}, u32[]{:S(2)}) collective-permute-start(f32[32,2048]{1,0:T(8,128)S(1)} %maximum_select_fusion.5), channel_id=1, source_target_pairs={{0,128},{16,144},{32,160},{48,176},{64,192},{80,208},{96,224},{112... | collective-permute-start | bytes 786440 | tf_op jit(solution)/shard_map/ppermute | solution.py:62
  193.9 31.4 %copy-start.3 = (f32[64]{0:T(128)S(1)}, f32[64]{0:T(128)}, u32[]{:S(2)}) copy-start(f32[64]{0:T(128)} %param.18) | copy-start | bytes 772
  209.4 5.5 %collective-permute-start.28 = (f32[16,512]{1,0:T(8,128)S(1)}, f32[16,512]{1,0:T(8,128)S(1)}, u32[]{:S(2)}, u32[]{:S(2)}) collective-permute-start(f32[16,512]{1,0:T(8,128)S(1)} %slice_select_fusion), channel_id=1, source_target_pairs={{0,8},{1,9},{2,10},{3,11},{4,12},{5,13},{6,14},{7,15},{8,0},{9,1},... | collective-permute-start | bytes 98312 | tf_op jit(solution)/shard_map/ppermute | solution.py:79
  214.9 5.3 %collective-permute-start.29 = (f32[16,256]{1,0:T(8,128)S(1)}, f32[16,256]{1,0:T(8,128)S(1)}, u32[]{:S(2)}, u32[]{:S(2)}) collective-permute-start(f32[16,256]{1,0:T(8,128)S(1)} %slice_select_fusion.1), channel_id=1, source_target_pairs={{0,4},{1,5},{2,6},{3,7},{4,0},{5,1},{6,2},{7,3},{8,12},{9,13},{10,... | collective-permute-start | bytes 49160 | tf_op jit(solution)/shard_map/ppermute | solution.py:79
  220.2 3.7 %collective-permute-start.30 = (f32[16,128]{1,0:T(8,128)S(1)}, f32[16,128]{1,0:T(8,128)S(1)}, u32[]{:S(2)}, u32[]{:S(2)}) collective-permute-start(f32[16,128]{1,0:T(8,128)S(1)} %slice_select_fusion.3), channel_id=1, source_target_pairs={{0,2},{1,3},{2,0},{3,1},{4,6},{5,7},{6,4},{7,5},{8,10},{9,11},{10,... | collective-permute-start | bytes 24584 | tf_op jit(solution)/shard_map/ppermute | solution.py:79
  224.1 1.2 collective-permute-start.31

commit v2 on v1

--- a/solution.py
+++ b/solution.py
@@ -4,6 +4,7 @@
 import jax.numpy as jnp
 from jax import lax
 from jax.sharding import PartitionSpec as P
+
 
 root_five = math.sqrt(5.0)
 contract_first = (((0,), (0,)), ((), ()))
@@ -47,8 +48,13 @@
         )
 
     start = jnp.zeros((vectors.shape[0], row_pts.shape[1]), jnp.float32)
-    result, ignored = lax.scan(one_block, start, (pts_blocks, sq_blocks, vec_blocks))
+    result, _ = lax.scan(one_block, start, (pts_blocks, sq_blocks, vec_blocks))
     return result
+
+
+def tied(x, dep):
+    x, dep = lax.optimization_barrier((x, dep))
+    return x
 
 
 def xor_perm(size, bit):
@@ -126,30 +132,47 @@
     partial_rows = kernel_apply(
         row_pts, row_sq, col_pts, col_sq, col_dir, signal_scalar, 256
     )
+    cand_blocks = []
+    width = col_pts.shape[1] // 2
+    for k in range(2):
+        lo, hi = k * width, (k + 1) * width
+        cand_blocks.append(
+            lax.optimization_barrier(
+                matern_block(
+                    row_cands, cand_sq, col_pts[:, lo:hi], col_sq[lo:hi],
+                    signal_scalar,
+                )
+            )
+        )
     kernel_row = all_sum(partial_rows, "col", n_col)
     image_row = kernel_row + noise_var[0] * dir_row
-    sums = all_sum(
-        jnp.concatenate(
-            [jnp.sum(res_row * res_row, axis=1), jnp.sum(dir_row * image_row, axis=1)]
-        ),
-        "row",
-        n_row,
-    )
+    local_sums = jnp.concatenate(
+        [jnp.sum(res_row * res_row, axis=1), jnp.sum(dir_row * image_row, axis=1)]
+    )
+    sums = all_sum(tied(local_sums, w_col), "row", n_row)
     norm_now, curvature = sums[:cols], sums[cols:]
     step_len = norm_now / curvature
     residual_new_row = res_row - step_len[:, None] * image_row
-    norm_next = all_sum(jnp.sum(residual_new_row * residual_new_row, axis=1), "row", n_row)
 
     me_col = lax.axis_index("col")
     image_vec = lax.dynamic_slice_in_dim(image_row, me_col * own, own, axis=1)
     weights_new = weights + step_len[:, None] * direction
     residual_new = residual - step_len[:, None] * image_vec
+
+    w_low_col = (w_col + step_len[:, None] * d_col).astype(jnp.bfloat16)
+    partial_fit = None
+    for k in range(2):
+        lo, hi = k * width, (k + 1) * width
+        part = lax.dot_general(
+            w_low_col[:, lo:hi], cand_blocks[k], contract_last,
+            preferred_element_type=jnp.float32,
+        )
+        partial_fit = part if partial_fit is None else partial_fit + part
+    norm_next = all_sum(
+        tied(jnp.sum(residual_new_row * residual_new_row, axis=1), partial_fit),
+        "row", n_row,
+    )
     direction_new = residual_new + (norm_next / norm_now)[:, None] * direction
-
-    w_low_col = (w_col + step_len[:, None] * d_col).astype(jnp.bfloat16)
-    partial_fit = kernel_apply(
-        row_cands, cand_sq, col_pts, col_sq, w_low_col, signal_scalar, 1024
-    )
     fitted = reduce_scatter_last(partial_fit, "col", n_col)
     cand_fit = cand_prior[None, :] + fitted
     return (weights_new, residual_new, direction_new, cand_fit)

time: 229 us -> 193 us (0.84)
  waiting for transfers between devices: 73 us -> 39 us
    ppermute x16, waiting for transfers between devices: 32.9 us -> 8.41 us  [gather_last(): recv = lax.ppermute(buf, axis_name, xor_perm(size, bit))]
    dot_general x20 -> x16, matrix products: 76.8 us -> 61.5 us  [one_block(): lax.dot_general(vec_blk, kern_vals, contract_last, preferred_element_type...]
    dot_general x0 -> x4, matrix products: none -> 14.6 us  [the longest x2 12.2 us: matern_block(): lax.dot_general(row_pts, col_pts, contract_first, preferred_element_type=...]
    ppermute x4, waiting for transfers between devices: 11.7 us -> 2.65 us  [reduce_scatter_last(): buf = keep + lax.ppermute(send, axis_name, xor_perm(size, bit))]
    ppermute x12, starting transfers between devices: 26.2 us -> 19.6 us  [all_sum(): x = x + lax.ppermute(x, axis_name, xor_perm(size, bit))]
    ppermute x4, starting transfers between devices: 4.03 us -> 8.05 us  [reduce_scatter_last(): buf = keep + lax.ppermute(send, axis_name, xor_perm(size, bit))]
  transfers between devices with their start and end apart: 32 -> 32, of which waited for: 27 -> 17; matrix products, arithmetic and copies ran while one was open for 2% -> 42% of each run, Pallas kernels for 0% -> 0%
where the time goes in v2:
time: 193 us; the launch traced here: 190 us
  matrix products  76.1 us (39%)
  starting transfers between devices  64.1 us (33%)
  waiting for transfers between devices  39 us (20%)
  other arithmetic  5.85 us (3%)
  between operations  2.37 us (1%)
  local copies, waits for them, and re-layouts  2.04 us (1%)
    dot_general x16, matrix products, one_block(): lax.dot_general(vec_blk, kern_vals, contract_last, preferred_element_type...  61.5 us
    ppermute x16, starting transfers between devices, gather_last(): recv = lax.ppermute(buf, axis_name, xor_perm(size, bit))  36.4 us
    ppermute x12, waiting for transfers between devices, all_sum(): x = x + lax.ppermute(x, axis_name, xor_perm(size, bit))  27.9 us
    ppermute x12, starting transfers between devices, all_sum(): x = x + lax.ppermute(x, axis_name, xor_perm(size, bit))  19.6 us
    dot_general x2, matrix products, matern_block(): lax.dot_general(row_pts, col_pts, contract_first, preferred_element_type=...  12.2 us
    ppermute x16, waiting for transfers between devices, gather_last(): recv = lax.ppermute(buf, axis_name, xor_perm(size, bit))  8.41 us
    ppermute x4, starting transfers between devices, reduce_scatter_last(): buf = keep + lax.ppermute(send, axis_name, xor_perm(size, bit))  8.05 us
  transfers between devices with their start and end apart: 32, of which 17 were waited for; matrix products, arithmetic and copies ran while one was open for 42% of the time, Pallas kernels for 0%

profile of v2, /device:TPU:2, one launch (start us, length us, event | category | flops | bytes accessed | tf_op | source)
XLA Modules:
  0.0 190.0 jit_solution(3087008192456654151)
XLA Ops:
  0.6 0.7 constant_dynamic-update-slice_fusion.1
  1.4 0.8 constant_dynamic-update-slice_fusion.2
  2.2 1.6 collective-permute-start.16
  3.7 0.8 divide_convert_fusion
  4.6 0.8 divide_convert_fusion.1
  5.4 0.6 collective-permute-start.8
  6.9 1.9 %collective-permute-start.9 = (bf16[32,640]{1,0:T(8,128)(2,1)S(1)}, bf16[32,640]{1,0:T(8,128)(2,1)S(1)}, u32[]{:S(2)}, u32[]{:S(2)}) collective-permute-start(bf16[32,640]{1,0:T(8,128)(2,1)S(1)} %maximum_select_fusion.17), channel_id=1, source_target_pairs={{0,2},{1,3},{2,0},{3,1},{4,6},{5,7},{6,4},{7,5},{8,10},{9,11},{10,... | collective-permute-start | bytes 122888 | tf_op jit(solution)/shard_map/ppermute | solution.py:68
  9.0 0.8 collective-permute-done.4
  9.8 2.0 %collective-permute-start.5 = (bf16[48,512]{1,0:T(8,128)(2,1)S(1)}, bf16[48,512]{1,0:T(8,128)(2,1)S(1)}, u32[]{:S(2)}, u32[]{:S(2)}) collective-permute-start(bf16[48,512]{1,0:T(8,128)(2,1)S(1)} %maximum_select_fusion.16), channel_id=1, source_target_pairs={{0,32},{16,48},{32,0},{48,16},{64,96},{80,112},{96,64},{112,80},{1... | collective-permute-start | bytes 147464 | tf_op jit(solution)/shard_map/ppermute | solution.py:68
  12.1 2.2 %collective-permute-start.10 = (bf16[32,1280]{1,0:T(8,128)(2,1)S(1)}, bf16[32,1280]{1,0:T(8,128)(2,1)S(1)}, u32[]{:S(2)}, u32[]{:S(2)}) collective-permute-start(bf16[32,1280]{1,0:T(8,128)(2,1)S(1)} %maximum_select_fusion.13), channel_id=1, source_target_pairs={{0,4},{1,5},{2,6},{3,7},{4,0},{5,1},{6,2},{7,3},{8,12},{9,13},{10,... | collective-permute-start | bytes 245768 | tf_op jit(solution)/shard_map/ppermute | solution.py:68
  14.7 3.4 %collective-permute-start.6 = (bf16[48,1024]{1,0:T(8,128)(2,1)S(1)}, bf16[48,1024]{1,0:T(8,128)(2,1)S(1)}, u32[]{:S(2)}, u32[]{:S(2)}) collective-permute-start(bf16[48,1024]{1,0:T(8,128)(2,1)S(1)} %maximum_select_fusion.11), channel_id=1, source_target_pairs={{0,64},{16,80},{32,96},{48,112},{64,0},{80,16},{96,32},{112,48},{1... | collective-permute-start | bytes 294920 | tf_op jit(solution)/shard_map/ppermute | solution.py:68
  18.2 3.0 %collective-permute-start.11 = (bf16[32,2560]{1,0:T(8,128)(2,1)S(1)}, bf16[32,2560]{1,0:T(8,128)(2,1)S(1)}, u32[]{:S(2)}, u32[]{:S(2)}) collective-permute-start(bf16[32,2560]{1,0:T(8,128)(2,1)S(1)} %maximum_select_fusion.8), channel_id=1, source_target_pairs={{0,8},{1,9},{2,10},{3,11},{4,12},{5,13},{6,14},{7,15},{8,0},{9,1},... | collective-permute-start | bytes 491528 | tf_op jit(solution)/shard_map/ppermute | solution.py:68
  22.1 6.7 %collective-permute-start.7 = (bf16[48,2048]{1,0:T(8,128)(2,1)S(1)}, bf16[48,2048]{1,0:T(8,128)(2,1)S(1)}, u32[]{:S(2)}, u32[]{:S(2)}) collective-permute-start(bf16[48,2048]{1,0:T(8,128)(2,1)S(1)} %maximum_select_fusion.6), channel_id=1, source_target_pairs={{0,128},{16,144},{32,160},{48,176},{64,192},{80,208},{96,224},{112... | collective-permute-start | bytes 589832 | tf_op jit(solution)/shard_map/ppermute | solution.py:68
  29.4 5.1 %collective-permute-done.7 = bf16[48,2048]{1,0:T(8,128)(2,1)S(1)} collective-permute-done((bf16[48,2048]{1,0:T(8,128)(2,1)S(1)}, bf16[48,2048]{1,0:T(8,128)(2,1)S(1)}, u32[]{:S(2)}, u32[]{:S(2)}) %collective-permute-start.7) | collective-permute-done | bytes 196640 | tf_op jit(solution)/shard_map/ppermute | solution.py:68
  35.0 62.2 %while.11 = (s32[]{:T(128)}, f32[16,4096]{1,0:T(8,128)S(1)}, bf16[16,16,256]{2,1,0:T(8,128)(2,1)S(1)}, f32[]{:T(128)}, f32[4096]{0:T(1024)S(1)}, /*index=5*/f32[...) while((s32[]{:T(128)}, f32[16,4096]{1,0:T(8,128)S(1)}, ...), condition=%wide.region_4.5_spmd.clone, body=%wide.region_3.4_spmd.clone.sunk | while | flops 113377280 | bytes 832126 | solution.py:51
  35.0 3.8 %convolution_add_fusion.3 = f32[16,4096]{1,0:T(8,128)S(1)} fusion(bf16[32,4096]{1,0:T(8,128)(2,1)S(1)} %get-tuple-element.193, f32[256]{0:T(256)S(1)} %bitcast.57, f32[4096]{0:T(1024)S(1)} %get-tuple-element.190, f32[]{:T(128)} %get-tuple-element.189, f32[16,4096]{1,0:T(8,128)S(1)} %get-tuple-element.177, pred[]{:T(512)S(6)} %compare.3, ...), kind=kOutput, calls=%fused_computation.4.clone.1 | convolution fusion | flops 113377280 | bytes 829956 | tf_op jit(solution)/shard_map/while/body/eval_jaxpr/dot_general | solution.py:44
  38.9 3.8 %convolution_add_fusion.3 = f32[16,4096]{1,0:T(8,128)S(1)} fusion(bf16[32,4096]{1,0:T(8,128)(2,1)S(1)} %get-tuple-element.193, f32[256]{0:T(256)S(1)} %bitcast.57, f32[4096]{0:T(1024)S(1)} %get-tuple-element.190, f32[]{:T(128)} %get-tuple-element.189, f32[16,4096]{1,0:T(8,128)S(1)} %get-tuple-element.177, pred[]{:T(512)S(6)} %compare.3, ...), kind=kOutput, calls=%fused_computation.4.clone.1 | convolution fusion | flops 113377280 | bytes 829956 | tf_op jit(solution)/shard_map/while/body/eval_jaxpr/dot_general | solution.py:44
  42.8 3.8 %convolution_add_fusion.3 = f32[16,4096]{1,0:T(8,128)S(1)} fusion(bf16[32,4096]{1,0:T(8,128)(2,1)S(1)} %get-tuple-element.193, f32[256]{0:T(256)S(1)} %bitcast.57, f32[4096]{0:T(1024)S(1)} %get-tuple-element.190, f32[]{:T(128)} %get-tuple-element.189, f32[16,4096]{1,0:T(8,128)S(1)} %get-tuple-element.177, pred[]{:T(512)S(6)} %compare.3, ...), kind=kOutput, calls=%fused_computation.4.clone.1 | convolution fusion | flops 113377280 | bytes 829956 | tf_op jit(solution)/shard_map/while/body/eval_jaxpr/dot_general | solution.py:44
  46.7 3.8 %convolution_add_fusion.3 = f32[16,4096]{1,0:T(8,128)S(1)} fusion(bf16[32,4096]{1,0:T(8,128)(2,1)S(1)} %get-tuple-element.193, f32[256]{0:T(256)S(1)} %bitcast.57, f32[4096]{0:T(1024)S(1)} %get-tuple-element.190, f32[]{:T(128)} %get-tuple-element.189, f32[16,4096]{1,0:T(8,128)S(1)} %get-tuple-element.177, pred[]{:T(512)S(6)} %compare.3, ...), kind=kOutput, calls=%fused_computation.4.clone.1 | convolution fusion | flops 113377280 | bytes 829956 | tf_op jit(solution)/shard_map/while/body/eval_jaxpr/dot_general | solution.py:44
  50.5 3.8 %convolution_add_fusion.3 = f32[16,4096]{1,0:T(8,128)S(1)} fusion(bf16[32,4096]{1,0:T(8,128)(2,1)S(1)} %get-tuple-element.193, f32[256]{0:T(256)S(1)} %bitcast.57, f32[4096]{0:T(1024)S(1)} %get-tuple-element.190, f32[]{:T(128)} %get-tuple-element.189, f32[16,4096]{1,0:T(8,128)S(1)} %get-tuple-element.177, pred[]{:T(512)S(6)} %compare.3, ...), kind=kOutput, calls=%fused_computation.4.clone.1 | convolution fusion | flops 113377280 | bytes 829956 | tf_op jit(solution)/shard_map/while/body/eval_jaxpr/dot_general | solution.py:44
  54.4 3.8 %convolution_add_fusion.3 = f32[16,4096]{1,0:T(8,128)S(1)} fusion(bf16[32,4096]{1,0:T(8,128)(2,1)S(1)} %get-tuple-element.193, f32[256]{0:T(256)S(1)} %bitcast.57, f32[4096]{0:T(1024)S(1)} %get-tuple-element.190, f32[]{:T(128)} %get-tuple-element.189, f32[16,4096]{1,0:T(8,128)S(1)} %get-tuple-element.177, pred[]{:T(512)S(6)} %compare.3, ...), kind=kOutput, calls=%fused_computation.4.clone.1 | convolution fusion | flops 113377280 | bytes 829956 | tf_op jit(solution)/shard_map/while/body/eval_jaxpr/dot_general | solution.py:44
  58.3 3.8 %convolution_add_fusion.3 = f32[16,4096]{1,0:T(8,128)S(1)} fusion(bf16[32,4096]{1,0:T(8,128)(2,1)S(1)} %get-tuple-element.193, f32[256]{0:T(256)S(1)} %bitcast.57, f32[4096]{0:T(1024)S(1)} %get-tuple-element.190, f32[]{:T(128)} %get-tuple-element.189, f32[16,4096]{1,0:T(8,128)S(1)} %get-tuple-element.177, pred[]{:T(512)S(6)} %compare.3, ...), kind=kOutput, calls=%fused_computation.4.clone.1 | convolution fusion | flops 113377280 | bytes 829956 | tf_op jit(solution)/shard_map/while/body/eval_jaxpr/dot_general | solution.py:44
  62.2 3.8 %convolution_add_fusion.3 = f32[16,4096]{1,0:T(8,128)S(1)} fusion(bf16[32,4096]{1,0:T(8,128)(2,1)S(1)} %get-tuple-element.193, f32[256]{0:T(256)S(1)} %bitcast.57, f32[4096]{0:T(1024)S(1)} %get-tuple-element.190, f32[]{:T(128)} %get-tuple-element.189, f32[16,4096]{1,0:T(8,128)S(1)} %get-tuple-element.177, pred[]{:T(512)S(6)} %compare.3, ...), kind=kOutput, calls=%fused_computation.4.clone.1 | convolution fusion | flops 113377280 | bytes 829956 | tf_op jit(solution)/shard_map/while/body/eval_jaxpr/dot_general | solution.py:44
  66.1 3.8 %convolution_add_fusion.3 = f32[16,4096]{1,0:T(8,128)S(1)} fusion(bf16[32,4096]{1,0:T(8,128)(2,1)S(1)} %get-tuple-element.193, f32[256]{0:T(256)S(1)} %bitcast.57, f32[4096]{0:T(1024)S(1)} %get-tuple-element.190, f32[]{:T(128)} %get-tuple-element.189, f32[16,4096]{1,0:T(8,128)S(1)} %get-tuple-element.177, pred[]{:T(512)S(6)} %compare.3, ...), kind=kOutput, calls=%fused_computation.4.clone.1 | convolution fusion | flops 113377280 | bytes 829956 | tf_op jit(solution)/shard_map/while/body/eval_jaxpr/dot_general | solution.py:44
  70.0 3.8 %convolution_add_fusion.3 = f32[16,4096]{1,0:T(8,128)S(1)} fusion(bf16[32,4096]{1,0:T(8,128)(2,1)S(1)} %get-tuple-element.193, f32[256]{0:T(256)S(1)} %bitcast.57, f32[4096]{0:T(1024)S(1)} %get-tuple-element.190, f32[]{:T(128)} %get-tuple-element.189, f32[16,4096]{1,0:T(8,128)S(1)} %get-tuple-element.177, pred[]{:T(512)S(6)} %compare.3, ...), kind=kOutput, calls=%fused_computation.4.clone.1 | convolution fusion | flops 113377280 | bytes 829956 | tf_op jit(solution)/shard_map/while/body/eval_jaxpr/dot_general | solution.py:44
  73.9 3.8 %convolution_add_fusion.3 = f32[16,4096]{1,0:T(8,128)S(1)} fusion(bf16[32,4096]{1,0:T(8,128)(2,1)S(1)} %get-tuple-element.193, f32[256]{0:T(256)S(1)} %bitcast.57, f32[4096]{0:T(1024)S(1)} %get-tuple-element.190, f32[]{:T(128)} %get-tuple-element.189, f32[16,4096]{1,0:T(8,128)S(1)} %get-tuple-element.177, pred[]{:T(512)S(6)} %compare.3, ...), kind=kOutput, calls=%fused_computation.4.clone.1 | convolution fusion | flops 113377280 | bytes 829956 | tf_op jit(solution)/shard_map/while/body/eval_jaxpr/dot_general | solution.py:44
  77.8 3.8 %convolution_add_fusion.3 = f32[16,4096]{1,0:T(8,128)S(1)} fusion(bf16[32,4096]{1,0:T(8,128)(2,1)S(1)} %get-tuple-element.193, f32[256]{0:T(256)S(1)} %bitcast.57, f32[4096]{0:T(1024)S(1)} %get-tuple-element.190, f32[]{:T(128)} %get-tuple-element.189, f32[16,4096]{1,0:T(8,128)S(1)} %get-tuple-element.177, pred[]{:T(512)S(6)} %compare.3, ...), kind=kOutput, calls=%fused_computation.4.clone.1 | convolution fusion | flops 113377280 | bytes 829956 | tf_op jit(solution)/shard_map/while/body/eval_jaxpr/dot_general | solution.py:44
  81.6 3.8 %convolution_add_fusion.3 = f32[16,4096]{1,0:T(8,128)S(1)} fusion(bf16[32,4096]{1,0:T(8,128)(2,1)S(1)} %get-tuple-element.193, f32[256]{0:T(256)S(1)} %bitcast.57, f32[4096]{0:T(1024)S(1)} %get-tuple-element.190, f32[]{:T(128)} %get-tuple-element.189, f32[16,4096]{1,0:T(8,128)S(1)} %get-tuple-element.177, pred[]{:T(512)S(6)} %compare.3, ...), kind=kOutput, calls=%fused_computation.4.clone.1 | convolution fusion | flops 113377280 | bytes 829956 | tf_op jit(solution)/shard_map/while/body/eval_jaxpr/dot_general | solution.py:44
  85.5 3.8 %convolution_add_fusion.3 = f32[16,4096]{1,0:T(8,128)S(1)} fusion(bf16[32,4096]{1,0:T(8,128)(2,1)S(1)} %get-tuple-element.193, f32[256]{0:T(256)S(1)} %bitcast.57, f32[4096]{0:T(1024)S(1)} %get-tuple-element.190, f32[]{:T(128)} %get-tuple-element.189, f32[16,4096]{1,0:T(8,128)S(1)} %get-tuple-element.177, pred[]{:T(512)S(6)} %compare.3, ...), kind=kOutput, calls=%fused_computation.4.clone.1 | convolution fusion | flops 113377280 | bytes 829956 | tf_op jit(solution)/shard_map/while/body/eval_jaxpr/dot_general | solution.py:44
  89.4 3.8 %convolution_add_fusion.3 = f32[16,4096]{1,0:T(8,128)S(1)} fusion(bf16[32,4096]{1,0:T(8,128)(2,1)S(1)} %get-tuple-element.193, f32[256]{0:T(256)S(1)} %bitcast.57, f32[4096]{0:T(1024)S(1)} %get-tuple-element.190, f32[]{:T(128)} %get-tuple-element.189, f32[16,4096]{1,0:T(8,128)S(1)} %get-tuple-element.177, pred[]{:T(512)S(6)} %compare.3, ...), kind=kOutput, calls=%fused_computation.4.clone.1 | convolution fusion | flops 113377280 | bytes 829956 | tf_op jit(solution)/shard_map/while/body/eval_jaxpr/dot_general | solution.py:44
  93.3 3.8 %convolution_add_fusion.3 = f32[16,4096]{1,0:T(8,128)S(1)} fusion(bf16[32,4096]{1,0:T(8,128)(2,1)S(1)} %get-tuple-element.193, f32[256]{0:T(256)S(1)} %bitcast.57, f32[4096]{0:T(1024)S(1)} %get-tuple-element.190, f32[]{:T(128)} %get-tuple-element.189, f32[16,4096]{1,0:T(8,128)S(1)} %get-tuple-element.177, pred[]{:T(512)S(6)} %compare.3, ...), kind=kOutput, calls=%fused_computation.4.clone.1 | convolution fusion | flops 113377280 | bytes 829956 | tf_op jit(solution)/shard_map/while/body/eval_jaxpr/dot_general | solution.py:44
  97.3 1.1 collective-permute-start.1
  98.4 2.9 %collective-permute-start.18 = (f32[32,1024]{1,0:T(8,128)S(1)}, f32[32,1024]{1,0:T(8,128)S(1)}, u32[]{:S(2)}, u32[]{:S(2)}) collective-permute-start(f32[32,1024]{1,0:T(8,128)S(1)} %maximum_select_fusion.10), channel_id=1, source_target_pairs={{0,64},{16,80},{32,96},{48,112},{64,0},{80,16},{96,32},{112,48},{1... | collective-permute-start | bytes 393224 | tf_op jit(solution)/shard_map/ppermute | solution.py:68
  102.6 2.1 %collective-permute-start.2 = (f32[32,1024]{1,0:T(8,128)S(1)}, f32[32,1024]{1,0:T(8,128)S(1)}, u32[]{:S(2)}, u32[]{:S(2)}) collective-permute-start(f32[32,1024]{1,0:T(8,128)S(1)} %maximum_select_fusion.9), channel_id=1, source_target_pairs={{0,4},{1,5},{2,6},{3,7},{4,0},{5,1},{6,2},{7,3},{8,12},{9,13},{10,... | collective-permute-start | bytes 393224 | tf_op jit(solution)/shard_map/ppermute | solution.py:68
  104.7 1.9 collective-permute-start.13
  106.6 1.3 collective-permute-done.18
  108.0 5.7 %collective-permute-start.19 = (f32[32,2048]{1,0:T(8,128)S(1)}, f32[32,2048]{1,0:T(8,128)S(1)}, u32[]{:S(2)}, u32[]{:S(2)}) collective-permute-start(f32[32,2048]{1,0:T(8,128)S(1)} %maximum_select_fusion.5), channel_id=1, source_target_pairs={{0,128},{16,144},{32,160},{48,176},{64,192},{80,208},{96,224},{112... | collective-permute-start | bytes 786440 | tf_op jit(solution)/shard_map/ppermute | solution.py:68
  113.8 2.6 %collective-permute-start.3 = (f32[32,2048]{1,0:T(8,128)S(1)}, f32[32,2048]{1,0:T(8,128)S(1)}, u32[]{:S(2)}, u32[]{:S(2)}) collective-permute-start(f32[32,2048]{1,0:T(8,128)S(1)} %maximum_select_fusion.4), channel_id=1, source_target_pairs={{0,8},{1,9},{2,10},{3,11},{4,12},{5,13},{6,14},{7,15},{8,0},{9,1},... | collective-permute-start | bytes 786440 | tf_op jit(solution)/shard_map/ppermute | solution.py:68
  116.4 1.0 collective-permute-start.14
  117.7 7.6 %collective-permute-done.14 = f32[16,4096]{1,0:T(8,128)S(1)} collective-permute-done((f32[16,4096]{1,0:T(8,128)S(1)}, f32[16,4096]{1,0:T(8,128)S(1)}, u32[]{:S(2)}, u32[]{:S(2)}) %collective-permute-start.14) | collective-permute-done | bytes 262176 | tf_op jit(solution)/shard_map/ppermute | solution.py:91
  125.3 1.6 collective-permute-start.15
  126.9 6.4 %collective-permute-done.15 = f32[16,4096]{1,0:T(8,128)S(1)} collective-permute-done((f32[16,4096]{1,0:T(8,128)S(1)}, f32[16,4096]{1,0:T(8,128)S(1)}, u32[]{:S(2)}, u32[]{:S(2)}) %collective-permute-start.15) | collective-permute-done | bytes 262176 | tf_op jit(solution)/shard_map/ppermute | solution.py:91
  133.8 6.1 %multiply_convert_fusion.2 = bf16[1024,2048]{1,0:T(8,128)(2,1)S(1)} fusion(bf16[32,1024]{1,0:T(8,128)(2,1)S(1)} %reshape.55, f32[2048]{0:T(1024)S(1)} %get-tuple-element.109, f32[1024]{0:T(1024)S(1)} %add.151, f32[]{:T(128)} %bitcast.47, bf16[48,4096]{1,0:T(8,128)(2,1)S(1)} %maximum_select_fusion.2), kind=kOutput, calls=%fused_computation.19 | convolution fusion | flops 159383552 | bytes 4403204 | tf_op jit(solution)/shard_map/dot_general | solution.py:19
  140.0 6.1 %multiply_convert_fusion.1 = bf16[1024,2048]{1,0:T(8,128)(2,1)S(1)} fusion(bf16[32,1024]{1,0:T(8,128)(2,1)S(1)} %reshape.55, f32[2048]{0:T(1024)S(1)} %get-tuple-element.108, f32[1024]{0:T(1024)S(1)} %add.151, f32[]{:T(128)} %bitcast.48, bf16[48,4096]{1,0:T(8,128)(2,1)S(1)} %maximum_select_fusion.2), kind=kOutput, calls=%fused_computation.18 | convolution fusion | flops 159383552 | bytes 4403204 | tf_op jit(solution)/shard_map/dot_general | solution.py:19
  146.1 2.8 %collective-permute-start.22 = (f32[32]{0:T(128)S(1)}, f32[32]{0:T(128)S(1)}, u32[]{:S(2)}, u32[]{:S(2)}) collective-permute-start(f32[32]{0:T(128)S(1)} %add.145), channel_id=1, source_target_pairs={{0,64},{16,80},{32,96},{48,112},{64,0},{80,16},{96,32},{112,48},{1... | collective-permute-start | bytes 392 | tf_op jit(solution)/shard_map/ppermute | solution.py:91
  149.0 1.9 %collective-permute-done.22 = f32[32]{0:T(128)S(1)} collective-permute-done((f32[32]{0:T(128)S(1)}, f32[32]{0:T(128)S(1)}, u32[]{:S(2)}, u32[]{:S(2)}) %collective-permute-start.22) | collective-permute-done | bytes 160 | tf_op jit(solution)/shard_map/ppermute | solution.py:91
  150.9 4.4 %collective-permute-start.23 = (f32[32]{0:T(128)S(1)}, f32[32]{0:T(128)S(1)}, u32[]{:S(2)}, u32[]{:S(2)}) collective-permute-start(f32[32]{0:T(128)S(1)} %add.146), channel_id=1, source_target_pairs={{0,128},{16,144},{32,160},{48,176},{64,192},{80,208},{96,224},{112... | collective-permute-start | bytes 392 | tf_op jit(solution)/shard_map/ppermute | solution.py:91
  155.4 3.0 %collective-permute-done.23 = f32[32]{0:T(128)S(1)} collective-permute-done((f32[32]{0:T(128)S(1)}, f32[32]{0:T(128)S(1)}, u32[]{:S(2)}, u32[]{:S(2)}) %collective-permute-start.23) | collective-permute-done | bytes 160 | tf_op jit(solution)/shard_map/ppermute | solution.py:91
  158.7 1.2 fusion.22
  159.9 1.2 convolution_add_fusion.1
  161.1 3.6 %collective-permute-start.28 = (f32[16,512]{1,0:T(8,128)S(1)}, f32[16,512]{1,0:T(8,128)S(1)}, u32[]{:S(2)}, u32[]{:S(2)}) collective-permute-start(f32[16,512]{1,0:T(8,128)S(1)} %slice_select_fusion), channel_id=1, source_target_pairs={{0,8},{1,9},{2,10},{3,11},{4,12},{5,13},{6,14},{7,15},{8,0},{9,1},... | collective-permute-start | bytes 98312 | tf_op jit(solution)/shard_map/ppermute | solution.py:85
  164.7 1.9 %collective-permute-done.28 = f32[16,512]{1,0:T(8,128)S(1)} collective-permute-done((f32[16,512]{1,0:T(8,128)S(1)}, f32[16,512]{1,0:T(8,128)S(1)}, u32[]{:S(2)}, u32[]{:S(2)}) %collective-permute-start.28) | collective-permute-done | bytes 32800 | tf_op jit(solution)/shard_map/ppermute | solution.py:85
  166.7 2.0 %collective-permute-start.29 = (f32[16,256]{1,0:T(8,128)S(1)}, f32[16,256]{1,0:T(8,128)S(1)}, u32[]{:S(2)}, u32[]{:S(2)}) collective-permute-start(f32[16,256]{1,0:T(8,128)S(1)} %slice_select_fusion.1), channel_id=1, source_target_pairs={{0,4},{1,5},{2,6},{3,7},{4,0},{5,1},{6,2},{7,3},{8,12},{9,13},{10,... | collective-permute-start | bytes 49160 | tf_op jit(solution)/shard_map/ppermute | solution.py:85
  168.6 1.6 collective-permute-start.24
  170.2 2.0 %collective-permute-done.24 = f32[16]{0:T(128)S(1)} collective-permute-done((f32[16]{0:T(128)S(1)}, f32[16]{0:T(128)S(1)}, u32[]{:S(2)}, u32[]{:S(2)}) %collective-permute-start.24) | collective-permute-done | bytes 96 | tf_op jit(solution)/shard_map/ppermute | solution.py:91
  172.2 1.0 collective-permute-start.25
  173.2 2.6 %collective-permute-done.25 = f32[16]{0:T(128)S(1)} collective-permute-done((f32[16]{0:T(128)S(1)}, f32[16]{0:T(128)S(1)}, u32[]{:S(2)}, u32[]{:S(2)}) %collective-permute-start.25) | collective-permute-done | bytes 96 | tf_op jit(solution)/shard_map/ppermute | solution.py:91
  175.8 1.4 collective-permute-start.26
  177.2 3.1 %collective-permute-done.26 = f32[16]{0:T(128)S(1)} collective-permute-done((f32[16]{0:T(128)S(1)}, f32[16]{0:T(128)S(1)}, u32[]{:S(2)}, u32[]{:S(2)}) %collective-permute-start.26) | collective-permute-done | bytes 96 | tf_op jit(solution)/shard_map/ppermute | solution.py:91
  180.2 3.6 %collective-permute-start.27 = (f32[16]{0:T(128)S(1)}, f32[16]{0:T(128)S(1)}, u32[]{:S(2)}, u32[]{:S(2)}) collective-permute-start(f32[16]{0:T(128)S(1)} %add.164), channel_id=1, source_target_pairs={{0,128},{16,144},{32,160},{48,176},{64,192},{80,208},{96,224},{112... | collective-permute-start | bytes 200 | tf_op jit(solution)/shard_map/ppermute | solution.py:91
  183.9 2.5 %collective-permute-start.30 = (f32[16,128]{1,0:T(8,128)S(1)}, f32[16,128]{1,0:T(8,128)S(1)}, u32[]{:S(2)}, u32[]{:S(2)}) collective-permute-start(f32[16,128]{1,0:T(8,128)S(1)} %slice_select_fusion.3), channel_id=1, source_target_pairs={{0,2},{1,3},{2,0},{3,1},{4,6},{5,7},{6,4},{7,5},{8,10},{9,11},{10,... | collective-permute-start | bytes 24584 | tf_op jit(solution)/shard_map/ppermute | solution.py:85
  186.4 1.3 collective-permute-done.27
  188.2 0.7 multiply_add_fusion.1
  189.3 0.7 add_add_fusion
  (115 shorter events, 6.2 us)
Async XLA Ops:
  2.2 9.7 %collective-permute-start.16 = (f32[32,256]{1,0:T(8,128)S(1)}, f32[32,256]{1,0:T(8,128)S(1)}, u32[]{:S(2)}, u32[]{:S(2)}) collective-permute-start(f32[32,256]{1,0:T(8,128)S(1)} %get-tuple-element.110), channel_id=1, source_target_pairs={{0,16},{16,0},{32,48},{48,32},{64,80},{80,64},{96,112},{112,96},{1... | collective-permute-start | bytes 98312 | tf_op jit(solution)/shard_map/ppermute | solution.py:68
  3.7 93.5 %collective-permute-start = (f32[32,256]{1,0:T(8,128)S(1)}, f32[32,256]{1,0:T(8,128)S(1)}, u32[]{:S(2)}, u32[]{:S(2)}) collective-permute-start(f32[32,256]{1,0:T(8,128)S(1)} %get-tuple-element.112), channel_id=1, source_target_pairs={{0,1},{1,0},{2,3},{3,2},{4,5},{5,4},{6,7},{7,6},{8,9},{9,8},{10,11... | collective-permute-start | bytes 98312 | tf_op jit(solution)/shard_map/ppermute | solution.py:68
  5.4 1.4 collective-permute-start.8
  6.0 3.8 %collective-permute-start.4 = (bf16[48,256]{1,0:T(8,128)(2,1)S(1)}, bf16[48,256]{1,0:T(8,128)(2,1)S(1)}, u32[]{:S(2)}, u32[]{:S(2)}) collective-permute-start(bf16[48,256]{1,0:T(8,128)(2,1)S(1)} %pad_maximum_fusion), channel_id=1, source_target_pairs={{0,16},{16,0},{32,48},{48,32},{64,80},{80,64},{96,112},{112,96},{1... | collective-permute-start | bytes 73736 | tf_op jit(solution)/shard_map/ppermute | solution.py:68
  6.9 5.1 %collective-permute-start.9 = (bf16[32,640]{1,0:T(8,128)(2,1)S(1)}, bf16[32,640]{1,0:T(8,128)(2,1)S(1)}, u32[]{:S(2)}, u32[]{:S(2)}) collective-permute-start(bf16[32,640]{1,0:T(8,128)(2,1)S(1)} %maximum_select_fusion.17), channel_id=1, source_target_pairs={{0,2},{1,3},{2,0},{3,1},{4,6},{5,7},{6,4},{7,5},{8,10},{9,11},{10,... | collective-permute-start | bytes 122888 | tf_op jit(solution)/shard_map/ppermute | solution.py:68
  9.8 4.8 %collective-permute-start.5 = (bf16[48,512]{1,0:T(8,128)(2,1)S(1)}, bf16[48,512]{1,0:T(8,128)(2,1)S(1)}, u32[]{:S(2)}, u32[]{:S(2)}) collective-permute-start(bf16[48,512]{1,0:T(8,128)(2,1)S(1)} %maximum_select_fusion.16), channel_id=1, source_target_pairs={{0,32},{16,48},{32,0},{48,16},{64,96},{80,112},{96,64},{112,80},{1... | collective-permute-start | bytes 147464 | tf_op jit(solution)/shard_map/ppermute | solution.py:68
  11.9 86.5 %collective-permute-start.17 = (f32[32,512]{1,0:T(8,128)S(1)}, f32[32,512]{1,0:T(8,128)S(1)}, u32[]{:S(2)}, u32[]{:S(2)}) collective-permute-start(f32[32,512]{1,0:T(8,128)S(1)} %maximum_select_fusion.15), channel_id=1, source_target_pairs={{0,32},{16,48},{32,0},{48,16},{64,96},{80,112},{96,64},{112,80},{1... | collective-permute-start | bytes 196616 | tf_op jit(solution)/shard_map/ppermute | solution.py:68
  12.1 6.0 %collective-permute-start.10 = (bf16[32,1280]{1,0:T(8,128)(2,1)S(1)}, bf16[32,1280]{1,0:T(8,128)(2,1)S(1)}, u32[]{:S(2)}, u32[]{:S(2)}) collective-permute-start(bf16[32,1280]{1,0:T(8,128)(2,1)S(1)} %maximum_select_fusion.13), channel_id=1, source_target_pairs={{0,4},{1,5},{2,6},{3,7},{4,0},{5,1},{6,2},{7,3},{8,12},{9,13},{10,... | collective-permute-start | bytes 245768 | tf_op jit(solution)/shard_map/ppermute | solution.py:68
  14.7 7.4 %collective-permute-start.6 = (bf16[48,1024]{1,0:T(8,128)(2,1)S(1)}, bf16[48,1024]{1,0:T(8,128)(2,1)S(1)}, u32[]{:S(2)}, u32[]{:S(2)}) collective-permute-start(bf16[48,1024]{1,0:T(8,128)(2,1)S(1)} %maximum_select_fusion.11), channel_id=1, source_target_pairs={{0,64},{16,80},{32,96},{48,112},{64,0},{80,16},{96,32},{112,48},{1... | collective-permute-start | bytes 294920 | tf_op jit(solution)/shard_map/ppermute | solution.py:68
  18.2 10.7 %collective-permute-start.11 = (bf16[32,2560]{1,0:T(8,128)(2,1)S(1)}, bf16[32,2560]{1,0:T(8,128)(2,1)S(1)}, u32[]{:S(2)}, u32[]{:S(2)}) collective-permute-start(bf16[32,2560]{1,0:T(8,128)(2,1)S(1)} %maximum_select_fusion.8), channel_id=1, source_target_pairs={{0,8},{1,9},{2,10},{3,11},{4,12},{5,13},{6,14},{7,15},{8,0},{9,1},... | collective-permute-start | bytes 491528 | tf_op jit(solution)/shard_map/ppermute | solution.py:68
  22.1 12.4 %collective-permute-start.7 = (bf16[48,2048]{1,0:T(8,128)(2,1)S(1)}, bf16[48,2048]{1,0:T(8,128)(2,1)S(1)}, u32[]{:S(2)}, u32[]{:S(2)}) collective-permute-start(bf16[48,2048]{1,0:T(8,128)(2,1)S(1)} %maximum_select_fusion.6), channel_id=1, source_target_pairs={{0,128},{16,144},{32,160},{48,176},{64,192},{80,208},{96,224},{112... | collective-permute-start | bytes 589832 | tf_op jit(solution)/shard_map/ppermute | solution.py:68
  97.2 7.5 %collective-permute-start.12 = (f32[16,4096]{1,0:T(8,128)S(1)}, f32[16,4096]{1,0:T(8,128)S(1)}, u32[]{:S(2)}, u32[]{:S(2)}) collective-permute-start(f32[16,4096]{1,0:T(8,128)S(1)} %get-tuple-element.48), channel_id=1, source_target_pairs={{0,1},{1,0},{2,3},{3,2},{4,5},{5,4},{6,7},{7,6},{8,9},{9,8},{10,11... | collective-permute-start | bytes 786440 | tf_op jit(solution)/shard_map/ppermute | solution.py:91
  97.3 5.3 %collective-permute-start.1 = (f32[32,512]{1,0:T(8,128)S(1)}, f32[32,512]{1,0:T(8,128)S(1)}, u32[]{:S(2)}, u32[]{:S(2)}) collective-permute-start(f32[32,512]{1,0:T(8,128)S(1)} %maximum_select_fusion.14), channel_id=1, source_target_pairs={{0,2},{1,3},{2,0},{3,1},{4,6},{5,7},{6,4},{7,5},{8,10},{9,11},{10,... | collective-permute-start | bytes 196616 | tf_op jit(solution)/shard_map/ppermute | solution.py:68
  98.4 9.6 %collective-permute-start.18 = (f32[32,1024]{1,0:T(8,128)S(1)}, f32[32,1024]{1,0:T(8,128)S(1)}, u32[]{:S(2)}, u32[]{:S(2)}) collective-permute-start(f32[32,1024]{1,0:T(8,128)S(1)} %maximum_select_fusion.10), channel_id=1, source_target_pairs={{0,64},{16,80},{32,96},{48,112},{64,0},{80,16},{96,32},{112,48},{1... | collective-permute-start | bytes 393224 | tf_op jit(solution)/shard_map/ppermute | solution.py:68
  102.6 11.1 %collective-permute-start.2 = (f32[32,1024]{1,0:T(8,128)S(1)}, f32[32,1024]{1,0:T(8,128)S(1)}, u32[]{:S(2)}, u32[]{:S(2)}) collective-permute-start(f32[32,1024]{1,0:T(8,128)S(1)} %maximum_select_fusion.9), channel_id=1, source_target_pairs={{0,4},{1,5},{2,6},{3,7},{4,0},{5,1},{6,2},{7,3},{8,12},{9,13},{10,... | collective-permute-start | bytes 393224 | tf_op jit(solution)/shard_map/ppermute | solution.py:68
  104.7 11.6 %collective-permute-start.13 = (f32[16,4096]{1,0:T(8,128)S(1)}, f32[16,4096]{1,0:T(8,128)S(1)}, u32[]{:S(2)}, u32[]{:S(2)}) collective-permute-start(f32[16,4096]{1,0:T(8,128)S(1)} %add.139), channel_id=1, source_target_pairs={{0,2},{1,3},{2,0},{3,1},{4,6},{5,7},{6,4},{7,5},{8,10},{9,11},{10,... | collective-permute-start | bytes 786440 | tf_op jit(solution)/shard_map/ppermute | solution.py:91
  108.0 47.3 %collective-permute-start.19 = (f32[32,2048]{1,0:T(8,128)S(1)}, f32[32,2048]{1,0:T(8,128)S(1)}, u32[]{:S(2)}, u32[]{:S(2)}) collective-permute-start(f32[32,2048]{1,0:T(8,128)S(1)} %maximum_select_fusion.5), channel_id=1, source_target_pairs={{0,128},{16,144},{32,160},{48,176},{64,192},{80,208},{96,224},{112... | collective-permute-start | bytes 786440 | tf_op jit(solution)/shard_map/ppermute | solution.py:68
  113.8 13.1 %collective-permute-start.3 = (f32[32,2048]{1,0:T(8,128)S(1)}, f32[32,2048]{1,0:T(8,128)S(1)}, u32[]{:S(2)}, u32[]{:S(2)}) collective-permute-start(f32[32,2048]{1,0:T(8,128)S(1)} %maximum_select_fusion.4), channel_id=1, source_target_pairs={{0,8},{1,9},{2,10},{3,11},{4,12},{5,13},{6,14},{7,15},{8,0},{9,1},... | collective-permute-start | bytes 786440 | tf_op jit(solution)/shard_map/ppermute | solution.py:68
  116.4 8.9 %collective-permute-start.14 = (f32[16,4096]{1,0:T(8,128)S(1)}, f32[16,4096]{1,0:T(8,128)S(1)}, u32[]{:S(2)}, u32[]{:S(2)}) collective-permute-start(f32[16,4096]{1,0:T(8,128)S(1)} %add.140), channel_id=1, source_target_pairs={{0,4},{1,5},{2,6},{3,7},{4,0},{5,1},{6,2},{7,3},{8,12},{9,13},{10,... | collective-permute-start | bytes 786440 | tf_op jit(solution)/shard_map/ppermute | solution.py:91
  125.3 8.0 %collective-permute-start.15 = (f32[16,4096]{1,0:T(8,128)S(1)}, f32[16,4096]{1,0:T(8,128)S(1)}, u32[]{:S(2)}, u32[]{:S(2)}) collective-permute-start(f32[16,4096]{1,0:T(8,128)S(1)} %add.141), channel_id=1, source_target_pairs={{0,8},{1,9},{2,10},{3,11},{4,12},{5,13},{6,14},{7,15},{8,0},{9,1},... | collective-permute-start | bytes 786440 | tf_op jit(solution)/shard_map/ppermute | solution.py:91
  133.6 6.3 %collective-permute-start.20 = (f32[32]{0:T(128)S(1)}, f32[32]{0:T(128)S(1)}, u32[]{:S(2)}, u32[]{:S(2)}) collective-permute-start(f32[32]{0:T(128)S(1)} %pad_maximum_fusion.2), channel_id=1, source_target_pairs={{0,16},{16,0},{32,48},{48,32},{64,80},{80,64},{96,112},{112,96},{1... | collective-permute-start | bytes 392 | tf_op jit(solution)/shard_map/ppermute | solution.py:91
  139.9 6.2 %collective-permute-start.21 = (f32[32]{0:T(128)S(1)}, f32[32]{0:T(128)S(1)}, u32[]{:S(2)}, u32[]{:S(2)}) collective-permute-start(f32[32]{0:T(128)S(1)} %add.144), channel_id=1, source_target_pairs={{0,32},{16,48},{32,0},{48,16},{64,96},{80,112},{96,64},{112,80},{1... | collective-permute-start | bytes 392 | tf_op jit(solution)/shard_map/ppermute | solution.py:91
  146.1 4.8 %collective-permute-start.22 = (f32[32]{0:T(128)S(1)}, f32[32]{0:T(128)S(1)}, u32[]{:S(2)}, u32[]{:S(2)}) collective-permute-start(f32[32]{0:T(128)S(1)} %add.145), channel_id=1, source_target_pairs={{0,64},{16,80},{32,96},{48,112},{64,0},{80,16},{96,32},{112,48},{1... | collective-permute-start | bytes 392 | tf_op jit(solution)/shard_map/ppermute | solution.py:91
  150.9 7.5 %collective-permute-start.23 = (f32[32]{0:T(128)S(1)}, f32[32]{0:T(128)S(1)}, u32[]{:S(2)}, u32[]{:S(2)}) collective-permute-start(f32[32]{0:T(128)S(1)} %add.146), channel_id=1, source_target_pairs={{0,128},{16,144},{32,160},{48,176},{64,192},{80,208},{96,224},{112... | collective-permute-start | bytes 392 | tf_op jit(solution)/shard_map/ppermute | solution.py:91
  158.7 29.5 %copy-start = (f32[16,256]{1,0:T(8,128)S(1)}, f32[16,256]{1,0:T(8,128)}, u32[]{:S(2)}) copy-start(f32[16,256]{1,0:T(8,128)} %param.19) | copy-start | bytes 49156
  158.7 29.5 %copy-start.1 = (f32[16,256]{1,0:T(8,128)S(1)}, f32[16,256]{1,0:T(8,128)}, u32[]{:S(2)}) copy-start(f32[16,256]{1,0:T(8,128)} %param.18) | copy-start | bytes 49156
  158.7 29.5 %copy-start.2 = (f32[16,256]{1,0:T(8,128)S(1)}, f32[16,256]{1,0:T(8,128)}, u32[]{:S(2)}) copy-start(f32[16,256]{1,0:T(8,128)} %param.17) | copy-start | bytes 49156
  158.7 30.6 %copy-start.3 = (f32[64]{0:T(128)S(1)}, f32[64]{0:T(128)}, u32[]{:S(2)}) copy-start(f32[64]{0:T(128)} %param.16) | copy-start | bytes 772
  161.1 5.5 %collective-permute-start.28 = (f32[16,512]{1,0:T(8,128)S(1)}, f32[16,512]{1,0:T(8,128)S(1)}, u32[]{:S(2)}, u32[]{:S(2)}) collective-permute-start(f32[16,512]{1,0:T(8,128)S(1)} %slice_select_fusion), channel_id=1, source_target_pairs={{0,8},{1,9},{2,10},{3,11},{4,12},{5,13},{6,14},{7,15},{8,0},{9,1},... | collective-permute-start | bytes 98312 | tf_op jit(solution)/shard_map/ppermute | solution.py:85
  166.7 17.2 %collective-permute-start.29 = (f32[16,256]{1,0:T(8,128)S(1)}, f32[16,256]{1,0:T(8,128)S(1)}, u32[]{:S(2)}, u32[]{:S(2)}) collective-permute-start(f32[16,256]{1,0:T(8,128)S(1)} %slice_select_fusion.1), channel_id=1, source_target_pairs={{0,4},{1,5},{2,6},{3,7},{4,0},{5,1},{6,2},{7,3},{8,12},{9,13},{10,... | collective-permute-start | bytes 49160 | tf_op jit(solution)/shard_map/ppermute | solution.py:85
  168.6 3.6 %collective-permute-start.24 = (f32[16]{0:T(128)S(1)}, f32[16]{0:T(128)S(1)}, u32[]{:S(2)}, u32[]{:S(2)}) collective-permute-start(f32[16]{0:T(128)S(1)} %get-tuple-element.50), channel_id=1, source_target_pairs={{0,16},{16,0},{32,48},{48,32},{64,80},{80,64},{96,112},{112,96},{1... | collective-permute-start | bytes 200 | tf_op jit(solution)/shard_map/ppermute | solution.py:91
  172.2 3.6 %collective-permute-start.25 = (f32[16]{0:T(128)S(1)}, f32[16]{0:T(128)S(1)}, u32[]{:S(2)}, u32[]{:S(2)}) collective-permute-start(f32[16]{0:T(128)S(1)} %add.162), channel_id=1, source_target_pairs={{0,32},{16,48},{32,0},{48,16},{64,96},{80,112},{96,64},{112,80},{1... | collective-permute-start | bytes 200 | tf_op jit(solution)/shard_map/ppermute | solution.py:91
  175.8 4.5 %collective-permute-start.26 = (f32[16]{0:T(128)S(1)}, f32[16]{0:T(128)S(1)}, u32[]{:S(2)}, u32[]{:S(2)}) collective-permute-start(f32[16]{0:T(128)S(1)} %add.163), channel_id=1, source_target_pairs={{0,64},{16,80},{32,96},{48,112},{64,0},{80,16},{96,32},{112,48},{1... | collective-permute-start | bytes 200 | tf_op jit(solution)/shard_map/ppermute | solution.py:91
  180.2 7.5 %collective-permute-start.27 = (f32[16]{0:T(128)S(1)}, f32[16]{0:T(128)S(1)}, u32[]{:S(2)}, u32[]{:S(2)}) collective-permute-start(f32[16]{0:T(128)S(1)} %add.164), channel_id=1, source_target_pairs={{0,128},{16,144},{32,160},{48,176},{64,192},{80,208},{96,224},{112... | collective-permute-start | bytes 200 | tf_op jit(solution)/shard_map/ppermute | solution.py:91
  183.9 4.1 %collective-permute-start.30 = (f32[16,128]{1,0:T(8,128)S(1)}, f32[16,128]{1,0:T(8,128)S(1)}, u32[]{:S(2)}, u32[]{:S(2)}) collective-permute-start(f32[16,128]{1,0:T(8,128)S(1)} %slice_select_fusion.3), channel_id=1, source_target_pairs={{0,2},{1,3},{2,0},{3,1},{4,6},{5,7},{6,4},{7,5},{8,10},{9,11},{10,... | collective-permute-start | bytes 24584 | tf_op jit(solution)/shard_map/ppermute | solution.py:85
  188.1 1.2 collective-permute-start.31

commit v3 on v2

--- a/solution.py
+++ b/solution.py
@@ -71,6 +71,26 @@
             low, jnp.concatenate([buf, recv], -1), jnp.concatenate([recv, buf], -1)
         )
     return buf
+
+
+def all_sum_grid(x, n_row, n_col):
+    rounds = min(n_row, n_col).bit_length() - 1
+    for bit in range(rounds):
+        step = 1 << bit
+        diag = [
+            (r * n_col + c, (r ^ step) * n_col + (c ^ step))
+            for r in range(n_row)
+            for c in range(n_col)
+        ]
+        from_col = lax.ppermute(x, "col", xor_perm(n_col, bit))
+        from_row = lax.ppermute(x, "row", xor_perm(n_row, bit))
+        from_diag = lax.ppermute(x, ("row", "col"), diag)
+        x = (x + from_col) + (from_row + from_diag)
+    for bit in range(rounds, n_row.bit_length() - 1):
+        x = x + lax.ppermute(x, "row", xor_perm(n_row, bit))
+    for bit in range(rounds, n_col.bit_length() - 1):
+        x = x + lax.ppermute(x, "col", xor_perm(n_col, bit))
+    return x
 
 
 def reduce_scatter_last(x, axis_name, size):
@@ -108,23 +128,43 @@
     scaled = (points / length_scales[:, None]).astype(jnp.bfloat16)
     cand_scaled = (candidates / length_scales[:, None]).astype(jnp.bfloat16)
     signal_scalar = signal_var[0]
-    dir_low = direction.astype(jnp.bfloat16)
     cols, own = direction.shape
     own_cand = cand_scaled.shape[1]
     feats = scaled.shape[0]
 
-    row_pack = gather_last(jnp.concatenate([scaled, cand_scaled], 1), "col", n_col)
-    row_pack = row_pack.reshape(feats, n_col, own + own_cand)
-    row_pts = row_pack[:, :, :own].reshape(feats, n_col * own)
-    row_cands = row_pack[:, :, own:].reshape(feats, n_col * own_cand)
-    col_pack = gather_last(jnp.concatenate([scaled, dir_low], 0), "row", n_row)
-    col_pts = col_pack[:feats]
-    col_dir = col_pack[feats:]
-    row_state = gather_last(jnp.concatenate([residual, direction], 0), "col", n_col)
-    res_row, dir_row = row_state[:cols], row_state[cols:]
-    col_state = gather_last(jnp.concatenate([weights, direction], 0), "row", n_row)
-    w_col, d_col = col_state[:cols], col_state[cols:]
-
+    cand_rows = own_cand * feats // own
+    row_pack = gather_last(
+        jnp.concatenate(
+            [
+                scaled.astype(jnp.float32),
+                cand_scaled.astype(jnp.float32).reshape(cand_rows, own),
+                direction,
+            ],
+            0,
+        ),
+        "col",
+        n_col,
+    )
+    row_pts = row_pack[:feats].astype(jnp.bfloat16)
+    row_cands = (
+        row_pack[feats:feats + cand_rows]
+        .reshape(cand_rows, n_col, own)
+        .transpose(1, 0, 2)
+        .reshape(n_col, feats, own_cand)
+        .transpose(1, 0, 2)
+        .reshape(feats, n_col * own_cand)
+        .astype(jnp.bfloat16)
+    )
+    dir_row = row_pack[feats + cand_rows:]
+    col_pack = gather_last(
+        jnp.concatenate([scaled.astype(jnp.float32), direction, weights], 0),
+        "row",
+        n_row,
+    )
+    col_pts = col_pack[:feats].astype(jnp.bfloat16)
+    d_col = col_pack[feats:feats + cols]
+    w_col = col_pack[feats + cols:]
+    col_dir = d_col.astype(jnp.bfloat16)
     row_sq = square_norms(row_pts)
     col_sq = square_norms(col_pts)
     cand_sq = square_norms(row_cands)
@@ -144,18 +184,22 @@
                 )
             )
         )
+    noise = noise_var[0]
+    local_sums = jnp.concatenate(
+        [
+            jnp.sum(residual * residual, axis=1),
+            jnp.sum(dir_row * partial_rows, axis=1)
+            + noise * jnp.sum(direction * direction, axis=1),
+        ]
+    )
+    sums = all_sum_grid(local_sums, n_row, n_col)
     kernel_row = all_sum(partial_rows, "col", n_col)
-    image_row = kernel_row + noise_var[0] * dir_row
-    local_sums = jnp.concatenate(
-        [jnp.sum(res_row * res_row, axis=1), jnp.sum(dir_row * image_row, axis=1)]
-    )
-    sums = all_sum(tied(local_sums, w_col), "row", n_row)
     norm_now, curvature = sums[:cols], sums[cols:]
     step_len = norm_now / curvature
-    residual_new_row = res_row - step_len[:, None] * image_row
 
     me_col = lax.axis_index("col")
-    image_vec = lax.dynamic_slice_in_dim(image_row, me_col * own, own, axis=1)
+    kernel_own = lax.dynamic_slice_in_dim(kernel_row, me_col * own, own, axis=1)
+    image_vec = kernel_own + noise * direction
     weights_new = weights + step_len[:, None] * direction
     residual_new = residual - step_len[:, None] * image_vec
 
@@ -168,9 +212,9 @@
             preferred_element_type=jnp.float32,
         )
         partial_fit = part if partial_fit is None else partial_fit + part
-    norm_next = all_sum(
-        tied(jnp.sum(residual_new_row * residual_new_row, axis=1), partial_fit),
-        "row", n_row,
+    norm_next = all_sum_grid(
+        tied(jnp.sum(residual_new * residual_new, axis=1), partial_fit),
+        n_row, n_col,
     )
     direction_new = residual_new + (norm_next / norm_now)[:, None] * direction
     fitted = reduce_scatter_last(partial_fit, "col", n_col)

time: 193 us -> 260 us (1.35)
  matrix products: 76.1 us -> 103 us
  waiting for transfers between devices: 39 us -> 65.2 us
  starting transfers between devices: 64.1 us -> 73.9 us
  other arithmetic: 5.85 us -> 11.5 us
    ppermute x0 -> x24, starting transfers between devices: none -> 41.9 us  [the longest x8 19.2 us: all_sum_grid(): from_diag = lax.ppermute(x, ('row', 'col'), diag)]
    dot_general x16, matrix products: 61.5 us -> 88.8 us  [one_block(): lax.dot_general(vec_blk, kern_vals, contract_last, preferred_element_type...]
    ppermute x12 -> x4, waiting for transfers between devices: 27.9 us -> 3.91 us  [all_sum(): x = x + lax.ppermute(x, axis_name, xor_perm(size, bit))]
    ppermute x0 -> x24, waiting for transfers between devices: none -> 23.7 us  [the longest x8 16.6 us: all_sum_grid(): from_diag = lax.ppermute(x, ('row', 'col'), diag)]
    ppermute x16 -> x8, waiting for transfers between devices: 8.41 us -> 27.3 us  [gather_last(): recv = lax.ppermute(buf, axis_name, xor_perm(size, bit))]
    ppermute x16 -> x8, starting transfers between devices: 36.4 us -> 20 us  [gather_last(): recv = lax.ppermute(buf, axis_name, xor_perm(size, bit))]
    ppermute x12 -> x4, starting transfers between devices: 19.6 us -> 7.28 us  [all_sum(): x = x + lax.ppermute(x, axis_name, xor_perm(size, bit))]
    ppermute x4, waiting for transfers between devices: 2.65 us -> 10.3 us  [reduce_scatter_last(): buf = keep + lax.ppermute(send, axis_name, xor_perm(size, bit))]
  transfers between devices with their start and end apart: 32 -> 40, of which waited for: 17 -> 24; matrix products, arithmetic and copies ran while one was open for 42% -> 8% of each run, Pallas kernels for 0% -> 0%
where the time goes in v3:
time: 260 us; the launch traced here: 258 us
  matrix products  103 us (40%)
  starting transfers between devices  73.9 us (28%)
  waiting for transfers between devices  65.2 us (25%)
  other arithmetic  11.5 us (4%)
    dot_general x16, matrix products, one_block(): lax.dot_general(vec_blk, kern_vals, contract_last, preferred_element_type...  88.8 us
    ppermute x8, waiting for transfers between devices, gather_last(): recv = lax.ppermute(buf, axis_name, xor_perm(size, bit))  27.3 us
    ppermute x8, starting transfers between devices, gather_last(): recv = lax.ppermute(buf, axis_name, xor_perm(size, bit))  20 us
    ppermute x8, starting transfers between devices, all_sum_grid(): from_diag = lax.ppermute(x, ('row', 'col'), diag)  19.2 us
    ppermute x8, waiting for transfers between devices, all_sum_grid(): from_diag = lax.ppermute(x, ('row', 'col'), diag)  16.6 us
    ppermute x8, starting transfers between devices, all_sum_grid(): from_row = lax.ppermute(x, 'row', xor_perm(n_row, bit))  12.6 us
    dot_general x2, matrix products, matern_block(): lax.dot_general(row_pts, col_pts, contract_first, preferred_element_type=...  12.2 us
    ppermute x4, waiting for transfers between devices, reduce_scatter_last(): buf = keep + lax.ppermute(send, axis_name, xor_perm(size, bit))  10.3 us
  transfers between devices with their start and end apart: 40, of which 24 were waited for; matrix products, arithmetic and copies ran while one was open for 8% of the time, Pallas kernels for 0%

profile of v3, /device:TPU:2, one launch (start us, length us, event | category | flops | bytes accessed | tf_op | source)
XLA Modules:
  0.0 258.1 jit_solution(7502662433563362314)
XLA Ops:
  3.8 1.6 collective-permute-start.4
  9.1 2.0 collective-permute-start.5
  11.6 2.2 collective-permute-start.2
  15.1 3.4 %collective-permute-start.6 = (f32[64,1024]{1,0:T(8,128)S(1)}, f32[64,1024]{1,0:T(8,128)S(1)}, u32[]{:S(2)}, u32[]{:S(2)}) collective-permute-start(f32[64,1024]{1,0:T(8,128)S(1)} %maximum_select_fusion.4), channel_id=1, source_target_pairs={{0,64},{16,80},{32,96},{48,112},{64,0},{80,16},{96,32},{112,48},{1... | collective-permute-start | bytes 786440 | tf_op jit(solution)/shard_map/ppermute | solution.py:68
  18.5 1.5 collective-permute-done.2
  20.1 3.0 %collective-permute-start.3 = (f32[56,2048]{1,0:T(8,128)S(1)}, f32[56,2048]{1,0:T(8,128)S(1)}, u32[]{:S(2)}, u32[]{:S(2)}) collective-permute-start(f32[56,2048]{1,0:T(8,128)S(1)} %maximum_select_fusion.3), channel_id=1, source_target_pairs={{0,8},{1,9},{2,10},{3,11},{4,12},{5,13},{6,14},{7,15},{8,0},{9,1},... | collective-permute-start | bytes 1376264 | tf_op jit(solution)/shard_map/ppermute | solution.py:68
  23.1 1.3 multiply_reduce_fusion.4
  24.4 1.4 multiply_reduce_fusion.5
  25.8 3.9 %collective-permute-done.6 = f32[64,1024]{1,0:T(8,128)S(1)} collective-permute-done((f32[64,1024]{1,0:T(8,128)S(1)}, f32[64,1024]{1,0:T(8,128)S(1)}, u32[]{:S(2)}, u32[]{:S(2)}) %collective-permute-start.6) | collective-permute-done | bytes 262176 | tf_op jit(solution)/shard_map/ppermute | solution.py:68
  29.7 6.6 %collective-permute-start.7 = (f32[64,2048]{1,0:T(8,128)S(1)}, f32[64,2048]{1,0:T(8,128)S(1)}, u32[]{:S(2)}, u32[]{:S(2)}) collective-permute-start(f32[64,2048]{1,0:T(8,128)S(1)} %maximum_select_fusion.2), channel_id=1, source_target_pairs={{0,128},{16,144},{32,160},{48,176},{64,192},{80,208},{96,224},{112... | collective-permute-start | bytes 1572872 | tf_op jit(solution)/shard_map/ppermute | solution.py:68
  38.9 20.5 %collective-permute-done.7 = f32[64,2048]{1,0:T(8,128)S(1)} collective-permute-done((f32[64,2048]{1,0:T(8,128)S(1)}, f32[64,2048]{1,0:T(8,128)S(1)}, u32[]{:S(2)}, u32[]{:S(2)}) %collective-permute-start.7) | collective-permute-done | bytes 524320 | tf_op jit(solution)/shard_map/ppermute | solution.py:68
  59.8 88.9 %while.11 = (s32[]{:T(128)}, f32[16,4096]{1,0:T(8,128)}, bf16[16,16,256]{2,1,0:T(8,128)(2,1)S(1)}, f32[]{:T(128)}, f32[4096]{0:T(1024)S(1)}, /*index=5*/f32[16,2...) while((s32[]{:T(128)}, f32[16,4096]{1,0:T(8,128)}, ...), condition=%wide.region_4.5_spmd.clone, body=%wide.region_3.4_spmd.clone.sunk | while | flops 113377280 | bytes 832126 | solution.py:51
  59.8 5.5 %convolution_add_fusion.3 = f32[16,4096]{1,0:T(8,128)} fusion(bf16[32,4096]{1,0:T(8,128)(2,1)} %get-tuple-element.179, f32[256]{0:T(256)S(1)} %bitcast.63, f32[4096]{0:T(1024)S(1)} %get-tuple-element.176, f32[]{:T(128)} %get-tuple-element.175, f32[16,4096]{1,0:T(8,128)} %get-tuple-element.163, pred[]{:T(512)S(6)} %compare.3, ...), kind=kOutput, calls=%fused_computation.4.clone.1 | convolution fusion | flops 113377280 | bytes 829956 | tf_op jit(solution)/shard_map/while/body/eval_jaxpr/dot_general | solution.py:44
  65.3 5.6 %convolution_add_fusion.3 = f32[16,4096]{1,0:T(8,128)} fusion(bf16[32,4096]{1,0:T(8,128)(2,1)} %get-tuple-element.179, f32[256]{0:T(256)S(1)} %bitcast.63, f32[4096]{0:T(1024)S(1)} %get-tuple-element.176, f32[]{:T(128)} %get-tuple-element.175, f32[16,4096]{1,0:T(8,128)} %get-tuple-element.163, pred[]{:T(512)S(6)} %compare.3, ...), kind=kOutput, calls=%fused_computation.4.clone.1 | convolution fusion | flops 113377280 | bytes 829956 | tf_op jit(solution)/shard_map/while/body/eval_jaxpr/dot_general | solution.py:44
  70.9 5.6 %convolution_add_fusion.3 = f32[16,4096]{1,0:T(8,128)} fusion(bf16[32,4096]{1,0:T(8,128)(2,1)} %get-tuple-element.179, f32[256]{0:T(256)S(1)} %bitcast.63, f32[4096]{0:T(1024)S(1)} %get-tuple-element.176, f32[]{:T(128)} %get-tuple-element.175, f32[16,4096]{1,0:T(8,128)} %get-tuple-element.163, pred[]{:T(512)S(6)} %compare.3, ...), kind=kOutput, calls=%fused_computation.4.clone.1 | convolution fusion | flops 113377280 | bytes 829956 | tf_op jit(solution)/shard_map/while/body/eval_jaxpr/dot_general | solution.py:44
  76.5 5.6 %convolution_add_fusion.3 = f32[16,4096]{1,0:T(8,128)} fusion(bf16[32,4096]{1,0:T(8,128)(2,1)} %get-tuple-element.179, f32[256]{0:T(256)S(1)} %bitcast.63, f32[4096]{0:T(1024)S(1)} %get-tuple-element.176, f32[]{:T(128)} %get-tuple-element.175, f32[16,4096]{1,0:T(8,128)} %get-tuple-element.163, pred[]{:T(512)S(6)} %compare.3, ...), kind=kOutput, calls=%fused_computation.4.clone.1 | convolution fusion | flops 113377280 | bytes 829956 | tf_op jit(solution)/shard_map/while/body/eval_jaxpr/dot_general | solution.py:44
  82.0 5.6 %convolution_add_fusion.3 = f32[16,4096]{1,0:T(8,128)} fusion(bf16[32,4096]{1,0:T(8,128)(2,1)} %get-tuple-element.179, f32[256]{0:T(256)S(1)} %bitcast.63, f32[4096]{0:T(1024)S(1)} %get-tuple-element.176, f32[]{:T(128)} %get-tuple-element.175, f32[16,4096]{1,0:T(8,128)} %get-tuple-element.163, pred[]{:T(512)S(6)} %compare.3, ...), kind=kOutput, calls=%fused_computation.4.clone.1 | convolution fusion | flops 113377280 | bytes 829956 | tf_op jit(solution)/shard_map/while/body/eval_jaxpr/dot_general | solution.py:44
  87.6 5.6 %convolution_add_fusion.3 = f32[16,4096]{1,0:T(8,128)} fusion(bf16[32,4096]{1,0:T(8,128)(2,1)} %get-tuple-element.179, f32[256]{0:T(256)S(1)} %bitcast.63, f32[4096]{0:T(1024)S(1)} %get-tuple-element.176, f32[]{:T(128)} %get-tuple-element.175, f32[16,4096]{1,0:T(8,128)} %get-tuple-element.163, pred[]{:T(512)S(6)} %compare.3, ...), kind=kOutput, calls=%fused_computation.4.clone.1 | convolution fusion | flops 113377280 | bytes 829956 | tf_op jit(solution)/shard_map/while/body/eval_jaxpr/dot_general | solution.py:44
  93.1 5.6 %convolution_add_fusion.3 = f32[16,4096]{1,0:T(8,128)} fusion(bf16[32,4096]{1,0:T(8,128)(2,1)} %get-tuple-element.179, f32[256]{0:T(256)S(1)} %bitcast.63, f32[4096]{0:T(1024)S(1)} %get-tuple-element.176, f32[]{:T(128)} %get-tuple-element.175, f32[16,4096]{1,0:T(8,128)} %get-tuple-element.163, pred[]{:T(512)S(6)} %compare.3, ...), kind=kOutput, calls=%fused_computation.4.clone.1 | convolution fusion | flops 113377280 | bytes 829956 | tf_op jit(solution)/shard_map/while/body/eval_jaxpr/dot_general | solution.py:44
  98.7 5.6 %convolution_add_fusion.3 = f32[16,4096]{1,0:T(8,128)} fusion(bf16[32,4096]{1,0:T(8,128)(2,1)} %get-tuple-element.179, f32[256]{0:T(256)S(1)} %bitcast.63, f32[4096]{0:T(1024)S(1)} %get-tuple-element.176, f32[]{:T(128)} %get-tuple-element.175, f32[16,4096]{1,0:T(8,128)} %get-tuple-element.163, pred[]{:T(512)S(6)} %compare.3, ...), kind=kOutput, calls=%fused_computation.4.clone.1 | convolution fusion | flops 113377280 | bytes 829956 | tf_op jit(solution)/shard_map/while/body/eval_jaxpr/dot_general | solution.py:44
  104.3 5.6 %convolution_add_fusion.3 = f32[16,4096]{1,0:T(8,128)} fusion(bf16[32,4096]{1,0:T(8,128)(2,1)} %get-tuple-element.179, f32[256]{0:T(256)S(1)} %bitcast.63, f32[4096]{0:T(1024)S(1)} %get-tuple-element.176, f32[]{:T(128)} %get-tuple-element.175, f32[16,4096]{1,0:T(8,128)} %get-tuple-element.163, pred[]{:T(512)S(6)} %compare.3, ...), kind=kOutput, calls=%fused_computation.4.clone.1 | convolution fusion | flops 113377280 | bytes 829956 | tf_op jit(solution)/shard_map/while/body/eval_jaxpr/dot_general | solution.py:44
  109.8 5.6 %convolution_add_fusion.3 = f32[16,4096]{1,0:T(8,128)} fusion(bf16[32,4096]{1,0:T(8,128)(2,1)} %get-tuple-element.179, f32[256]{0:T(256)S(1)} %bitcast.63, f32[4096]{0:T(1024)S(1)} %get-tuple-element.176, f32[]{:T(128)} %get-tuple-element.175, f32[16,4096]{1,0:T(8,128)} %get-tuple-element.163, pred[]{:T(512)S(6)} %compare.3, ...), kind=kOutput, calls=%fused_computation.4.clone.1 | convolution fusion | flops 113377280 | bytes 829956 | tf_op jit(solution)/shard_map/while/body/eval_jaxpr/dot_general | solution.py:44
  115.4 5.6 %convolution_add_fusion.3 = f32[16,4096]{1,0:T(8,128)} fusion(bf16[32,4096]{1,0:T(8,128)(2,1)} %get-tuple-element.179, f32[256]{0:T(256)S(1)} %bitcast.63, f32[4096]{0:T(1024)S(1)} %get-tuple-element.176, f32[]{:T(128)} %get-tuple-element.175, f32[16,4096]{1,0:T(8,128)} %get-tuple-element.163, pred[]{:T(512)S(6)} %compare.3, ...), kind=kOutput, calls=%fused_computation.4.clone.1 | convolution fusion | flops 113377280 | bytes 829956 | tf_op jit(solution)/shard_map/while/body/eval_jaxpr/dot_general | solution.py:44
  120.9 5.6 %convolution_add_fusion.3 = f32[16,4096]{1,0:T(8,128)} fusion(bf16[32,4096]{1,0:T(8,128)(2,1)} %get-tuple-element.179, f32[256]{0:T(256)S(1)} %bitcast.63, f32[4096]{0:T(1024)S(1)} %get-tuple-element.176, f32[]{:T(128)} %get-tuple-element.175, f32[16,4096]{1,0:T(8,128)} %get-tuple-element.163, pred[]{:T(512)S(6)} %compare.3, ...), kind=kOutput, calls=%fused_computation.4.clone.1 | convolution fusion | flops 113377280 | bytes 829956 | tf_op jit(solution)/shard_map/while/body/eval_jaxpr/dot_general | solution.py:44
  126.5 5.6 %convolution_add_fusion.3 = f32[16,4096]{1,0:T(8,128)} fusion(bf16[32,4096]{1,0:T(8,128)(2,1)} %get-tuple-element.179, f32[256]{0:T(256)S(1)} %bitcast.63, f32[4096]{0:T(1024)S(1)} %get-tuple-element.176, f32[]{:T(128)} %get-tuple-element.175, f32[16,4096]{1,0:T(8,128)} %get-tuple-element.163, pred[]{:T(512)S(6)} %compare.3, ...), kind=kOutput, calls=%fused_computation.4.clone.1 | convolution fusion | flops 113377280 | bytes 829956 | tf_op jit(solution)/shard_map/while/body/eval_jaxpr/dot_general | solution.py:44
  132.1 5.6 %convolution_add_fusion.3 = f32[16,4096]{1,0:T(8,128)} fusion(bf16[32,4096]{1,0:T(8,128)(2,1)} %get-tuple-element.179, f32[256]{0:T(256)S(1)} %bitcast.63, f32[4096]{0:T(1024)S(1)} %get-tuple-element.176, f32[]{:T(128)} %get-tuple-element.175, f32[16,4096]{1,0:T(8,128)} %get-tuple-element.163, pred[]{:T(512)S(6)} %compare.3, ...), kind=kOutput, calls=%fused_computation.4.clone.1 | convolution fusion | flops 113377280 | bytes 829956 | tf_op jit(solution)/shard_map/while/body/eval_jaxpr/dot_general | solution.py:44
  137.6 5.6 %convolution_add_fusion.3 = f32[16,4096]{1,0:T(8,128)} fusion(bf16[32,4096]{1,0:T(8,128)(2,1)} %get-tuple-element.179, f32[256]{0:T(256)S(1)} %bitcast.63, f32[4096]{0:T(1024)S(1)} %get-tuple-element.176, f32[]{:T(128)} %get-tuple-element.175, f32[16,4096]{1,0:T(8,128)} %get-tuple-element.163, pred[]{:T(512)S(6)} %compare.3, ...), kind=kOutput, calls=%fused_computation.4.clone.1 | convolution fusion | flops 113377280 | bytes 829956 | tf_op jit(solution)/shard_map/while/body/eval_jaxpr/dot_general | solution.py:44
  143.2 5.6 %convolution_add_fusion.3 = f32[16,4096]{1,0:T(8,128)} fusion(bf16[32,4096]{1,0:T(8,128)(2,1)} %get-tuple-element.179, f32[256]{0:T(256)S(1)} %bitcast.63, f32[4096]{0:T(1024)S(1)} %get-tuple-element.176, f32[]{:T(128)} %get-tuple-element.175, f32[16,4096]{1,0:T(8,128)} %get-tuple-element.163, pred[]{:T(512)S(6)} %compare.3, ...), kind=kOutput, calls=%fused_computation.4.clone.1 | convolution fusion | flops 113377280 | bytes 829956 | tf_op jit(solution)/shard_map/while/body/eval_jaxpr/dot_general | solution.py:44
  148.7 6.1 %multiply_convert_fusion.2 = bf16[1024,2048]{1,0:T(8,128)(2,1)S(1)} fusion(bf16[32,1024]{1,0:T(8,128)(2,1)S(1)} %copy-done.3, f32[2048]{0:T(1024)S(1)} %get-tuple-element.102, f32[1024]{0:T(1024)S(1)} %copy-done.6, f32[]{:T(128)} %bitcast.53, bf16[64,4096]{1,0:T(8,128)(2,1)S(1)} %get-tuple-element.94), kind=kOutput, calls=%fused_computation.19 | convolution fusion | flops 159383552 | bytes 4403204 | tf_op jit(solution)/shard_map/dot_general | solution.py:19
  154.9 6.1 %multiply_convert_fusion.1 = bf16[1024,2048]{1,0:T(8,128)(2,1)S(1)} fusion(bf16[32,1024]{1,0:T(8,128)(2,1)S(1)} %copy-done.3, f32[2048]{0:T(1024)S(1)} %get-tuple-element.101, f32[1024]{0:T(1024)S(1)} %copy-done.6, f32[]{:T(128)} %bitcast.54, bf16[64,4096]{1,0:T(8,128)(2,1)S(1)} %get-tuple-element.94), kind=kOutput, calls=%fused_computation.18 | convolution fusion | flops 159383552 | bytes 4403204 | tf_op jit(solution)/shard_map/dot_general | solution.py:19
  161.7 1.4 collective-permute-start.10
  163.5 1.4 collective-permute-done.9
  165.0 2.9 %collective-permute-start.13 = (f32[32]{0:T(128)S(1)}, f32[32]{0:T(128)S(1)}, u32[]{:S(2)}, u32[]{:S(2)}) collective-permute-start(f32[32]{0:T(128)S(1)} %add_add_fusion.7), channel_id=1, source_target_pairs={{0,34},{1,35},{2,32},{3,33},{4,38},{5,39},{6,36},{7,37},{8,42},{9,... | collective-permute-start | bytes 392 | tf_op jit(solution)/shard_map/ppermute | solution.py:87
  169.6 1.9 collective-permute-done.11
  171.5 1.7 collective-permute-start.15
  173.1 2.0 collective-permute-start.16
  175.2 2.2 collective-permute-start.14
  177.4 2.6 %collective-permute-done.16 = f32[32]{0:T(128)S(1)} collective-permute-done((f32[32]{0:T(128)S(1)}, f32[32]{0:T(128)S(1)}, u32[]{:S(2)}, u32[]{:S(2)}) %collective-permute-start.16) | collective-permute-done | bytes 160 | tf_op jit(solution)/shard_map/ppermute | solution.py:87
  180.3 3.1 %collective-permute-start.18 = (f32[32]{0:T(128)S(1)}, f32[32]{0:T(128)S(1)}, u32[]{:S(2)}, u32[]{:S(2)}) collective-permute-start(f32[32]{0:T(128)S(1)} %add_add_fusion.5), channel_id=1, source_target_pairs={{0,128},{16,144},{32,160},{48,176},{64,192},{80,208},{96,224},{112... | collective-permute-start | bytes 392 | tf_op jit(solution)/shard_map/ppermute | solution.py:86
  183.4 5.4 %collective-permute-start.19 = (f32[32]{0:T(128)S(1)}, f32[32]{0:T(128)S(1)}, u32[]{:S(2)}, u32[]{:S(2)}) collective-permute-start(f32[32]{0:T(128)S(1)} %add_add_fusion.5), channel_id=1, source_target_pairs={{0,136},{1,137},{2,138},{3,139},{4,140},{5,141},{6,142},{7,143},{8... | collective-permute-start | bytes 392 | tf_op jit(solution)/shard_map/ppermute | solution.py:87
  189.2 4.1 %collective-permute-done.19 = f32[32]{0:T(128)S(1)} collective-permute-done((f32[32]{0:T(128)S(1)}, f32[32]{0:T(128)S(1)}, u32[]{:S(2)}, u32[]{:S(2)}) %collective-permute-start.19) | collective-permute-done | bytes 160 | tf_op jit(solution)/shard_map/ppermute | solution.py:87
  196.5 2.4 collective-permute-start.36
  198.9 1.8 collective-permute-start.21
  200.7 1.3 collective-permute-done.36
  202.1 2.1 collective-permute-start.37
  204.2 3.4 %collective-permute-done.37 = f32[16,256]{1,0:T(8,128)S(1)} collective-permute-done((f32[16,256]{1,0:T(8,128)S(1)}, f32[16,256]{1,0:T(8,128)S(1)}, u32[]{:S(2)}, u32[]{:S(2)}) %collective-permute-start.37) | collective-permute-done | bytes 16416 | tf_op jit(solution)/shard_map/ppermute | solution.py:105
  207.6 3.1 %collective-permute-start.22 = (f32[16,4096]{1,0:T(8,128)S(1)}, f32[16,4096]{1,0:T(8,128)S(1)}, u32[]{:S(2)}, u32[]{:S(2)}) collective-permute-start(f32[16,4096]{1,0:T(8,128)S(1)} %add.205), channel_id=1, source_target_pairs={{0,4},{1,5},{2,6},{3,7},{4,0},{5,1},{6,2},{7,3},{8,12},{9,13},{10,... | collective-permute-start | bytes 786440 | tf_op jit(solution)/shard_map/ppermute | solution.py:111
  210.9 4.4 %collective-permute-done.38 = f32[16,128]{1,0:T(8,128)S(1)} collective-permute-done((f32[16,128]{1,0:T(8,128)S(1)}, f32[16,128]{1,0:T(8,128)S(1)}, u32[]{:S(2)}, u32[]{:S(2)}) %collective-permute-start.38) | collective-permute-done | bytes 8224 | tf_op jit(solution)/shard_map/ppermute | solution.py:105
  215.6 2.4 collective-permute-start.23
  219.9 3.7 %collective-permute-done.23 = f32[16,4096]{1,0:T(8,128)S(1)} collective-permute-done((f32[16,4096]{1,0:T(8,128)S(1)}, f32[16,4096]{1,0:T(8,128)S(1)}, u32[]{:S(2)}, u32[]{:S(2)}) %collective-permute-start.23) | collective-permute-done | bytes 262176 | tf_op jit(solution)/shard_map/ppermute | solution.py:111
  224.8 1.8 collective-permute-start.24
  226.6 1.4 collective-permute-done.25
  228.1 2.0 collective-permute-start.28
  230.1 2.3 collective-permute-start.29
  232.3 2.2 collective-permute-done.29
  234.5 1.4 collective-permute-done.27
  235.9 1.3 collective-permute-start.31
  237.2 1.4 collective-permute-start.32
  238.6 3.2 %collective-permute-start.30 = (f32[16]{0:T(128)S(1)}, f32[16]{0:T(128)S(1)}, u32[]{:S(2)}, u32[]{:S(2)}) collective-permute-start(f32[16]{0:T(128)S(1)} %add_add_fusion.2), channel_id=1, source_target_pairs={{0,4},{1,5},{2,6},{3,7},{4,0},{5,1},{6,2},{7,3},{8,12},{9,13},{10,... | collective-permute-start | bytes 200 | tf_op jit(solution)/shard_map/ppermute | solution.py:85
  241.8 2.3 collective-permute-done.32
  244.1 3.5 %collective-permute-start.34 = (f32[16]{0:T(128)S(1)}, f32[16]{0:T(128)S(1)}, u32[]{:S(2)}, u32[]{:S(2)}) collective-permute-start(f32[16]{0:T(128)S(1)} %add_add_fusion.1), channel_id=1, source_target_pairs={{0,128},{16,144},{32,160},{48,176},{64,192},{80,208},{96,224},{112... | collective-permute-start | bytes 200 | tf_op jit(solution)/shard_map/ppermute | solution.py:86
  247.6 3.8 %collective-permute-start.35 = (f32[16]{0:T(128)S(1)}, f32[16]{0:T(128)S(1)}, u32[]{:S(2)}, u32[]{:S(2)}) collective-permute-start(f32[16]{0:T(128)S(1)} %add_add_fusion.1), channel_id=1, source_target_pairs={{0,136},{1,137},{2,138},{3,139},{4,140},{5,141},{6,142},{7,143},{8... | collective-permute-start | bytes 200 | tf_op jit(solution)/shard_map/ppermute | solution.py:87
  251.3 1.7 collective-permute-start.33
  253.1 4.3 %collective-permute-done.35 = f32[16]{0:T(128)S(1)} collective-permute-done((f32[16]{0:T(128)S(1)}, f32[16]{0:T(128)S(1)}, u32[]{:S(2)}, u32[]{:S(2)}) %collective-permute-start.35) | collective-permute-done | bytes 96 | tf_op jit(solution)/shard_map/ppermute | solution.py:87
  (128 shorter events, 21.3 us)
Async XLA Ops:
  3.1 2.3 collective-permute-start
  3.8 4.5 %collective-permute-start.4 = (f32[64,256]{1,0:T(8,128)S(1)}, f32[64,256]{1,0:T(8,128)S(1)}, u32[]{:S(2)}, u32[]{:S(2)}) collective-permute-start(f32[64,256]{1,0:T(8,128)S(1)} %pad_maximum_fusion), channel_id=1, source_target_pairs={{0,16},{16,0},{32,48},{48,32},{64,80},{80,64},{96,112},{112,96},{1... | collective-permute-start | bytes 196616 | tf_op jit(solution)/shard_map/ppermute | solution.py:68
  6.2 5.4 %collective-permute-start.1 = (f32[56,512]{1,0:T(8,128)S(1)}, f32[56,512]{1,0:T(8,128)S(1)}, u32[]{:S(2)}, u32[]{:S(2)}) collective-permute-start(f32[56,512]{1,0:T(8,128)S(1)} %maximum_select_fusion.7), channel_id=1, source_target_pairs={{0,2},{1,3},{2,0},{3,1},{4,6},{5,7},{6,4},{7,5},{8,10},{9,11},{10,... | collective-permute-start | bytes 344072 | tf_op jit(solution)/shard_map/ppermute | solution.py:68
  9.1 6.0 %collective-permute-start.5 = (f32[64,512]{1,0:T(8,128)S(1)}, f32[64,512]{1,0:T(8,128)S(1)}, u32[]{:S(2)}, u32[]{:S(2)}) collective-permute-start(f32[64,512]{1,0:T(8,128)S(1)} %maximum_select_fusion.6), channel_id=1, source_target_pairs={{0,32},{16,48},{32,0},{48,16},{64,96},{80,112},{96,64},{112,80},{1... | collective-permute-start | bytes 393224 | tf_op jit(solution)/shard_map/ppermute | solution.py:68
  11.6 8.5 %collective-permute-start.2 = (f32[56,1024]{1,0:T(8,128)S(1)}, f32[56,1024]{1,0:T(8,128)S(1)}, u32[]{:S(2)}, u32[]{:S(2)}) collective-permute-start(f32[56,1024]{1,0:T(8,128)S(1)} %maximum_select_fusion.5), channel_id=1, source_target_pairs={{0,4},{1,5},{2,6},{3,7},{4,0},{5,1},{6,2},{7,3},{8,12},{9,13},{10,... | collective-permute-start | bytes 688136 | tf_op jit(solution)/shard_map/ppermute | solution.py:68
  15.1 14.5 %collective-permute-start.6 = (f32[64,1024]{1,0:T(8,128)S(1)}, f32[64,1024]{1,0:T(8,128)S(1)}, u32[]{:S(2)}, u32[]{:S(2)}) collective-permute-start(f32[64,1024]{1,0:T(8,128)S(1)} %maximum_select_fusion.4), channel_id=1, source_target_pairs={{0,64},{16,80},{32,96},{48,112},{64,0},{80,16},{96,32},{112,48},{1... | collective-permute-start | bytes 786440 | tf_op jit(solution)/shard_map/ppermute | solution.py:68
  20.1 16.3 %collective-permute-start.3 = (f32[56,2048]{1,0:T(8,128)S(1)}, f32[56,2048]{1,0:T(8,128)S(1)}, u32[]{:S(2)}, u32[]{:S(2)}) collective-permute-start(f32[56,2048]{1,0:T(8,128)S(1)} %maximum_select_fusion.3), channel_id=1, source_target_pairs={{0,8},{1,9},{2,10},{3,11},{4,12},{5,13},{6,14},{7,15},{8,0},{9,1},... | collective-permute-start | bytes 1376264 | tf_op jit(solution)/shard_map/ppermute | solution.py:68
  29.7 29.7 %collective-permute-start.7 = (f32[64,2048]{1,0:T(8,128)S(1)}, f32[64,2048]{1,0:T(8,128)S(1)}, u32[]{:S(2)}, u32[]{:S(2)}) collective-permute-start(f32[64,2048]{1,0:T(8,128)S(1)} %maximum_select_fusion.2), channel_id=1, source_target_pairs={{0,128},{16,144},{32,160},{48,176},{64,192},{80,208},{96,224},{112... | collective-permute-start | bytes 1572872 | tf_op jit(solution)/shard_map/ppermute | solution.py:68
  59.8 89.0 %copy-start.3 = (bf16[32,1024]{1,0:T(8,128)(2,1)S(1)}, bf16[32,1024]{1,0:T(8,128)(2,1)}, u32[]{:S(2)}) copy-start(bf16[32,1024]{1,0:T(8,128)(2,1)} %convert_element_type.71) | copy-start | bytes 196612
  59.8 88.9 %copy-start.6 = (f32[1024]{0:T(1024)S(1)}, f32[1024]{0:T(1024)}, u32[]{:S(2)}) copy-start(f32[1024]{0:T(1024)} %add.211) | copy-start | bytes 12292
  148.7 12.3 %collective-permute-start.20 = (f32[16,4096]{1,0:T(8,128)}, f32[16,4096]{1,0:T(8,128)S(1)}, u32[]{:S(2)}, u32[]{:S(2)}) collective-permute-start(f32[16,4096]{1,0:T(8,128)} %get-tuple-element.47), channel_id=1, source_target_pairs={{0,1},{1,0},{2,3},{3,2},{4,5},{5,4},{6,7},{7,6},{8,9},{9,8},{10,11... | collective-permute-start | bytes 786440 | tf_op jit(solution)/shard_map/ppermute | solution.py:111
  154.9 6.2 %copy-start.1 = (f32[16,4096]{1,0:T(8,128)S(1)}, f32[16,4096]{1,0:T(8,128)}, u32[]{:S(2)}) copy-start(f32[16,4096]{1,0:T(8,128)} %get-tuple-element.47) | copy-start | bytes 786436
  154.9 6.3 %copy-start.7 = (f32[16]{0:T(128)S(1)}, f32[16]{0:T(128)}, u32[]{:S(2)}) copy-start(f32[16]{0:T(128)} %multiply_reduce_fusion.4) | copy-start | bytes 196
  154.9 6.3 %copy-start.9 = (f32[16]{0:T(128)S(1)}, f32[16]{0:T(128)}, u32[]{:S(2)}) copy-start(f32[16]{0:T(128)} %multiply_reduce_fusion.5) | copy-start | bytes 196
  161.3 3.6 %collective-permute-start.9 = (f32[32]{0:T(128)S(1)}, f32[32]{0:T(128)S(1)}, u32[]{:S(2)}, u32[]{:S(2)}) collective-permute-start(f32[32]{0:T(128)S(1)} %pad_maximum_fusion.2), channel_id=1, source_target_pairs={{0,16},{16,0},{32,48},{48,32},{64,80},{80,64},{96,112},{112,96},{1... | collective-permute-start | bytes 392 | tf_op jit(solution)/shard_map/ppermute | solution.py:86
  161.7 3.2 %collective-permute-start.10 = (f32[32]{0:T(128)S(1)}, f32[32]{0:T(128)S(1)}, u32[]{:S(2)}, u32[]{:S(2)}) collective-permute-start(f32[32]{0:T(128)S(1)} %pad_maximum_fusion.2), channel_id=1, source_target_pairs={{0,17},{1,16},{2,19},{3,18},{4,21},{5,20},{6,23},{7,22},{8,25},{9,... | collective-permute-start | bytes 392 | tf_op jit(solution)/shard_map/ppermute | solution.py:87
  163.2 1.7 collective-permute-start.8
  164.9 3.7 %collective-permute-start.12 = (f32[32]{0:T(128)S(1)}, f32[32]{0:T(128)S(1)}, u32[]{:S(2)}, u32[]{:S(2)}) collective-permute-start(f32[32]{0:T(128)S(1)} %add_add_fusion.7), channel_id=1, source_target_pairs={{0,32},{16,48},{32,0},{48,16},{64,96},{80,112},{96,64},{112,80},{1... | collective-permute-start | bytes 392 | tf_op jit(solution)/shard_map/ppermute | solution.py:86
  165.0 4.6 %collective-permute-start.13 = (f32[32]{0:T(128)S(1)}, f32[32]{0:T(128)S(1)}, u32[]{:S(2)}, u32[]{:S(2)}) collective-permute-start(f32[32]{0:T(128)S(1)} %add_add_fusion.7), channel_id=1, source_target_pairs={{0,34},{1,35},{2,32},{3,33},{4,38},{5,39},{6,36},{7,37},{8,42},{9,... | collective-permute-start | bytes 392 | tf_op jit(solution)/shard_map/ppermute | solution.py:87
  167.9 3.6 %collective-permute-start.11 = (f32[32]{0:T(128)S(1)}, f32[32]{0:T(128)S(1)}, u32[]{:S(2)}, u32[]{:S(2)}) collective-permute-start(f32[32]{0:T(128)S(1)} %add_add_fusion.7), channel_id=1, source_target_pairs={{0,2},{1,3},{2,0},{3,1},{4,6},{5,7},{6,4},{7,5},{8,10},{9,11},{10,... | collective-permute-start | bytes 392 | tf_op jit(solution)/shard_map/ppermute | solution.py:85
  171.5 5.9 %collective-permute-start.15 = (f32[32]{0:T(128)S(1)}, f32[32]{0:T(128)S(1)}, u32[]{:S(2)}, u32[]{:S(2)}) collective-permute-start(f32[32]{0:T(128)S(1)} %add_add_fusion.6), channel_id=1, source_target_pairs={{0,64},{16,80},{32,96},{48,112},{64,0},{80,16},{96,32},{112,48},{1... | collective-permute-start | bytes 392 | tf_op jit(solution)/shard_map/ppermute | solution.py:86
  173.1 6.9 %collective-permute-start.16 = (f32[32]{0:T(128)S(1)}, f32[32]{0:T(128)S(1)}, u32[]{:S(2)}, u32[]{:S(2)}) collective-permute-start(f32[32]{0:T(128)S(1)} %add_add_fusion.6), channel_id=1, source_target_pairs={{0,68},{1,69},{2,70},{3,71},{4,64},{5,65},{6,66},{7,67},{8,76},{9,... | collective-permute-start | bytes 392 | tf_op jit(solution)/shard_map/ppermute | solution.py:87
  175.2 5.1 %collective-permute-start.14 = (f32[32]{0:T(128)S(1)}, f32[32]{0:T(128)S(1)}, u32[]{:S(2)}, u32[]{:S(2)}) collective-permute-start(f32[32]{0:T(128)S(1)} %add_add_fusion.6), channel_id=1, source_target_pairs={{0,4},{1,5},{2,6},{3,7},{4,0},{5,1},{6,2},{7,3},{8,12},{9,13},{10,... | collective-permute-start | bytes 392 | tf_op jit(solution)/shard_map/ppermute | solution.py:85
  180.3 8.9 %collective-permute-start.18 = (f32[32]{0:T(128)S(1)}, f32[32]{0:T(128)S(1)}, u32[]{:S(2)}, u32[]{:S(2)}) collective-permute-start(f32[32]{0:T(128)S(1)} %add_add_fusion.5), channel_id=1, source_target_pairs={{0,128},{16,144},{32,160},{48,176},{64,192},{80,208},{96,224},{112... | collective-permute-start | bytes 392 | tf_op jit(solution)/shard_map/ppermute | solution.py:86
  183.4 9.9 %collective-permute-start.19 = (f32[32]{0:T(128)S(1)}, f32[32]{0:T(128)S(1)}, u32[]{:S(2)}, u32[]{:S(2)}) collective-permute-start(f32[32]{0:T(128)S(1)} %add_add_fusion.5), channel_id=1, source_target_pairs={{0,136},{1,137},{2,138},{3,139},{4,140},{5,141},{6,142},{7,143},{8... | collective-permute-start | bytes 392 | tf_op jit(solution)/shard_map/ppermute | solution.py:87
  188.8 5.1 %collective-permute-start.17 = (f32[32]{0:T(128)S(1)}, f32[32]{0:T(128)S(1)}, u32[]{:S(2)}, u32[]{:S(2)}) collective-permute-start(f32[32]{0:T(128)S(1)} %add_add_fusion.5), channel_id=1, source_target_pairs={{0,8},{1,9},{2,10},{3,11},{4,12},{5,13},{6,14},{7,15},{8,0},{9,1},... | collective-permute-start | bytes 392 | tf_op jit(solution)/shard_map/ppermute | solution.py:85
  195.3 24.0 %copy-start.8 = (f32[64]{0:T(128)S(1)}, f32[64]{0:T(128)}, u32[]{:S(2)}) copy-start(f32[64]{0:T(128)} %param.16) | copy-start | bytes 772
  195.3 28.3 %copy-start = (f32[16,256]{1,0:T(8,128)S(1)}, f32[16,256]{1,0:T(8,128)}, u32[]{:S(2)}) copy-start(f32[16,256]{1,0:T(8,128)} %param.19) | copy-start | bytes 49156
  195.3 28.3 %copy-start.2 = (f32[16,256]{1,0:T(8,128)S(1)}, f32[16,256]{1,0:T(8,128)}, u32[]{:S(2)}) copy-start(f32[16,256]{1,0:T(8,128)} %param.17) | copy-start | bytes 49156
  195.3 28.3 %copy-start.5 = (f32[16,256]{1,0:T(8,128)S(1)}, f32[16,256]{1,0:T(8,128)}, u32[]{:S(2)}) copy-start(f32[16,256]{1,0:T(8,128)} %param.18) | copy-start | bytes 49156
  196.5 5.5 %collective-permute-start.36 = (f32[16,512]{1,0:T(8,128)S(1)}, f32[16,512]{1,0:T(8,128)S(1)}, u32[]{:S(2)}, u32[]{:S(2)}) collective-permute-start(f32[16,512]{1,0:T(8,128)S(1)} %slice_select_fusion), channel_id=1, source_target_pairs={{0,8},{1,9},{2,10},{3,11},{4,12},{5,13},{6,14},{7,15},{8,0},{9,1},... | collective-permute-start | bytes 98312 | tf_op jit(solution)/shard_map/ppermute | solution.py:105
  198.9 8.7 %collective-permute-start.21 = (f32[16,4096]{1,0:T(8,128)S(1)}, f32[16,4096]{1,0:T(8,128)S(1)}, u32[]{:S(2)}, u32[]{:S(2)}) collective-permute-start(f32[16,4096]{1,0:T(8,128)S(1)} %get-tuple-element.98), channel_id=1, source_target_pairs={{0,2},{1,3},{2,0},{3,1},{4,6},{5,7},{6,4},{7,5},{8,10},{9,11},{10,... | collective-permute-start | bytes 786440 | tf_op jit(solution)/shard_map/ppermute | solution.py:111
  202.1 5.5 %collective-permute-start.37 = (f32[16,256]{1,0:T(8,128)S(1)}, f32[16,256]{1,0:T(8,128)S(1)}, u32[]{:S(2)}, u32[]{:S(2)}) collective-permute-start(f32[16,256]{1,0:T(8,128)S(1)} %slice_select_fusion.1), channel_id=1, source_target_pairs={{0,4},{1,5},{2,6},{3,7},{4,0},{5,1},{6,2},{7,3},{8,12},{9,13},{10,... | collective-permute-start | bytes 49160 | tf_op jit(solution)/shard_map/ppermute | solution.py:105
  207.6 8.0 %collective-permute-start.22 = (f32[16,4096]{1,0:T(8,128)S(1)}, f32[16,4096]{1,0:T(8,128)S(1)}, u32[]{:S(2)}, u32[]{:S(2)}) collective-permute-start(f32[16,4096]{1,0:T(8,128)S(1)} %add.205), channel_id=1, source_target_pairs={{0,4},{1,5},{2,6},{3,7},{4,0},{5,1},{6,2},{7,3},{8,12},{9,13},{10,... | collective-permute-start | bytes 786440 | tf_op jit(solution)/shard_map/ppermute | solution.py:111
  210.7 4.6 %collective-permute-start.38 = (f32[16,128]{1,0:T(8,128)S(1)}, f32[16,128]{1,0:T(8,128)S(1)}, u32[]{:S(2)}, u32[]{:S(2)}) collective-permute-start(f32[16,128]{1,0:T(8,128)S(1)} %slice_select_fusion.3), channel_id=1, source_target_pairs={{0,2},{1,3},{2,0},{3,1},{4,6},{5,7},{6,4},{7,5},{8,10},{9,11},{10,... | collective-permute-start | bytes 24584 | tf_op jit(solution)/shard_map/ppermute | solution.py:105
  215.6 8.0 %collective-permute-start.23 = (f32[16,4096]{1,0:T(8,128)S(1)}, f32[16,4096]{1,0:T(8,128)S(1)}, u32[]{:S(2)}, u32[]{:S(2)}) collective-permute-start(f32[16,4096]{1,0:T(8,128)S(1)} %add.206), channel_id=1, source_target_pairs={{0,8},{1,9},{2,10},{3,11},{4,12},{5,13},{6,14},{7,15},{8,0},{9,1},... | collective-permute-start | bytes 786440 | tf_op jit(solution)/shard_map/ppermute | solution.py:111
  218.1 1.2 collective-permute-start.39
  224.4 33.8 %copy-start.4 = (f32[16,256]{1,0:T(8,128)}, f32[16,256]{1,0:T(8,128)S(1)}, u32[]{:S(2)}) copy-start(f32[16,256]{1,0:T(8,128)S(1)} %get-tuple-element.93) | copy-start | bytes 49156
  224.4 3.7 %collective-permute-start.25 = (f32[16]{0:T(128)S(1)}, f32[16]{0:T(128)S(1)}, u32[]{:S(2)}, u32[]{:S(2)}) collective-permute-start(f32[16]{0:T(128)S(1)} %get-tuple-element.48), channel_id=1, source_target_pairs={{0,16},{16,0},{32,48},{48,32},{64,80},{80,64},{96,112},{112,96},{1... | collective-permute-start | bytes 200 | tf_op jit(solution)/shard_map/ppermute | solution.py:86
  224.8 3.2 %collective-permute-start.26 = (f32[16]{0:T(128)S(1)}, f32[16]{0:T(128)S(1)}, u32[]{:S(2)}, u32[]{:S(2)}) collective-permute-start(f32[16]{0:T(128)S(1)} %get-tuple-element.48), channel_id=1, source_target_pairs={{0,17},{1,16},{2,19},{3,18},{4,21},{5,20},{6,23},{7,22},{8,25},{9,... | collective-permute-start | bytes 200 | tf_op jit(solution)/shard_map/ppermute | solution.py:87
  224.8 3.2 %collective-permute-start.24 = (f32[16]{0:T(128)S(1)}, f32[16]{0:T(128)S(1)}, u32[]{:S(2)}, u32[]{:S(2)}) collective-permute-start(f32[16]{0:T(128)S(1)} %get-tuple-element.48), channel_id=1, source_target_pairs={{0,1},{1,0},{2,3},{3,2},{4,5},{5,4},{6,7},{7,6},{8,9},{9,8},{10,11... | collective-permute-start | bytes 200 | tf_op jit(solution)/shard_map/ppermute | solution.py:85
  228.1 4.3 %collective-permute-start.28 = (f32[16]{0:T(128)S(1)}, f32[16]{0:T(128)S(1)}, u32[]{:S(2)}, u32[]{:S(2)}) collective-permute-start(f32[16]{0:T(128)S(1)} %add_add_fusion.3), channel_id=1, source_target_pairs={{0,32},{16,48},{32,0},{48,16},{64,96},{80,112},{96,64},{112,80},{1... | collective-permute-start | bytes 200 | tf_op jit(solution)/shard_map/ppermute | solution.py:86
  230.1 4.5 %collective-permute-start.29 = (f32[16]{0:T(128)S(1)}, f32[16]{0:T(128)S(1)}, u32[]{:S(2)}, u32[]{:S(2)}) collective-permute-start(f32[16]{0:T(128)S(1)} %add_add_fusion.3), channel_id=1, source_target_pairs={{0,34},{1,35},{2,32},{3,33},{4,38},{5,39},{6,36},{7,37},{8,42},{9,... | collective-permute-start | bytes 200 | tf_op jit(solution)/shard_map/ppermute | solution.py:87
  232.3 3.6 %collective-permute-start.27 = (f32[16]{0:T(128)S(1)}, f32[16]{0:T(128)S(1)}, u32[]{:S(2)}, u32[]{:S(2)}) collective-permute-start(f32[16]{0:T(128)S(1)} %add_add_fusion.3), channel_id=1, source_target_pairs={{0,2},{1,3},{2,0},{3,1},{4,6},{5,7},{6,4},{7,5},{8,10},{9,11},{10,... | collective-permute-start | bytes 200 | tf_op jit(solution)/shard_map/ppermute | solution.py:85
  235.9 5.9 %collective-permute-start.31 = (f32[16]{0:T(128)S(1)}, f32[16]{0:T(128)S(1)}, u32[]{:S(2)}, u32[]{:S(2)}) collective-permute-start(f32[16]{0:T(128)S(1)} %add_add_fusion.2), channel_id=1, source_target_pairs={{0,64},{16,80},{32,96},{48,112},{64,0},{80,16},{96,32},{112,48},{1... | collective-permute-start | bytes 200 | tf_op jit(solution)/shard_map/ppermute | solution.py:86
  237.2 6.9 %collective-permute-start.32 = (f32[16]{0:T(128)S(1)}, f32[16]{0:T(128)S(1)}, u32[]{:S(2)}, u32[]{:S(2)}) collective-permute-start(f32[16]{0:T(128)S(1)} %add_add_fusion.2), channel_id=1, source_target_pairs={{0,68},{1,69},{2,70},{3,71},{4,64},{5,65},{6,66},{7,67},{8,76},{9,... | collective-permute-start | bytes 200 | tf_op jit(solution)/shard_map/ppermute | solution.py:87
  238.6 5.5 %collective-permute-start.30 = (f32[16]{0:T(128)S(1)}, f32[16]{0:T(128)S(1)}, u32[]{:S(2)}, u32[]{:S(2)}) collective-permute-start(f32[16]{0:T(128)S(1)} %add_add_fusion.2), channel_id=1, source_target_pairs={{0,4},{1,5},{2,6},{3,7},{4,0},{5,1},{6,2},{7,3},{8,12},{9,13},{10,... | collective-permute-start | bytes 200 | tf_op jit(solution)/shard_map/ppermute | solution.py:85
  244.1 9.0 %collective-permute-start.34 = (f32[16]{0:T(128)S(1)}, f32[16]{0:T(128)S(1)}, u32[]{:S(2)}, u32[]{:S(2)}) collective-permute-start(f32[16]{0:T(128)S(1)} %add_add_fusion.1), channel_id=1, source_target_pairs={{0,128},{16,144},{32,160},{48,176},{64,192},{80,208},{96,224},{112... | collective-permute-start | bytes 200 | tf_op jit(solution)/shard_map/ppermute | solution.py:86
  247.6 9.9 %collective-permute-start.35 = (f32[16]{0:T(128)S(1)}, f32[16]{0:T(128)S(1)}, u32[]{:S(2)}, u32[]{:S(2)}) collective-permute-start(f32[16]{0:T(128)S(1)} %add_add_fusion.1), channel_id=1, source_target_pairs={{0,136},{1,137},{2,138},{3,139},{4,140},{5,141},{6,142},{7,143},{8... | collective-permute-start | bytes 200 | tf_op jit(solution)/shard_map/ppermute | solution.py:87
  251.3 6.1 %collective-permute-start.33 = (f32[16]{0:T(128)S(1)}, f32[16]{0:T(128)S(1)}, u32[]{:S(2)}, u32[]{:S(2)}) collective-permute-start(f32[16]{0:T(128)S(1)} %add_add_fusion.1), channel_id=1, source_target_pairs={{0,8},{1,9},{2,10},{3,11},{4,12},{5,13},{6,14},{7,15},{8,0},{9,1},... | collective-permute-start | bytes 200 | tf_op jit(solution)/shard_map/ppermute | solution.py:85

commit v4 on v2

--- a/solution.py
+++ b/solution.py
@@ -61,10 +61,17 @@
     return [(i, i ^ (1 << bit)) for i in range(size)]
 
 
+def bit_reversed(index, nbits):
+    out = 0
+    for bit in range(nbits):
+        out = out | (((index >> bit) & 1) << (nbits - 1 - bit))
+    return out
+
+
 def gather_last(x, axis_name, size):
     me = lax.axis_index(axis_name)
     buf = x
-    for bit in range(size.bit_length() - 1):
+    for bit in reversed(range(size.bit_length() - 1)):
         recv = lax.ppermute(buf, axis_name, xor_perm(size, bit))
         low = ((me >> bit) & 1) == 0
         buf = jnp.where(
@@ -76,7 +83,7 @@
 def reduce_scatter_last(x, axis_name, size):
     me = lax.axis_index(axis_name)
     buf = x
-    for bit in reversed(range(size.bit_length() - 1)):
+    for bit in range(size.bit_length() - 1):
         half = buf.shape[-1] // 2
         lower, upper = buf[..., :half], buf[..., half:]
         low = ((me >> bit) & 1) == 0
@@ -155,7 +162,8 @@
     residual_new_row = res_row - step_len[:, None] * image_row
 
     me_col = lax.axis_index("col")
-    image_vec = lax.dynamic_slice_in_dim(image_row, me_col * own, own, axis=1)
+    own_at = bit_reversed(me_col, n_col.bit_length() - 1) * own
+    image_vec = lax.dynamic_slice_in_dim(image_row, own_at, own, axis=1)
     weights_new = weights + step_len[:, None] * direction
     residual_new = residual - step_len[:, None] * image_vec
 

time: 193 us -> 193 us (level)
  waiting for transfers between devices: 39 us -> 56.5 us
  starting transfers between devices: 64.1 us -> 48.4 us
    ppermute x16, starting transfers between devices: 36.4 us -> 26.4 us  [gather_last(): recv = lax.ppermute(buf, axis_name, xor_perm(size, bit))]
    ppermute x12, waiting for transfers between devices: 27.9 us -> 37.1 us  [all_sum(): x = x + lax.ppermute(x, axis_name, xor_perm(size, bit))]
    ppermute x16, waiting for transfers between devices: 8.41 us -> 16.6 us  [gather_last(): recv = lax.ppermute(buf, axis_name, xor_perm(size, bit))]
    ppermute x12, starting transfers between devices: 19.6 us -> 16.6 us  [all_sum(): x = x + lax.ppermute(x, axis_name, xor_perm(size, bit))]
    ppermute x4, starting transfers between devices: 8.05 us -> 5.36 us  [reduce_scatter_last(): buf = keep + lax.ppermute(send, axis_name, xor_perm(size, bit))]
  transfers between devices with their start and end apart: 32 -> 32, of which waited for: 17 -> 19; matrix products, arithmetic and copies ran while one was open for 42% -> 41% of each run, Pallas kernels for 0% -> 0%
where the time goes in v4:
time: 193 us; the launch traced here: 192 us
  matrix products  76.1 us (39%)
  waiting for transfers between devices  56.5 us (29%)
  starting transfers between devices  48.4 us (25%)
  other arithmetic  5.84 us (3%)
  between operations  2.35 us (1%)
  local copies, waits for them, and re-layouts  2.04 us (1%)
    dot_general x16, matrix products, one_block(): lax.dot_general(vec_blk, kern_vals, contract_last, preferred_element_type...  61.5 us
    ppermute x12, waiting for transfers between devices, all_sum(): x = x + lax.ppermute(x, axis_name, xor_perm(size, bit))  37.1 us
    ppermute x16, starting transfers between devices, gather_last(): recv = lax.ppermute(buf, axis_name, xor_perm(size, bit))  26.4 us
    ppermute x12, starting transfers between devices, all_sum(): x = x + lax.ppermute(x, axis_name, xor_perm(size, bit))  16.6 us
    ppermute x16, waiting for transfers between devices, gather_last(): recv = lax.ppermute(buf, axis_name, xor_perm(size, bit))  16.6 us
    dot_general x2, matrix products, matern_block(): lax.dot_general(row_pts, col_pts, contract_first, preferred_element_type=...  12.2 us
    ppermute x4, starting transfers between devices, reduce_scatter_last(): buf = keep + lax.ppermute(send, axis_name, xor_perm(size, bit))  5.36 us
  transfers between devices with their start and end apart: 32, of which 19 were waited for; matrix products, arithmetic and copies ran while one was open for 41% of the time, Pallas kernels for 0%

profile of v4, /device:TPU:2, one launch (start us, length us, event | category | flops | bytes accessed | tf_op | source)
XLA Modules:
  0.0 191.7 jit_solution(13728960579138138253)
XLA Ops:
  2.2 7.2 %collective-permute-start.16 = (f32[32,256]{1,0:T(8,128)S(1)}, f32[32,256]{1,0:T(8,128)S(1)}, u32[]{:S(2)}, u32[]{:S(2)}) collective-permute-start(f32[32,256]{1,0:T(8,128)S(1)} %get-tuple-element.110), channel_id=1, source_target_pairs={{0,128},{16,144},{32,160},{48,176},{64,192},{80,208},{96,224},{112... | collective-permute-start | bytes 98312 | tf_op jit(solution)/shard_map/ppermute | solution.py:75
  9.4 3.2 %collective-permute-start = (f32[32,256]{1,0:T(8,128)S(1)}, f32[32,256]{1,0:T(8,128)S(1)}, u32[]{:S(2)}, u32[]{:S(2)}) collective-permute-start(f32[32,256]{1,0:T(8,128)S(1)} %get-tuple-element.112), channel_id=1, source_target_pairs={{0,8},{1,9},{2,10},{3,11},{4,12},{5,13},{6,14},{7,15},{8,0},{9,1},... | collective-permute-start | bytes 98312 | tf_op jit(solution)/shard_map/ppermute | solution.py:75
  12.6 0.8 divide_convert_fusion
  13.4 0.8 divide_convert_fusion.1
  14.7 4.9 %collective-permute-done.8 = bf16[32,320]{1,0:T(8,128)(2,1)S(1)} collective-permute-done((bf16[32,320]{1,0:T(8,128)(2,1)S(1)}, bf16[32,320]{1,0:T(8,128)(2,1)S(1)}, u32[]{:S(2)}, u32[]{:S(2)}) %collective-permute-start.8) | collective-permute-done | bytes 20512 | tf_op jit(solution)/shard_map/ppermute | solution.py:75
  19.7 2.2 %collective-permute-start.9 = (bf16[32,640]{1,0:T(8,128)(2,1)S(1)}, bf16[32,640]{1,0:T(8,128)(2,1)S(1)}, u32[]{:S(2)}, u32[]{:S(2)}) collective-permute-start(bf16[32,640]{1,0:T(8,128)(2,1)S(1)} %maximum_select_fusion.17), channel_id=1, source_target_pairs={{0,4},{1,5},{2,6},{3,7},{4,0},{5,1},{6,2},{7,3},{8,12},{9,13},{10,... | collective-permute-start | bytes 122888 | tf_op jit(solution)/shard_map/ppermute | solution.py:75
  22.4 1.6 collective-permute-start.5
  24.0 1.5 collective-permute-start.17
  25.5 1.2 collective-permute-start.10
  27.6 1.1 collective-permute-start.6
  28.7 1.4 collective-permute-done.10
  30.5 1.7 collective-permute-done.6
  32.3 1.6 collective-permute-start.7
  34.5 3.6 %collective-permute-done.7 = bf16[48,2048]{1,0:T(8,128)(2,1)S(1)} collective-permute-done((bf16[48,2048]{1,0:T(8,128)(2,1)S(1)}, bf16[48,2048]{1,0:T(8,128)(2,1)S(1)}, u32[]{:S(2)}, u32[]{:S(2)}) %collective-permute-start.7) | collective-permute-done | bytes 196640 | tf_op jit(solution)/shard_map/ppermute | solution.py:75
  38.6 62.2 %while.11 = (s32[]{:T(128)}, f32[16,4096]{1,0:T(8,128)S(1)}, bf16[16,16,256]{2,1,0:T(8,128)(2,1)S(1)}, f32[]{:T(128)}, f32[4096]{0:T(1024)S(1)}, /*index=5*/f32[...) while((s32[]{:T(128)}, f32[16,4096]{1,0:T(8,128)S(1)}, ...), condition=%wide.region_4.5_spmd.clone, body=%wide.region_3.4_spmd.clone.sunk | while | flops 113377280 | bytes 832126 | solution.py:51
  38.6 3.8 %convolution_add_fusion.3 = f32[16,4096]{1,0:T(8,128)S(1)} fusion(bf16[32,4096]{1,0:T(8,128)(2,1)S(1)} %get-tuple-element.193, f32[256]{0:T(256)S(1)} %bitcast.57, f32[4096]{0:T(1024)S(1)} %get-tuple-element.190, f32[]{:T(128)} %get-tuple-element.189, f32[16,4096]{1,0:T(8,128)S(1)} %get-tuple-element.177, pred[]{:T(512)S(6)} %compare.3, ...), kind=kOutput, calls=%fused_computation.4.clone.1 | convolution fusion | flops 113377280 | bytes 829956 | tf_op jit(solution)/shard_map/while/body/eval_jaxpr/dot_general | solution.py:44
  42.5 3.8 %convolution_add_fusion.3 = f32[16,4096]{1,0:T(8,128)S(1)} fusion(bf16[32,4096]{1,0:T(8,128)(2,1)S(1)} %get-tuple-element.193, f32[256]{0:T(256)S(1)} %bitcast.57, f32[4096]{0:T(1024)S(1)} %get-tuple-element.190, f32[]{:T(128)} %get-tuple-element.189, f32[16,4096]{1,0:T(8,128)S(1)} %get-tuple-element.177, pred[]{:T(512)S(6)} %compare.3, ...), kind=kOutput, calls=%fused_computation.4.clone.1 | convolution fusion | flops 113377280 | bytes 829956 | tf_op jit(solution)/shard_map/while/body/eval_jaxpr/dot_general | solution.py:44
  46.4 3.8 %convolution_add_fusion.3 = f32[16,4096]{1,0:T(8,128)S(1)} fusion(bf16[32,4096]{1,0:T(8,128)(2,1)S(1)} %get-tuple-element.193, f32[256]{0:T(256)S(1)} %bitcast.57, f32[4096]{0:T(1024)S(1)} %get-tuple-element.190, f32[]{:T(128)} %get-tuple-element.189, f32[16,4096]{1,0:T(8,128)S(1)} %get-tuple-element.177, pred[]{:T(512)S(6)} %compare.3, ...), kind=kOutput, calls=%fused_computation.4.clone.1 | convolution fusion | flops 113377280 | bytes 829956 | tf_op jit(solution)/shard_map/while/body/eval_jaxpr/dot_general | solution.py:44
  50.3 3.8 %convolution_add_fusion.3 = f32[16,4096]{1,0:T(8,128)S(1)} fusion(bf16[32,4096]{1,0:T(8,128)(2,1)S(1)} %get-tuple-element.193, f32[256]{0:T(256)S(1)} %bitcast.57, f32[4096]{0:T(1024)S(1)} %get-tuple-element.190, f32[]{:T(128)} %get-tuple-element.189, f32[16,4096]{1,0:T(8,128)S(1)} %get-tuple-element.177, pred[]{:T(512)S(6)} %compare.3, ...), kind=kOutput, calls=%fused_computation.4.clone.1 | convolution fusion | flops 113377280 | bytes 829956 | tf_op jit(solution)/shard_map/while/body/eval_jaxpr/dot_general | solution.py:44
  54.2 3.8 %convolution_add_fusion.3 = f32[16,4096]{1,0:T(8,128)S(1)} fusion(bf16[32,4096]{1,0:T(8,128)(2,1)S(1)} %get-tuple-element.193, f32[256]{0:T(256)S(1)} %bitcast.57, f32[4096]{0:T(1024)S(1)} %get-tuple-element.190, f32[]{:T(128)} %get-tuple-element.189, f32[16,4096]{1,0:T(8,128)S(1)} %get-tuple-element.177, pred[]{:T(512)S(6)} %compare.3, ...), kind=kOutput, calls=%fused_computation.4.clone.1 | convolution fusion | flops 113377280 | bytes 829956 | tf_op jit(solution)/shard_map/while/body/eval_jaxpr/dot_general | solution.py:44
  58.0 3.8 %convolution_add_fusion.3 = f32[16,4096]{1,0:T(8,128)S(1)} fusion(bf16[32,4096]{1,0:T(8,128)(2,1)S(1)} %get-tuple-element.193, f32[256]{0:T(256)S(1)} %bitcast.57, f32[4096]{0:T(1024)S(1)} %get-tuple-element.190, f32[]{:T(128)} %get-tuple-element.189, f32[16,4096]{1,0:T(8,128)S(1)} %get-tuple-element.177, pred[]{:T(512)S(6)} %compare.3, ...), kind=kOutput, calls=%fused_computation.4.clone.1 | convolution fusion | flops 113377280 | bytes 829956 | tf_op jit(solution)/shard_map/while/body/eval_jaxpr/dot_general | solution.py:44
  61.9 3.8 %convolution_add_fusion.3 = f32[16,4096]{1,0:T(8,128)S(1)} fusion(bf16[32,4096]{1,0:T(8,128)(2,1)S(1)} %get-tuple-element.193, f32[256]{0:T(256)S(1)} %bitcast.57, f32[4096]{0:T(1024)S(1)} %get-tuple-element.190, f32[]{:T(128)} %get-tuple-element.189, f32[16,4096]{1,0:T(8,128)S(1)} %get-tuple-element.177, pred[]{:T(512)S(6)} %compare.3, ...), kind=kOutput, calls=%fused_computation.4.clone.1 | convolution fusion | flops 113377280 | bytes 829956 | tf_op jit(solution)/shard_map/while/body/eval_jaxpr/dot_general | solution.py:44
  65.8 3.8 %convolution_add_fusion.3 = f32[16,4096]{1,0:T(8,128)S(1)} fusion(bf16[32,4096]{1,0:T(8,128)(2,1)S(1)} %get-tuple-element.193, f32[256]{0:T(256)S(1)} %bitcast.57, f32[4096]{0:T(1024)S(1)} %get-tuple-element.190, f32[]{:T(128)} %get-tuple-element.189, f32[16,4096]{1,0:T(8,128)S(1)} %get-tuple-element.177, pred[]{:T(512)S(6)} %compare.3, ...), kind=kOutput, calls=%fused_computation.4.clone.1 | convolution fusion | flops 113377280 | bytes 829956 | tf_op jit(solution)/shard_map/while/body/eval_jaxpr/dot_general | solution.py:44
  69.7 3.8 %convolution_add_fusion.3 = f32[16,4096]{1,0:T(8,128)S(1)} fusion(bf16[32,4096]{1,0:T(8,128)(2,1)S(1)} %get-tuple-element.193, f32[256]{0:T(256)S(1)} %bitcast.57, f32[4096]{0:T(1024)S(1)} %get-tuple-element.190, f32[]{:T(128)} %get-tuple-element.189, f32[16,4096]{1,0:T(8,128)S(1)} %get-tuple-element.177, pred[]{:T(512)S(6)} %compare.3, ...), kind=kOutput, calls=%fused_computation.4.clone.1 | convolution fusion | flops 113377280 | bytes 829956 | tf_op jit(solution)/shard_map/while/body/eval_jaxpr/dot_general | solution.py:44
  73.6 3.8 %convolution_add_fusion.3 = f32[16,4096]{1,0:T(8,128)S(1)} fusion(bf16[32,4096]{1,0:T(8,128)(2,1)S(1)} %get-tuple-element.193, f32[256]{0:T(256)S(1)} %bitcast.57, f32[4096]{0:T(1024)S(1)} %get-tuple-element.190, f32[]{:T(128)} %get-tuple-element.189, f32[16,4096]{1,0:T(8,128)S(1)} %get-tuple-element.177, pred[]{:T(512)S(6)} %compare.3, ...), kind=kOutput, calls=%fused_computation.4.clone.1 | convolution fusion | flops 113377280 | bytes 829956 | tf_op jit(solution)/shard_map/while/body/eval_jaxpr/dot_general | solution.py:44
  77.5 3.8 %convolution_add_fusion.3 = f32[16,4096]{1,0:T(8,128)S(1)} fusion(bf16[32,4096]{1,0:T(8,128)(2,1)S(1)} %get-tuple-element.193, f32[256]{0:T(256)S(1)} %bitcast.57, f32[4096]{0:T(1024)S(1)} %get-tuple-element.190, f32[]{:T(128)} %get-tuple-element.189, f32[16,4096]{1,0:T(8,128)S(1)} %get-tuple-element.177, pred[]{:T(512)S(6)} %compare.3, ...), kind=kOutput, calls=%fused_computation.4.clone.1 | convolution fusion | flops 113377280 | bytes 829956 | tf_op jit(solution)/shard_map/while/body/eval_jaxpr/dot_general | solution.py:44
  81.4 3.8 %convolution_add_fusion.3 = f32[16,4096]{1,0:T(8,128)S(1)} fusion(bf16[32,4096]{1,0:T(8,128)(2,1)S(1)} %get-tuple-element.193, f32[256]{0:T(256)S(1)} %bitcast.57, f32[4096]{0:T(1024)S(1)} %get-tuple-element.190, f32[]{:T(128)} %get-tuple-element.189, f32[16,4096]{1,0:T(8,128)S(1)} %get-tuple-element.177, pred[]{:T(512)S(6)} %compare.3, ...), kind=kOutput, calls=%fused_computation.4.clone.1 | convolution fusion | flops 113377280 | bytes 829956 | tf_op jit(solution)/shard_map/while/body/eval_jaxpr/dot_general | solution.py:44
  85.2 3.8 %convolution_add_fusion.3 = f32[16,4096]{1,0:T(8,128)S(1)} fusion(bf16[32,4096]{1,0:T(8,128)(2,1)S(1)} %get-tuple-element.193, f32[256]{0:T(256)S(1)} %bitcast.57, f32[4096]{0:T(1024)S(1)} %get-tuple-element.190, f32[]{:T(128)} %get-tuple-element.189, f32[16,4096]{1,0:T(8,128)S(1)} %get-tuple-element.177, pred[]{:T(512)S(6)} %compare.3, ...), kind=kOutput, calls=%fused_computation.4.clone.1 | convolution fusion | flops 113377280 | bytes 829956 | tf_op jit(solution)/shard_map/while/body/eval_jaxpr/dot_general | solution.py:44
  89.1 3.8 %convolution_add_fusion.3 = f32[16,4096]{1,0:T(8,128)S(1)} fusion(bf16[32,4096]{1,0:T(8,128)(2,1)S(1)} %get-tuple-element.193, f32[256]{0:T(256)S(1)} %bitcast.57, f32[4096]{0:T(1024)S(1)} %get-tuple-element.190, f32[]{:T(128)} %get-tuple-element.189, f32[16,4096]{1,0:T(8,128)S(1)} %get-tuple-element.177, pred[]{:T(512)S(6)} %compare.3, ...), kind=kOutput, calls=%fused_computation.4.clone.1 | convolution fusion | flops 113377280 | bytes 829956 | tf_op jit(solution)/shard_map/while/body/eval_jaxpr/dot_general | solution.py:44
  93.0 3.8 %convolution_add_fusion.3 = f32[16,4096]{1,0:T(8,128)S(1)} fusion(bf16[32,4096]{1,0:T(8,128)(2,1)S(1)} %get-tuple-element.193, f32[256]{0:T(256)S(1)} %bitcast.57, f32[4096]{0:T(1024)S(1)} %get-tuple-element.190, f32[]{:T(128)} %get-tuple-element.189, f32[16,4096]{1,0:T(8,128)S(1)} %get-tuple-element.177, pred[]{:T(512)S(6)} %compare.3, ...), kind=kOutput, calls=%fused_computation.4.clone.1 | convolution fusion | flops 113377280 | bytes 829956 | tf_op jit(solution)/shard_map/while/body/eval_jaxpr/dot_general | solution.py:44
  96.9 3.8 %convolution_add_fusion.3 = f32[16,4096]{1,0:T(8,128)S(1)} fusion(bf16[32,4096]{1,0:T(8,128)(2,1)S(1)} %get-tuple-element.193, f32[256]{0:T(256)S(1)} %bitcast.57, f32[4096]{0:T(1024)S(1)} %get-tuple-element.190, f32[]{:T(128)} %get-tuple-element.189, f32[16,4096]{1,0:T(8,128)S(1)} %get-tuple-element.177, pred[]{:T(512)S(6)} %compare.3, ...), kind=kOutput, calls=%fused_computation.4.clone.1 | convolution fusion | flops 113377280 | bytes 829956 | tf_op jit(solution)/shard_map/while/body/eval_jaxpr/dot_general | solution.py:44
  100.9 2.4 %collective-permute-start.1 = (f32[32,512]{1,0:T(8,128)S(1)}, f32[32,512]{1,0:T(8,128)S(1)}, u32[]{:S(2)}, u32[]{:S(2)}) collective-permute-start(f32[32,512]{1,0:T(8,128)S(1)} %maximum_select_fusion.14), channel_id=1, source_target_pairs={{0,4},{1,5},{2,6},{3,7},{4,0},{5,1},{6,2},{7,3},{8,12},{9,13},{10,... | collective-permute-start | bytes 196616 | tf_op jit(solution)/shard_map/ppermute | solution.py:75
  103.3 1.1 collective-permute-start.18
  105.7 1.5 collective-permute-done.1
  107.2 1.1 collective-permute-start.2
  108.3 1.1 collective-permute-start.13
  109.4 1.6 collective-permute-start.19
  111.0 2.6 %collective-permute-done.2 = f32[32,1024]{1,0:T(8,128)S(1)} collective-permute-done((f32[32,1024]{1,0:T(8,128)S(1)}, f32[32,1024]{1,0:T(8,128)S(1)}, u32[]{:S(2)}, u32[]{:S(2)}) %collective-permute-start.2) | collective-permute-done | bytes 131104 | tf_op jit(solution)/shard_map/ppermute | solution.py:75
  113.7 4.2 %collective-permute-done.13 = f32[16,4096]{1,0:T(8,128)S(1)} collective-permute-done((f32[16,4096]{1,0:T(8,128)S(1)}, f32[16,4096]{1,0:T(8,128)S(1)}, u32[]{:S(2)}, u32[]{:S(2)}) %collective-permute-start.13) | collective-permute-done | bytes 262176 | tf_op jit(solution)/shard_map/ppermute | solution.py:98
  117.9 2.2 %collective-permute-start.14 = (f32[16,4096]{1,0:T(8,128)S(1)}, f32[16,4096]{1,0:T(8,128)S(1)}, u32[]{:S(2)}, u32[]{:S(2)}) collective-permute-start(f32[16,4096]{1,0:T(8,128)S(1)} %add.140), channel_id=1, source_target_pairs={{0,4},{1,5},{2,6},{3,7},{4,0},{5,1},{6,2},{7,3},{8,12},{9,13},{10,... | collective-permute-start | bytes 786440 | tf_op jit(solution)/shard_map/ppermute | solution.py:98
  120.4 6.1 %collective-permute-done.14 = f32[16,4096]{1,0:T(8,128)S(1)} collective-permute-done((f32[16,4096]{1,0:T(8,128)S(1)}, f32[16,4096]{1,0:T(8,128)S(1)}, u32[]{:S(2)}, u32[]{:S(2)}) %collective-permute-start.14) | collective-permute-done | bytes 262176 | tf_op jit(solution)/shard_map/ppermute | solution.py:98
  126.5 3.3 %collective-permute-start.15 = (f32[16,4096]{1,0:T(8,128)S(1)}, f32[16,4096]{1,0:T(8,128)S(1)}, u32[]{:S(2)}, u32[]{:S(2)}) collective-permute-start(f32[16,4096]{1,0:T(8,128)S(1)} %add.141), channel_id=1, source_target_pairs={{0,8},{1,9},{2,10},{3,11},{4,12},{5,13},{6,14},{7,15},{8,0},{9,1},... | collective-permute-start | bytes 786440 | tf_op jit(solution)/shard_map/ppermute | solution.py:98
  129.9 4.6 %collective-permute-done.15 = f32[16,4096]{1,0:T(8,128)S(1)} collective-permute-done((f32[16,4096]{1,0:T(8,128)S(1)}, f32[16,4096]{1,0:T(8,128)S(1)}, u32[]{:S(2)}, u32[]{:S(2)}) %collective-permute-start.15) | collective-permute-done | bytes 262176 | tf_op jit(solution)/shard_map/ppermute | solution.py:98
  134.8 1.5 collective-permute-start.20
  136.3 6.1 %multiply_convert_fusion.2 = bf16[1024,2048]{1,0:T(8,128)(2,1)S(1)} fusion(bf16[32,1024]{1,0:T(8,128)(2,1)S(1)} %reshape.55, f32[2048]{0:T(1024)S(1)} %get-tuple-element.109, f32[1024]{0:T(1024)S(1)} %add.151, f32[]{:T(128)} %bitcast.47, bf16[48,4096]{1,0:T(8,128)(2,1)S(1)} %maximum_select_fusion.2), kind=kOutput, calls=%fused_computation.19 | convolution fusion | flops 159383552 | bytes 4403204 | tf_op jit(solution)/shard_map/dot_general | solution.py:19
  142.4 1.1 collective-permute-start.21
  143.6 6.1 %multiply_convert_fusion.1 = bf16[1024,2048]{1,0:T(8,128)(2,1)S(1)} fusion(bf16[32,1024]{1,0:T(8,128)(2,1)S(1)} %reshape.55, f32[2048]{0:T(1024)S(1)} %get-tuple-element.108, f32[1024]{0:T(1024)S(1)} %add.151, f32[]{:T(128)} %bitcast.48, bf16[48,4096]{1,0:T(8,128)(2,1)S(1)} %maximum_select_fusion.2), kind=kOutput, calls=%fused_computation.18 | convolution fusion | flops 159383552 | bytes 4403204 | tf_op jit(solution)/shard_map/dot_general | solution.py:19
  149.7 1.7 collective-permute-start.22
  151.4 3.0 %collective-permute-done.22 = f32[32]{0:T(128)S(1)} collective-permute-done((f32[32]{0:T(128)S(1)}, f32[32]{0:T(128)S(1)}, u32[]{:S(2)}, u32[]{:S(2)}) %collective-permute-start.22) | collective-permute-done | bytes 160 | tf_op jit(solution)/shard_map/ppermute | solution.py:98
  155.2 6.7 %collective-permute-done.23 = f32[32]{0:T(128)S(1)} collective-permute-done((f32[32]{0:T(128)S(1)}, f32[32]{0:T(128)S(1)}, u32[]{:S(2)}, u32[]{:S(2)}) %collective-permute-start.23) | collective-permute-done | bytes 160 | tf_op jit(solution)/shard_map/ppermute | solution.py:98
  162.3 1.2 fusion.22
  163.5 1.2 convolution_add_fusion.1
  164.8 1.2 collective-permute-done.28
  166.7 1.0 collective-permute-start.24
  167.7 2.5 %collective-permute-done.24 = f32[16]{0:T(128)S(1)} collective-permute-done((f32[16]{0:T(128)S(1)}, f32[16]{0:T(128)S(1)}, u32[]{:S(2)}, u32[]{:S(2)}) %collective-permute-start.24) | collective-permute-done | bytes 96 | tf_op jit(solution)/shard_map/ppermute | solution.py:98
  170.2 1.0 collective-permute-start.25
  171.2 2.6 %collective-permute-done.25 = f32[16]{0:T(128)S(1)} collective-permute-done((f32[16]{0:T(128)S(1)}, f32[16]{0:T(128)S(1)}, u32[]{:S(2)}, u32[]{:S(2)}) %collective-permute-start.25) | collective-permute-done | bytes 96 | tf_op jit(solution)/shard_map/ppermute | solution.py:98
  173.8 1.4 collective-permute-start.26
  175.2 3.0 %collective-permute-done.26 = f32[16]{0:T(128)S(1)} collective-permute-done((f32[16]{0:T(128)S(1)}, f32[16]{0:T(128)S(1)}, u32[]{:S(2)}, u32[]{:S(2)}) %collective-permute-start.26) | collective-permute-done | bytes 96 | tf_op jit(solution)/shard_map/ppermute | solution.py:98
  178.3 1.5 collective-permute-start.27
  179.8 1.7 collective-permute-start.30
  181.5 4.2 %collective-permute-done.27 = f32[16]{0:T(128)S(1)} collective-permute-done((f32[16]{0:T(128)S(1)}, f32[16]{0:T(128)S(1)}, u32[]{:S(2)}, u32[]{:S(2)}) %collective-permute-start.27) | collective-permute-done | bytes 96 | tf_op jit(solution)/shard_map/ppermute | solution.py:98
  185.8 2.9 %collective-permute-start.31 = (f32[16,64]{1,0:T(8,128)S(1)}, f32[16,64]{1,0:T(8,128)S(1)}, u32[]{:S(2)}, u32[]{:S(2)}) collective-permute-start(f32[16,64]{1,0:T(8,128)S(1)} %slice_select_fusion.2), channel_id=1, source_target_pairs={{0,8},{1,9},{2,10},{3,11},{4,12},{5,13},{6,14},{7,15},{8,0},{9,1},... | collective-permute-start | bytes 12296 | tf_op jit(solution)/shard_map/ppermute | solution.py:92
  189.5 1.6 collective-permute-done.31
  (115 shorter events, 9.3 us)
Async XLA Ops:
  2.2 21.8 %collective-permute-start.16 = (f32[32,256]{1,0:T(8,128)S(1)}, f32[32,256]{1,0:T(8,128)S(1)}, u32[]{:S(2)}, u32[]{:S(2)}) collective-permute-start(f32[32,256]{1,0:T(8,128)S(1)} %get-tuple-element.110), channel_id=1, source_target_pairs={{0,128},{16,144},{32,160},{48,176},{64,192},{80,208},{96,224},{112... | collective-permute-start | bytes 98312 | tf_op jit(solution)/shard_map/ppermute | solution.py:75
  9.4 91.5 %collective-permute-start = (f32[32,256]{1,0:T(8,128)S(1)}, f32[32,256]{1,0:T(8,128)S(1)}, u32[]{:S(2)}, u32[]{:S(2)}) collective-permute-start(f32[32,256]{1,0:T(8,128)S(1)} %get-tuple-element.112), channel_id=1, source_target_pairs={{0,8},{1,9},{2,10},{3,11},{4,12},{5,13},{6,14},{7,15},{8,0},{9,1},... | collective-permute-start | bytes 98312 | tf_op jit(solution)/shard_map/ppermute | solution.py:75
  14.2 5.4 %collective-permute-start.8 = (bf16[32,320]{1,0:T(8,128)(2,1)S(1)}, bf16[32,320]{1,0:T(8,128)(2,1)S(1)}, u32[]{:S(2)}, u32[]{:S(2)}) collective-permute-start(bf16[32,320]{1,0:T(8,128)(2,1)S(1)} %pad_maximum_fusion.1), channel_id=1, source_target_pairs={{0,8},{1,9},{2,10},{3,11},{4,12},{5,13},{6,14},{7,15},{8,0},{9,1},... | collective-permute-start | bytes 61448 | tf_op jit(solution)/shard_map/ppermute | solution.py:75
  14.6 7.7 %collective-permute-start.4 = (bf16[48,256]{1,0:T(8,128)(2,1)S(1)}, bf16[48,256]{1,0:T(8,128)(2,1)S(1)}, u32[]{:S(2)}, u32[]{:S(2)}) collective-permute-start(bf16[48,256]{1,0:T(8,128)(2,1)S(1)} %pad_maximum_fusion), channel_id=1, source_target_pairs={{0,128},{16,144},{32,160},{48,176},{64,192},{80,208},{96,224},{112... | collective-permute-start | bytes 73736 | tf_op jit(solution)/shard_map/ppermute | solution.py:75
  19.7 5.8 %collective-permute-start.9 = (bf16[32,640]{1,0:T(8,128)(2,1)S(1)}, bf16[32,640]{1,0:T(8,128)(2,1)S(1)}, u32[]{:S(2)}, u32[]{:S(2)}) collective-permute-start(bf16[32,640]{1,0:T(8,128)(2,1)S(1)} %maximum_select_fusion.17), channel_id=1, source_target_pairs={{0,4},{1,5},{2,6},{3,7},{4,0},{5,1},{6,2},{7,3},{8,12},{9,13},{10,... | collective-permute-start | bytes 122888 | tf_op jit(solution)/shard_map/ppermute | solution.py:75
  22.4 5.2 %collective-permute-start.5 = (bf16[48,512]{1,0:T(8,128)(2,1)S(1)}, bf16[48,512]{1,0:T(8,128)(2,1)S(1)}, u32[]{:S(2)}, u32[]{:S(2)}) collective-permute-start(bf16[48,512]{1,0:T(8,128)(2,1)S(1)} %maximum_select_fusion.16), channel_id=1, source_target_pairs={{0,64},{16,80},{32,96},{48,112},{64,0},{80,16},{96,32},{112,48},{1... | collective-permute-start | bytes 147464 | tf_op jit(solution)/shard_map/ppermute | solution.py:75
  24.0 79.3 %collective-permute-start.17 = (f32[32,512]{1,0:T(8,128)S(1)}, f32[32,512]{1,0:T(8,128)S(1)}, u32[]{:S(2)}, u32[]{:S(2)}) collective-permute-start(f32[32,512]{1,0:T(8,128)S(1)} %maximum_select_fusion.15), channel_id=1, source_target_pairs={{0,64},{16,80},{32,96},{48,112},{64,0},{80,16},{96,32},{112,48},{1... | collective-permute-start | bytes 196616 | tf_op jit(solution)/shard_map/ppermute | solution.py:75
  25.5 4.5 %collective-permute-start.10 = (bf16[32,1280]{1,0:T(8,128)(2,1)S(1)}, bf16[32,1280]{1,0:T(8,128)(2,1)S(1)}, u32[]{:S(2)}, u32[]{:S(2)}) collective-permute-start(bf16[32,1280]{1,0:T(8,128)(2,1)S(1)} %maximum_select_fusion.13), channel_id=1, source_target_pairs={{0,2},{1,3},{2,0},{3,1},{4,6},{5,7},{6,4},{7,5},{8,10},{9,11},{10,... | collective-permute-start | bytes 245768 | tf_op jit(solution)/shard_map/ppermute | solution.py:75
  27.6 4.7 %collective-permute-start.6 = (bf16[48,1024]{1,0:T(8,128)(2,1)S(1)}, bf16[48,1024]{1,0:T(8,128)(2,1)S(1)}, u32[]{:S(2)}, u32[]{:S(2)}) collective-permute-start(bf16[48,1024]{1,0:T(8,128)(2,1)S(1)} %maximum_select_fusion.11), channel_id=1, source_target_pairs={{0,32},{16,48},{32,0},{48,16},{64,96},{80,112},{96,64},{112,80},{1... | collective-permute-start | bytes 294920 | tf_op jit(solution)/shard_map/ppermute | solution.py:75
  30.1 3.8 %collective-permute-start.11 = (bf16[32,2560]{1,0:T(8,128)(2,1)S(1)}, bf16[32,2560]{1,0:T(8,128)(2,1)S(1)}, u32[]{:S(2)}, u32[]{:S(2)}) collective-permute-start(bf16[32,2560]{1,0:T(8,128)(2,1)S(1)} %maximum_select_fusion.8), channel_id=1, source_target_pairs={{0,1},{1,0},{2,3},{3,2},{4,5},{5,4},{6,7},{7,6},{8,9},{9,8},{10,11... | collective-permute-start | bytes 491528 | tf_op jit(solution)/shard_map/ppermute | solution.py:75
  32.3 5.8 %collective-permute-start.7 = (bf16[48,2048]{1,0:T(8,128)(2,1)S(1)}, bf16[48,2048]{1,0:T(8,128)(2,1)S(1)}, u32[]{:S(2)}, u32[]{:S(2)}) collective-permute-start(bf16[48,2048]{1,0:T(8,128)(2,1)S(1)} %maximum_select_fusion.6), channel_id=1, source_target_pairs={{0,16},{16,0},{32,48},{48,32},{64,80},{80,64},{96,112},{112,96},{1... | collective-permute-start | bytes 589832 | tf_op jit(solution)/shard_map/ppermute | solution.py:75
  100.8 7.5 %collective-permute-start.12 = (f32[16,4096]{1,0:T(8,128)S(1)}, f32[16,4096]{1,0:T(8,128)S(1)}, u32[]{:S(2)}, u32[]{:S(2)}) collective-permute-start(f32[16,4096]{1,0:T(8,128)S(1)} %get-tuple-element.48), channel_id=1, source_target_pairs={{0,1},{1,0},{2,3},{3,2},{4,5},{5,4},{6,7},{7,6},{8,9},{9,8},{10,11... | collective-permute-start | bytes 786440 | tf_op jit(solution)/shard_map/ppermute | solution.py:98
  100.9 6.3 %collective-permute-start.1 = (f32[32,512]{1,0:T(8,128)S(1)}, f32[32,512]{1,0:T(8,128)S(1)}, u32[]{:S(2)}, u32[]{:S(2)}) collective-permute-start(f32[32,512]{1,0:T(8,128)S(1)} %maximum_select_fusion.14), channel_id=1, source_target_pairs={{0,4},{1,5},{2,6},{3,7},{4,0},{5,1},{6,2},{7,3},{8,12},{9,13},{10,... | collective-permute-start | bytes 196616 | tf_op jit(solution)/shard_map/ppermute | solution.py:75
  103.3 6.1 %collective-permute-start.18 = (f32[32,1024]{1,0:T(8,128)S(1)}, f32[32,1024]{1,0:T(8,128)S(1)}, u32[]{:S(2)}, u32[]{:S(2)}) collective-permute-start(f32[32,1024]{1,0:T(8,128)S(1)} %maximum_select_fusion.10), channel_id=1, source_target_pairs={{0,32},{16,48},{32,0},{48,16},{64,96},{80,112},{96,64},{112,80},{1... | collective-permute-start | bytes 393224 | tf_op jit(solution)/shard_map/ppermute | solution.py:75
  107.2 6.5 %collective-permute-start.2 = (f32[32,1024]{1,0:T(8,128)S(1)}, f32[32,1024]{1,0:T(8,128)S(1)}, u32[]{:S(2)}, u32[]{:S(2)}) collective-permute-start(f32[32,1024]{1,0:T(8,128)S(1)} %maximum_select_fusion.9), channel_id=1, source_target_pairs={{0,2},{1,3},{2,0},{3,1},{4,6},{5,7},{6,4},{7,5},{8,10},{9,11},{10,... | collective-permute-start | bytes 393224 | tf_op jit(solution)/shard_map/ppermute | solution.py:75
  108.3 9.6 %collective-permute-start.13 = (f32[16,4096]{1,0:T(8,128)S(1)}, f32[16,4096]{1,0:T(8,128)S(1)}, u32[]{:S(2)}, u32[]{:S(2)}) collective-permute-start(f32[16,4096]{1,0:T(8,128)S(1)} %add.139), channel_id=1, source_target_pairs={{0,2},{1,3},{2,0},{3,1},{4,6},{5,7},{6,4},{7,5},{8,10},{9,11},{10,... | collective-permute-start | bytes 786440 | tf_op jit(solution)/shard_map/ppermute | solution.py:98
  109.4 45.7 %collective-permute-start.19 = (f32[32,2048]{1,0:T(8,128)S(1)}, f32[32,2048]{1,0:T(8,128)S(1)}, u32[]{:S(2)}, u32[]{:S(2)}) collective-permute-start(f32[32,2048]{1,0:T(8,128)S(1)} %maximum_select_fusion.5), channel_id=1, source_target_pairs={{0,16},{16,0},{32,48},{48,32},{64,80},{80,64},{96,112},{112,96},{1... | collective-permute-start | bytes 786440 | tf_op jit(solution)/shard_map/ppermute | solution.py:75
  113.6 16.2 %collective-permute-start.3 = (f32[32,2048]{1,0:T(8,128)S(1)}, f32[32,2048]{1,0:T(8,128)S(1)}, u32[]{:S(2)}, u32[]{:S(2)}) collective-permute-start(f32[32,2048]{1,0:T(8,128)S(1)} %maximum_select_fusion.4), channel_id=1, source_target_pairs={{0,1},{1,0},{2,3},{3,2},{4,5},{5,4},{6,7},{7,6},{8,9},{9,8},{10,11... | collective-permute-start | bytes 786440 | tf_op jit(solution)/shard_map/ppermute | solution.py:75
  117.9 8.6 %collective-permute-start.14 = (f32[16,4096]{1,0:T(8,128)S(1)}, f32[16,4096]{1,0:T(8,128)S(1)}, u32[]{:S(2)}, u32[]{:S(2)}) collective-permute-start(f32[16,4096]{1,0:T(8,128)S(1)} %add.140), channel_id=1, source_target_pairs={{0,4},{1,5},{2,6},{3,7},{4,0},{5,1},{6,2},{7,3},{8,12},{9,13},{10,... | collective-permute-start | bytes 786440 | tf_op jit(solution)/shard_map/ppermute | solution.py:98
  126.5 8.0 %collective-permute-start.15 = (f32[16,4096]{1,0:T(8,128)S(1)}, f32[16,4096]{1,0:T(8,128)S(1)}, u32[]{:S(2)}, u32[]{:S(2)}) collective-permute-start(f32[16,4096]{1,0:T(8,128)S(1)} %add.141), channel_id=1, source_target_pairs={{0,8},{1,9},{2,10},{3,11},{4,12},{5,13},{6,14},{7,15},{8,0},{9,1},... | collective-permute-start | bytes 786440 | tf_op jit(solution)/shard_map/ppermute | solution.py:98
  134.8 7.6 %collective-permute-start.20 = (f32[32]{0:T(128)S(1)}, f32[32]{0:T(128)S(1)}, u32[]{:S(2)}, u32[]{:S(2)}) collective-permute-start(f32[32]{0:T(128)S(1)} %pad_maximum_fusion.2), channel_id=1, source_target_pairs={{0,16},{16,0},{32,48},{48,32},{64,80},{80,64},{96,112},{112,96},{1... | collective-permute-start | bytes 392 | tf_op jit(solution)/shard_map/ppermute | solution.py:98
  142.4 7.2 %collective-permute-start.21 = (f32[32]{0:T(128)S(1)}, f32[32]{0:T(128)S(1)}, u32[]{:S(2)}, u32[]{:S(2)}) collective-permute-start(f32[32]{0:T(128)S(1)} %add.144), channel_id=1, source_target_pairs={{0,32},{16,48},{32,0},{48,16},{64,96},{80,112},{96,64},{112,80},{1... | collective-permute-start | bytes 392 | tf_op jit(solution)/shard_map/ppermute | solution.py:98
  149.7 4.8 %collective-permute-start.22 = (f32[32]{0:T(128)S(1)}, f32[32]{0:T(128)S(1)}, u32[]{:S(2)}, u32[]{:S(2)}) collective-permute-start(f32[32]{0:T(128)S(1)} %add.145), channel_id=1, source_target_pairs={{0,64},{16,80},{32,96},{48,112},{64,0},{80,16},{96,32},{112,48},{1... | collective-permute-start | bytes 392 | tf_op jit(solution)/shard_map/ppermute | solution.py:98
  154.5 7.5 %collective-permute-start.23 = (f32[32]{0:T(128)S(1)}, f32[32]{0:T(128)S(1)}, u32[]{:S(2)}, u32[]{:S(2)}) collective-permute-start(f32[32]{0:T(128)S(1)} %add.146), channel_id=1, source_target_pairs={{0,128},{16,144},{32,160},{48,176},{64,192},{80,208},{96,224},{112... | collective-permute-start | bytes 392 | tf_op jit(solution)/shard_map/ppermute | solution.py:98
  162.2 26.5 %copy-start = (f32[16,256]{1,0:T(8,128)S(1)}, f32[16,256]{1,0:T(8,128)}, u32[]{:S(2)}) copy-start(f32[16,256]{1,0:T(8,128)} %param.19) | copy-start | bytes 49156
  162.3 26.5 %copy-start.1 = (f32[16,256]{1,0:T(8,128)S(1)}, f32[16,256]{1,0:T(8,128)}, u32[]{:S(2)}) copy-start(f32[16,256]{1,0:T(8,128)} %param.18) | copy-start | bytes 49156
  162.3 26.5 %copy-start.2 = (f32[16,256]{1,0:T(8,128)S(1)}, f32[16,256]{1,0:T(8,128)}, u32[]{:S(2)}) copy-start(f32[16,256]{1,0:T(8,128)} %param.17) | copy-start | bytes 49156
  162.3 28.7 %copy-start.3 = (f32[64]{0:T(128)S(1)}, f32[64]{0:T(128)}, u32[]{:S(2)}) copy-start(f32[64]{0:T(128)} %param.16) | copy-start | bytes 772
  164.7 1.3 collective-permute-start.28
  166.0 13.7 %collective-permute-start.29 = (f32[16,256]{1,0:T(8,128)S(1)}, f32[16,256]{1,0:T(8,128)S(1)}, u32[]{:S(2)}, u32[]{:S(2)}) collective-permute-start(f32[16,256]{1,0:T(8,128)S(1)} %slice_select_fusion.1), channel_id=1, source_target_pairs={{0,2},{1,3},{2,0},{3,1},{4,6},{5,7},{6,4},{7,5},{8,10},{9,11},{10,... | collective-permute-start | bytes 49160 | tf_op jit(solution)/shard_map/ppermute | solution.py:92
  166.7 3.6 %collective-permute-start.24 = (f32[16]{0:T(128)S(1)}, f32[16]{0:T(128)S(1)}, u32[]{:S(2)}, u32[]{:S(2)}) collective-permute-start(f32[16]{0:T(128)S(1)} %get-tuple-element.50), channel_id=1, source_target_pairs={{0,16},{16,0},{32,48},{48,32},{64,80},{80,64},{96,112},{112,96},{1... | collective-permute-start | bytes 200 | tf_op jit(solution)/shard_map/ppermute | solution.py:98
  170.2 3.6 %collective-permute-start.25 = (f32[16]{0:T(128)S(1)}, f32[16]{0:T(128)S(1)}, u32[]{:S(2)}, u32[]{:S(2)}) collective-permute-start(f32[16]{0:T(128)S(1)} %add.162), channel_id=1, source_target_pairs={{0,32},{16,48},{32,0},{48,16},{64,96},{80,112},{96,64},{112,80},{1... | collective-permute-start | bytes 200 | tf_op jit(solution)/shard_map/ppermute | solution.py:98
  173.8 4.5 %collective-permute-start.26 = (f32[16]{0:T(128)S(1)}, f32[16]{0:T(128)S(1)}, u32[]{:S(2)}, u32[]{:S(2)}) collective-permute-start(f32[16]{0:T(128)S(1)} %add.163), channel_id=1, source_target_pairs={{0,64},{16,80},{32,96},{48,112},{64,0},{80,16},{96,32},{112,48},{1... | collective-permute-start | bytes 200 | tf_op jit(solution)/shard_map/ppermute | solution.py:98
  178.3 7.5 %collective-permute-start.27 = (f32[16]{0:T(128)S(1)}, f32[16]{0:T(128)S(1)}, u32[]{:S(2)}, u32[]{:S(2)}) collective-permute-start(f32[16]{0:T(128)S(1)} %add.164), channel_id=1, source_target_pairs={{0,128},{16,144},{32,160},{48,176},{64,192},{80,208},{96,224},{112... | collective-permute-start | bytes 200 | tf_op jit(solution)/shard_map/ppermute | solution.py:98
  179.8 6.0 %collective-permute-start.30 = (f32[16,128]{1,0:T(8,128)S(1)}, f32[16,128]{1,0:T(8,128)S(1)}, u32[]{:S(2)}, u32[]{:S(2)}) collective-permute-start(f32[16,128]{1,0:T(8,128)S(1)} %slice_select_fusion.3), channel_id=1, source_target_pairs={{0,4},{1,5},{2,6},{3,7},{4,0},{5,1},{6,2},{7,3},{8,12},{9,13},{10,... | collective-permute-start | bytes 24584 | tf_op jit(solution)/shard_map/ppermute | solution.py:92
  185.8 5.2 %collective-permute-start.31 = (f32[16,64]{1,0:T(8,128)S(1)}, f32[16,64]{1,0:T(8,128)S(1)}, u32[]{:S(2)}, u32[]{:S(2)}) collective-permute-start(f32[16,64]{1,0:T(8,128)S(1)} %slice_select_fusion.2), channel_id=1, source_target_pairs={{0,8},{1,9},{2,10},{3,11},{4,12},{5,13},{6,14},{7,15},{8,0},{9,1},... | collective-permute-start | bytes 12296 | tf_op jit(solution)/shard_map/ppermute | solution.py:92

commit v5 on v4

--- a/solution.py
+++ b/solution.py
@@ -115,23 +115,50 @@
     scaled = (points / length_scales[:, None]).astype(jnp.bfloat16)
     cand_scaled = (candidates / length_scales[:, None]).astype(jnp.bfloat16)
     signal_scalar = signal_var[0]
-    dir_low = direction.astype(jnp.bfloat16)
     cols, own = direction.shape
     own_cand = cand_scaled.shape[1]
     feats = scaled.shape[0]
 
-    row_pack = gather_last(jnp.concatenate([scaled, cand_scaled], 1), "col", n_col)
-    row_pack = row_pack.reshape(feats, n_col, own + own_cand)
-    row_pts = row_pack[:, :, :own].reshape(feats, n_col * own)
-    row_cands = row_pack[:, :, own:].reshape(feats, n_col * own_cand)
-    col_pack = gather_last(jnp.concatenate([scaled, dir_low], 0), "row", n_row)
+    def split(x):
+        lo = x - lax.reduce_precision(x, exponent_bits=8, mantissa_bits=7)
+        return x.astype(jnp.bfloat16), lo.astype(jnp.bfloat16)
+
+    def join(hi, lo):
+        return hi.astype(jnp.float32) + lo.astype(jnp.float32)
+
+    dir_hi, dir_lo = split(direction)
+    res_hi, res_lo = split(residual)
+    w_hi, w_lo = split(weights)
+    cand_rows = own_cand * feats // own
+    row_pack = gather_last(
+        jnp.concatenate(
+            [scaled, cand_scaled.reshape(cand_rows, own), dir_hi, dir_lo, res_hi, res_lo],
+            0,
+        ),
+        "col",
+        n_col,
+    )
+    row_pts = row_pack[:feats]
+    row_cands = (
+        row_pack[feats:feats + cand_rows]
+        .reshape(cand_rows, n_col, own)
+        .transpose(1, 0, 2)
+        .reshape(n_col, feats, own_cand)
+        .transpose(1, 0, 2)
+        .reshape(feats, n_col * own_cand)
+    )
+    at = feats + cand_rows
+    dir_row = join(row_pack[at:at + cols], row_pack[at + cols:at + 2 * cols])
+    at += 2 * cols
+    res_row = join(row_pack[at:at + cols], row_pack[at + cols:at + 2 * cols])
+    col_pack = gather_last(
+        jnp.concatenate([scaled, dir_hi, dir_lo, w_hi, w_lo], 0), "row", n_row
+    )
     col_pts = col_pack[:feats]
-    col_dir = col_pack[feats:]
-    row_state = gather_last(jnp.concatenate([residual, direction], 0), "col", n_col)
-    res_row, dir_row = row_state[:cols], row_state[cols:]
-    col_state = gather_last(jnp.concatenate([weights, direction], 0), "row", n_row)
-    w_col, d_col = col_state[:cols], col_state[cols:]
-
+    col_dir = col_pack[feats:feats + cols]
+    d_col = join(col_dir, col_pack[feats + cols:feats + 2 * cols])
+    at = feats + 2 * cols
+    w_col = join(col_pack[at:at + cols], col_pack[at + cols:at + 2 * cols])
     row_sq = square_norms(row_pts)
     col_sq = square_norms(col_pts)
     cand_sq = square_norms(row_cands)
@@ -163,7 +190,10 @@
 
     me_col = lax.axis_index("col")
     own_at = bit_reversed(me_col, n_col.bit_length() - 1) * own
-    image_vec = lax.dynamic_slice_in_dim(image_row, own_at, own, axis=1)
+    image_vec = (
+        lax.dynamic_slice_in_dim(kernel_row, own_at, own, axis=1)
+        + noise_var[0] * direction
+    )
     weights_new = weights + step_len[:, None] * direction
     residual_new = residual - step_len[:, None] * image_vec
 

time: 193 us -> 189 us (0.979)
  starting transfers between devices: 48.4 us -> 32 us
  waiting for transfers between devices: 56.5 us -> 66.3 us
  other arithmetic: 5.84 us -> 9.15 us
    ppermute x16 -> x8, starting transfers between devices: 26.4 us -> 15.7 us  [gather_last(): recv = lax.ppermute(buf, axis_name, xor_perm(size, bit))]
    ppermute x12, waiting for transfers between devices: 37.1 us -> 45 us  [all_sum(): x = x + lax.ppermute(x, axis_name, xor_perm(size, bit))]
    ppermute x12, starting transfers between devices: 16.6 us -> 11 us  [all_sum(): x = x + lax.ppermute(x, axis_name, xor_perm(size, bit))]
    unnamed x1 -> x6, other arithmetic: 0.01 us -> 3.72 us
    ppermute x16 -> x8, waiting for transfers between devices: 16.6 us -> 17.6 us  [gather_last(): recv = lax.ppermute(buf, axis_name, xor_perm(size, bit))]
  transfers between devices with their start and end apart: 32 -> 24, of which waited for: 19 -> 18; matrix products, arithmetic and copies ran while one was open for 41% -> 8% of each run, Pallas kernels for 0% -> 0%
where the time goes in v5:
time: 189 us; the launch traced here: 187 us
  matrix products  76.2 us (40%)
  waiting for transfers between devices  66.3 us (35%)
  starting transfers between devices  32 us (17%)
  other arithmetic  9.15 us (5%)
  between operations  2.29 us (1%)
    dot_general x16, matrix products, one_block(): lax.dot_general(vec_blk, kern_vals, contract_last, preferred_element_type...  61.6 us
    ppermute x12, waiting for transfers between devices, all_sum(): x = x + lax.ppermute(x, axis_name, xor_perm(size, bit))  45 us
    ppermute x8, waiting for transfers between devices, gather_last(): recv = lax.ppermute(buf, axis_name, xor_perm(size, bit))  17.6 us
    ppermute x8, starting transfers between devices, gather_last(): recv = lax.ppermute(buf, axis_name, xor_perm(size, bit))  15.7 us
    dot_general x2, matrix products, matern_block(): lax.dot_general(row_pts, col_pts, contract_first, preferred_element_type=...  12.2 us
    ppermute x12, starting transfers between devices, all_sum(): x = x + lax.ppermute(x, axis_name, xor_perm(size, bit))  11 us
    ppermute x4, starting transfers between devices, reduce_scatter_last(): buf = keep + lax.ppermute(send, axis_name, xor_perm(size, bit))  5.27 us
    ppermute x4, waiting for transfers between devices, reduce_scatter_last(): buf = keep + lax.ppermute(send, axis_name, xor_perm(size, bit))  3.79 us
  transfers between devices with their start and end apart: 24, of which 18 were waited for; matrix products, arithmetic and copies ran while one was open for 8% of the time, Pallas kernels for 0%

profile of v5, /device:TPU:2, one launch (start us, length us, event | category | flops | bytes accessed | tf_op | source)
XLA Modules:
  0.0 187.2 jit_solution(4334730949950630265)
XLA Ops:
  0.6 0.8 constant_dynamic-update-slice_fusion.10
  1.5 0.8 divide_convert_fusion.1
  2.4 0.7 constant_dynamic-update-slice_fusion.9
  3.1 0.7 constant_dynamic-update-slice_fusion.8
  3.8 0.7 constant_dynamic-update-slice_fusion.7
  4.5 0.7 constant_dynamic-update-slice_fusion.6
  5.3 7.2 %collective-permute-start.4 = (bf16[96,256]{1,0:T(8,128)(2,1)S(1)}, bf16[96,256]{1,0:T(8,128)(2,1)S(1)}, u32[]{:S(2)}, u32[]{:S(2)}) collective-permute-start(bf16[96,256]{1,0:T(8,128)(2,1)S(1)} %constant_dynamic-update-slice_fusion.6), channel_id=1, source_target_pairs={{0,128},{16,144},{32,160},{48,176},{64,192},{80,208},{96,224},{112... | collective-permute-start | bytes 147464 | tf_op jit(solution)/shard_map/ppermute | solution.py:75
  12.4 0.7 constant_dynamic-update-slice_fusion.1
  13.2 0.7 constant_dynamic-update-slice_fusion
  13.9 3.2 %collective-permute-start = (bf16[104,256]{1,0:T(8,128)(2,1)S(1)}, bf16[104,256]{1,0:T(8,128)(2,1)S(1)}, u32[]{:S(2)}, u32[]{:S(2)}) collective-permute-start(bf16[104,256]{1,0:T(8,128)(2,1)S(1)} %constant_dynamic-update-slice_fusion), channel_id=1, source_target_pairs={{0,8},{1,9},{2,10},{3,11},{4,12},{5,13},{6,14},{7,15},{8,0},{9,1},... | collective-permute-start | bytes 159752 | tf_op jit(solution)/shard_map/ppermute | solution.py:75
  17.1 1.6 collective-permute-start.5
  18.7 0.9 collective-permute-done
  19.5 2.2 %collective-permute-start.1 = (bf16[104,512]{1,0:T(8,128)(2,1)S(1)}, bf16[104,512]{1,0:T(8,128)(2,1)S(1)}, u32[]{:S(2)}, u32[]{:S(2)}) collective-permute-start(bf16[104,512]{1,0:T(8,128)(2,1)S(1)} %maximum_select_fusion.6), channel_id=1, source_target_pairs={{0,4},{1,5},{2,6},{3,7},{4,0},{5,1},{6,2},{7,3},{8,12},{9,13},{10,... | collective-permute-start | bytes 319496 | tf_op jit(solution)/shard_map/ppermute | solution.py:75
  21.8 2.4 %collective-permute-done.5 = bf16[96,512]{1,0:T(8,128)(2,1)S(1)} collective-permute-done((bf16[96,512]{1,0:T(8,128)(2,1)S(1)}, bf16[96,512]{1,0:T(8,128)(2,1)S(1)}, u32[]{:S(2)}, u32[]{:S(2)}) %collective-permute-start.5) | collective-permute-done | bytes 98336 | tf_op jit(solution)/shard_map/ppermute | solution.py:75
  24.4 1.5 collective-permute-done.1
  25.9 0.6 collective-permute-start.2
  26.5 4.1 %collective-permute-done.6 = bf16[96,1024]{1,0:T(8,128)(2,1)S(1)} collective-permute-done((bf16[96,1024]{1,0:T(8,128)(2,1)S(1)}, bf16[96,1024]{1,0:T(8,128)(2,1)S(1)}, u32[]{:S(2)}, u32[]{:S(2)}) %collective-permute-start.6) | collective-permute-done | bytes 196640 | tf_op jit(solution)/shard_map/ppermute | solution.py:75
  30.7 0.8 collective-permute-start.7
  32.1 8.4 %collective-permute-done.7 = bf16[96,2048]{1,0:T(8,128)(2,1)S(1)} collective-permute-done((bf16[96,2048]{1,0:T(8,128)(2,1)S(1)}, bf16[96,2048]{1,0:T(8,128)(2,1)S(1)}, u32[]{:S(2)}, u32[]{:S(2)}) %collective-permute-start.7) | collective-permute-done | bytes 393248 | tf_op jit(solution)/shard_map/ppermute | solution.py:75
  41.1 62.3 %while.11 = (s32[]{:T(128)}, f32[16,4096]{1,0:T(8,128)S(1)}, bf16[16,16,256]{2,1,0:T(8,128)(2,1)S(1)}, f32[]{:T(128)}, f32[4096]{0:T(1024)S(1)}, /*index=5*/f32[...) while((s32[]{:T(128)}, f32[16,4096]{1,0:T(8,128)S(1)}, ...), condition=%wide.region_4.5_spmd.clone, body=%wide.region_3.4_spmd.clone.sunk | while | flops 113377280 | bytes 832126 | solution.py:51
  41.2 3.9 %convolution_add_fusion.3 = f32[16,4096]{1,0:T(8,128)S(1)} fusion(bf16[32,4096]{1,0:T(8,128)(2,1)S(1)} %get-tuple-element.186, f32[256]{0:T(256)S(1)} %bitcast.65, f32[4096]{0:T(1024)S(1)} %get-tuple-element.183, f32[]{:T(128)} %get-tuple-element.182, f32[16,4096]{1,0:T(8,128)S(1)} %get-tuple-element.170, pred[]{:T(512)S(6)} %compare.3, ...), kind=kOutput, calls=%fused_computation.4.clone.1 | convolution fusion | flops 113377280 | bytes 829956 | tf_op jit(solution)/shard_map/while/body/eval_jaxpr/dot_general | solution.py:44
  45.1 3.9 %convolution_add_fusion.3 = f32[16,4096]{1,0:T(8,128)S(1)} fusion(bf16[32,4096]{1,0:T(8,128)(2,1)S(1)} %get-tuple-element.186, f32[256]{0:T(256)S(1)} %bitcast.65, f32[4096]{0:T(1024)S(1)} %get-tuple-element.183, f32[]{:T(128)} %get-tuple-element.182, f32[16,4096]{1,0:T(8,128)S(1)} %get-tuple-element.170, pred[]{:T(512)S(6)} %compare.3, ...), kind=kOutput, calls=%fused_computation.4.clone.1 | convolution fusion | flops 113377280 | bytes 829956 | tf_op jit(solution)/shard_map/while/body/eval_jaxpr/dot_general | solution.py:44
  49.0 3.8 %convolution_add_fusion.3 = f32[16,4096]{1,0:T(8,128)S(1)} fusion(bf16[32,4096]{1,0:T(8,128)(2,1)S(1)} %get-tuple-element.186, f32[256]{0:T(256)S(1)} %bitcast.65, f32[4096]{0:T(1024)S(1)} %get-tuple-element.183, f32[]{:T(128)} %get-tuple-element.182, f32[16,4096]{1,0:T(8,128)S(1)} %get-tuple-element.170, pred[]{:T(512)S(6)} %compare.3, ...), kind=kOutput, calls=%fused_computation.4.clone.1 | convolution fusion | flops 113377280 | bytes 829956 | tf_op jit(solution)/shard_map/while/body/eval_jaxpr/dot_general | solution.py:44
  52.9 3.8 %convolution_add_fusion.3 = f32[16,4096]{1,0:T(8,128)S(1)} fusion(bf16[32,4096]{1,0:T(8,128)(2,1)S(1)} %get-tuple-element.186, f32[256]{0:T(256)S(1)} %bitcast.65, f32[4096]{0:T(1024)S(1)} %get-tuple-element.183, f32[]{:T(128)} %get-tuple-element.182, f32[16,4096]{1,0:T(8,128)S(1)} %get-tuple-element.170, pred[]{:T(512)S(6)} %compare.3, ...), kind=kOutput, calls=%fused_computation.4.clone.1 | convolution fusion | flops 113377280 | bytes 829956 | tf_op jit(solution)/shard_map/while/body/eval_jaxpr/dot_general | solution.py:44
  56.7 3.8 %convolution_add_fusion.3 = f32[16,4096]{1,0:T(8,128)S(1)} fusion(bf16[32,4096]{1,0:T(8,128)(2,1)S(1)} %get-tuple-element.186, f32[256]{0:T(256)S(1)} %bitcast.65, f32[4096]{0:T(1024)S(1)} %get-tuple-element.183, f32[]{:T(128)} %get-tuple-element.182, f32[16,4096]{1,0:T(8,128)S(1)} %get-tuple-element.170, pred[]{:T(512)S(6)} %compare.3, ...), kind=kOutput, calls=%fused_computation.4.clone.1 | convolution fusion | flops 113377280 | bytes 829956 | tf_op jit(solution)/shard_map/while/body/eval_jaxpr/dot_general | solution.py:44
  60.6 3.8 %convolution_add_fusion.3 = f32[16,4096]{1,0:T(8,128)S(1)} fusion(bf16[32,4096]{1,0:T(8,128)(2,1)S(1)} %get-tuple-element.186, f32[256]{0:T(256)S(1)} %bitcast.65, f32[4096]{0:T(1024)S(1)} %get-tuple-element.183, f32[]{:T(128)} %get-tuple-element.182, f32[16,4096]{1,0:T(8,128)S(1)} %get-tuple-element.170, pred[]{:T(512)S(6)} %compare.3, ...), kind=kOutput, calls=%fused_computation.4.clone.1 | convolution fusion | flops 113377280 | bytes 829956 | tf_op jit(solution)/shard_map/while/body/eval_jaxpr/dot_general | solution.py:44
  64.5 3.8 %convolution_add_fusion.3 = f32[16,4096]{1,0:T(8,128)S(1)} fusion(bf16[32,4096]{1,0:T(8,128)(2,1)S(1)} %get-tuple-element.186, f32[256]{0:T(256)S(1)} %bitcast.65, f32[4096]{0:T(1024)S(1)} %get-tuple-element.183, f32[]{:T(128)} %get-tuple-element.182, f32[16,4096]{1,0:T(8,128)S(1)} %get-tuple-element.170, pred[]{:T(512)S(6)} %compare.3, ...), kind=kOutput, calls=%fused_computation.4.clone.1 | convolution fusion | flops 113377280 | bytes 829956 | tf_op jit(solution)/shard_map/while/body/eval_jaxpr/dot_general | solution.py:44
  68.4 3.8 %convolution_add_fusion.3 = f32[16,4096]{1,0:T(8,128)S(1)} fusion(bf16[32,4096]{1,0:T(8,128)(2,1)S(1)} %get-tuple-element.186, f32[256]{0:T(256)S(1)} %bitcast.65, f32[4096]{0:T(1024)S(1)} %get-tuple-element.183, f32[]{:T(128)} %get-tuple-element.182, f32[16,4096]{1,0:T(8,128)S(1)} %get-tuple-element.170, pred[]{:T(512)S(6)} %compare.3, ...), kind=kOutput, calls=%fused_computation.4.clone.1 | convolution fusion | flops 113377280 | bytes 829956 | tf_op jit(solution)/shard_map/while/body/eval_jaxpr/dot_general | solution.py:44
  72.3 3.8 %convolution_add_fusion.3 = f32[16,4096]{1,0:T(8,128)S(1)} fusion(bf16[32,4096]{1,0:T(8,128)(2,1)S(1)} %get-tuple-element.186, f32[256]{0:T(256)S(1)} %bitcast.65, f32[4096]{0:T(1024)S(1)} %get-tuple-element.183, f32[]{:T(128)} %get-tuple-element.182, f32[16,4096]{1,0:T(8,128)S(1)} %get-tuple-element.170, pred[]{:T(512)S(6)} %compare.3, ...), kind=kOutput, calls=%fused_computation.4.clone.1 | convolution fusion | flops 113377280 | bytes 829956 | tf_op jit(solution)/shard_map/while/body/eval_jaxpr/dot_general | solution.py:44
  76.2 3.8 %convolution_add_fusion.3 = f32[16,4096]{1,0:T(8,128)S(1)} fusion(bf16[32,4096]{1,0:T(8,128)(2,1)S(1)} %get-tuple-element.186, f32[256]{0:T(256)S(1)} %bitcast.65, f32[4096]{0:T(1024)S(1)} %get-tuple-element.183, f32[]{:T(128)} %get-tuple-element.182, f32[16,4096]{1,0:T(8,128)S(1)} %get-tuple-element.170, pred[]{:T(512)S(6)} %compare.3, ...), kind=kOutput, calls=%fused_computation.4.clone.1 | convolution fusion | flops 113377280 | bytes 829956 | tf_op jit(solution)/shard_map/while/body/eval_jaxpr/dot_general | solution.py:44
  80.1 3.8 %convolution_add_fusion.3 = f32[16,4096]{1,0:T(8,128)S(1)} fusion(bf16[32,4096]{1,0:T(8,128)(2,1)S(1)} %get-tuple-element.186, f32[256]{0:T(256)S(1)} %bitcast.65, f32[4096]{0:T(1024)S(1)} %get-tuple-element.183, f32[]{:T(128)} %get-tuple-element.182, f32[16,4096]{1,0:T(8,128)S(1)} %get-tuple-element.170, pred[]{:T(512)S(6)} %compare.3, ...), kind=kOutput, calls=%fused_computation.4.clone.1 | convolution fusion | flops 113377280 | bytes 829956 | tf_op jit(solution)/shard_map/while/body/eval_jaxpr/dot_general | solution.py:44
  84.0 3.8 %convolution_add_fusion.3 = f32[16,4096]{1,0:T(8,128)S(1)} fusion(bf16[32,4096]{1,0:T(8,128)(2,1)S(1)} %get-tuple-element.186, f32[256]{0:T(256)S(1)} %bitcast.65, f32[4096]{0:T(1024)S(1)} %get-tuple-element.183, f32[]{:T(128)} %get-tuple-element.182, f32[16,4096]{1,0:T(8,128)S(1)} %get-tuple-element.170, pred[]{:T(512)S(6)} %compare.3, ...), kind=kOutput, calls=%fused_computation.4.clone.1 | convolution fusion | flops 113377280 | bytes 829956 | tf_op jit(solution)/shard_map/while/body/eval_jaxpr/dot_general | solution.py:44
  87.9 3.8 %convolution_add_fusion.3 = f32[16,4096]{1,0:T(8,128)S(1)} fusion(bf16[32,4096]{1,0:T(8,128)(2,1)S(1)} %get-tuple-element.186, f32[256]{0:T(256)S(1)} %bitcast.65, f32[4096]{0:T(1024)S(1)} %get-tuple-element.183, f32[]{:T(128)} %get-tuple-element.182, f32[16,4096]{1,0:T(8,128)S(1)} %get-tuple-element.170, pred[]{:T(512)S(6)} %compare.3, ...), kind=kOutput, calls=%fused_computation.4.clone.1 | convolution fusion | flops 113377280 | bytes 829956 | tf_op jit(solution)/shard_map/while/body/eval_jaxpr/dot_general | solution.py:44
  91.8 3.8 %convolution_add_fusion.3 = f32[16,4096]{1,0:T(8,128)S(1)} fusion(bf16[32,4096]{1,0:T(8,128)(2,1)S(1)} %get-tuple-element.186, f32[256]{0:T(256)S(1)} %bitcast.65, f32[4096]{0:T(1024)S(1)} %get-tuple-element.183, f32[]{:T(128)} %get-tuple-element.182, f32[16,4096]{1,0:T(8,128)S(1)} %get-tuple-element.170, pred[]{:T(512)S(6)} %compare.3, ...), kind=kOutput, calls=%fused_computation.4.clone.1 | convolution fusion | flops 113377280 | bytes 829956 | tf_op jit(solution)/shard_map/while/body/eval_jaxpr/dot_general | solution.py:44
  95.7 3.8 %convolution_add_fusion.3 = f32[16,4096]{1,0:T(8,128)S(1)} fusion(bf16[32,4096]{1,0:T(8,128)(2,1)S(1)} %get-tuple-element.186, f32[256]{0:T(256)S(1)} %bitcast.65, f32[4096]{0:T(1024)S(1)} %get-tuple-element.183, f32[]{:T(128)} %get-tuple-element.182, f32[16,4096]{1,0:T(8,128)S(1)} %get-tuple-element.170, pred[]{:T(512)S(6)} %compare.3, ...), kind=kOutput, calls=%fused_computation.4.clone.1 | convolution fusion | flops 113377280 | bytes 829956 | tf_op jit(solution)/shard_map/while/body/eval_jaxpr/dot_general | solution.py:44
  99.5 3.8 %convolution_add_fusion.3 = f32[16,4096]{1,0:T(8,128)S(1)} fusion(bf16[32,4096]{1,0:T(8,128)(2,1)S(1)} %get-tuple-element.186, f32[256]{0:T(256)S(1)} %bitcast.65, f32[4096]{0:T(1024)S(1)} %get-tuple-element.183, f32[]{:T(128)} %get-tuple-element.182, f32[16,4096]{1,0:T(8,128)S(1)} %get-tuple-element.170, pred[]{:T(512)S(6)} %compare.3, ...), kind=kOutput, calls=%fused_computation.4.clone.1 | convolution fusion | flops 113377280 | bytes 829956 | tf_op jit(solution)/shard_map/while/body/eval_jaxpr/dot_general | solution.py:44
  103.5 1.5 collective-permute-done.8
  105.7 7.8 %collective-permute-done.9 = f32[16,4096]{1,0:T(8,128)S(1)} collective-permute-done((f32[16,4096]{1,0:T(8,128)S(1)}, f32[16,4096]{1,0:T(8,128)S(1)}, u32[]{:S(2)}, u32[]{:S(2)}) %collective-permute-start.9) | collective-permute-done | bytes 262176 | tf_op jit(solution)/shard_map/ppermute | solution.py:98
  113.5 2.2 %collective-permute-start.10 = (f32[16,4096]{1,0:T(8,128)S(1)}, f32[16,4096]{1,0:T(8,128)S(1)}, u32[]{:S(2)}, u32[]{:S(2)}) collective-permute-start(f32[16,4096]{1,0:T(8,128)S(1)} %add.157), channel_id=1, source_target_pairs={{0,4},{1,5},{2,6},{3,7},{4,0},{5,1},{6,2},{7,3},{8,12},{9,13},{10,... | collective-permute-start | bytes 786440 | tf_op jit(solution)/shard_map/ppermute | solution.py:98
  117.0 5.6 %collective-permute-done.10 = f32[16,4096]{1,0:T(8,128)S(1)} collective-permute-done((f32[16,4096]{1,0:T(8,128)S(1)}, f32[16,4096]{1,0:T(8,128)S(1)}, u32[]{:S(2)}, u32[]{:S(2)}) %collective-permute-start.10) | collective-permute-done | bytes 262176 | tf_op jit(solution)/shard_map/ppermute | solution.py:98
  122.7 0.9 collective-permute-start.11
  123.8 7.1 %collective-permute-done.11 = f32[16,4096]{1,0:T(8,128)S(1)} collective-permute-done((f32[16,4096]{1,0:T(8,128)S(1)}, f32[16,4096]{1,0:T(8,128)S(1)}, u32[]{:S(2)}, u32[]{:S(2)}) %collective-permute-start.11) | collective-permute-done | bytes 262176 | tf_op jit(solution)/shard_map/ppermute | solution.py:98
  131.2 0.9 collective-permute-start.12
  132.3 2.6 %collective-permute-done.12 = f32[32]{0:T(128)S(1)} collective-permute-done((f32[32]{0:T(128)S(1)}, f32[32]{0:T(128)S(1)}, u32[]{:S(2)}, u32[]{:S(2)}) %collective-permute-start.12) | collective-permute-done | bytes 160 | tf_op jit(solution)/shard_map/ppermute | solution.py:98
  135.5 6.1 %multiply_convert_fusion.2 = bf16[1024,2048]{1,0:T(8,128)(2,1)S(1)} fusion(bf16[32,1024]{1,0:T(8,128)(2,1)S(1)} %reshape.45, f32[2048]{0:T(1024)S(1)} %get-tuple-element.103, f32[1024]{0:T(1024)S(1)} %add.171, f32[]{:T(128)} %bitcast.54, bf16[96,4096]{1,0:T(8,128)(2,1)S(1)} %maximum_select_fusion.1), kind=kOutput, calls=%fused_computation.19 | convolution fusion | flops 159383552 | bytes 4403204 | tf_op jit(solution)/shard_map/dot_general | solution.py:19
  141.6 2.0 %collective-permute-start.14 = (f32[32]{0:T(128)S(1)}, f32[32]{0:T(128)S(1)}, u32[]{:S(2)}, u32[]{:S(2)}) collective-permute-start(f32[32]{0:T(128)S(1)} %add.163), channel_id=1, source_target_pairs={{0,64},{16,80},{32,96},{48,112},{64,0},{80,16},{96,32},{112,48},{1... | collective-permute-start | bytes 392 | tf_op jit(solution)/shard_map/ppermute | solution.py:98
  143.6 6.1 %multiply_convert_fusion.1 = bf16[1024,2048]{1,0:T(8,128)(2,1)S(1)} fusion(bf16[32,1024]{1,0:T(8,128)(2,1)S(1)} %reshape.45, f32[2048]{0:T(1024)S(1)} %get-tuple-element.102, f32[1024]{0:T(1024)S(1)} %add.171, f32[]{:T(128)} %bitcast.55, bf16[96,4096]{1,0:T(8,128)(2,1)S(1)} %maximum_select_fusion.1), kind=kOutput, calls=%fused_computation.18 | convolution fusion | flops 159383552 | bytes 4403204 | tf_op jit(solution)/shard_map/dot_general | solution.py:19
  149.8 0.8 collective-permute-start.15
  150.6 6.8 %collective-permute-done.15 = f32[32]{0:T(128)S(1)} collective-permute-done((f32[32]{0:T(128)S(1)}, f32[32]{0:T(128)S(1)}, u32[]{:S(2)}, u32[]{:S(2)}) %collective-permute-start.15) | collective-permute-done | bytes 160 | tf_op jit(solution)/shard_map/ppermute | solution.py:98
  157.7 1.2 fusion.20
  158.9 1.2 convolution_add_fusion.1
  160.2 1.2 collective-permute-done.20
  161.4 0.7 collective-permute-start.21
  162.7 3.0 %collective-permute-done.16 = f32[16]{0:T(128)S(1)} collective-permute-done((f32[16]{0:T(128)S(1)}, f32[16]{0:T(128)S(1)}, u32[]{:S(2)}, u32[]{:S(2)}) %collective-permute-start.16) | collective-permute-done | bytes 96 | tf_op jit(solution)/shard_map/ppermute | solution.py:98
  166.2 3.1 %collective-permute-done.17 = f32[16]{0:T(128)S(1)} collective-permute-done((f32[16]{0:T(128)S(1)}, f32[16]{0:T(128)S(1)}, u32[]{:S(2)}, u32[]{:S(2)}) %collective-permute-start.17) | collective-permute-done | bytes 96 | tf_op jit(solution)/shard_map/ppermute | solution.py:98
  169.3 0.9 collective-permute-start.18
  170.2 3.5 %collective-permute-done.18 = f32[16]{0:T(128)S(1)} collective-permute-done((f32[16]{0:T(128)S(1)}, f32[16]{0:T(128)S(1)}, u32[]{:S(2)}, u32[]{:S(2)}) %collective-permute-start.18) | collective-permute-done | bytes 96 | tf_op jit(solution)/shard_map/ppermute | solution.py:98
  173.7 0.8 collective-permute-start.19
  174.6 2.6 %collective-permute-start.22 = (f32[16,128]{1,0:T(8,128)S(1)}, f32[16,128]{1,0:T(8,128)S(1)}, u32[]{:S(2)}, u32[]{:S(2)}) collective-permute-start(f32[16,128]{1,0:T(8,128)S(1)} %slice_select_fusion.3), channel_id=1, source_target_pairs={{0,4},{1,5},{2,6},{3,7},{4,0},{5,1},{6,2},{7,3},{8,12},{9,13},{10,... | collective-permute-start | bytes 24584 | tf_op jit(solution)/shard_map/ppermute | solution.py:92
  177.2 4.0 %collective-permute-done.19 = f32[16]{0:T(128)S(1)} collective-permute-done((f32[16]{0:T(128)S(1)}, f32[16]{0:T(128)S(1)}, u32[]{:S(2)}, u32[]{:S(2)}) %collective-permute-start.19) | collective-permute-done | bytes 96 | tf_op jit(solution)/shard_map/ppermute | solution.py:98
  181.3 1.9 %collective-permute-start.23 = (f32[16,64]{1,0:T(8,128)S(1)}, f32[16,64]{1,0:T(8,128)S(1)}, u32[]{:S(2)}, u32[]{:S(2)}) collective-permute-start(f32[16,64]{1,0:T(8,128)S(1)} %slice_select_fusion.2), channel_id=1, source_target_pairs={{0,8},{1,9},{2,10},{3,11},{4,12},{5,13},{6,14},{7,15},{8,0},{9,1},... | collective-permute-start | bytes 12296 | tf_op jit(solution)/shard_map/ppermute | solution.py:92
  183.2 0.7 multiply_add_fusion.1
  183.9 2.6 %collective-permute-done.23 = f32[16,64]{1,0:T(8,128)S(1)} collective-permute-done((f32[16,64]{1,0:T(8,128)S(1)}, f32[16,64]{1,0:T(8,128)S(1)}, u32[]{:S(2)}, u32[]{:S(2)}) %collective-permute-start.23) | collective-permute-done | bytes 4128 | tf_op jit(solution)/shard_map/ppermute | solution.py:92
  186.5 0.7 add_add_fusion
  (87 shorter events, 5.6 us)
Async XLA Ops:
  5.3 11.8 %collective-permute-start.4 = (bf16[96,256]{1,0:T(8,128)(2,1)S(1)}, bf16[96,256]{1,0:T(8,128)(2,1)S(1)}, u32[]{:S(2)}, u32[]{:S(2)}) collective-permute-start(bf16[96,256]{1,0:T(8,128)(2,1)S(1)} %constant_dynamic-update-slice_fusion.6), channel_id=1, source_target_pairs={{0,128},{16,144},{32,160},{48,176},{64,192},{80,208},{96,224},{112... | collective-permute-start | bytes 147464 | tf_op jit(solution)/shard_map/ppermute | solution.py:75
  13.9 5.6 %collective-permute-start = (bf16[104,256]{1,0:T(8,128)(2,1)S(1)}, bf16[104,256]{1,0:T(8,128)(2,1)S(1)}, u32[]{:S(2)}, u32[]{:S(2)}) collective-permute-start(bf16[104,256]{1,0:T(8,128)(2,1)S(1)} %constant_dynamic-update-slice_fusion), channel_id=1, source_target_pairs={{0,8},{1,9},{2,10},{3,11},{4,12},{5,13},{6,14},{7,15},{8,0},{9,1},... | collective-permute-start | bytes 159752 | tf_op jit(solution)/shard_map/ppermute | solution.py:75
  17.1 7.1 %collective-permute-start.5 = (bf16[96,512]{1,0:T(8,128)(2,1)S(1)}, bf16[96,512]{1,0:T(8,128)(2,1)S(1)}, u32[]{:S(2)}, u32[]{:S(2)}) collective-permute-start(bf16[96,512]{1,0:T(8,128)(2,1)S(1)} %maximum_select_fusion.7), channel_id=1, source_target_pairs={{0,64},{16,80},{32,96},{48,112},{64,0},{80,16},{96,32},{112,48},{1... | collective-permute-start | bytes 294920 | tf_op jit(solution)/shard_map/ppermute | solution.py:75
  19.5 6.3 %collective-permute-start.1 = (bf16[104,512]{1,0:T(8,128)(2,1)S(1)}, bf16[104,512]{1,0:T(8,128)(2,1)S(1)}, u32[]{:S(2)}, u32[]{:S(2)}) collective-permute-start(bf16[104,512]{1,0:T(8,128)(2,1)S(1)} %maximum_select_fusion.6), channel_id=1, source_target_pairs={{0,4},{1,5},{2,6},{3,7},{4,0},{5,1},{6,2},{7,3},{8,12},{9,13},{10,... | collective-permute-start | bytes 319496 | tf_op jit(solution)/shard_map/ppermute | solution.py:75
  24.2 6.4 %collective-permute-start.6 = (bf16[96,1024]{1,0:T(8,128)(2,1)S(1)}, bf16[96,1024]{1,0:T(8,128)(2,1)S(1)}, u32[]{:S(2)}, u32[]{:S(2)}) collective-permute-start(bf16[96,1024]{1,0:T(8,128)(2,1)S(1)} %maximum_select_fusion.5), channel_id=1, source_target_pairs={{0,32},{16,48},{32,0},{48,16},{64,96},{80,112},{96,64},{112,80},{1... | collective-permute-start | bytes 589832 | tf_op jit(solution)/shard_map/ppermute | solution.py:75
  25.9 5.9 %collective-permute-start.2 = (bf16[104,1024]{1,0:T(8,128)(2,1)S(1)}, bf16[104,1024]{1,0:T(8,128)(2,1)S(1)}, u32[]{:S(2)}, u32[]{:S(2)}) collective-permute-start(bf16[104,1024]{1,0:T(8,128)(2,1)S(1)} %maximum_select_fusion.4), channel_id=1, source_target_pairs={{0,2},{1,3},{2,0},{3,1},{4,6},{5,7},{6,4},{7,5},{8,10},{9,11},{10,... | collective-permute-start | bytes 638984 | tf_op jit(solution)/shard_map/ppermute | solution.py:75
  30.7 9.7 %collective-permute-start.7 = (bf16[96,2048]{1,0:T(8,128)(2,1)S(1)}, bf16[96,2048]{1,0:T(8,128)(2,1)S(1)}, u32[]{:S(2)}, u32[]{:S(2)}) collective-permute-start(bf16[96,2048]{1,0:T(8,128)(2,1)S(1)} %maximum_select_fusion.3), channel_id=1, source_target_pairs={{0,16},{16,0},{32,48},{48,32},{64,80},{80,64},{96,112},{112,96},{1... | collective-permute-start | bytes 1179656 | tf_op jit(solution)/shard_map/ppermute | solution.py:75
  32.0 8.9 %collective-permute-start.3 = (bf16[104,2048]{1,0:T(8,128)(2,1)S(1)}, bf16[104,2048]{1,0:T(8,128)(2,1)S(1)}, u32[]{:S(2)}, u32[]{:S(2)}) collective-permute-start(bf16[104,2048]{1,0:T(8,128)(2,1)S(1)} %maximum_select_fusion.2), channel_id=1, source_target_pairs={{0,1},{1,0},{2,3},{3,2},{4,5},{5,4},{6,7},{7,6},{8,9},{9,8},{10,11... | collective-permute-start | bytes 1277960 | tf_op jit(solution)/shard_map/ppermute | solution.py:75
  103.4 1.6 collective-permute-start.8
  105.1 8.4 %collective-permute-start.9 = (f32[16,4096]{1,0:T(8,128)S(1)}, f32[16,4096]{1,0:T(8,128)S(1)}, u32[]{:S(2)}, u32[]{:S(2)}) collective-permute-start(f32[16,4096]{1,0:T(8,128)S(1)} %add.156), channel_id=1, source_target_pairs={{0,2},{1,3},{2,0},{3,1},{4,6},{5,7},{6,4},{7,5},{8,10},{9,11},{10,... | collective-permute-start | bytes 786440 | tf_op jit(solution)/shard_map/ppermute | solution.py:98
  113.5 9.1 %collective-permute-start.10 = (f32[16,4096]{1,0:T(8,128)S(1)}, f32[16,4096]{1,0:T(8,128)S(1)}, u32[]{:S(2)}, u32[]{:S(2)}) collective-permute-start(f32[16,4096]{1,0:T(8,128)S(1)} %add.157), channel_id=1, source_target_pairs={{0,4},{1,5},{2,6},{3,7},{4,0},{5,1},{6,2},{7,3},{8,12},{9,13},{10,... | collective-permute-start | bytes 786440 | tf_op jit(solution)/shard_map/ppermute | solution.py:98
  122.7 8.2 %collective-permute-start.11 = (f32[16,4096]{1,0:T(8,128)S(1)}, f32[16,4096]{1,0:T(8,128)S(1)}, u32[]{:S(2)}, u32[]{:S(2)}) collective-permute-start(f32[16,4096]{1,0:T(8,128)S(1)} %add.158), channel_id=1, source_target_pairs={{0,8},{1,9},{2,10},{3,11},{4,12},{5,13},{6,14},{7,15},{8,0},{9,1},... | collective-permute-start | bytes 786440 | tf_op jit(solution)/shard_map/ppermute | solution.py:98
  131.2 3.8 %collective-permute-start.12 = (f32[32]{0:T(128)S(1)}, f32[32]{0:T(128)S(1)}, u32[]{:S(2)}, u32[]{:S(2)}) collective-permute-start(f32[32]{0:T(128)S(1)} %pad_maximum_fusion), channel_id=1, source_target_pairs={{0,16},{16,0},{32,48},{48,32},{64,80},{80,64},{96,112},{112,96},{1... | collective-permute-start | bytes 392 | tf_op jit(solution)/shard_map/ppermute | solution.py:98
  135.0 6.7 %collective-permute-start.13 = (f32[32]{0:T(128)S(1)}, f32[32]{0:T(128)S(1)}, u32[]{:S(2)}, u32[]{:S(2)}) collective-permute-start(f32[32]{0:T(128)S(1)} %add.162), channel_id=1, source_target_pairs={{0,32},{16,48},{32,0},{48,16},{64,96},{80,112},{96,64},{112,80},{1... | collective-permute-start | bytes 392 | tf_op jit(solution)/shard_map/ppermute | solution.py:98
  141.6 8.1 %collective-permute-start.14 = (f32[32]{0:T(128)S(1)}, f32[32]{0:T(128)S(1)}, u32[]{:S(2)}, u32[]{:S(2)}) collective-permute-start(f32[32]{0:T(128)S(1)} %add.163), channel_id=1, source_target_pairs={{0,64},{16,80},{32,96},{48,112},{64,0},{80,16},{96,32},{112,48},{1... | collective-permute-start | bytes 392 | tf_op jit(solution)/shard_map/ppermute | solution.py:98
  149.8 7.6 %collective-permute-start.15 = (f32[32]{0:T(128)S(1)}, f32[32]{0:T(128)S(1)}, u32[]{:S(2)}, u32[]{:S(2)}) collective-permute-start(f32[32]{0:T(128)S(1)} %add.164), channel_id=1, source_target_pairs={{0,128},{16,144},{32,160},{48,176},{64,192},{80,208},{96,224},{112... | collective-permute-start | bytes 392 | tf_op jit(solution)/shard_map/ppermute | solution.py:98
  157.6 25.6 %copy-start = (f32[16,256]{1,0:T(8,128)S(1)}, f32[16,256]{1,0:T(8,128)}, u32[]{:S(2)}) copy-start(f32[16,256]{1,0:T(8,128)} %param.19) | copy-start | bytes 49156
  157.7 25.5 %copy-start.1 = (f32[16,256]{1,0:T(8,128)S(1)}, f32[16,256]{1,0:T(8,128)}, u32[]{:S(2)}) copy-start(f32[16,256]{1,0:T(8,128)} %param.17) | copy-start | bytes 49156
  157.7 25.5 %copy-start.2 = (f32[16,256]{1,0:T(8,128)S(1)}, f32[16,256]{1,0:T(8,128)}, u32[]{:S(2)}) copy-start(f32[16,256]{1,0:T(8,128)} %param.18) | copy-start | bytes 49156
  157.7 28.8 %copy-start.3 = (f32[64]{0:T(128)S(1)}, f32[64]{0:T(128)}, u32[]{:S(2)}) copy-start(f32[64]{0:T(128)} %param.16) | copy-start | bytes 772
  160.1 1.3 collective-permute-start.20
  161.4 13.2 %collective-permute-start.21 = (f32[16,256]{1,0:T(8,128)S(1)}, f32[16,256]{1,0:T(8,128)S(1)}, u32[]{:S(2)}, u32[]{:S(2)}) collective-permute-start(f32[16,256]{1,0:T(8,128)S(1)} %slice_select_fusion.1), channel_id=1, source_target_pairs={{0,2},{1,3},{2,0},{3,1},{4,6},{5,7},{6,4},{7,5},{8,10},{9,11},{10,... | collective-permute-start | bytes 49160 | tf_op jit(solution)/shard_map/ppermute | solution.py:92
  162.1 3.6 %collective-permute-start.16 = (f32[16]{0:T(128)S(1)}, f32[16]{0:T(128)S(1)}, u32[]{:S(2)}, u32[]{:S(2)}) collective-permute-start(f32[16]{0:T(128)S(1)} %get-tuple-element.50), channel_id=1, source_target_pairs={{0,16},{16,0},{32,48},{48,32},{64,80},{80,64},{96,112},{112,96},{1... | collective-permute-start | bytes 200 | tf_op jit(solution)/shard_map/ppermute | solution.py:98
  165.7 3.6 %collective-permute-start.17 = (f32[16]{0:T(128)S(1)}, f32[16]{0:T(128)S(1)}, u32[]{:S(2)}, u32[]{:S(2)}) collective-permute-start(f32[16]{0:T(128)S(1)} %add.182), channel_id=1, source_target_pairs={{0,32},{16,48},{32,0},{48,16},{64,96},{80,112},{96,64},{112,80},{1... | collective-permute-start | bytes 200 | tf_op jit(solution)/shard_map/ppermute | solution.py:98
  169.3 4.5 %collective-permute-start.18 = (f32[16]{0:T(128)S(1)}, f32[16]{0:T(128)S(1)}, u32[]{:S(2)}, u32[]{:S(2)}) collective-permute-start(f32[16]{0:T(128)S(1)} %add.183), channel_id=1, source_target_pairs={{0,64},{16,80},{32,96},{48,112},{64,0},{80,16},{96,32},{112,48},{1... | collective-permute-start | bytes 200 | tf_op jit(solution)/shard_map/ppermute | solution.py:98
  173.7 7.5 %collective-permute-start.19 = (f32[16]{0:T(128)S(1)}, f32[16]{0:T(128)S(1)}, u32[]{:S(2)}, u32[]{:S(2)}) collective-permute-start(f32[16]{0:T(128)S(1)} %add.184), channel_id=1, source_target_pairs={{0,128},{16,144},{32,160},{48,176},{64,192},{80,208},{96,224},{112... | collective-permute-start | bytes 200 | tf_op jit(solution)/shard_map/ppermute | solution.py:98
  174.6 6.6 %collective-permute-start.22 = (f32[16,128]{1,0:T(8,128)S(1)}, f32[16,128]{1,0:T(8,128)S(1)}, u32[]{:S(2)}, u32[]{:S(2)}) collective-permute-start(f32[16,128]{1,0:T(8,128)S(1)} %slice_select_fusion.3), channel_id=1, source_target_pairs={{0,4},{1,5},{2,6},{3,7},{4,0},{5,1},{6,2},{7,3},{8,12},{9,13},{10,... | collective-permute-start | bytes 24584 | tf_op jit(solution)/shard_map/ppermute | solution.py:92
  181.3 5.2 %collective-permute-start.23 = (f32[16,64]{1,0:T(8,128)S(1)}, f32[16,64]{1,0:T(8,128)S(1)}, u32[]{:S(2)}, u32[]{:S(2)}) collective-permute-start(f32[16,64]{1,0:T(8,128)S(1)} %slice_select_fusion.2), channel_id=1, source_target_pairs={{0,8},{1,9},{2,10},{3,11},{4,12},{5,13},{6,14},{7,15},{8,0},{9,1},... | collective-permute-start | bytes 12296 | tf_op jit(solution)/shard_map/ppermute | solution.py:92

commit v6 on v5

--- a/solution.py
+++ b/solution.py
@@ -15,11 +15,11 @@
     return jnp.sum(jnp.square(scaled.astype(jnp.float32)), axis=0)
 
 
-def matern_block(row_pts, row_sq, col_pts, col_sq, signal_scalar):
-    inner_prod = lax.dot_general(
-        row_pts, col_pts, contract_first, preferred_element_type=jnp.float32
-    )
-    dist_sq = jnp.maximum(row_sq[:, None] + col_sq[None, :] - 2.0 * inner_prod, 0.0)
+def matern_block(row_pts_m2, row_sq, col_pts, col_sq, signal_scalar):
+    inner_m2 = lax.dot_general(
+        row_pts_m2, col_pts, contract_first, preferred_element_type=jnp.float32
+    )
+    dist_sq = jnp.maximum(row_sq[:, None] + col_sq[None, :] + inner_m2, 0.0)
     distance = jnp.sqrt(dist_sq)
     kern_vals = (
         signal_scalar
@@ -29,7 +29,7 @@
     return kern_vals.astype(jnp.bfloat16)
 
 
-def kernel_apply(row_pts, row_sq, col_pts, col_sq, vectors, signal_scalar, block_len):
+def kernel_apply(row_pts_m2, row_sq, col_pts, col_sq, vectors, signal_scalar, block_len):
     feature_count = col_pts.shape[0]
     num_blocks = col_pts.shape[1] // block_len
     pts_blocks = col_pts.reshape(feature_count, num_blocks, block_len).transpose(1, 0, 2)
@@ -38,18 +38,18 @@
 
     def one_block(total, pieces):
         pts_blk, sq_blk, vec_blk = pieces
-        kern_vals = matern_block(row_pts, row_sq, pts_blk, sq_blk, signal_scalar)
+        kern_vals = matern_block(row_pts_m2, row_sq, pts_blk, sq_blk, signal_scalar)
         return (
             total
             + lax.dot_general(
-                vec_blk, kern_vals, contract_last, preferred_element_type=jnp.float32
+                kern_vals, vec_blk, contract_last, preferred_element_type=jnp.float32
             ),
             None,
         )
 
-    start = jnp.zeros((vectors.shape[0], row_pts.shape[1]), jnp.float32)
+    start = jnp.zeros((row_pts_m2.shape[1], vectors.shape[0]), jnp.float32)
     result, _ = lax.scan(one_block, start, (pts_blocks, sq_blocks, vec_blocks))
-    return result
+    return result.T
 
 
 def tied(x, dep):
@@ -164,16 +164,17 @@
     cand_sq = square_norms(row_cands)
 
     partial_rows = kernel_apply(
-        row_pts, row_sq, col_pts, col_sq, col_dir, signal_scalar, 256
+        row_pts * jnp.asarray(-2.0, jnp.bfloat16), row_sq, col_pts, col_sq, col_dir, signal_scalar, 256
     )
     cand_blocks = []
-    width = col_pts.shape[1] // 2
-    for k in range(2):
+    pieces = 4
+    width = col_pts.shape[1] // pieces
+    for k in range(pieces):
         lo, hi = k * width, (k + 1) * width
         cand_blocks.append(
             lax.optimization_barrier(
                 matern_block(
-                    row_cands, cand_sq, col_pts[:, lo:hi], col_sq[lo:hi],
+                    row_cands * jnp.asarray(-2.0, jnp.bfloat16), cand_sq, col_pts[:, lo:hi], col_sq[lo:hi],
                     signal_scalar,
                 )
             )
@@ -199,7 +200,7 @@
 
     w_low_col = (w_col + step_len[:, None] * d_col).astype(jnp.bfloat16)
     partial_fit = None
-    for k in range(2):
+    for k in range(pieces):
         lo, hi = k * width, (k + 1) * width
         part = lax.dot_general(
             w_low_col[:, lo:hi], cand_blocks[k], contract_last,

time: 189 us -> 181 us (0.958)
  waiting for transfers between devices: 66.3 us -> 54.8 us
  starting transfers between devices: 32 us -> 37.2 us
    ppermute x12, waiting for transfers between devices: 45 us -> 35.3 us  [all_sum(): x = x + lax.ppermute(x, axis_name, xor_perm(size, bit))]
    ppermute x12, starting transfers between devices: 11 us -> 15.5 us  [all_sum(): x = x + lax.ppermute(x, axis_name, xor_perm(size, bit))]
    dot_general x18 -> x20, matrix products: 73.8 us -> 71.8 us  [the longest x16 59.6 us: one_block(): lax.dot_general(kern_vals, vec_blk, contract_last, preferred_element_type...]
  transfers between devices with their start and end apart: 24 -> 24, of which waited for: 18 -> 17; matrix products, arithmetic and copies ran while one was open for 8% -> 9% of each run, Pallas kernels for 0% -> 0%
where the time goes in v6:
time: 181 us; the launch traced here: 179 us
  matrix products  74.4 us (41%)
  waiting for transfers between devices  54.8 us (30%)
  starting transfers between devices  37.2 us (21%)
  other arithmetic  9.17 us (5%)
  between operations  2.33 us (1%)
    dot_general x16, matrix products, one_block(): lax.dot_general(kern_vals, vec_blk, contract_last, preferred_element_type...  59.6 us
    ppermute x12, waiting for transfers between devices, all_sum(): x = x + lax.ppermute(x, axis_name, xor_perm(size, bit))  35.3 us
    ppermute x8, waiting for transfers between devices, gather_last(): recv = lax.ppermute(buf, axis_name, xor_perm(size, bit))  16.3 us
    ppermute x8, starting transfers between devices, gather_last(): recv = lax.ppermute(buf, axis_name, xor_perm(size, bit))  15.7 us
    ppermute x12, starting transfers between devices, all_sum(): x = x + lax.ppermute(x, axis_name, xor_perm(size, bit))  15.5 us
    dot_general x4, matrix products, matern_block(): lax.dot_general(row_pts_m2, col_pts, contract_first, preferred_element_ty...  12.2 us
    ppermute x4, starting transfers between devices, reduce_scatter_last(): buf = keep + lax.ppermute(send, axis_name, xor_perm(size, bit))  5.93 us
    unnamed x6, other arithmetic  3.72 us
  transfers between devices with their start and end apart: 24, of which 17 were waited for; matrix products, arithmetic and copies ran while one was open for 9% of the time, Pallas kernels for 0%

profile of v6, /device:TPU:2, one launch (start us, length us, event | category | flops | bytes accessed | tf_op | source)
XLA Modules:
  0.0 179.2 jit_solution(11284374282567301697)
XLA Ops:
  0.6 0.8 constant_dynamic-update-slice_fusion.10
  1.5 0.8 divide_convert_fusion.1
  2.4 0.7 constant_dynamic-update-slice_fusion.9
  3.1 0.7 constant_dynamic-update-slice_fusion.8
  3.8 0.7 constant_dynamic-update-slice_fusion.7
  4.5 0.7 constant_dynamic-update-slice_fusion.6
  5.3 7.2 %collective-permute-start.4 = (bf16[96,256]{1,0:T(8,128)(2,1)S(1)}, bf16[96,256]{1,0:T(8,128)(2,1)S(1)}, u32[]{:S(2)}, u32[]{:S(2)}) collective-permute-start(bf16[96,256]{1,0:T(8,128)(2,1)S(1)} %constant_dynamic-update-slice_fusion.6), channel_id=1, source_target_pairs={{0,128},{16,144},{32,160},{48,176},{64,192},{80,208},{96,224},{112... | collective-permute-start | bytes 147464 | tf_op jit(solution)/shard_map/ppermute | solution.py:75
  12.4 0.7 constant_dynamic-update-slice_fusion.1
  13.2 0.7 constant_dynamic-update-slice_fusion
  13.9 3.2 %collective-permute-start = (bf16[104,256]{1,0:T(8,128)(2,1)S(1)}, bf16[104,256]{1,0:T(8,128)(2,1)S(1)}, u32[]{:S(2)}, u32[]{:S(2)}) collective-permute-start(bf16[104,256]{1,0:T(8,128)(2,1)S(1)} %constant_dynamic-update-slice_fusion), channel_id=1, source_target_pairs={{0,8},{1,9},{2,10},{3,11},{4,12},{5,13},{6,14},{7,15},{8,0},{9,1},... | collective-permute-start | bytes 159752 | tf_op jit(solution)/shard_map/ppermute | solution.py:75
  17.1 1.6 collective-permute-start.5
  18.7 0.9 collective-permute-done
  19.5 2.2 %collective-permute-start.1 = (bf16[104,512]{1,0:T(8,128)(2,1)S(1)}, bf16[104,512]{1,0:T(8,128)(2,1)S(1)}, u32[]{:S(2)}, u32[]{:S(2)}) collective-permute-start(bf16[104,512]{1,0:T(8,128)(2,1)S(1)} %maximum_select_fusion.6), channel_id=1, source_target_pairs={{0,4},{1,5},{2,6},{3,7},{4,0},{5,1},{6,2},{7,3},{8,12},{9,13},{10,... | collective-permute-start | bytes 319496 | tf_op jit(solution)/shard_map/ppermute | solution.py:75
  21.8 2.4 %collective-permute-done.5 = bf16[96,512]{1,0:T(8,128)(2,1)S(1)} collective-permute-done((bf16[96,512]{1,0:T(8,128)(2,1)S(1)}, bf16[96,512]{1,0:T(8,128)(2,1)S(1)}, u32[]{:S(2)}, u32[]{:S(2)}) %collective-permute-start.5) | collective-permute-done | bytes 98336 | tf_op jit(solution)/shard_map/ppermute | solution.py:75
  24.4 1.5 collective-permute-done.1
  26.5 4.1 %collective-permute-done.6 = bf16[96,1024]{1,0:T(8,128)(2,1)S(1)} collective-permute-done((bf16[96,1024]{1,0:T(8,128)(2,1)S(1)}, bf16[96,1024]{1,0:T(8,128)(2,1)S(1)}, u32[]{:S(2)}, u32[]{:S(2)}) %collective-permute-start.6) | collective-permute-done | bytes 196640 | tf_op jit(solution)/shard_map/ppermute | solution.py:75
  30.7 0.8 collective-permute-start.7
  33.0 7.4 %collective-permute-done.7 = bf16[96,2048]{1,0:T(8,128)(2,1)S(1)} collective-permute-done((bf16[96,2048]{1,0:T(8,128)(2,1)S(1)}, bf16[96,2048]{1,0:T(8,128)(2,1)S(1)}, u32[]{:S(2)}, u32[]{:S(2)}) %collective-permute-start.7) | collective-permute-done | bytes 393248 | tf_op jit(solution)/shard_map/ppermute | solution.py:75
  41.2 60.3 %while.11 = (s32[]{:T(128)}, f32[4096,16]{0,1:T(8,128)S(1)}, f32[]{:T(128)}, f32[4096]{0:T(1024)S(1)}, f32[16,256]{1,0:T(8,128)S(1)}, /*index=5*/bf16[16,32,256]...) while((s32[]{:T(128)}, f32[4096,16]{0,1:T(8,128)S(1)}, ...), condition=%wide.region_4.5_spmd.clone, body=%wide.region_3.4_spmd.clone.sunk | while | flops 112328704 | bytes 832126 | solution.py:51
  41.2 3.7 %convolution_add_fusion.5 = f32[4096,16]{0,1:T(8,128)S(1)} fusion(bf16[32,4096]{1,0:T(8,128)(2,1)S(1)} %get-tuple-element.187, f32[256]{0:T(256)S(1)} %bitcast.77, f32[4096]{0:T(1024)S(1)} %get-tuple-element.184, f32[]{:T(128)} %get-tuple-element.183, f32[4096,16]{0,1:T(8,128)S(1)} %get-tuple-element.172, pred[]{:T(512)S(6)} %compare.3, ...), kind=kOutput, calls=%fused_computation.3.clone.1 | convolution fusion | flops 112328704 | bytes 829956 | tf_op jit(solution)/shard_map/while/body/eval_jaxpr/dot_general | solution.py:44
  45.0 3.7 %convolution_add_fusion.5 = f32[4096,16]{0,1:T(8,128)S(1)} fusion(bf16[32,4096]{1,0:T(8,128)(2,1)S(1)} %get-tuple-element.187, f32[256]{0:T(256)S(1)} %bitcast.77, f32[4096]{0:T(1024)S(1)} %get-tuple-element.184, f32[]{:T(128)} %get-tuple-element.183, f32[4096,16]{0,1:T(8,128)S(1)} %get-tuple-element.172, pred[]{:T(512)S(6)} %compare.3, ...), kind=kOutput, calls=%fused_computation.3.clone.1 | convolution fusion | flops 112328704 | bytes 829956 | tf_op jit(solution)/shard_map/while/body/eval_jaxpr/dot_general | solution.py:44
  48.7 3.7 %convolution_add_fusion.5 = f32[4096,16]{0,1:T(8,128)S(1)} fusion(bf16[32,4096]{1,0:T(8,128)(2,1)S(1)} %get-tuple-element.187, f32[256]{0:T(256)S(1)} %bitcast.77, f32[4096]{0:T(1024)S(1)} %get-tuple-element.184, f32[]{:T(128)} %get-tuple-element.183, f32[4096,16]{0,1:T(8,128)S(1)} %get-tuple-element.172, pred[]{:T(512)S(6)} %compare.3, ...), kind=kOutput, calls=%fused_computation.3.clone.1 | convolution fusion | flops 112328704 | bytes 829956 | tf_op jit(solution)/shard_map/while/body/eval_jaxpr/dot_general | solution.py:44
  52.5 3.7 %convolution_add_fusion.5 = f32[4096,16]{0,1:T(8,128)S(1)} fusion(bf16[32,4096]{1,0:T(8,128)(2,1)S(1)} %get-tuple-element.187, f32[256]{0:T(256)S(1)} %bitcast.77, f32[4096]{0:T(1024)S(1)} %get-tuple-element.184, f32[]{:T(128)} %get-tuple-element.183, f32[4096,16]{0,1:T(8,128)S(1)} %get-tuple-element.172, pred[]{:T(512)S(6)} %compare.3, ...), kind=kOutput, calls=%fused_computation.3.clone.1 | convolution fusion | flops 112328704 | bytes 829956 | tf_op jit(solution)/shard_map/while/body/eval_jaxpr/dot_general | solution.py:44
  56.3 3.7 %convolution_add_fusion.5 = f32[4096,16]{0,1:T(8,128)S(1)} fusion(bf16[32,4096]{1,0:T(8,128)(2,1)S(1)} %get-tuple-element.187, f32[256]{0:T(256)S(1)} %bitcast.77, f32[4096]{0:T(1024)S(1)} %get-tuple-element.184, f32[]{:T(128)} %get-tuple-element.183, f32[4096,16]{0,1:T(8,128)S(1)} %get-tuple-element.172, pred[]{:T(512)S(6)} %compare.3, ...), kind=kOutput, calls=%fused_computation.3.clone.1 | convolution fusion | flops 112328704 | bytes 829956 | tf_op jit(solution)/shard_map/while/body/eval_jaxpr/dot_general | solution.py:44
  60.0 3.7 %convolution_add_fusion.5 = f32[4096,16]{0,1:T(8,128)S(1)} fusion(bf16[32,4096]{1,0:T(8,128)(2,1)S(1)} %get-tuple-element.187, f32[256]{0:T(256)S(1)} %bitcast.77, f32[4096]{0:T(1024)S(1)} %get-tuple-element.184, f32[]{:T(128)} %get-tuple-element.183, f32[4096,16]{0,1:T(8,128)S(1)} %get-tuple-element.172, pred[]{:T(512)S(6)} %compare.3, ...), kind=kOutput, calls=%fused_computation.3.clone.1 | convolution fusion | flops 112328704 | bytes 829956 | tf_op jit(solution)/shard_map/while/body/eval_jaxpr/dot_general | solution.py:44
  63.8 3.7 %convolution_add_fusion.5 = f32[4096,16]{0,1:T(8,128)S(1)} fusion(bf16[32,4096]{1,0:T(8,128)(2,1)S(1)} %get-tuple-element.187, f32[256]{0:T(256)S(1)} %bitcast.77, f32[4096]{0:T(1024)S(1)} %get-tuple-element.184, f32[]{:T(128)} %get-tuple-element.183, f32[4096,16]{0,1:T(8,128)S(1)} %get-tuple-element.172, pred[]{:T(512)S(6)} %compare.3, ...), kind=kOutput, calls=%fused_computation.3.clone.1 | convolution fusion | flops 112328704 | bytes 829956 | tf_op jit(solution)/shard_map/while/body/eval_jaxpr/dot_general | solution.py:44
  67.6 3.7 %convolution_add_fusion.5 = f32[4096,16]{0,1:T(8,128)S(1)} fusion(bf16[32,4096]{1,0:T(8,128)(2,1)S(1)} %get-tuple-element.187, f32[256]{0:T(256)S(1)} %bitcast.77, f32[4096]{0:T(1024)S(1)} %get-tuple-element.184, f32[]{:T(128)} %get-tuple-element.183, f32[4096,16]{0,1:T(8,128)S(1)} %get-tuple-element.172, pred[]{:T(512)S(6)} %compare.3, ...), kind=kOutput, calls=%fused_computation.3.clone.1 | convolution fusion | flops 112328704 | bytes 829956 | tf_op jit(solution)/shard_map/while/body/eval_jaxpr/dot_general | solution.py:44
  71.3 3.7 %convolution_add_fusion.5 = f32[4096,16]{0,1:T(8,128)S(1)} fusion(bf16[32,4096]{1,0:T(8,128)(2,1)S(1)} %get-tuple-element.187, f32[256]{0:T(256)S(1)} %bitcast.77, f32[4096]{0:T(1024)S(1)} %get-tuple-element.184, f32[]{:T(128)} %get-tuple-element.183, f32[4096,16]{0,1:T(8,128)S(1)} %get-tuple-element.172, pred[]{:T(512)S(6)} %compare.3, ...), kind=kOutput, calls=%fused_computation.3.clone.1 | convolution fusion | flops 112328704 | bytes 829956 | tf_op jit(solution)/shard_map/while/body/eval_jaxpr/dot_general | solution.py:44
  75.1 3.7 %convolution_add_fusion.5 = f32[4096,16]{0,1:T(8,128)S(1)} fusion(bf16[32,4096]{1,0:T(8,128)(2,1)S(1)} %get-tuple-element.187, f32[256]{0:T(256)S(1)} %bitcast.77, f32[4096]{0:T(1024)S(1)} %get-tuple-element.184, f32[]{:T(128)} %get-tuple-element.183, f32[4096,16]{0,1:T(8,128)S(1)} %get-tuple-element.172, pred[]{:T(512)S(6)} %compare.3, ...), kind=kOutput, calls=%fused_computation.3.clone.1 | convolution fusion | flops 112328704 | bytes 829956 | tf_op jit(solution)/shard_map/while/body/eval_jaxpr/dot_general | solution.py:44
  78.9 3.7 %convolution_add_fusion.5 = f32[4096,16]{0,1:T(8,128)S(1)} fusion(bf16[32,4096]{1,0:T(8,128)(2,1)S(1)} %get-tuple-element.187, f32[256]{0:T(256)S(1)} %bitcast.77, f32[4096]{0:T(1024)S(1)} %get-tuple-element.184, f32[]{:T(128)} %get-tuple-element.183, f32[4096,16]{0,1:T(8,128)S(1)} %get-tuple-element.172, pred[]{:T(512)S(6)} %compare.3, ...), kind=kOutput, calls=%fused_computation.3.clone.1 | convolution fusion | flops 112328704 | bytes 829956 | tf_op jit(solution)/shard_map/while/body/eval_jaxpr/dot_general | solution.py:44
  82.6 3.7 %convolution_add_fusion.5 = f32[4096,16]{0,1:T(8,128)S(1)} fusion(bf16[32,4096]{1,0:T(8,128)(2,1)S(1)} %get-tuple-element.187, f32[256]{0:T(256)S(1)} %bitcast.77, f32[4096]{0:T(1024)S(1)} %get-tuple-element.184, f32[]{:T(128)} %get-tuple-element.183, f32[4096,16]{0,1:T(8,128)S(1)} %get-tuple-element.172, pred[]{:T(512)S(6)} %compare.3, ...), kind=kOutput, calls=%fused_computation.3.clone.1 | convolution fusion | flops 112328704 | bytes 829956 | tf_op jit(solution)/shard_map/while/body/eval_jaxpr/dot_general | solution.py:44
  86.4 3.7 %convolution_add_fusion.5 = f32[4096,16]{0,1:T(8,128)S(1)} fusion(bf16[32,4096]{1,0:T(8,128)(2,1)S(1)} %get-tuple-element.187, f32[256]{0:T(256)S(1)} %bitcast.77, f32[4096]{0:T(1024)S(1)} %get-tuple-element.184, f32[]{:T(128)} %get-tuple-element.183, f32[4096,16]{0,1:T(8,128)S(1)} %get-tuple-element.172, pred[]{:T(512)S(6)} %compare.3, ...), kind=kOutput, calls=%fused_computation.3.clone.1 | convolution fusion | flops 112328704 | bytes 829956 | tf_op jit(solution)/shard_map/while/body/eval_jaxpr/dot_general | solution.py:44
  90.2 3.7 %convolution_add_fusion.5 = f32[4096,16]{0,1:T(8,128)S(1)} fusion(bf16[32,4096]{1,0:T(8,128)(2,1)S(1)} %get-tuple-element.187, f32[256]{0:T(256)S(1)} %bitcast.77, f32[4096]{0:T(1024)S(1)} %get-tuple-element.184, f32[]{:T(128)} %get-tuple-element.183, f32[4096,16]{0,1:T(8,128)S(1)} %get-tuple-element.172, pred[]{:T(512)S(6)} %compare.3, ...), kind=kOutput, calls=%fused_computation.3.clone.1 | convolution fusion | flops 112328704 | bytes 829956 | tf_op jit(solution)/shard_map/while/body/eval_jaxpr/dot_general | solution.py:44
  93.9 3.7 %convolution_add_fusion.5 = f32[4096,16]{0,1:T(8,128)S(1)} fusion(bf16[32,4096]{1,0:T(8,128)(2,1)S(1)} %get-tuple-element.187, f32[256]{0:T(256)S(1)} %bitcast.77, f32[4096]{0:T(1024)S(1)} %get-tuple-element.184, f32[]{:T(128)} %get-tuple-element.183, f32[4096,16]{0,1:T(8,128)S(1)} %get-tuple-element.172, pred[]{:T(512)S(6)} %compare.3, ...), kind=kOutput, calls=%fused_computation.3.clone.1 | convolution fusion | flops 112328704 | bytes 829956 | tf_op jit(solution)/shard_map/while/body/eval_jaxpr/dot_general | solution.py:44
  97.7 3.7 %convolution_add_fusion.5 = f32[4096,16]{0,1:T(8,128)S(1)} fusion(bf16[32,4096]{1,0:T(8,128)(2,1)S(1)} %get-tuple-element.187, f32[256]{0:T(256)S(1)} %bitcast.77, f32[4096]{0:T(1024)S(1)} %get-tuple-element.184, f32[]{:T(128)} %get-tuple-element.183, f32[4096,16]{0,1:T(8,128)S(1)} %get-tuple-element.172, pred[]{:T(512)S(6)} %compare.3, ...), kind=kOutput, calls=%fused_computation.3.clone.1 | convolution fusion | flops 112328704 | bytes 829956 | tf_op jit(solution)/shard_map/while/body/eval_jaxpr/dot_general | solution.py:44
  101.5 1.5 collective-permute-done.8
  104.3 7.3 %collective-permute-done.9 = f32[16,4096]{1,0:T(8,128)S(1)} collective-permute-done((f32[16,4096]{1,0:T(8,128)S(1)}, f32[16,4096]{1,0:T(8,128)S(1)}, u32[]{:S(2)}, u32[]{:S(2)}) %collective-permute-start.9) | collective-permute-done | bytes 262176 | tf_op jit(solution)/shard_map/ppermute | solution.py:98
  111.5 2.4 %collective-permute-start.10 = (f32[16,4096]{1,0:T(8,128)S(1)}, f32[16,4096]{1,0:T(8,128)S(1)}, u32[]{:S(2)}, u32[]{:S(2)}) collective-permute-start(f32[16,4096]{1,0:T(8,128)S(1)} %add.212), channel_id=1, source_target_pairs={{0,4},{1,5},{2,6},{3,7},{4,0},{5,1},{6,2},{7,3},{8,12},{9,13},{10,... | collective-permute-start | bytes 786440 | tf_op jit(solution)/shard_map/ppermute | solution.py:98
  113.9 3.0 %multiply_convert_fusion.4 = bf16[1024,1024]{1,0:T(8,128)(2,1)S(1)} fusion(bf16[32,1024]{1,0:T(8,128)(2,1)S(1)} %mul.189, f32[1024]{0:T(1024)S(1)} %get-tuple-element.105, f32[1024]{0:T(1024)S(1)} %add.226, f32[]{:T(128)} %bitcast.62, bf16[96,4096]{1,0:T(8,128)(2,1)S(1)} %maximum_select_fusion.1), kind=kOutput, calls=%fused_computation.19 | convolution fusion | flops 78643200 | bytes 2236420 | tf_op jit(solution)/shard_map/dot_general | solution.py:19
  117.0 3.8 %collective-permute-done.10 = f32[16,4096]{1,0:T(8,128)S(1)} collective-permute-done((f32[16,4096]{1,0:T(8,128)S(1)}, f32[16,4096]{1,0:T(8,128)S(1)}, u32[]{:S(2)}, u32[]{:S(2)}) %collective-permute-start.10) | collective-permute-done | bytes 262176 | tf_op jit(solution)/shard_map/ppermute | solution.py:98
  120.8 0.9 collective-permute-start.11
  121.7 3.0 %multiply_convert_fusion.3 = bf16[1024,1024]{1,0:T(8,128)(2,1)S(1)} fusion(bf16[32,1024]{1,0:T(8,128)(2,1)S(1)} %mul.189, f32[1024]{0:T(1024)S(1)} %get-tuple-element.104, f32[1024]{0:T(1024)S(1)} %add.226, f32[]{:T(128)} %bitcast.65, bf16[96,4096]{1,0:T(8,128)(2,1)S(1)} %maximum_select_fusion.1), kind=kOutput, calls=%fused_computation.18 | convolution fusion | flops 78643200 | bytes 2236420 | tf_op jit(solution)/shard_map/dot_general | solution.py:19
  124.8 4.3 %collective-permute-done.11 = f32[16,4096]{1,0:T(8,128)S(1)} collective-permute-done((f32[16,4096]{1,0:T(8,128)S(1)}, f32[16,4096]{1,0:T(8,128)S(1)}, u32[]{:S(2)}, u32[]{:S(2)}) %collective-permute-start.11) | collective-permute-done | bytes 262176 | tf_op jit(solution)/shard_map/ppermute | solution.py:98
  129.4 0.7 collective-permute-start.12
  130.1 3.0 %multiply_convert_fusion.2 = bf16[1024,1024]{1,0:T(8,128)(2,1)S(1)} fusion(bf16[32,1024]{1,0:T(8,128)(2,1)S(1)} %mul.189, f32[1024]{0:T(1024)S(1)} %get-tuple-element.103, f32[1024]{0:T(1024)S(1)} %add.226, f32[]{:T(128)} %bitcast.64, bf16[96,4096]{1,0:T(8,128)(2,1)S(1)} %maximum_select_fusion.1), kind=kOutput, calls=%fused_computation.17 | convolution fusion | flops 78643200 | bytes 2236420 | tf_op jit(solution)/shard_map/dot_general | solution.py:19
  133.8 3.0 %multiply_convert_fusion.1 = bf16[1024,1024]{1,0:T(8,128)(2,1)S(1)} fusion(bf16[32,1024]{1,0:T(8,128)(2,1)S(1)} %mul.189, f32[1024]{0:T(1024)S(1)} %get-tuple-element.102, f32[1024]{0:T(1024)S(1)} %add.226, f32[]{:T(128)} %bitcast.63, bf16[96,4096]{1,0:T(8,128)(2,1)S(1)} %maximum_select_fusion.1), kind=kOutput, calls=%fused_computation.16 | convolution fusion | flops 78643200 | bytes 2236420 | tf_op jit(solution)/shard_map/dot_general | solution.py:19
  136.9 2.0 %collective-permute-start.14 = (f32[32]{0:T(128)S(1)}, f32[32]{0:T(128)S(1)}, u32[]{:S(2)}, u32[]{:S(2)}) collective-permute-start(f32[32]{0:T(128)S(1)} %add.218), channel_id=1, source_target_pairs={{0,64},{16,80},{32,96},{48,112},{64,0},{80,16},{96,32},{112,48},{1... | collective-permute-start | bytes 392 | tf_op jit(solution)/shard_map/ppermute | solution.py:98
  138.9 2.5 %collective-permute-done.14 = f32[32]{0:T(128)S(1)} collective-permute-done((f32[32]{0:T(128)S(1)}, f32[32]{0:T(128)S(1)}, u32[]{:S(2)}, u32[]{:S(2)}) %collective-permute-start.14) | collective-permute-done | bytes 160 | tf_op jit(solution)/shard_map/ppermute | solution.py:98
  141.5 1.8 %collective-permute-start.15 = (f32[32]{0:T(128)S(1)}, f32[32]{0:T(128)S(1)}, u32[]{:S(2)}, u32[]{:S(2)}) collective-permute-start(f32[32]{0:T(128)S(1)} %add.219), channel_id=1, source_target_pairs={{0,128},{16,144},{32,160},{48,176},{64,192},{80,208},{96,224},{112... | collective-permute-start | bytes 392 | tf_op jit(solution)/shard_map/ppermute | solution.py:98
  143.2 5.7 %collective-permute-done.15 = f32[32]{0:T(128)S(1)} collective-permute-done((f32[32]{0:T(128)S(1)}, f32[32]{0:T(128)S(1)}, u32[]{:S(2)}, u32[]{:S(2)}) %collective-permute-start.15) | collective-permute-done | bytes 160 | tf_op jit(solution)/shard_map/ppermute | solution.py:98
  152.0 1.2 collective-permute-done.20
  153.2 0.9 collective-permute-start.21
  154.1 1.3 collective-permute-start.16
  155.4 2.3 %collective-permute-done.16 = f32[16]{0:T(128)S(1)} collective-permute-done((f32[16]{0:T(128)S(1)}, f32[16]{0:T(128)S(1)}, u32[]{:S(2)}, u32[]{:S(2)}) %collective-permute-start.16) | collective-permute-done | bytes 96 | tf_op jit(solution)/shard_map/ppermute | solution.py:98
  157.7 1.4 collective-permute-start.17
  159.1 2.1 %collective-permute-done.17 = f32[16]{0:T(128)S(1)} collective-permute-done((f32[16]{0:T(128)S(1)}, f32[16]{0:T(128)S(1)}, u32[]{:S(2)}, u32[]{:S(2)}) %collective-permute-start.17) | collective-permute-done | bytes 96 | tf_op jit(solution)/shard_map/ppermute | solution.py:98
  161.3 1.9 %collective-permute-start.18 = (f32[16]{0:T(128)S(1)}, f32[16]{0:T(128)S(1)}, u32[]{:S(2)}, u32[]{:S(2)}) collective-permute-start(f32[16]{0:T(128)S(1)} %add.252), channel_id=1, source_target_pairs={{0,64},{16,80},{32,96},{48,112},{64,0},{80,16},{96,32},{112,48},{1... | collective-permute-start | bytes 200 | tf_op jit(solution)/shard_map/ppermute | solution.py:98
  163.2 2.6 %collective-permute-done.18 = f32[16]{0:T(128)S(1)} collective-permute-done((f32[16]{0:T(128)S(1)}, f32[16]{0:T(128)S(1)}, u32[]{:S(2)}, u32[]{:S(2)}) %collective-permute-start.18) | collective-permute-done | bytes 96 | tf_op jit(solution)/shard_map/ppermute | solution.py:98
  165.7 1.8 collective-permute-start.19
  167.5 2.5 %collective-permute-start.22 = (f32[16,128]{1,0:T(8,128)S(1)}, f32[16,128]{1,0:T(8,128)S(1)}, u32[]{:S(2)}, u32[]{:S(2)}) collective-permute-start(f32[16,128]{1,0:T(8,128)S(1)} %slice_select_fusion.3), channel_id=1, source_target_pairs={{0,4},{1,5},{2,6},{3,7},{4,0},{5,1},{6,2},{7,3},{8,12},{9,13},{10,... | collective-permute-start | bytes 24584 | tf_op jit(solution)/shard_map/ppermute | solution.py:92
  170.0 3.2 %collective-permute-done.19 = f32[16]{0:T(128)S(1)} collective-permute-done((f32[16]{0:T(128)S(1)}, f32[16]{0:T(128)S(1)}, u32[]{:S(2)}, u32[]{:S(2)}) %collective-permute-start.19) | collective-permute-done | bytes 96 | tf_op jit(solution)/shard_map/ppermute | solution.py:98
  173.3 2.5 %collective-permute-start.23 = (f32[16,64]{1,0:T(8,128)S(1)}, f32[16,64]{1,0:T(8,128)S(1)}, u32[]{:S(2)}, u32[]{:S(2)}) collective-permute-start(f32[16,64]{1,0:T(8,128)S(1)} %slice_select_fusion.2), channel_id=1, source_target_pairs={{0,8},{1,9},{2,10},{3,11},{4,12},{5,13},{6,14},{7,15},{8,0},{9,1},... | collective-permute-start | bytes 12296 | tf_op jit(solution)/shard_map/ppermute | solution.py:92
  175.8 0.7 multiply_add_fusion.1
  176.5 2.0 %collective-permute-done.23 = f32[16,64]{1,0:T(8,128)S(1)} collective-permute-done((f32[16,64]{1,0:T(8,128)S(1)}, f32[16,64]{1,0:T(8,128)S(1)}, u32[]{:S(2)}, u32[]{:S(2)}) %collective-permute-start.23) | collective-permute-done | bytes 4128 | tf_op jit(solution)/shard_map/ppermute | solution.py:92
  (93 shorter events, 8.2 us)
Async XLA Ops:
  5.3 11.8 %collective-permute-start.4 = (bf16[96,256]{1,0:T(8,128)(2,1)S(1)}, bf16[96,256]{1,0:T(8,128)(2,1)S(1)}, u32[]{:S(2)}, u32[]{:S(2)}) collective-permute-start(bf16[96,256]{1,0:T(8,128)(2,1)S(1)} %constant_dynamic-update-slice_fusion.6), channel_id=1, source_target_pairs={{0,128},{16,144},{32,160},{48,176},{64,192},{80,208},{96,224},{112... | collective-permute-start | bytes 147464 | tf_op jit(solution)/shard_map/ppermute | solution.py:75
  13.9 5.6 %collective-permute-start = (bf16[104,256]{1,0:T(8,128)(2,1)S(1)}, bf16[104,256]{1,0:T(8,128)(2,1)S(1)}, u32[]{:S(2)}, u32[]{:S(2)}) collective-permute-start(bf16[104,256]{1,0:T(8,128)(2,1)S(1)} %constant_dynamic-update-slice_fusion), channel_id=1, source_target_pairs={{0,8},{1,9},{2,10},{3,11},{4,12},{5,13},{6,14},{7,15},{8,0},{9,1},... | collective-permute-start | bytes 159752 | tf_op jit(solution)/shard_map/ppermute | solution.py:75
  17.1 7.1 %collective-permute-start.5 = (bf16[96,512]{1,0:T(8,128)(2,1)S(1)}, bf16[96,512]{1,0:T(8,128)(2,1)S(1)}, u32[]{:S(2)}, u32[]{:S(2)}) collective-permute-start(bf16[96,512]{1,0:T(8,128)(2,1)S(1)} %maximum_select_fusion.7), channel_id=1, source_target_pairs={{0,64},{16,80},{32,96},{48,112},{64,0},{80,16},{96,32},{112,48},{1... | collective-permute-start | bytes 294920 | tf_op jit(solution)/shard_map/ppermute | solution.py:75
  19.5 6.3 %collective-permute-start.1 = (bf16[104,512]{1,0:T(8,128)(2,1)S(1)}, bf16[104,512]{1,0:T(8,128)(2,1)S(1)}, u32[]{:S(2)}, u32[]{:S(2)}) collective-permute-start(bf16[104,512]{1,0:T(8,128)(2,1)S(1)} %maximum_select_fusion.6), channel_id=1, source_target_pairs={{0,4},{1,5},{2,6},{3,7},{4,0},{5,1},{6,2},{7,3},{8,12},{9,13},{10,... | collective-permute-start | bytes 319496 | tf_op jit(solution)/shard_map/ppermute | solution.py:75
  24.2 6.4 %collective-permute-start.6 = (bf16[96,1024]{1,0:T(8,128)(2,1)S(1)}, bf16[96,1024]{1,0:T(8,128)(2,1)S(1)}, u32[]{:S(2)}, u32[]{:S(2)}) collective-permute-start(bf16[96,1024]{1,0:T(8,128)(2,1)S(1)} %maximum_select_fusion.5), channel_id=1, source_target_pairs={{0,32},{16,48},{32,0},{48,16},{64,96},{80,112},{96,64},{112,80},{1... | collective-permute-start | bytes 589832 | tf_op jit(solution)/shard_map/ppermute | solution.py:75
  25.9 6.9 %collective-permute-start.2 = (bf16[104,1024]{1,0:T(8,128)(2,1)S(1)}, bf16[104,1024]{1,0:T(8,128)(2,1)S(1)}, u32[]{:S(2)}, u32[]{:S(2)}) collective-permute-start(bf16[104,1024]{1,0:T(8,128)(2,1)S(1)} %maximum_select_fusion.4), channel_id=1, source_target_pairs={{0,2},{1,3},{2,0},{3,1},{4,6},{5,7},{6,4},{7,5},{8,10},{9,11},{10,... | collective-permute-start | bytes 638984 | tf_op jit(solution)/shard_map/ppermute | solution.py:75
  30.7 9.7 %collective-permute-start.7 = (bf16[96,2048]{1,0:T(8,128)(2,1)S(1)}, bf16[96,2048]{1,0:T(8,128)(2,1)S(1)}, u32[]{:S(2)}, u32[]{:S(2)}) collective-permute-start(bf16[96,2048]{1,0:T(8,128)(2,1)S(1)} %maximum_select_fusion.3), channel_id=1, source_target_pairs={{0,16},{16,0},{32,48},{48,32},{64,80},{80,64},{96,112},{112,96},{1... | collective-permute-start | bytes 1179656 | tf_op jit(solution)/shard_map/ppermute | solution.py:75
  32.9 7.9 %collective-permute-start.3 = (bf16[104,2048]{1,0:T(8,128)(2,1)S(1)}, bf16[104,2048]{1,0:T(8,128)(2,1)S(1)}, u32[]{:S(2)}, u32[]{:S(2)}) collective-permute-start(bf16[104,2048]{1,0:T(8,128)(2,1)S(1)} %maximum_select_fusion.2), channel_id=1, source_target_pairs={{0,1},{1,0},{2,3},{3,2},{4,5},{5,4},{6,7},{7,6},{8,9},{9,8},{10,11... | collective-permute-start | bytes 1277960 | tf_op jit(solution)/shard_map/ppermute | solution.py:75
  101.4 1.6 collective-permute-start.8
  103.1 8.4 %collective-permute-start.9 = (f32[16,4096]{1,0:T(8,128)S(1)}, f32[16,4096]{1,0:T(8,128)S(1)}, u32[]{:S(2)}, u32[]{:S(2)}) collective-permute-start(f32[16,4096]{1,0:T(8,128)S(1)} %bitcast_add_fusion), channel_id=1, source_target_pairs={{0,2},{1,3},{2,0},{3,1},{4,6},{5,7},{6,4},{7,5},{8,10},{9,11},{10,... | collective-permute-start | bytes 786440 | tf_op jit(solution)/shard_map/ppermute | solution.py:98
  111.5 9.3 %collective-permute-start.10 = (f32[16,4096]{1,0:T(8,128)S(1)}, f32[16,4096]{1,0:T(8,128)S(1)}, u32[]{:S(2)}, u32[]{:S(2)}) collective-permute-start(f32[16,4096]{1,0:T(8,128)S(1)} %add.212), channel_id=1, source_target_pairs={{0,4},{1,5},{2,6},{3,7},{4,0},{5,1},{6,2},{7,3},{8,12},{9,13},{10,... | collective-permute-start | bytes 786440 | tf_op jit(solution)/shard_map/ppermute | solution.py:98
  120.8 8.2 %collective-permute-start.11 = (f32[16,4096]{1,0:T(8,128)S(1)}, f32[16,4096]{1,0:T(8,128)S(1)}, u32[]{:S(2)}, u32[]{:S(2)}) collective-permute-start(f32[16,4096]{1,0:T(8,128)S(1)} %add.213), channel_id=1, source_target_pairs={{0,8},{1,9},{2,10},{3,11},{4,12},{5,13},{6,14},{7,15},{8,0},{9,1},... | collective-permute-start | bytes 786440 | tf_op jit(solution)/shard_map/ppermute | solution.py:98
  129.4 3.8 %collective-permute-start.12 = (f32[32]{0:T(128)S(1)}, f32[32]{0:T(128)S(1)}, u32[]{:S(2)}, u32[]{:S(2)}) collective-permute-start(f32[32]{0:T(128)S(1)} %pad_maximum_fusion), channel_id=1, source_target_pairs={{0,16},{16,0},{32,48},{48,32},{64,80},{80,64},{96,112},{112,96},{1... | collective-permute-start | bytes 392 | tf_op jit(solution)/shard_map/ppermute | solution.py:98
  133.2 3.7 %collective-permute-start.13 = (f32[32]{0:T(128)S(1)}, f32[32]{0:T(128)S(1)}, u32[]{:S(2)}, u32[]{:S(2)}) collective-permute-start(f32[32]{0:T(128)S(1)} %add.217), channel_id=1, source_target_pairs={{0,32},{16,48},{32,0},{48,16},{64,96},{80,112},{96,64},{112,80},{1... | collective-permute-start | bytes 392 | tf_op jit(solution)/shard_map/ppermute | solution.py:98
  136.9 4.6 %collective-permute-start.14 = (f32[32]{0:T(128)S(1)}, f32[32]{0:T(128)S(1)}, u32[]{:S(2)}, u32[]{:S(2)}) collective-permute-start(f32[32]{0:T(128)S(1)} %add.218), channel_id=1, source_target_pairs={{0,64},{16,80},{32,96},{48,112},{64,0},{80,16},{96,32},{112,48},{1... | collective-permute-start | bytes 392 | tf_op jit(solution)/shard_map/ppermute | solution.py:98
  141.5 7.5 %collective-permute-start.15 = (f32[32]{0:T(128)S(1)}, f32[32]{0:T(128)S(1)}, u32[]{:S(2)}, u32[]{:S(2)}) collective-permute-start(f32[32]{0:T(128)S(1)} %add.219), channel_id=1, source_target_pairs={{0,128},{16,144},{32,160},{48,176},{64,192},{80,208},{96,224},{112... | collective-permute-start | bytes 392 | tf_op jit(solution)/shard_map/ppermute | solution.py:98
  150.6 25.2 %copy-start = (f32[16,256]{1,0:T(8,128)S(1)}, f32[16,256]{1,0:T(8,128)}, u32[]{:S(2)}) copy-start(f32[16,256]{1,0:T(8,128)} %param.19) | copy-start | bytes 49156
  150.6 25.2 %copy-start.1 = (f32[16,256]{1,0:T(8,128)S(1)}, f32[16,256]{1,0:T(8,128)}, u32[]{:S(2)}) copy-start(f32[16,256]{1,0:T(8,128)} %param.17) | copy-start | bytes 49156
  150.6 25.2 %copy-start.2 = (f32[16,256]{1,0:T(8,128)S(1)}, f32[16,256]{1,0:T(8,128)}, u32[]{:S(2)}) copy-start(f32[16,256]{1,0:T(8,128)} %param.18) | copy-start | bytes 49156
  150.6 27.9 %copy-start.3 = (f32[64]{0:T(128)S(1)}, f32[64]{0:T(128)}, u32[]{:S(2)}) copy-start(f32[64]{0:T(128)} %param.16) | copy-start | bytes 772
  151.9 1.3 collective-permute-start.20
  153.2 14.3 %collective-permute-start.21 = (f32[16,256]{1,0:T(8,128)S(1)}, f32[16,256]{1,0:T(8,128)S(1)}, u32[]{:S(2)}, u32[]{:S(2)}) collective-permute-start(f32[16,256]{1,0:T(8,128)S(1)} %slice_select_fusion.1), channel_id=1, source_target_pairs={{0,2},{1,3},{2,0},{3,1},{4,6},{5,7},{6,4},{7,5},{8,10},{9,11},{10,... | collective-permute-start | bytes 49160 | tf_op jit(solution)/shard_map/ppermute | solution.py:92
  154.1 3.6 %collective-permute-start.16 = (f32[16]{0:T(128)S(1)}, f32[16]{0:T(128)S(1)}, u32[]{:S(2)}, u32[]{:S(2)}) collective-permute-start(f32[16]{0:T(128)S(1)} %get-tuple-element.50), channel_id=1, source_target_pairs={{0,16},{16,0},{32,48},{48,32},{64,80},{80,64},{96,112},{112,96},{1... | collective-permute-start | bytes 200 | tf_op jit(solution)/shard_map/ppermute | solution.py:98
  157.7 3.6 %collective-permute-start.17 = (f32[16]{0:T(128)S(1)}, f32[16]{0:T(128)S(1)}, u32[]{:S(2)}, u32[]{:S(2)}) collective-permute-start(f32[16]{0:T(128)S(1)} %add.251), channel_id=1, source_target_pairs={{0,32},{16,48},{32,0},{48,16},{64,96},{80,112},{96,64},{112,80},{1... | collective-permute-start | bytes 200 | tf_op jit(solution)/shard_map/ppermute | solution.py:98
  161.3 4.5 %collective-permute-start.18 = (f32[16]{0:T(128)S(1)}, f32[16]{0:T(128)S(1)}, u32[]{:S(2)}, u32[]{:S(2)}) collective-permute-start(f32[16]{0:T(128)S(1)} %add.252), channel_id=1, source_target_pairs={{0,64},{16,80},{32,96},{48,112},{64,0},{80,16},{96,32},{112,48},{1... | collective-permute-start | bytes 200 | tf_op jit(solution)/shard_map/ppermute | solution.py:98
  165.7 7.5 %collective-permute-start.19 = (f32[16]{0:T(128)S(1)}, f32[16]{0:T(128)S(1)}, u32[]{:S(2)}, u32[]{:S(2)}) collective-permute-start(f32[16]{0:T(128)S(1)} %add.253), channel_id=1, source_target_pairs={{0,128},{16,144},{32,160},{48,176},{64,192},{80,208},{96,224},{112... | collective-permute-start | bytes 200 | tf_op jit(solution)/shard_map/ppermute | solution.py:98
  167.5 5.7 %collective-permute-start.22 = (f32[16,128]{1,0:T(8,128)S(1)}, f32[16,128]{1,0:T(8,128)S(1)}, u32[]{:S(2)}, u32[]{:S(2)}) collective-permute-start(f32[16,128]{1,0:T(8,128)S(1)} %slice_select_fusion.3), channel_id=1, source_target_pairs={{0,4},{1,5},{2,6},{3,7},{4,0},{5,1},{6,2},{7,3},{8,12},{9,13},{10,... | collective-permute-start | bytes 24584 | tf_op jit(solution)/shard_map/ppermute | solution.py:92
  173.3 5.2 %collective-permute-start.23 = (f32[16,64]{1,0:T(8,128)S(1)}, f32[16,64]{1,0:T(8,128)S(1)}, u32[]{:S(2)}, u32[]{:S(2)}) collective-permute-start(f32[16,64]{1,0:T(8,128)S(1)} %slice_select_fusion.2), channel_id=1, source_target_pairs={{0,8},{1,9},{2,10},{3,11},{4,12},{5,13},{6,14},{7,15},{8,0},{9,1},... | collective-permute-start | bytes 12296 | tf_op jit(solution)/shard_map/ppermute | solution.py:92

commit v7 on v6

--- a/solution.py
+++ b/solution.py
@@ -7,6 +7,7 @@
 
 
 root_five = math.sqrt(5.0)
+exp2_scale = -root_five / math.log(2.0)
 contract_first = (((0,), (0,)), ((), ()))
 contract_last = (((1,), (1,)), ((), ()))
 
@@ -24,7 +25,7 @@
     kern_vals = (
         signal_scalar
         * (1.0 + root_five * distance + 5.0 / 3.0 * dist_sq)
-        * jnp.exp(-root_five * distance)
+        * jnp.exp2(distance * exp2_scale)
     )
     return kern_vals.astype(jnp.bfloat16)
 
@@ -167,9 +168,8 @@
         row_pts * jnp.asarray(-2.0, jnp.bfloat16), row_sq, col_pts, col_sq, col_dir, signal_scalar, 256
     )
     cand_blocks = []
-    pieces = 4
-    width = col_pts.shape[1] // pieces
-    for k in range(pieces):
+    width = col_pts.shape[1] // 2
+    for k in range(2):
         lo, hi = k * width, (k + 1) * width
         cand_blocks.append(
             lax.optimization_barrier(
@@ -200,7 +200,7 @@
 
     w_low_col = (w_col + step_len[:, None] * d_col).astype(jnp.bfloat16)
     partial_fit = None
-    for k in range(pieces):
+    for k in range(2):
         lo, hi = k * width, (k + 1) * width
         part = lax.dot_general(
             w_low_col[:, lo:hi], cand_blocks[k], contract_last,

time: 181 us -> 187 us (1.033)
  waiting for transfers between devices: 54.8 us -> 66.1 us
  starting transfers between devices: 37.2 us -> 32 us
    ppermute x12, waiting for transfers between devices: 35.3 us -> 44.7 us  [all_sum(): x = x + lax.ppermute(x, axis_name, xor_perm(size, bit))]
    ppermute x12, starting transfers between devices: 15.5 us -> 11.1 us  [all_sum(): x = x + lax.ppermute(x, axis_name, xor_perm(size, bit))]
    dot_general x4 -> x2, matrix products: 12.2 us -> 11.6 us  [matern_block(): lax.dot_general(row_pts_m2, col_pts, contract_first, preferred_element_ty...]
  transfers between devices with their start and end apart: 24 -> 24, of which waited for: 17 -> 18; matrix products, arithmetic and copies ran while one was open for 9% -> 8% of each run, Pallas kernels for 0% -> 0%
where the time goes in v7:
time: 187 us; the launch traced here: 185 us
  matrix products  73.7 us (39%)
  waiting for transfers between devices  66.1 us (35%)
  starting transfers between devices  32 us (17%)
  other arithmetic  9.16 us (5%)
  between operations  2.31 us (1%)
    dot_general x16, matrix products, one_block(): lax.dot_general(kern_vals, vec_blk, contract_last, preferred_element_type...  59.7 us
    ppermute x12, waiting for transfers between devices, all_sum(): x = x + lax.ppermute(x, axis_name, xor_perm(size, bit))  44.7 us
    ppermute x8, waiting for transfers between devices, gather_last(): recv = lax.ppermute(buf, axis_name, xor_perm(size, bit))  17.6 us
    ppermute x8, starting transfers between devices, gather_last(): recv = lax.ppermute(buf, axis_name, xor_perm(size, bit))  15.7 us
    dot_general x2, matrix products, matern_block(): lax.dot_general(row_pts_m2, col_pts, contract_first, preferred_element_ty...  11.6 us
    ppermute x12, starting transfers between devices, all_sum(): x = x + lax.ppermute(x, axis_name, xor_perm(size, bit))  11.1 us
    ppermute x4, starting transfers between devices, reduce_scatter_last(): buf = keep + lax.ppermute(send, axis_name, xor_perm(size, bit))  5.2 us
    ppermute x4, waiting for transfers between devices, reduce_scatter_last(): buf = keep + lax.ppermute(send, axis_name, xor_perm(size, bit))  3.86 us
  transfers between devices with their start and end apart: 24, of which 18 were waited for; matrix products, arithmetic and copies ran while one was open for 8% of the time, Pallas kernels for 0%

profile of v7, /device:TPU:2, one launch (start us, length us, event | category | flops | bytes accessed | tf_op | source)
XLA Modules:
  0.0 184.6 jit_solution(10019343988074571816)
XLA Ops:
  0.6 0.8 constant_dynamic-update-slice_fusion.10
  1.5 0.8 divide_convert_fusion.1
  2.4 0.7 constant_dynamic-update-slice_fusion.9
  3.1 0.7 constant_dynamic-update-slice_fusion.8
  3.8 0.7 constant_dynamic-update-slice_fusion.7
  4.5 0.7 constant_dynamic-update-slice_fusion.6
  5.3 7.2 %collective-permute-start.4 = (bf16[96,256]{1,0:T(8,128)(2,1)S(1)}, bf16[96,256]{1,0:T(8,128)(2,1)S(1)}, u32[]{:S(2)}, u32[]{:S(2)}) collective-permute-start(bf16[96,256]{1,0:T(8,128)(2,1)S(1)} %constant_dynamic-update-slice_fusion.6), channel_id=1, source_target_pairs={{0,128},{16,144},{32,160},{48,176},{64,192},{80,208},{96,224},{112... | collective-permute-start | bytes 147464 | tf_op jit(solution)/shard_map/ppermute | solution.py:76
  12.4 0.7 constant_dynamic-update-slice_fusion.1
  13.2 0.7 constant_dynamic-update-slice_fusion
  13.9 3.2 %collective-permute-start = (bf16[104,256]{1,0:T(8,128)(2,1)S(1)}, bf16[104,256]{1,0:T(8,128)(2,1)S(1)}, u32[]{:S(2)}, u32[]{:S(2)}) collective-permute-start(bf16[104,256]{1,0:T(8,128)(2,1)S(1)} %constant_dynamic-update-slice_fusion), channel_id=1, source_target_pairs={{0,8},{1,9},{2,10},{3,11},{4,12},{5,13},{6,14},{7,15},{8,0},{9,1},... | collective-permute-start | bytes 159752 | tf_op jit(solution)/shard_map/ppermute | solution.py:76
  17.1 1.6 collective-permute-start.5
  18.7 0.9 collective-permute-done
  19.5 2.2 %collective-permute-start.1 = (bf16[104,512]{1,0:T(8,128)(2,1)S(1)}, bf16[104,512]{1,0:T(8,128)(2,1)S(1)}, u32[]{:S(2)}, u32[]{:S(2)}) collective-permute-start(bf16[104,512]{1,0:T(8,128)(2,1)S(1)} %maximum_select_fusion.6), channel_id=1, source_target_pairs={{0,4},{1,5},{2,6},{3,7},{4,0},{5,1},{6,2},{7,3},{8,12},{9,13},{10,... | collective-permute-start | bytes 319496 | tf_op jit(solution)/shard_map/ppermute | solution.py:76
  21.8 2.4 %collective-permute-done.5 = bf16[96,512]{1,0:T(8,128)(2,1)S(1)} collective-permute-done((bf16[96,512]{1,0:T(8,128)(2,1)S(1)}, bf16[96,512]{1,0:T(8,128)(2,1)S(1)}, u32[]{:S(2)}, u32[]{:S(2)}) %collective-permute-start.5) | collective-permute-done | bytes 98336 | tf_op jit(solution)/shard_map/ppermute | solution.py:76
  24.4 1.5 collective-permute-done.1
  26.5 4.1 %collective-permute-done.6 = bf16[96,1024]{1,0:T(8,128)(2,1)S(1)} collective-permute-done((bf16[96,1024]{1,0:T(8,128)(2,1)S(1)}, bf16[96,1024]{1,0:T(8,128)(2,1)S(1)}, u32[]{:S(2)}, u32[]{:S(2)}) %collective-permute-start.6) | collective-permute-done | bytes 196640 | tf_op jit(solution)/shard_map/ppermute | solution.py:76
  30.7 0.8 collective-permute-start.7
  32.1 8.4 %collective-permute-done.7 = bf16[96,2048]{1,0:T(8,128)(2,1)S(1)} collective-permute-done((bf16[96,2048]{1,0:T(8,128)(2,1)S(1)}, bf16[96,2048]{1,0:T(8,128)(2,1)S(1)}, u32[]{:S(2)}, u32[]{:S(2)}) %collective-permute-start.7) | collective-permute-done | bytes 393248 | tf_op jit(solution)/shard_map/ppermute | solution.py:76
  41.1 60.4 %while.13 = (s32[]{:T(128)}, f32[4096,16]{0,1:T(8,128)S(1)}, f32[]{:T(128)}, f32[4096]{0:T(1024)S(1)}, f32[16,256]{1,0:T(8,128)S(1)}, /*index=5*/bf16[16,32,256]...) while((s32[]{:T(128)}, f32[4096,16]{0,1:T(8,128)S(1)}, ...), condition=%wide.region_4.5_spmd.clone, body=%wide.region_3.4_spmd.clone.sunk | while | flops 112328704 | bytes 832126 | solution.py:52
  41.2 3.7 %convolution_add_fusion.3 = f32[4096,16]{0,1:T(8,128)S(1)} fusion(bf16[32,4096]{1,0:T(8,128)(2,1)S(1)} %get-tuple-element.244, f32[256]{0:T(256)S(1)} %bitcast.71, f32[4096]{0:T(1024)S(1)} %get-tuple-element.241, f32[]{:T(128)} %get-tuple-element.240, f32[4096,16]{0,1:T(8,128)S(1)} %get-tuple-element.229, pred[]{:T(512)S(6)} %compare.3, ...), kind=kOutput, calls=%fused_computation.3.clone.1 | convolution fusion | flops 112328704 | bytes 829956 | tf_op jit(solution)/shard_map/while/body/eval_jaxpr/dot_general | solution.py:45
  44.9 3.7 %convolution_add_fusion.3 = f32[4096,16]{0,1:T(8,128)S(1)} fusion(bf16[32,4096]{1,0:T(8,128)(2,1)S(1)} %get-tuple-element.244, f32[256]{0:T(256)S(1)} %bitcast.71, f32[4096]{0:T(1024)S(1)} %get-tuple-element.241, f32[]{:T(128)} %get-tuple-element.240, f32[4096,16]{0,1:T(8,128)S(1)} %get-tuple-element.229, pred[]{:T(512)S(6)} %compare.3, ...), kind=kOutput, calls=%fused_computation.3.clone.1 | convolution fusion | flops 112328704 | bytes 829956 | tf_op jit(solution)/shard_map/while/body/eval_jaxpr/dot_general | solution.py:45
  48.7 3.7 %convolution_add_fusion.3 = f32[4096,16]{0,1:T(8,128)S(1)} fusion(bf16[32,4096]{1,0:T(8,128)(2,1)S(1)} %get-tuple-element.244, f32[256]{0:T(256)S(1)} %bitcast.71, f32[4096]{0:T(1024)S(1)} %get-tuple-element.241, f32[]{:T(128)} %get-tuple-element.240, f32[4096,16]{0,1:T(8,128)S(1)} %get-tuple-element.229, pred[]{:T(512)S(6)} %compare.3, ...), kind=kOutput, calls=%fused_computation.3.clone.1 | convolution fusion | flops 112328704 | bytes 829956 | tf_op jit(solution)/shard_map/while/body/eval_jaxpr/dot_general | solution.py:45
  52.5 3.7 %convolution_add_fusion.3 = f32[4096,16]{0,1:T(8,128)S(1)} fusion(bf16[32,4096]{1,0:T(8,128)(2,1)S(1)} %get-tuple-element.244, f32[256]{0:T(256)S(1)} %bitcast.71, f32[4096]{0:T(1024)S(1)} %get-tuple-element.241, f32[]{:T(128)} %get-tuple-element.240, f32[4096,16]{0,1:T(8,128)S(1)} %get-tuple-element.229, pred[]{:T(512)S(6)} %compare.3, ...), kind=kOutput, calls=%fused_computation.3.clone.1 | convolution fusion | flops 112328704 | bytes 829956 | tf_op jit(solution)/shard_map/while/body/eval_jaxpr/dot_general | solution.py:45
  56.3 3.7 %convolution_add_fusion.3 = f32[4096,16]{0,1:T(8,128)S(1)} fusion(bf16[32,4096]{1,0:T(8,128)(2,1)S(1)} %get-tuple-element.244, f32[256]{0:T(256)S(1)} %bitcast.71, f32[4096]{0:T(1024)S(1)} %get-tuple-element.241, f32[]{:T(128)} %get-tuple-element.240, f32[4096,16]{0,1:T(8,128)S(1)} %get-tuple-element.229, pred[]{:T(512)S(6)} %compare.3, ...), kind=kOutput, calls=%fused_computation.3.clone.1 | convolution fusion | flops 112328704 | bytes 829956 | tf_op jit(solution)/shard_map/while/body/eval_jaxpr/dot_general | solution.py:45
  60.0 3.7 %convolution_add_fusion.3 = f32[4096,16]{0,1:T(8,128)S(1)} fusion(bf16[32,4096]{1,0:T(8,128)(2,1)S(1)} %get-tuple-element.244, f32[256]{0:T(256)S(1)} %bitcast.71, f32[4096]{0:T(1024)S(1)} %get-tuple-element.241, f32[]{:T(128)} %get-tuple-element.240, f32[4096,16]{0,1:T(8,128)S(1)} %get-tuple-element.229, pred[]{:T(512)S(6)} %compare.3, ...), kind=kOutput, calls=%fused_computation.3.clone.1 | convolution fusion | flops 112328704 | bytes 829956 | tf_op jit(solution)/shard_map/while/body/eval_jaxpr/dot_general | solution.py:45
  63.8 3.7 %convolution_add_fusion.3 = f32[4096,16]{0,1:T(8,128)S(1)} fusion(bf16[32,4096]{1,0:T(8,128)(2,1)S(1)} %get-tuple-element.244, f32[256]{0:T(256)S(1)} %bitcast.71, f32[4096]{0:T(1024)S(1)} %get-tuple-element.241, f32[]{:T(128)} %get-tuple-element.240, f32[4096,16]{0,1:T(8,128)S(1)} %get-tuple-element.229, pred[]{:T(512)S(6)} %compare.3, ...), kind=kOutput, calls=%fused_computation.3.clone.1 | convolution fusion | flops 112328704 | bytes 829956 | tf_op jit(solution)/shard_map/while/body/eval_jaxpr/dot_general | solution.py:45
  67.6 3.7 %convolution_add_fusion.3 = f32[4096,16]{0,1:T(8,128)S(1)} fusion(bf16[32,4096]{1,0:T(8,128)(2,1)S(1)} %get-tuple-element.244, f32[256]{0:T(256)S(1)} %bitcast.71, f32[4096]{0:T(1024)S(1)} %get-tuple-element.241, f32[]{:T(128)} %get-tuple-element.240, f32[4096,16]{0,1:T(8,128)S(1)} %get-tuple-element.229, pred[]{:T(512)S(6)} %compare.3, ...), kind=kOutput, calls=%fused_computation.3.clone.1 | convolution fusion | flops 112328704 | bytes 829956 | tf_op jit(solution)/shard_map/while/body/eval_jaxpr/dot_general | solution.py:45
  71.4 3.7 %convolution_add_fusion.3 = f32[4096,16]{0,1:T(8,128)S(1)} fusion(bf16[32,4096]{1,0:T(8,128)(2,1)S(1)} %get-tuple-element.244, f32[256]{0:T(256)S(1)} %bitcast.71, f32[4096]{0:T(1024)S(1)} %get-tuple-element.241, f32[]{:T(128)} %get-tuple-element.240, f32[4096,16]{0,1:T(8,128)S(1)} %get-tuple-element.229, pred[]{:T(512)S(6)} %compare.3, ...), kind=kOutput, calls=%fused_computation.3.clone.1 | convolution fusion | flops 112328704 | bytes 829956 | tf_op jit(solution)/shard_map/while/body/eval_jaxpr/dot_general | solution.py:45
  75.1 3.7 %convolution_add_fusion.3 = f32[4096,16]{0,1:T(8,128)S(1)} fusion(bf16[32,4096]{1,0:T(8,128)(2,1)S(1)} %get-tuple-element.244, f32[256]{0:T(256)S(1)} %bitcast.71, f32[4096]{0:T(1024)S(1)} %get-tuple-element.241, f32[]{:T(128)} %get-tuple-element.240, f32[4096,16]{0,1:T(8,128)S(1)} %get-tuple-element.229, pred[]{:T(512)S(6)} %compare.3, ...), kind=kOutput, calls=%fused_computation.3.clone.1 | convolution fusion | flops 112328704 | bytes 829956 | tf_op jit(solution)/shard_map/while/body/eval_jaxpr/dot_general | solution.py:45
  78.9 3.7 %convolution_add_fusion.3 = f32[4096,16]{0,1:T(8,128)S(1)} fusion(bf16[32,4096]{1,0:T(8,128)(2,1)S(1)} %get-tuple-element.244, f32[256]{0:T(256)S(1)} %bitcast.71, f32[4096]{0:T(1024)S(1)} %get-tuple-element.241, f32[]{:T(128)} %get-tuple-element.240, f32[4096,16]{0,1:T(8,128)S(1)} %get-tuple-element.229, pred[]{:T(512)S(6)} %compare.3, ...), kind=kOutput, calls=%fused_computation.3.clone.1 | convolution fusion | flops 112328704 | bytes 829956 | tf_op jit(solution)/shard_map/while/body/eval_jaxpr/dot_general | solution.py:45
  82.7 3.7 %convolution_add_fusion.3 = f32[4096,16]{0,1:T(8,128)S(1)} fusion(bf16[32,4096]{1,0:T(8,128)(2,1)S(1)} %get-tuple-element.244, f32[256]{0:T(256)S(1)} %bitcast.71, f32[4096]{0:T(1024)S(1)} %get-tuple-element.241, f32[]{:T(128)} %get-tuple-element.240, f32[4096,16]{0,1:T(8,128)S(1)} %get-tuple-element.229, pred[]{:T(512)S(6)} %compare.3, ...), kind=kOutput, calls=%fused_computation.3.clone.1 | convolution fusion | flops 112328704 | bytes 829956 | tf_op jit(solution)/shard_map/while/body/eval_jaxpr/dot_general | solution.py:45
  86.4 3.7 %convolution_add_fusion.3 = f32[4096,16]{0,1:T(8,128)S(1)} fusion(bf16[32,4096]{1,0:T(8,128)(2,1)S(1)} %get-tuple-element.244, f32[256]{0:T(256)S(1)} %bitcast.71, f32[4096]{0:T(1024)S(1)} %get-tuple-element.241, f32[]{:T(128)} %get-tuple-element.240, f32[4096,16]{0,1:T(8,128)S(1)} %get-tuple-element.229, pred[]{:T(512)S(6)} %compare.3, ...), kind=kOutput, calls=%fused_computation.3.clone.1 | convolution fusion | flops 112328704 | bytes 829956 | tf_op jit(solution)/shard_map/while/body/eval_jaxpr/dot_general | solution.py:45
  90.2 3.7 %convolution_add_fusion.3 = f32[4096,16]{0,1:T(8,128)S(1)} fusion(bf16[32,4096]{1,0:T(8,128)(2,1)S(1)} %get-tuple-element.244, f32[256]{0:T(256)S(1)} %bitcast.71, f32[4096]{0:T(1024)S(1)} %get-tuple-element.241, f32[]{:T(128)} %get-tuple-element.240, f32[4096,16]{0,1:T(8,128)S(1)} %get-tuple-element.229, pred[]{:T(512)S(6)} %compare.3, ...), kind=kOutput, calls=%fused_computation.3.clone.1 | convolution fusion | flops 112328704 | bytes 829956 | tf_op jit(solution)/shard_map/while/body/eval_jaxpr/dot_general | solution.py:45
  94.0 3.7 %convolution_add_fusion.3 = f32[4096,16]{0,1:T(8,128)S(1)} fusion(bf16[32,4096]{1,0:T(8,128)(2,1)S(1)} %get-tuple-element.244, f32[256]{0:T(256)S(1)} %bitcast.71, f32[4096]{0:T(1024)S(1)} %get-tuple-element.241, f32[]{:T(128)} %get-tuple-element.240, f32[4096,16]{0,1:T(8,128)S(1)} %get-tuple-element.229, pred[]{:T(512)S(6)} %compare.3, ...), kind=kOutput, calls=%fused_computation.3.clone.1 | convolution fusion | flops 112328704 | bytes 829956 | tf_op jit(solution)/shard_map/while/body/eval_jaxpr/dot_general | solution.py:45
  97.8 3.7 %convolution_add_fusion.3 = f32[4096,16]{0,1:T(8,128)S(1)} fusion(bf16[32,4096]{1,0:T(8,128)(2,1)S(1)} %get-tuple-element.244, f32[256]{0:T(256)S(1)} %bitcast.71, f32[4096]{0:T(1024)S(1)} %get-tuple-element.241, f32[]{:T(128)} %get-tuple-element.240, f32[4096,16]{0,1:T(8,128)S(1)} %get-tuple-element.229, pred[]{:T(512)S(6)} %compare.3, ...), kind=kOutput, calls=%fused_computation.3.clone.1 | convolution fusion | flops 112328704 | bytes 829956 | tf_op jit(solution)/shard_map/while/body/eval_jaxpr/dot_general | solution.py:45
  101.6 1.5 collective-permute-done.8
  105.1 6.5 %collective-permute-done.9 = f32[16,4096]{1,0:T(8,128)S(1)} collective-permute-done((f32[16,4096]{1,0:T(8,128)S(1)}, f32[16,4096]{1,0:T(8,128)S(1)}, u32[]{:S(2)}, u32[]{:S(2)}) %collective-permute-start.9) | collective-permute-done | bytes 262176 | tf_op jit(solution)/shard_map/ppermute | solution.py:99
  111.6 2.2 %collective-permute-start.10 = (f32[16,4096]{1,0:T(8,128)S(1)}, f32[16,4096]{1,0:T(8,128)S(1)}, u32[]{:S(2)}, u32[]{:S(2)}) collective-permute-start(f32[16,4096]{1,0:T(8,128)S(1)} %add.193), channel_id=1, source_target_pairs={{0,4},{1,5},{2,6},{3,7},{4,0},{5,1},{6,2},{7,3},{8,12},{9,13},{10,... | collective-permute-start | bytes 786440 | tf_op jit(solution)/shard_map/ppermute | solution.py:99
  113.9 6.9 %collective-permute-done.10 = f32[16,4096]{1,0:T(8,128)S(1)} collective-permute-done((f32[16,4096]{1,0:T(8,128)S(1)}, f32[16,4096]{1,0:T(8,128)S(1)}, u32[]{:S(2)}, u32[]{:S(2)}) %collective-permute-start.10) | collective-permute-done | bytes 262176 | tf_op jit(solution)/shard_map/ppermute | solution.py:99
  120.7 0.9 collective-permute-start.11
  122.0 6.9 %collective-permute-done.11 = f32[16,4096]{1,0:T(8,128)S(1)} collective-permute-done((f32[16,4096]{1,0:T(8,128)S(1)}, f32[16,4096]{1,0:T(8,128)S(1)}, u32[]{:S(2)}, u32[]{:S(2)}) %collective-permute-start.11) | collective-permute-done | bytes 262176 | tf_op jit(solution)/shard_map/ppermute | solution.py:99
  129.3 0.9 collective-permute-start.12
  130.3 2.8 %collective-permute-done.12 = f32[32]{0:T(128)S(1)} collective-permute-done((f32[32]{0:T(128)S(1)}, f32[32]{0:T(128)S(1)}, u32[]{:S(2)}, u32[]{:S(2)}) %collective-permute-start.12) | collective-permute-done | bytes 160 | tf_op jit(solution)/shard_map/ppermute | solution.py:99
  133.6 5.8 %multiply_convert_fusion.2 = bf16[1024,2048]{1,0:T(8,128)(2,1)S(1)} fusion(bf16[32,1024]{1,0:T(8,128)(2,1)S(1)} %mul.164, f32[2048]{0:T(1024)S(1)} %get-tuple-element.162, f32[1024]{0:T(1024)S(1)} %add.207, f32[]{:T(128)} %bitcast.58, bf16[96,4096]{1,0:T(8,128)(2,1)S(1)} %maximum_select_fusion.1), kind=kOutput, calls=%fused_computation.17 | convolution fusion | flops 157286400 | bytes 4403204 | tf_op jit(solution)/shard_map/dot_general | solution.py:20
  139.4 2.0 %collective-permute-start.14 = (f32[32]{0:T(128)S(1)}, f32[32]{0:T(128)S(1)}, u32[]{:S(2)}, u32[]{:S(2)}) collective-permute-start(f32[32]{0:T(128)S(1)} %add.199), channel_id=1, source_target_pairs={{0,64},{16,80},{32,96},{48,112},{64,0},{80,16},{96,32},{112,48},{1... | collective-permute-start | bytes 392 | tf_op jit(solution)/shard_map/ppermute | solution.py:99
  141.5 5.8 %multiply_convert_fusion.1 = bf16[1024,2048]{1,0:T(8,128)(2,1)S(1)} fusion(bf16[32,1024]{1,0:T(8,128)(2,1)S(1)} %mul.164, f32[2048]{0:T(1024)S(1)} %get-tuple-element.161, f32[1024]{0:T(1024)S(1)} %add.207, f32[]{:T(128)} %bitcast.59, bf16[96,4096]{1,0:T(8,128)(2,1)S(1)} %maximum_select_fusion.1), kind=kOutput, calls=%fused_computation.16 | convolution fusion | flops 157286400 | bytes 4403204 | tf_op jit(solution)/shard_map/dot_general | solution.py:20
  147.3 0.8 collective-permute-start.15
  148.1 6.8 %collective-permute-done.15 = f32[32]{0:T(128)S(1)} collective-permute-done((f32[32]{0:T(128)S(1)}, f32[32]{0:T(128)S(1)}, u32[]{:S(2)}, u32[]{:S(2)}) %collective-permute-start.15) | collective-permute-done | bytes 160 | tf_op jit(solution)/shard_map/ppermute | solution.py:99
  155.2 1.2 fusion.18
  156.4 1.2 convolution_add_fusion.1
  157.7 1.2 collective-permute-done.20
  158.9 0.6 collective-permute-start.21
  159.6 0.7 collective-permute-start.16
  160.2 2.9 %collective-permute-done.16 = f32[16]{0:T(128)S(1)} collective-permute-done((f32[16]{0:T(128)S(1)}, f32[16]{0:T(128)S(1)}, u32[]{:S(2)}, u32[]{:S(2)}) %collective-permute-start.16) | collective-permute-done | bytes 96 | tf_op jit(solution)/shard_map/ppermute | solution.py:99
  163.7 3.0 %collective-permute-done.17 = f32[16]{0:T(128)S(1)} collective-permute-done((f32[16]{0:T(128)S(1)}, f32[16]{0:T(128)S(1)}, u32[]{:S(2)}, u32[]{:S(2)}) %collective-permute-start.17) | collective-permute-done | bytes 96 | tf_op jit(solution)/shard_map/ppermute | solution.py:99
  166.7 1.0 collective-permute-start.18
  167.7 3.5 %collective-permute-done.18 = f32[16]{0:T(128)S(1)} collective-permute-done((f32[16]{0:T(128)S(1)}, f32[16]{0:T(128)S(1)}, u32[]{:S(2)}, u32[]{:S(2)}) %collective-permute-start.18) | collective-permute-done | bytes 96 | tf_op jit(solution)/shard_map/ppermute | solution.py:99
  171.2 0.8 collective-permute-start.19
  172.0 2.7 %collective-permute-start.22 = (f32[16,128]{1,0:T(8,128)S(1)}, f32[16,128]{1,0:T(8,128)S(1)}, u32[]{:S(2)}, u32[]{:S(2)}) collective-permute-start(f32[16,128]{1,0:T(8,128)S(1)} %slice_select_fusion.3), channel_id=1, source_target_pairs={{0,4},{1,5},{2,6},{3,7},{4,0},{5,1},{6,2},{7,3},{8,12},{9,13},{10,... | collective-permute-start | bytes 24584 | tf_op jit(solution)/shard_map/ppermute | solution.py:93
  174.7 3.9 %collective-permute-done.19 = f32[16]{0:T(128)S(1)} collective-permute-done((f32[16]{0:T(128)S(1)}, f32[16]{0:T(128)S(1)}, u32[]{:S(2)}, u32[]{:S(2)}) %collective-permute-start.19) | collective-permute-done | bytes 96 | tf_op jit(solution)/shard_map/ppermute | solution.py:99
  178.7 1.8 collective-permute-start.23
  180.6 0.7 multiply_add_fusion.1
  181.3 2.7 %collective-permute-done.23 = f32[16,64]{1,0:T(8,128)S(1)} collective-permute-done((f32[16,64]{1,0:T(8,128)S(1)}, f32[16,64]{1,0:T(8,128)S(1)}, u32[]{:S(2)}, u32[]{:S(2)}) %collective-permute-start.23) | collective-permute-done | bytes 4128 | tf_op jit(solution)/shard_map/ppermute | solution.py:93
  183.9 0.7 add_add_fusion
  (89 shorter events, 5.8 us)
Async XLA Ops:
  5.3 11.8 %collective-permute-start.4 = (bf16[96,256]{1,0:T(8,128)(2,1)S(1)}, bf16[96,256]{1,0:T(8,128)(2,1)S(1)}, u32[]{:S(2)}, u32[]{:S(2)}) collective-permute-start(bf16[96,256]{1,0:T(8,128)(2,1)S(1)} %constant_dynamic-update-slice_fusion.6), channel_id=1, source_target_pairs={{0,128},{16,144},{32,160},{48,176},{64,192},{80,208},{96,224},{112... | collective-permute-start | bytes 147464 | tf_op jit(solution)/shard_map/ppermute | solution.py:76
  13.9 5.6 %collective-permute-start = (bf16[104,256]{1,0:T(8,128)(2,1)S(1)}, bf16[104,256]{1,0:T(8,128)(2,1)S(1)}, u32[]{:S(2)}, u32[]{:S(2)}) collective-permute-start(bf16[104,256]{1,0:T(8,128)(2,1)S(1)} %constant_dynamic-update-slice_fusion), channel_id=1, source_target_pairs={{0,8},{1,9},{2,10},{3,11},{4,12},{5,13},{6,14},{7,15},{8,0},{9,1},... | collective-permute-start | bytes 159752 | tf_op jit(solution)/shard_map/ppermute | solution.py:76
  17.1 7.1 %collective-permute-start.5 = (bf16[96,512]{1,0:T(8,128)(2,1)S(1)}, bf16[96,512]{1,0:T(8,128)(2,1)S(1)}, u32[]{:S(2)}, u32[]{:S(2)}) collective-permute-start(bf16[96,512]{1,0:T(8,128)(2,1)S(1)} %maximum_select_fusion.7), channel_id=1, source_target_pairs={{0,64},{16,80},{32,96},{48,112},{64,0},{80,16},{96,32},{112,48},{1... | collective-permute-start | bytes 294920 | tf_op jit(solution)/shard_map/ppermute | solution.py:76
  19.5 6.3 %collective-permute-start.1 = (bf16[104,512]{1,0:T(8,128)(2,1)S(1)}, bf16[104,512]{1,0:T(8,128)(2,1)S(1)}, u32[]{:S(2)}, u32[]{:S(2)}) collective-permute-start(bf16[104,512]{1,0:T(8,128)(2,1)S(1)} %maximum_select_fusion.6), channel_id=1, source_target_pairs={{0,4},{1,5},{2,6},{3,7},{4,0},{5,1},{6,2},{7,3},{8,12},{9,13},{10,... | collective-permute-start | bytes 319496 | tf_op jit(solution)/shard_map/ppermute | solution.py:76
  24.2 6.4 %collective-permute-start.6 = (bf16[96,1024]{1,0:T(8,128)(2,1)S(1)}, bf16[96,1024]{1,0:T(8,128)(2,1)S(1)}, u32[]{:S(2)}, u32[]{:S(2)}) collective-permute-start(bf16[96,1024]{1,0:T(8,128)(2,1)S(1)} %maximum_select_fusion.5), channel_id=1, source_target_pairs={{0,32},{16,48},{32,0},{48,16},{64,96},{80,112},{96,64},{112,80},{1... | collective-permute-start | bytes 589832 | tf_op jit(solution)/shard_map/ppermute | solution.py:76
  25.9 5.9 %collective-permute-start.2 = (bf16[104,1024]{1,0:T(8,128)(2,1)S(1)}, bf16[104,1024]{1,0:T(8,128)(2,1)S(1)}, u32[]{:S(2)}, u32[]{:S(2)}) collective-permute-start(bf16[104,1024]{1,0:T(8,128)(2,1)S(1)} %maximum_select_fusion.4), channel_id=1, source_target_pairs={{0,2},{1,3},{2,0},{3,1},{4,6},{5,7},{6,4},{7,5},{8,10},{9,11},{10,... | collective-permute-start | bytes 638984 | tf_op jit(solution)/shard_map/ppermute | solution.py:76
  30.7 9.7 %collective-permute-start.7 = (bf16[96,2048]{1,0:T(8,128)(2,1)S(1)}, bf16[96,2048]{1,0:T(8,128)(2,1)S(1)}, u32[]{:S(2)}, u32[]{:S(2)}) collective-permute-start(bf16[96,2048]{1,0:T(8,128)(2,1)S(1)} %maximum_select_fusion.3), channel_id=1, source_target_pairs={{0,16},{16,0},{32,48},{48,32},{64,80},{80,64},{96,112},{112,96},{1... | collective-permute-start | bytes 1179656 | tf_op jit(solution)/shard_map/ppermute | solution.py:76
  32.0 8.9 %collective-permute-start.3 = (bf16[104,2048]{1,0:T(8,128)(2,1)S(1)}, bf16[104,2048]{1,0:T(8,128)(2,1)S(1)}, u32[]{:S(2)}, u32[]{:S(2)}) collective-permute-start(bf16[104,2048]{1,0:T(8,128)(2,1)S(1)} %maximum_select_fusion.2), channel_id=1, source_target_pairs={{0,1},{1,0},{2,3},{3,2},{4,5},{5,4},{6,7},{7,6},{8,9},{9,8},{10,11... | collective-permute-start | bytes 1277960 | tf_op jit(solution)/shard_map/ppermute | solution.py:76
  101.5 1.6 collective-permute-start.8
  103.2 8.4 %collective-permute-start.9 = (f32[16,4096]{1,0:T(8,128)S(1)}, f32[16,4096]{1,0:T(8,128)S(1)}, u32[]{:S(2)}, u32[]{:S(2)}) collective-permute-start(f32[16,4096]{1,0:T(8,128)S(1)} %bitcast_add_fusion), channel_id=1, source_target_pairs={{0,2},{1,3},{2,0},{3,1},{4,6},{5,7},{6,4},{7,5},{8,10},{9,11},{10,... | collective-permute-start | bytes 786440 | tf_op jit(solution)/shard_map/ppermute | solution.py:99
  111.6 9.1 %collective-permute-start.10 = (f32[16,4096]{1,0:T(8,128)S(1)}, f32[16,4096]{1,0:T(8,128)S(1)}, u32[]{:S(2)}, u32[]{:S(2)}) collective-permute-start(f32[16,4096]{1,0:T(8,128)S(1)} %add.193), channel_id=1, source_target_pairs={{0,4},{1,5},{2,6},{3,7},{4,0},{5,1},{6,2},{7,3},{8,12},{9,13},{10,... | collective-permute-start | bytes 786440 | tf_op jit(solution)/shard_map/ppermute | solution.py:99
  120.7 8.2 %collective-permute-start.11 = (f32[16,4096]{1,0:T(8,128)S(1)}, f32[16,4096]{1,0:T(8,128)S(1)}, u32[]{:S(2)}, u32[]{:S(2)}) collective-permute-start(f32[16,4096]{1,0:T(8,128)S(1)} %add.194), channel_id=1, source_target_pairs={{0,8},{1,9},{2,10},{3,11},{4,12},{5,13},{6,14},{7,15},{8,0},{9,1},... | collective-permute-start | bytes 786440 | tf_op jit(solution)/shard_map/ppermute | solution.py:99
  129.3 3.8 %collective-permute-start.12 = (f32[32]{0:T(128)S(1)}, f32[32]{0:T(128)S(1)}, u32[]{:S(2)}, u32[]{:S(2)}) collective-permute-start(f32[32]{0:T(128)S(1)} %pad_maximum_fusion), channel_id=1, source_target_pairs={{0,16},{16,0},{32,48},{48,32},{64,80},{80,64},{96,112},{112,96},{1... | collective-permute-start | bytes 392 | tf_op jit(solution)/shard_map/ppermute | solution.py:99
  133.1 6.4 %collective-permute-start.13 = (f32[32]{0:T(128)S(1)}, f32[32]{0:T(128)S(1)}, u32[]{:S(2)}, u32[]{:S(2)}) collective-permute-start(f32[32]{0:T(128)S(1)} %add.198), channel_id=1, source_target_pairs={{0,32},{16,48},{32,0},{48,16},{64,96},{80,112},{96,64},{112,80},{1... | collective-permute-start | bytes 392 | tf_op jit(solution)/shard_map/ppermute | solution.py:99
  139.4 7.8 %collective-permute-start.14 = (f32[32]{0:T(128)S(1)}, f32[32]{0:T(128)S(1)}, u32[]{:S(2)}, u32[]{:S(2)}) collective-permute-start(f32[32]{0:T(128)S(1)} %add.199), channel_id=1, source_target_pairs={{0,64},{16,80},{32,96},{48,112},{64,0},{80,16},{96,32},{112,48},{1... | collective-permute-start | bytes 392 | tf_op jit(solution)/shard_map/ppermute | solution.py:99
  147.3 7.6 %collective-permute-start.15 = (f32[32]{0:T(128)S(1)}, f32[32]{0:T(128)S(1)}, u32[]{:S(2)}, u32[]{:S(2)}) collective-permute-start(f32[32]{0:T(128)S(1)} %add.200), channel_id=1, source_target_pairs={{0,128},{16,144},{32,160},{48,176},{64,192},{80,208},{96,224},{112... | collective-permute-start | bytes 392 | tf_op jit(solution)/shard_map/ppermute | solution.py:99
  155.2 25.4 %copy-start = (f32[16,256]{1,0:T(8,128)S(1)}, f32[16,256]{1,0:T(8,128)}, u32[]{:S(2)}) copy-start(f32[16,256]{1,0:T(8,128)} %param.19) | copy-start | bytes 49156
  155.2 25.4 %copy-start.1 = (f32[16,256]{1,0:T(8,128)S(1)}, f32[16,256]{1,0:T(8,128)}, u32[]{:S(2)}) copy-start(f32[16,256]{1,0:T(8,128)} %param.17) | copy-start | bytes 49156
  155.2 25.4 %copy-start.2 = (f32[16,256]{1,0:T(8,128)S(1)}, f32[16,256]{1,0:T(8,128)}, u32[]{:S(2)}) copy-start(f32[16,256]{1,0:T(8,128)} %param.18) | copy-start | bytes 49156
  155.2 28.7 %copy-start.3 = (f32[64]{0:T(128)S(1)}, f32[64]{0:T(128)}, u32[]{:S(2)}) copy-start(f32[64]{0:T(128)} %param.16) | copy-start | bytes 772
  157.6 1.3 collective-permute-start.20
  158.9 13.1 %collective-permute-start.21 = (f32[16,256]{1,0:T(8,128)S(1)}, f32[16,256]{1,0:T(8,128)S(1)}, u32[]{:S(2)}, u32[]{:S(2)}) collective-permute-start(f32[16,256]{1,0:T(8,128)S(1)} %slice_select_fusion.1), channel_id=1, source_target_pairs={{0,2},{1,3},{2,0},{3,1},{4,6},{5,7},{6,4},{7,5},{8,10},{9,11},{10,... | collective-permute-start | bytes 49160 | tf_op jit(solution)/shard_map/ppermute | solution.py:93
  159.6 3.6 %collective-permute-start.16 = (f32[16]{0:T(128)S(1)}, f32[16]{0:T(128)S(1)}, u32[]{:S(2)}, u32[]{:S(2)}) collective-permute-start(f32[16]{0:T(128)S(1)} %get-tuple-element.109), channel_id=1, source_target_pairs={{0,16},{16,0},{32,48},{48,32},{64,80},{80,64},{96,112},{112,96},{1... | collective-permute-start | bytes 200 | tf_op jit(solution)/shard_map/ppermute | solution.py:99
  163.1 3.6 %collective-permute-start.17 = (f32[16]{0:T(128)S(1)}, f32[16]{0:T(128)S(1)}, u32[]{:S(2)}, u32[]{:S(2)}) collective-permute-start(f32[16]{0:T(128)S(1)} %add.220), channel_id=1, source_target_pairs={{0,32},{16,48},{32,0},{48,16},{64,96},{80,112},{96,64},{112,80},{1... | collective-permute-start | bytes 200 | tf_op jit(solution)/shard_map/ppermute | solution.py:99
  166.7 4.5 %collective-permute-start.18 = (f32[16]{0:T(128)S(1)}, f32[16]{0:T(128)S(1)}, u32[]{:S(2)}, u32[]{:S(2)}) collective-permute-start(f32[16]{0:T(128)S(1)} %add.221), channel_id=1, source_target_pairs={{0,64},{16,80},{32,96},{48,112},{64,0},{80,16},{96,32},{112,48},{1... | collective-permute-start | bytes 200 | tf_op jit(solution)/shard_map/ppermute | solution.py:99
  171.2 7.5 %collective-permute-start.19 = (f32[16]{0:T(128)S(1)}, f32[16]{0:T(128)S(1)}, u32[]{:S(2)}, u32[]{:S(2)}) collective-permute-start(f32[16]{0:T(128)S(1)} %add.222), channel_id=1, source_target_pairs={{0,128},{16,144},{32,160},{48,176},{64,192},{80,208},{96,224},{112... | collective-permute-start | bytes 200 | tf_op jit(solution)/shard_map/ppermute | solution.py:99
  172.0 6.6 %collective-permute-start.22 = (f32[16,128]{1,0:T(8,128)S(1)}, f32[16,128]{1,0:T(8,128)S(1)}, u32[]{:S(2)}, u32[]{:S(2)}) collective-permute-start(f32[16,128]{1,0:T(8,128)S(1)} %slice_select_fusion.3), channel_id=1, source_target_pairs={{0,4},{1,5},{2,6},{3,7},{4,0},{5,1},{6,2},{7,3},{8,12},{9,13},{10,... | collective-permute-start | bytes 24584 | tf_op jit(solution)/shard_map/ppermute | solution.py:93
  178.7 5.2 %collective-permute-start.23 = (f32[16,64]{1,0:T(8,128)S(1)}, f32[16,64]{1,0:T(8,128)S(1)}, u32[]{:S(2)}, u32[]{:S(2)}) collective-permute-start(f32[16,64]{1,0:T(8,128)S(1)} %slice_select_fusion.2), channel_id=1, source_target_pairs={{0,8},{1,9},{2,10},{3,11},{4,12},{5,13},{6,14},{7,15},{8,0},{9,1},... | collective-permute-start | bytes 12296 | tf_op jit(solution)/shard_map/ppermute | solution.py:93

commit v8 on v7

--- a/solution.py
+++ b/solution.py
@@ -7,7 +7,6 @@
 
 
 root_five = math.sqrt(5.0)
-exp2_scale = -root_five / math.log(2.0)
 contract_first = (((0,), (0,)), ((), ()))
 contract_last = (((1,), (1,)), ((), ()))
 
@@ -25,7 +24,7 @@
     kern_vals = (
         signal_scalar
         * (1.0 + root_five * distance + 5.0 / 3.0 * dist_sq)
-        * jnp.exp2(distance * exp2_scale)
+        * jnp.exp(-root_five * distance)
     )
     return kern_vals.astype(jnp.bfloat16)
 
@@ -81,23 +80,26 @@
     return buf
 
 
-def reduce_scatter_last(x, axis_name, size):
-    me = lax.axis_index(axis_name)
-    buf = x
+def all_sum(x, axis_name, size):
     for bit in range(size.bit_length() - 1):
+        x = x + lax.ppermute(x, axis_name, xor_perm(size, bit))
+    return x
+
+
+def tail_sums(fit, local, axis_rs, axis_ar, size_rs, size_ar):
+    me = lax.axis_index(axis_rs)
+    buf, x = fit, local
+    for bit in range(size_rs.bit_length() - 1):
         half = buf.shape[-1] // 2
         lower, upper = buf[..., :half], buf[..., half:]
         low = ((me >> bit) & 1) == 0
         keep = jnp.where(low, lower, upper)
         send = jnp.where(low, upper, lower)
-        buf = keep + lax.ppermute(send, axis_name, xor_perm(size, bit))
-    return buf
-
-
-def all_sum(x, axis_name, size):
-    for bit in range(size.bit_length() - 1):
-        x = x + lax.ppermute(x, axis_name, xor_perm(size, bit))
-    return x
+        send, x = lax.optimization_barrier((send, x))
+        got = lax.ppermute(send, axis_rs, xor_perm(size_rs, bit))
+        x = x + lax.ppermute(x, axis_ar, xor_perm(size_ar, bit))
+        buf = keep + got
+    return buf, x
 
 
 def per_device(
@@ -207,12 +209,11 @@
             preferred_element_type=jnp.float32,
         )
         partial_fit = part if partial_fit is None else partial_fit + part
-    norm_next = all_sum(
-        tied(jnp.sum(residual_new_row * residual_new_row, axis=1), partial_fit),
-        "row", n_row,
+    fitted, norm_next = tail_sums(
+        partial_fit, jnp.sum(residual_new_row * residual_new_row, axis=1),
+        "col", "row", n_col, n_row,
     )
     direction_new = residual_new + (norm_next / norm_now)[:, None] * direction
-    fitted = reduce_scatter_last(partial_fit, "col", n_col)
     cand_fit = cand_prior[None, :] + fitted
     return (weights_new, residual_new, direction_new, cand_fit)
 

time: 187 us -> 184 us (0.984)
  waiting for transfers between devices: 66.1 us -> 61.6 us
    ppermute x12 -> x8, waiting for transfers between devices: 44.7 us -> 31.4 us  [all_sum(): x = x + lax.ppermute(x, axis_name, xor_perm(size, bit))]
    ppermute x4 -> x8, waiting for transfers between devices: 3.86 us -> 12.6 us  [the longest x4 12.6 us: tail_sums(): x = x + lax.ppermute(x, axis_ar, xor_perm(size_ar, bit))]
    ppermute x4 -> x8, starting transfers between devices: 5.2 us -> 9.79 us  [the longest x4 6.41 us: tail_sums(): got = lax.ppermute(send, axis_rs, xor_perm(size_rs, bit))]
    ppermute x12 -> x8, starting transfers between devices: 11.1 us -> 8.03 us  [all_sum(): x = x + lax.ppermute(x, axis_name, xor_perm(size, bit))]
  transfers between devices with their start and end apart: 24 -> 24, of which waited for: 18 -> 16; matrix products, arithmetic and copies ran while one was open for 8% -> 8% of each run, Pallas kernels for 0% -> 0%
where the time goes in v8:
time: 184 us; the launch traced here: 182 us
  matrix products  73.7 us (40%)
  waiting for transfers between devices  61.6 us (33%)
  starting transfers between devices  33.5 us (18%)
  other arithmetic  9.16 us (5%)
  between operations  2.31 us (1%)
    dot_general x16, matrix products, one_block(): lax.dot_general(kern_vals, vec_blk, contract_last, preferred_element_type...  59.7 us
    ppermute x8, waiting for transfers between devices, all_sum(): x = x + lax.ppermute(x, axis_name, xor_perm(size, bit))  31.4 us
    ppermute x8, waiting for transfers between devices, gather_last(): recv = lax.ppermute(buf, axis_name, xor_perm(size, bit))  17.6 us
    ppermute x8, starting transfers between devices, gather_last(): recv = lax.ppermute(buf, axis_name, xor_perm(size, bit))  15.7 us
    ppermute x4, waiting for transfers between devices, tail_sums(): x = x + lax.ppermute(x, axis_ar, xor_perm(size_ar, bit))  12.6 us
    dot_general x2, matrix products, matern_block(): lax.dot_general(row_pts_m2, col_pts, contract_first, preferred_element_ty...  11.6 us
    ppermute x8, starting transfers between devices, all_sum(): x = x + lax.ppermute(x, axis_name, xor_perm(size, bit))  8.03 us
    ppermute x4, starting transfers between devices, tail_sums(): got = lax.ppermute(send, axis_rs, xor_perm(size_rs, bit))  6.41 us
  transfers between devices with their start and end apart: 24, of which 16 were waited for; matrix products, arithmetic and copies ran while one was open for 8% of the time, Pallas kernels for 0%

profile of v8, /device:TPU:2, one launch (start us, length us, event | category | flops | bytes accessed | tf_op | source)
XLA Modules:
  0.0 181.6 jit_solution(15320625627533279328)
XLA Ops:
  0.6 0.8 constant_dynamic-update-slice_fusion.10
  1.5 0.8 divide_convert_fusion.1
  2.4 0.7 constant_dynamic-update-slice_fusion.9
  3.1 0.7 constant_dynamic-update-slice_fusion.8
  3.8 0.7 constant_dynamic-update-slice_fusion.7
  4.5 0.7 constant_dynamic-update-slice_fusion.6
  5.3 7.2 %collective-permute-start.4 = (bf16[96,256]{1,0:T(8,128)(2,1)S(1)}, bf16[96,256]{1,0:T(8,128)(2,1)S(1)}, u32[]{:S(2)}, u32[]{:S(2)}) collective-permute-start(bf16[96,256]{1,0:T(8,128)(2,1)S(1)} %constant_dynamic-update-slice_fusion.6), channel_id=1, source_target_pairs={{0,128},{16,144},{32,160},{48,176},{64,192},{80,208},{96,224},{112... | collective-permute-start | bytes 147464 | tf_op jit(solution)/shard_map/ppermute | solution.py:75
  12.4 0.7 constant_dynamic-update-slice_fusion.1
  13.2 0.7 constant_dynamic-update-slice_fusion
  13.9 3.2 %collective-permute-start = (bf16[104,256]{1,0:T(8,128)(2,1)S(1)}, bf16[104,256]{1,0:T(8,128)(2,1)S(1)}, u32[]{:S(2)}, u32[]{:S(2)}) collective-permute-start(bf16[104,256]{1,0:T(8,128)(2,1)S(1)} %constant_dynamic-update-slice_fusion), channel_id=1, source_target_pairs={{0,8},{1,9},{2,10},{3,11},{4,12},{5,13},{6,14},{7,15},{8,0},{9,1},... | collective-permute-start | bytes 159752 | tf_op jit(solution)/shard_map/ppermute | solution.py:75
  17.1 1.6 collective-permute-start.5
  18.7 0.9 collective-permute-done
  19.5 2.2 %collective-permute-start.1 = (bf16[104,512]{1,0:T(8,128)(2,1)S(1)}, bf16[104,512]{1,0:T(8,128)(2,1)S(1)}, u32[]{:S(2)}, u32[]{:S(2)}) collective-permute-start(bf16[104,512]{1,0:T(8,128)(2,1)S(1)} %maximum_select_fusion.6), channel_id=1, source_target_pairs={{0,4},{1,5},{2,6},{3,7},{4,0},{5,1},{6,2},{7,3},{8,12},{9,13},{10,... | collective-permute-start | bytes 319496 | tf_op jit(solution)/shard_map/ppermute | solution.py:75
  21.8 2.4 %collective-permute-done.5 = bf16[96,512]{1,0:T(8,128)(2,1)S(1)} collective-permute-done((bf16[96,512]{1,0:T(8,128)(2,1)S(1)}, bf16[96,512]{1,0:T(8,128)(2,1)S(1)}, u32[]{:S(2)}, u32[]{:S(2)}) %collective-permute-start.5) | collective-permute-done | bytes 98336 | tf_op jit(solution)/shard_map/ppermute | solution.py:75
  24.4 1.5 collective-permute-done.1
  25.9 0.6 collective-permute-start.2
  26.5 4.1 %collective-permute-done.6 = bf16[96,1024]{1,0:T(8,128)(2,1)S(1)} collective-permute-done((bf16[96,1024]{1,0:T(8,128)(2,1)S(1)}, bf16[96,1024]{1,0:T(8,128)(2,1)S(1)}, u32[]{:S(2)}, u32[]{:S(2)}) %collective-permute-start.6) | collective-permute-done | bytes 196640 | tf_op jit(solution)/shard_map/ppermute | solution.py:75
  30.7 0.8 collective-permute-start.7
  32.1 8.4 %collective-permute-done.7 = bf16[96,2048]{1,0:T(8,128)(2,1)S(1)} collective-permute-done((bf16[96,2048]{1,0:T(8,128)(2,1)S(1)}, bf16[96,2048]{1,0:T(8,128)(2,1)S(1)}, u32[]{:S(2)}, u32[]{:S(2)}) %collective-permute-start.7) | collective-permute-done | bytes 393248 | tf_op jit(solution)/shard_map/ppermute | solution.py:75
  41.1 60.4 %while.11 = (s32[]{:T(128)}, f32[4096,16]{0,1:T(8,128)S(1)}, f32[]{:T(128)}, f32[4096]{0:T(1024)S(1)}, f32[16,256]{1,0:T(8,128)S(1)}, /*index=5*/bf16[16,32,256]...) while((s32[]{:T(128)}, f32[4096,16]{0,1:T(8,128)S(1)}, ...), condition=%wide.region_4.5_spmd.clone, body=%wide.region_3.4_spmd.clone.sunk | while | flops 112328704 | bytes 832126 | solution.py:51
  41.2 3.7 %convolution_add_fusion.3 = f32[4096,16]{0,1:T(8,128)S(1)} fusion(bf16[32,4096]{1,0:T(8,128)(2,1)S(1)} %get-tuple-element.199, f32[256]{0:T(256)S(1)} %bitcast.71, f32[4096]{0:T(1024)S(1)} %get-tuple-element.196, f32[]{:T(128)} %get-tuple-element.195, f32[4096,16]{0,1:T(8,128)S(1)} %get-tuple-element.184, pred[]{:T(512)S(6)} %compare.3, ...), kind=kOutput, calls=%fused_computation.3.clone.1 | convolution fusion | flops 112328704 | bytes 829956 | tf_op jit(solution)/shard_map/while/body/eval_jaxpr/dot_general | solution.py:44
  44.9 3.7 %convolution_add_fusion.3 = f32[4096,16]{0,1:T(8,128)S(1)} fusion(bf16[32,4096]{1,0:T(8,128)(2,1)S(1)} %get-tuple-element.199, f32[256]{0:T(256)S(1)} %bitcast.71, f32[4096]{0:T(1024)S(1)} %get-tuple-element.196, f32[]{:T(128)} %get-tuple-element.195, f32[4096,16]{0,1:T(8,128)S(1)} %get-tuple-element.184, pred[]{:T(512)S(6)} %compare.3, ...), kind=kOutput, calls=%fused_computation.3.clone.1 | convolution fusion | flops 112328704 | bytes 829956 | tf_op jit(solution)/shard_map/while/body/eval_jaxpr/dot_general | solution.py:44
  48.7 3.7 %convolution_add_fusion.3 = f32[4096,16]{0,1:T(8,128)S(1)} fusion(bf16[32,4096]{1,0:T(8,128)(2,1)S(1)} %get-tuple-element.199, f32[256]{0:T(256)S(1)} %bitcast.71, f32[4096]{0:T(1024)S(1)} %get-tuple-element.196, f32[]{:T(128)} %get-tuple-element.195, f32[4096,16]{0,1:T(8,128)S(1)} %get-tuple-element.184, pred[]{:T(512)S(6)} %compare.3, ...), kind=kOutput, calls=%fused_computation.3.clone.1 | convolution fusion | flops 112328704 | bytes 829956 | tf_op jit(solution)/shard_map/while/body/eval_jaxpr/dot_general | solution.py:44
  52.5 3.7 %convolution_add_fusion.3 = f32[4096,16]{0,1:T(8,128)S(1)} fusion(bf16[32,4096]{1,0:T(8,128)(2,1)S(1)} %get-tuple-element.199, f32[256]{0:T(256)S(1)} %bitcast.71, f32[4096]{0:T(1024)S(1)} %get-tuple-element.196, f32[]{:T(128)} %get-tuple-element.195, f32[4096,16]{0,1:T(8,128)S(1)} %get-tuple-element.184, pred[]{:T(512)S(6)} %compare.3, ...), kind=kOutput, calls=%fused_computation.3.clone.1 | convolution fusion | flops 112328704 | bytes 829956 | tf_op jit(solution)/shard_map/while/body/eval_jaxpr/dot_general | solution.py:44
  56.3 3.7 %convolution_add_fusion.3 = f32[4096,16]{0,1:T(8,128)S(1)} fusion(bf16[32,4096]{1,0:T(8,128)(2,1)S(1)} %get-tuple-element.199, f32[256]{0:T(256)S(1)} %bitcast.71, f32[4096]{0:T(1024)S(1)} %get-tuple-element.196, f32[]{:T(128)} %get-tuple-element.195, f32[4096,16]{0,1:T(8,128)S(1)} %get-tuple-element.184, pred[]{:T(512)S(6)} %compare.3, ...), kind=kOutput, calls=%fused_computation.3.clone.1 | convolution fusion | flops 112328704 | bytes 829956 | tf_op jit(solution)/shard_map/while/body/eval_jaxpr/dot_general | solution.py:44
  60.0 3.7 %convolution_add_fusion.3 = f32[4096,16]{0,1:T(8,128)S(1)} fusion(bf16[32,4096]{1,0:T(8,128)(2,1)S(1)} %get-tuple-element.199, f32[256]{0:T(256)S(1)} %bitcast.71, f32[4096]{0:T(1024)S(1)} %get-tuple-element.196, f32[]{:T(128)} %get-tuple-element.195, f32[4096,16]{0,1:T(8,128)S(1)} %get-tuple-element.184, pred[]{:T(512)S(6)} %compare.3, ...), kind=kOutput, calls=%fused_computation.3.clone.1 | convolution fusion | flops 112328704 | bytes 829956 | tf_op jit(solution)/shard_map/while/body/eval_jaxpr/dot_general | solution.py:44
  63.8 3.7 %convolution_add_fusion.3 = f32[4096,16]{0,1:T(8,128)S(1)} fusion(bf16[32,4096]{1,0:T(8,128)(2,1)S(1)} %get-tuple-element.199, f32[256]{0:T(256)S(1)} %bitcast.71, f32[4096]{0:T(1024)S(1)} %get-tuple-element.196, f32[]{:T(128)} %get-tuple-element.195, f32[4096,16]{0,1:T(8,128)S(1)} %get-tuple-element.184, pred[]{:T(512)S(6)} %compare.3, ...), kind=kOutput, calls=%fused_computation.3.clone.1 | convolution fusion | flops 112328704 | bytes 829956 | tf_op jit(solution)/shard_map/while/body/eval_jaxpr/dot_general | solution.py:44
  67.6 3.7 %convolution_add_fusion.3 = f32[4096,16]{0,1:T(8,128)S(1)} fusion(bf16[32,4096]{1,0:T(8,128)(2,1)S(1)} %get-tuple-element.199, f32[256]{0:T(256)S(1)} %bitcast.71, f32[4096]{0:T(1024)S(1)} %get-tuple-element.196, f32[]{:T(128)} %get-tuple-element.195, f32[4096,16]{0,1:T(8,128)S(1)} %get-tuple-element.184, pred[]{:T(512)S(6)} %compare.3, ...), kind=kOutput, calls=%fused_computation.3.clone.1 | convolution fusion | flops 112328704 | bytes 829956 | tf_op jit(solution)/shard_map/while/body/eval_jaxpr/dot_general | solution.py:44
  71.4 3.7 %convolution_add_fusion.3 = f32[4096,16]{0,1:T(8,128)S(1)} fusion(bf16[32,4096]{1,0:T(8,128)(2,1)S(1)} %get-tuple-element.199, f32[256]{0:T(256)S(1)} %bitcast.71, f32[4096]{0:T(1024)S(1)} %get-tuple-element.196, f32[]{:T(128)} %get-tuple-element.195, f32[4096,16]{0,1:T(8,128)S(1)} %get-tuple-element.184, pred[]{:T(512)S(6)} %compare.3, ...), kind=kOutput, calls=%fused_computation.3.clone.1 | convolution fusion | flops 112328704 | bytes 829956 | tf_op jit(solution)/shard_map/while/body/eval_jaxpr/dot_general | solution.py:44
  75.1 3.7 %convolution_add_fusion.3 = f32[4096,16]{0,1:T(8,128)S(1)} fusion(bf16[32,4096]{1,0:T(8,128)(2,1)S(1)} %get-tuple-element.199, f32[256]{0:T(256)S(1)} %bitcast.71, f32[4096]{0:T(1024)S(1)} %get-tuple-element.196, f32[]{:T(128)} %get-tuple-element.195, f32[4096,16]{0,1:T(8,128)S(1)} %get-tuple-element.184, pred[]{:T(512)S(6)} %compare.3, ...), kind=kOutput, calls=%fused_computation.3.clone.1 | convolution fusion | flops 112328704 | bytes 829956 | tf_op jit(solution)/shard_map/while/body/eval_jaxpr/dot_general | solution.py:44
  78.9 3.7 %convolution_add_fusion.3 = f32[4096,16]{0,1:T(8,128)S(1)} fusion(bf16[32,4096]{1,0:T(8,128)(2,1)S(1)} %get-tuple-element.199, f32[256]{0:T(256)S(1)} %bitcast.71, f32[4096]{0:T(1024)S(1)} %get-tuple-element.196, f32[]{:T(128)} %get-tuple-element.195, f32[4096,16]{0,1:T(8,128)S(1)} %get-tuple-element.184, pred[]{:T(512)S(6)} %compare.3, ...), kind=kOutput, calls=%fused_computation.3.clone.1 | convolution fusion | flops 112328704 | bytes 829956 | tf_op jit(solution)/shard_map/while/body/eval_jaxpr/dot_general | solution.py:44
  82.7 3.7 %convolution_add_fusion.3 = f32[4096,16]{0,1:T(8,128)S(1)} fusion(bf16[32,4096]{1,0:T(8,128)(2,1)S(1)} %get-tuple-element.199, f32[256]{0:T(256)S(1)} %bitcast.71, f32[4096]{0:T(1024)S(1)} %get-tuple-element.196, f32[]{:T(128)} %get-tuple-element.195, f32[4096,16]{0,1:T(8,128)S(1)} %get-tuple-element.184, pred[]{:T(512)S(6)} %compare.3, ...), kind=kOutput, calls=%fused_computation.3.clone.1 | convolution fusion | flops 112328704 | bytes 829956 | tf_op jit(solution)/shard_map/while/body/eval_jaxpr/dot_general | solution.py:44
  86.4 3.7 %convolution_add_fusion.3 = f32[4096,16]{0,1:T(8,128)S(1)} fusion(bf16[32,4096]{1,0:T(8,128)(2,1)S(1)} %get-tuple-element.199, f32[256]{0:T(256)S(1)} %bitcast.71, f32[4096]{0:T(1024)S(1)} %get-tuple-element.196, f32[]{:T(128)} %get-tuple-element.195, f32[4096,16]{0,1:T(8,128)S(1)} %get-tuple-element.184, pred[]{:T(512)S(6)} %compare.3, ...), kind=kOutput, calls=%fused_computation.3.clone.1 | convolution fusion | flops 112328704 | bytes 829956 | tf_op jit(solution)/shard_map/while/body/eval_jaxpr/dot_general | solution.py:44
  90.2 3.7 %convolution_add_fusion.3 = f32[4096,16]{0,1:T(8,128)S(1)} fusion(bf16[32,4096]{1,0:T(8,128)(2,1)S(1)} %get-tuple-element.199, f32[256]{0:T(256)S(1)} %bitcast.71, f32[4096]{0:T(1024)S(1)} %get-tuple-element.196, f32[]{:T(128)} %get-tuple-element.195, f32[4096,16]{0,1:T(8,128)S(1)} %get-tuple-element.184, pred[]{:T(512)S(6)} %compare.3, ...), kind=kOutput, calls=%fused_computation.3.clone.1 | convolution fusion | flops 112328704 | bytes 829956 | tf_op jit(solution)/shard_map/while/body/eval_jaxpr/dot_general | solution.py:44
  94.0 3.7 %convolution_add_fusion.3 = f32[4096,16]{0,1:T(8,128)S(1)} fusion(bf16[32,4096]{1,0:T(8,128)(2,1)S(1)} %get-tuple-element.199, f32[256]{0:T(256)S(1)} %bitcast.71, f32[4096]{0:T(1024)S(1)} %get-tuple-element.196, f32[]{:T(128)} %get-tuple-element.195, f32[4096,16]{0,1:T(8,128)S(1)} %get-tuple-element.184, pred[]{:T(512)S(6)} %compare.3, ...), kind=kOutput, calls=%fused_computation.3.clone.1 | convolution fusion | flops 112328704 | bytes 829956 | tf_op jit(solution)/shard_map/while/body/eval_jaxpr/dot_general | solution.py:44
  97.8 3.7 %convolution_add_fusion.3 = f32[4096,16]{0,1:T(8,128)S(1)} fusion(bf16[32,4096]{1,0:T(8,128)(2,1)S(1)} %get-tuple-element.199, f32[256]{0:T(256)S(1)} %bitcast.71, f32[4096]{0:T(1024)S(1)} %get-tuple-element.196, f32[]{:T(128)} %get-tuple-element.195, f32[4096,16]{0,1:T(8,128)S(1)} %get-tuple-element.184, pred[]{:T(512)S(6)} %compare.3, ...), kind=kOutput, calls=%fused_computation.3.clone.1 | convolution fusion | flops 112328704 | bytes 829956 | tf_op jit(solution)/shard_map/while/body/eval_jaxpr/dot_general | solution.py:44
  101.6 1.5 collective-permute-done.8
  103.2 0.6 collective-permute-start.9
  105.1 6.5 %collective-permute-done.9 = f32[16,4096]{1,0:T(8,128)S(1)} collective-permute-done((f32[16,4096]{1,0:T(8,128)S(1)}, f32[16,4096]{1,0:T(8,128)S(1)}, u32[]{:S(2)}, u32[]{:S(2)}) %collective-permute-start.9) | collective-permute-done | bytes 262176 | tf_op jit(solution)/shard_map/ppermute | solution.py:85
  111.6 2.2 %collective-permute-start.10 = (f32[16,4096]{1,0:T(8,128)S(1)}, f32[16,4096]{1,0:T(8,128)S(1)}, u32[]{:S(2)}, u32[]{:S(2)}) collective-permute-start(f32[16,4096]{1,0:T(8,128)S(1)} %add.166), channel_id=1, source_target_pairs={{0,4},{1,5},{2,6},{3,7},{4,0},{5,1},{6,2},{7,3},{8,12},{9,13},{10,... | collective-permute-start | bytes 786440 | tf_op jit(solution)/shard_map/ppermute | solution.py:85
  113.9 6.9 %collective-permute-done.10 = f32[16,4096]{1,0:T(8,128)S(1)} collective-permute-done((f32[16,4096]{1,0:T(8,128)S(1)}, f32[16,4096]{1,0:T(8,128)S(1)}, u32[]{:S(2)}, u32[]{:S(2)}) %collective-permute-start.10) | collective-permute-done | bytes 262176 | tf_op jit(solution)/shard_map/ppermute | solution.py:85
  120.7 0.9 collective-permute-start.11
  122.0 6.9 %collective-permute-done.11 = f32[16,4096]{1,0:T(8,128)S(1)} collective-permute-done((f32[16,4096]{1,0:T(8,128)S(1)}, f32[16,4096]{1,0:T(8,128)S(1)}, u32[]{:S(2)}, u32[]{:S(2)}) %collective-permute-start.11) | collective-permute-done | bytes 262176 | tf_op jit(solution)/shard_map/ppermute | solution.py:85
  129.3 0.9 collective-permute-start.12
  130.3 2.8 %collective-permute-done.12 = f32[32]{0:T(128)S(1)} collective-permute-done((f32[32]{0:T(128)S(1)}, f32[32]{0:T(128)S(1)}, u32[]{:S(2)}, u32[]{:S(2)}) %collective-permute-start.12) | collective-permute-done | bytes 160 | tf_op jit(solution)/shard_map/ppermute | solution.py:85
  133.6 5.8 %multiply_convert_fusion.2 = bf16[1024,2048]{1,0:T(8,128)(2,1)S(1)} fusion(bf16[32,1024]{1,0:T(8,128)(2,1)S(1)} %mul.153, f32[2048]{0:T(1024)S(1)} %get-tuple-element.117, f32[1024]{0:T(1024)S(1)} %add.180, f32[]{:T(128)} %bitcast.58, bf16[96,4096]{1,0:T(8,128)(2,1)S(1)} %maximum_select_fusion.1), kind=kOutput, calls=%fused_computation.17 | convolution fusion | flops 157286400 | bytes 4403204 | tf_op jit(solution)/shard_map/dot_general | solution.py:19
  139.4 2.0 %collective-permute-start.14 = (f32[32]{0:T(128)S(1)}, f32[32]{0:T(128)S(1)}, u32[]{:S(2)}, u32[]{:S(2)}) collective-permute-start(f32[32]{0:T(128)S(1)} %add.172), channel_id=1, source_target_pairs={{0,64},{16,80},{32,96},{48,112},{64,0},{80,16},{96,32},{112,48},{1... | collective-permute-start | bytes 392 | tf_op jit(solution)/shard_map/ppermute | solution.py:85
  141.5 5.8 %multiply_convert_fusion.1 = bf16[1024,2048]{1,0:T(8,128)(2,1)S(1)} fusion(bf16[32,1024]{1,0:T(8,128)(2,1)S(1)} %mul.153, f32[2048]{0:T(1024)S(1)} %get-tuple-element.116, f32[1024]{0:T(1024)S(1)} %add.180, f32[]{:T(128)} %bitcast.59, bf16[96,4096]{1,0:T(8,128)(2,1)S(1)} %maximum_select_fusion.1), kind=kOutput, calls=%fused_computation.16 | convolution fusion | flops 157286400 | bytes 4403204 | tf_op jit(solution)/shard_map/dot_general | solution.py:19
  147.3 0.8 collective-permute-start.15
  148.1 6.8 %collective-permute-done.15 = f32[32]{0:T(128)S(1)} collective-permute-done((f32[32]{0:T(128)S(1)}, f32[32]{0:T(128)S(1)}, u32[]{:S(2)}, u32[]{:S(2)}) %collective-permute-start.15) | collective-permute-done | bytes 160 | tf_op jit(solution)/shard_map/ppermute | solution.py:85
  155.2 1.2 fusion.18
  156.4 1.2 convolution_add_fusion.1
  157.7 0.8 collective-permute-start.17
  158.5 2.9 %collective-permute-done.17 = f32[16]{0:T(128)S(1)} collective-permute-done((f32[16]{0:T(128)S(1)}, f32[16]{0:T(128)S(1)}, u32[]{:S(2)}, u32[]{:S(2)}) %collective-permute-start.17) | collective-permute-done | bytes 96 | tf_op jit(solution)/shard_map/ppermute | solution.py:100
  161.4 0.6 collective-permute-start.18
  162.6 3.0 %collective-permute-done.19 = f32[16]{0:T(128)S(1)} collective-permute-done((f32[16]{0:T(128)S(1)}, f32[16]{0:T(128)S(1)}, u32[]{:S(2)}, u32[]{:S(2)}) %collective-permute-start.19) | collective-permute-done | bytes 96 | tf_op jit(solution)/shard_map/ppermute | solution.py:100
  165.6 2.5 %collective-permute-start.20 = (f32[16,128]{1,0:T(8,128)S(1)}, f32[16,128]{1,0:T(8,128)S(1)}, u32[]{:S(2)}, u32[]{:S(2)}) collective-permute-start(f32[16,128]{1,0:T(8,128)S(1)} %slice_select_fusion.3), channel_id=1, source_target_pairs={{0,4},{1,5},{2,6},{3,7},{4,0},{5,1},{6,2},{7,3},{8,12},{9,13},{10,... | collective-permute-start | bytes 24584 | tf_op jit(solution)/shard_map/ppermute | solution.py:99
  168.1 1.0 collective-permute-start.21
  169.1 3.5 %collective-permute-done.21 = f32[16]{0:T(128)S(1)} collective-permute-done((f32[16]{0:T(128)S(1)}, f32[16]{0:T(128)S(1)}, u32[]{:S(2)}, u32[]{:S(2)}) %collective-permute-start.21) | collective-permute-done | bytes 96 | tf_op jit(solution)/shard_map/ppermute | solution.py:100
  172.7 1.0 collective-permute-start.22
  173.7 3.2 %collective-permute-start.23 = (f32[16,64]{1,0:T(8,128)S(1)}, f32[16,64]{1,0:T(8,128)S(1)}, u32[]{:S(2)}, u32[]{:S(2)}) collective-permute-start(f32[16,64]{1,0:T(8,128)S(1)} %slice_select_fusion.2), channel_id=1, source_target_pairs={{0,8},{1,9},{2,10},{3,11},{4,12},{5,13},{6,14},{7,15},{8,0},{9,1},... | collective-permute-start | bytes 12296 | tf_op jit(solution)/shard_map/ppermute | solution.py:99
  176.9 3.3 %collective-permute-done.22 = f32[16]{0:T(128)S(1)} collective-permute-done((f32[16]{0:T(128)S(1)}, f32[16]{0:T(128)S(1)}, u32[]{:S(2)}, u32[]{:S(2)}) %collective-permute-start.22) | collective-permute-done | bytes 96 | tf_op jit(solution)/shard_map/ppermute | solution.py:100
  180.2 0.7 multiply_add_fusion.1
  180.9 0.7 add_add_fusion
  (89 shorter events, 4.5 us)
Async XLA Ops:
  5.3 11.8 %collective-permute-start.4 = (bf16[96,256]{1,0:T(8,128)(2,1)S(1)}, bf16[96,256]{1,0:T(8,128)(2,1)S(1)}, u32[]{:S(2)}, u32[]{:S(2)}) collective-permute-start(bf16[96,256]{1,0:T(8,128)(2,1)S(1)} %constant_dynamic-update-slice_fusion.6), channel_id=1, source_target_pairs={{0,128},{16,144},{32,160},{48,176},{64,192},{80,208},{96,224},{112... | collective-permute-start | bytes 147464 | tf_op jit(solution)/shard_map/ppermute | solution.py:75
  13.9 5.6 %collective-permute-start = (bf16[104,256]{1,0:T(8,128)(2,1)S(1)}, bf16[104,256]{1,0:T(8,128)(2,1)S(1)}, u32[]{:S(2)}, u32[]{:S(2)}) collective-permute-start(bf16[104,256]{1,0:T(8,128)(2,1)S(1)} %constant_dynamic-update-slice_fusion), channel_id=1, source_target_pairs={{0,8},{1,9},{2,10},{3,11},{4,12},{5,13},{6,14},{7,15},{8,0},{9,1},... | collective-permute-start | bytes 159752 | tf_op jit(solution)/shard_map/ppermute | solution.py:75
  17.1 7.1 %collective-permute-start.5 = (bf16[96,512]{1,0:T(8,128)(2,1)S(1)}, bf16[96,512]{1,0:T(8,128)(2,1)S(1)}, u32[]{:S(2)}, u32[]{:S(2)}) collective-permute-start(bf16[96,512]{1,0:T(8,128)(2,1)S(1)} %maximum_select_fusion.7), channel_id=1, source_target_pairs={{0,64},{16,80},{32,96},{48,112},{64,0},{80,16},{96,32},{112,48},{1... | collective-permute-start | bytes 294920 | tf_op jit(solution)/shard_map/ppermute | solution.py:75
  19.5 6.3 %collective-permute-start.1 = (bf16[104,512]{1,0:T(8,128)(2,1)S(1)}, bf16[104,512]{1,0:T(8,128)(2,1)S(1)}, u32[]{:S(2)}, u32[]{:S(2)}) collective-permute-start(bf16[104,512]{1,0:T(8,128)(2,1)S(1)} %maximum_select_fusion.6), channel_id=1, source_target_pairs={{0,4},{1,5},{2,6},{3,7},{4,0},{5,1},{6,2},{7,3},{8,12},{9,13},{10,... | collective-permute-start | bytes 319496 | tf_op jit(solution)/shard_map/ppermute | solution.py:75
  24.2 6.4 %collective-permute-start.6 = (bf16[96,1024]{1,0:T(8,128)(2,1)S(1)}, bf16[96,1024]{1,0:T(8,128)(2,1)S(1)}, u32[]{:S(2)}, u32[]{:S(2)}) collective-permute-start(bf16[96,1024]{1,0:T(8,128)(2,1)S(1)} %maximum_select_fusion.5), channel_id=1, source_target_pairs={{0,32},{16,48},{32,0},{48,16},{64,96},{80,112},{96,64},{112,80},{1... | collective-permute-start | bytes 589832 | tf_op jit(solution)/shard_map/ppermute | solution.py:75
  25.9 5.9 %collective-permute-start.2 = (bf16[104,1024]{1,0:T(8,128)(2,1)S(1)}, bf16[104,1024]{1,0:T(8,128)(2,1)S(1)}, u32[]{:S(2)}, u32[]{:S(2)}) collective-permute-start(bf16[104,1024]{1,0:T(8,128)(2,1)S(1)} %maximum_select_fusion.4), channel_id=1, source_target_pairs={{0,2},{1,3},{2,0},{3,1},{4,6},{5,7},{6,4},{7,5},{8,10},{9,11},{10,... | collective-permute-start | bytes 638984 | tf_op jit(solution)/shard_map/ppermute | solution.py:75
  30.7 9.7 %collective-permute-start.7 = (bf16[96,2048]{1,0:T(8,128)(2,1)S(1)}, bf16[96,2048]{1,0:T(8,128)(2,1)S(1)}, u32[]{:S(2)}, u32[]{:S(2)}) collective-permute-start(bf16[96,2048]{1,0:T(8,128)(2,1)S(1)} %maximum_select_fusion.3), channel_id=1, source_target_pairs={{0,16},{16,0},{32,48},{48,32},{64,80},{80,64},{96,112},{112,96},{1... | collective-permute-start | bytes 1179656 | tf_op jit(solution)/shard_map/ppermute | solution.py:75
  32.0 8.9 %collective-permute-start.3 = (bf16[104,2048]{1,0:T(8,128)(2,1)S(1)}, bf16[104,2048]{1,0:T(8,128)(2,1)S(1)}, u32[]{:S(2)}, u32[]{:S(2)}) collective-permute-start(bf16[104,2048]{1,0:T(8,128)(2,1)S(1)} %maximum_select_fusion.2), channel_id=1, source_target_pairs={{0,1},{1,0},{2,3},{3,2},{4,5},{5,4},{6,7},{7,6},{8,9},{9,8},{10,11... | collective-permute-start | bytes 1277960 | tf_op jit(solution)/shard_map/ppermute | solution.py:75
  101.5 1.6 collective-permute-start.8
  103.2 8.4 %collective-permute-start.9 = (f32[16,4096]{1,0:T(8,128)S(1)}, f32[16,4096]{1,0:T(8,128)S(1)}, u32[]{:S(2)}, u32[]{:S(2)}) collective-permute-start(f32[16,4096]{1,0:T(8,128)S(1)} %bitcast_add_fusion), channel_id=1, source_target_pairs={{0,2},{1,3},{2,0},{3,1},{4,6},{5,7},{6,4},{7,5},{8,10},{9,11},{10,... | collective-permute-start | bytes 786440 | tf_op jit(solution)/shard_map/ppermute | solution.py:85
  111.6 9.1 %collective-permute-start.10 = (f32[16,4096]{1,0:T(8,128)S(1)}, f32[16,4096]{1,0:T(8,128)S(1)}, u32[]{:S(2)}, u32[]{:S(2)}) collective-permute-start(f32[16,4096]{1,0:T(8,128)S(1)} %add.166), channel_id=1, source_target_pairs={{0,4},{1,5},{2,6},{3,7},{4,0},{5,1},{6,2},{7,3},{8,12},{9,13},{10,... | collective-permute-start | bytes 786440 | tf_op jit(solution)/shard_map/ppermute | solution.py:85
  120.7 8.2 %collective-permute-start.11 = (f32[16,4096]{1,0:T(8,128)S(1)}, f32[16,4096]{1,0:T(8,128)S(1)}, u32[]{:S(2)}, u32[]{:S(2)}) collective-permute-start(f32[16,4096]{1,0:T(8,128)S(1)} %add.167), channel_id=1, source_target_pairs={{0,8},{1,9},{2,10},{3,11},{4,12},{5,13},{6,14},{7,15},{8,0},{9,1},... | collective-permute-start | bytes 786440 | tf_op jit(solution)/shard_map/ppermute | solution.py:85
  129.3 3.8 %collective-permute-start.12 = (f32[32]{0:T(128)S(1)}, f32[32]{0:T(128)S(1)}, u32[]{:S(2)}, u32[]{:S(2)}) collective-permute-start(f32[32]{0:T(128)S(1)} %pad_maximum_fusion), channel_id=1, source_target_pairs={{0,16},{16,0},{32,48},{48,32},{64,80},{80,64},{96,112},{112,96},{1... | collective-permute-start | bytes 392 | tf_op jit(solution)/shard_map/ppermute | solution.py:85
  133.1 6.4 %collective-permute-start.13 = (f32[32]{0:T(128)S(1)}, f32[32]{0:T(128)S(1)}, u32[]{:S(2)}, u32[]{:S(2)}) collective-permute-start(f32[32]{0:T(128)S(1)} %add.171), channel_id=1, source_target_pairs={{0,32},{16,48},{32,0},{48,16},{64,96},{80,112},{96,64},{112,80},{1... | collective-permute-start | bytes 392 | tf_op jit(solution)/shard_map/ppermute | solution.py:85
  139.4 7.8 %collective-permute-start.14 = (f32[32]{0:T(128)S(1)}, f32[32]{0:T(128)S(1)}, u32[]{:S(2)}, u32[]{:S(2)}) collective-permute-start(f32[32]{0:T(128)S(1)} %add.172), channel_id=1, source_target_pairs={{0,64},{16,80},{32,96},{48,112},{64,0},{80,16},{96,32},{112,48},{1... | collective-permute-start | bytes 392 | tf_op jit(solution)/shard_map/ppermute | solution.py:85
  147.3 7.6 %collective-permute-start.15 = (f32[32]{0:T(128)S(1)}, f32[32]{0:T(128)S(1)}, u32[]{:S(2)}, u32[]{:S(2)}) collective-permute-start(f32[32]{0:T(128)S(1)} %add.173), channel_id=1, source_target_pairs={{0,128},{16,144},{32,160},{48,176},{64,192},{80,208},{96,224},{112... | collective-permute-start | bytes 392 | tf_op jit(solution)/shard_map/ppermute | solution.py:85
  155.2 25.0 %copy-start = (f32[16,256]{1,0:T(8,128)S(1)}, f32[16,256]{1,0:T(8,128)}, u32[]{:S(2)}) copy-start(f32[16,256]{1,0:T(8,128)} %param.19) | copy-start | bytes 49156
  155.2 25.0 %copy-start.1 = (f32[16,256]{1,0:T(8,128)S(1)}, f32[16,256]{1,0:T(8,128)}, u32[]{:S(2)}) copy-start(f32[16,256]{1,0:T(8,128)} %param.18) | copy-start | bytes 49156
  155.2 25.0 %copy-start.2 = (f32[16,256]{1,0:T(8,128)S(1)}, f32[16,256]{1,0:T(8,128)}, u32[]{:S(2)}) copy-start(f32[16,256]{1,0:T(8,128)} %param.17) | copy-start | bytes 49156
  155.2 25.7 %copy-start.3 = (f32[64]{0:T(128)S(1)}, f32[64]{0:T(128)}, u32[]{:S(2)}) copy-start(f32[64]{0:T(128)} %param.16) | copy-start | bytes 772
  157.6 3.8 %collective-permute-start.16 = (f32[16,512]{1,0:T(8,128)S(1)}, f32[16,512]{1,0:T(8,128)S(1)}, u32[]{:S(2)}, u32[]{:S(2)}) collective-permute-start(f32[16,512]{1,0:T(8,128)S(1)} %slice_select_fusion), channel_id=1, source_target_pairs={{0,1},{1,0},{2,3},{3,2},{4,5},{5,4},{6,7},{7,6},{8,9},{9,8},{10,11... | collective-permute-start | bytes 98312 | tf_op jit(solution)/shard_map/ppermute | solution.py:99
  157.7 3.7 %collective-permute-start.17 = (f32[16]{0:T(128)S(1)}, f32[16]{0:T(128)S(1)}, u32[]{:S(2)}, u32[]{:S(2)}) collective-permute-start(f32[16]{0:T(128)S(1)} %get-tuple-element.58), channel_id=1, source_target_pairs={{0,16},{16,0},{32,48},{48,32},{64,80},{80,64},{96,112},{112,96},{1... | collective-permute-start | bytes 200 | tf_op jit(solution)/shard_map/ppermute | solution.py:100
  161.4 4.2 %collective-permute-start.18 = (f32[16,256]{1,0:T(8,128)S(1)}, f32[16,256]{1,0:T(8,128)S(1)}, u32[]{:S(2)}, u32[]{:S(2)}) collective-permute-start(f32[16,256]{1,0:T(8,128)S(1)} %slice_select_fusion.1), channel_id=1, source_target_pairs={{0,2},{1,3},{2,0},{3,1},{4,6},{5,7},{6,4},{7,5},{8,10},{9,11},{10,... | collective-permute-start | bytes 49160 | tf_op jit(solution)/shard_map/ppermute | solution.py:99
  162.0 3.6 %collective-permute-start.19 = (f32[16]{0:T(128)S(1)}, f32[16]{0:T(128)S(1)}, u32[]{:S(2)}, u32[]{:S(2)}) collective-permute-start(f32[16]{0:T(128)S(1)} %add.194), channel_id=1, source_target_pairs={{0,32},{16,48},{32,0},{48,16},{64,96},{80,112},{96,64},{112,80},{1... | collective-permute-start | bytes 200 | tf_op jit(solution)/shard_map/ppermute | solution.py:100
  165.6 7.0 %collective-permute-start.20 = (f32[16,128]{1,0:T(8,128)S(1)}, f32[16,128]{1,0:T(8,128)S(1)}, u32[]{:S(2)}, u32[]{:S(2)}) collective-permute-start(f32[16,128]{1,0:T(8,128)S(1)} %slice_select_fusion.3), channel_id=1, source_target_pairs={{0,4},{1,5},{2,6},{3,7},{4,0},{5,1},{6,2},{7,3},{8,12},{9,13},{10,... | collective-permute-start | bytes 24584 | tf_op jit(solution)/shard_map/ppermute | solution.py:99
  168.1 4.5 %collective-permute-start.21 = (f32[16]{0:T(128)S(1)}, f32[16]{0:T(128)S(1)}, u32[]{:S(2)}, u32[]{:S(2)}) collective-permute-start(f32[16]{0:T(128)S(1)} %add.196), channel_id=1, source_target_pairs={{0,64},{16,80},{32,96},{48,112},{64,0},{80,16},{96,32},{112,48},{1... | collective-permute-start | bytes 200 | tf_op jit(solution)/shard_map/ppermute | solution.py:100
  172.7 7.5 %collective-permute-start.22 = (f32[16]{0:T(128)S(1)}, f32[16]{0:T(128)S(1)}, u32[]{:S(2)}, u32[]{:S(2)}) collective-permute-start(f32[16]{0:T(128)S(1)} %add.198), channel_id=1, source_target_pairs={{0,128},{16,144},{32,160},{48,176},{64,192},{80,208},{96,224},{112... | collective-permute-start | bytes 200 | tf_op jit(solution)/shard_map/ppermute | solution.py:100
  173.7 7.2 %collective-permute-start.23 = (f32[16,64]{1,0:T(8,128)S(1)}, f32[16,64]{1,0:T(8,128)S(1)}, u32[]{:S(2)}, u32[]{:S(2)}) collective-permute-start(f32[16,64]{1,0:T(8,128)S(1)} %slice_select_fusion.2), channel_id=1, source_target_pairs={{0,8},{1,9},{2,10},{3,11},{4,12},{5,13},{6,14},{7,15},{8,0},{9,1},... | collective-permute-start | bytes 12296 | tf_op jit(solution)/shard_map/ppermute | solution.py:99

commit v9 on v8

--- a/solution.py
+++ b/solution.py
@@ -52,11 +52,6 @@
     return result.T
 
 
-def tied(x, dep):
-    x, dep = lax.optimization_barrier((x, dep))
-    return x
-
-
 def xor_perm(size, bit):
     return [(i, i ^ (1 << bit)) for i in range(size)]
 
@@ -80,10 +75,24 @@
     return buf
 
 
-def all_sum(x, axis_name, size):
-    for bit in range(size.bit_length() - 1):
-        x = x + lax.ppermute(x, axis_name, xor_perm(size, bit))
-    return x
+def col_sum_with_grid(rows, sums, n_row, n_col):
+    cols = rows.shape[0]
+    extra = sums.shape[0] // cols
+    for bit in range(n_col.bit_length() - 1):
+        packed = jnp.concatenate([rows, sums.reshape(cols, extra)], 1)
+        got = lax.ppermute(packed, "col", xor_perm(n_col, bit))
+        step = 1 << bit
+        diag = [
+            (r * n_col + c, (r ^ step) * n_col + (c ^ step))
+            for r in range(n_row)
+            for c in range(n_col)
+        ]
+        from_row = lax.ppermute(sums, "row", xor_perm(n_row, bit))
+        from_diag = lax.ppermute(sums, ("row", "col"), diag)
+        rows = rows + got[:, : rows.shape[1]]
+        from_col = got[:, rows.shape[1]:].reshape(-1)
+        sums = (sums + from_col) + (from_row + from_diag)
+    return rows, sums
 
 
 def tail_sums(fit, local, axis_rs, axis_ar, size_rs, size_ar):
@@ -181,12 +190,16 @@
                 )
             )
         )
-    kernel_row = all_sum(partial_rows, "col", n_col)
-    image_row = kernel_row + noise_var[0] * dir_row
+    noise = noise_var[0]
     local_sums = jnp.concatenate(
-        [jnp.sum(res_row * res_row, axis=1), jnp.sum(dir_row * image_row, axis=1)]
-    )
-    sums = all_sum(tied(local_sums, w_col), "row", n_row)
+        [
+            jnp.sum(residual * residual, axis=1),
+            jnp.sum(dir_row * partial_rows, axis=1)
+            + noise * jnp.sum(direction * direction, axis=1),
+        ]
+    )
+    kernel_row, sums = col_sum_with_grid(partial_rows, local_sums, n_row, n_col)
+    image_row = kernel_row + noise * dir_row
     norm_now, curvature = sums[:cols], sums[cols:]
     step_len = norm_now / curvature
     residual_new_row = res_row - step_len[:, None] * image_row

time: 184 us -> 185 us (level)
  waiting for transfers between devices: 61.6 us -> 40.1 us
  starting transfers between devices: 33.5 us -> 47.9 us
  matrix products: 73.7 us -> 78.6 us
    ppermute x8 -> x12, waiting for transfers between devices: 31.4 us -> 15.2 us  [the longest x4 8.63 us: col_sum_with_grid(): from_diag = lax.ppermute(sums, ('row', 'col'), diag)]
    ppermute x8 -> x12, starting transfers between devices: 8.03 us -> 20.7 us  [the longest x4 11.1 us: col_sum_with_grid(): from_diag = lax.ppermute(sums, ('row', 'col'), diag)]
    ppermute x4, starting transfers between devices: 3.38 us -> 6.68 us  [tail_sums(): x = x + lax.ppermute(x, axis_ar, xor_perm(size_ar, bit))]
    ppermute x8, waiting for transfers between devices: 17.6 us -> 14.5 us  [gather_last(): recv = lax.ppermute(buf, axis_name, xor_perm(size, bit))]
    ppermute x4, waiting for transfers between devices: 12.6 us -> 9.77 us  [tail_sums(): x = x + lax.ppermute(x, axis_ar, xor_perm(size_ar, bit))]
    dot_general x2, matrix products: 11.6 us -> 14.3 us  [matern_block(): lax.dot_general(row_pts_m2, col_pts, contract_first, preferred_element_ty...]
    dot_general x2, matrix products: 2.38 us -> 4.59 us  [per_device(): lax.dot_general(w_low_col[:, lo:hi], cand_blocks[k], contract_last, prefe...]
  transfers between devices with their start and end apart: 24 -> 28, of which waited for: 16 -> 16; matrix products, arithmetic and copies ran while one was open for 8% -> 11% of each run, Pallas kernels for 0% -> 0%
where the time goes in v9:
time: 185 us; the launch traced here: 182 us
  matrix products  78.6 us (42%)
  starting transfers between devices  47.9 us (26%)
  waiting for transfers between devices  40.1 us (22%)
  other arithmetic  11 us (6%)
  between operations  2.39 us (1%)
    dot_general x16, matrix products, one_block(): lax.dot_general(kern_vals, vec_blk, contract_last, preferred_element_type...  59.7 us
    ppermute x8, starting transfers between devices, gather_last(): recv = lax.ppermute(buf, axis_name, xor_perm(size, bit))  15.7 us
    ppermute x8, waiting for transfers between devices, gather_last(): recv = lax.ppermute(buf, axis_name, xor_perm(size, bit))  14.5 us
    dot_general x2, matrix products, matern_block(): lax.dot_general(row_pts_m2, col_pts, contract_first, preferred_element_ty...  14.3 us
    ppermute x4, starting transfers between devices, col_sum_with_grid(): from_diag = lax.ppermute(sums, ('row', 'col'), diag)  11.1 us
    ppermute x4, waiting for transfers between devices, tail_sums(): x = x + lax.ppermute(x, axis_ar, xor_perm(size_ar, bit))  9.77 us
    ppermute x4, waiting for transfers between devices, col_sum_with_grid(): from_diag = lax.ppermute(sums, ('row', 'col'), diag)  8.63 us
    ppermute x4, starting transfers between devices, tail_sums(): x = x + lax.ppermute(x, axis_ar, xor_perm(size_ar, bit))  6.68 us
  transfers between devices with their start and end apart: 28, of which 16 were waited for; matrix products, arithmetic and copies ran while one was open for 11% of the time, Pallas kernels for 0%

profile of v9, /device:TPU:2, one launch (start us, length us, event | category | flops | bytes accessed | tf_op | source)
XLA Modules:
  0.0 182.0 jit_solution(3801222038410778542)
XLA Ops:
  0.6 0.8 constant_dynamic-update-slice_fusion.10
  1.5 0.8 divide_convert_fusion.1
  2.4 0.7 constant_dynamic-update-slice_fusion.9
  3.1 0.7 constant_dynamic-update-slice_fusion.8
  3.8 0.7 constant_dynamic-update-slice_fusion.7
  4.5 0.7 constant_dynamic-update-slice_fusion.6
  5.3 7.2 %collective-permute-start.4 = (bf16[96,256]{1,0:T(8,128)(2,1)S(1)}, bf16[96,256]{1,0:T(8,128)(2,1)S(1)}, u32[]{:S(2)}, u32[]{:S(2)}) collective-permute-start(bf16[96,256]{1,0:T(8,128)(2,1)S(1)} %constant_dynamic-update-slice_fusion.6), channel_id=1, source_target_pairs={{0,128},{16,144},{32,160},{48,176},{64,192},{80,208},{96,224},{112... | collective-permute-start | bytes 147464 | tf_op jit(solution)/shard_map/ppermute | solution.py:70
  12.4 0.7 constant_dynamic-update-slice_fusion.1
  13.2 0.7 constant_dynamic-update-slice_fusion
  13.9 3.2 %collective-permute-start = (bf16[104,256]{1,0:T(8,128)(2,1)S(1)}, bf16[104,256]{1,0:T(8,128)(2,1)S(1)}, u32[]{:S(2)}, u32[]{:S(2)}) collective-permute-start(bf16[104,256]{1,0:T(8,128)(2,1)S(1)} %constant_dynamic-update-slice_fusion), channel_id=1, source_target_pairs={{0,8},{1,9},{2,10},{3,11},{4,12},{5,13},{6,14},{7,15},{8,0},{9,1},... | collective-permute-start | bytes 159752 | tf_op jit(solution)/shard_map/ppermute | solution.py:70
  17.1 1.6 collective-permute-start.5
  18.7 0.9 collective-permute-done
  19.5 2.2 %collective-permute-start.1 = (bf16[104,512]{1,0:T(8,128)(2,1)S(1)}, bf16[104,512]{1,0:T(8,128)(2,1)S(1)}, u32[]{:S(2)}, u32[]{:S(2)}) collective-permute-start(bf16[104,512]{1,0:T(8,128)(2,1)S(1)} %maximum_select_fusion.6), channel_id=1, source_target_pairs={{0,4},{1,5},{2,6},{3,7},{4,0},{5,1},{6,2},{7,3},{8,12},{9,13},{10,... | collective-permute-start | bytes 319496 | tf_op jit(solution)/shard_map/ppermute | solution.py:70
  21.8 2.4 %collective-permute-done.5 = bf16[96,512]{1,0:T(8,128)(2,1)S(1)} collective-permute-done((bf16[96,512]{1,0:T(8,128)(2,1)S(1)}, bf16[96,512]{1,0:T(8,128)(2,1)S(1)}, u32[]{:S(2)}, u32[]{:S(2)}) %collective-permute-start.5) | collective-permute-done | bytes 98336 | tf_op jit(solution)/shard_map/ppermute | solution.py:70
  24.4 1.5 collective-permute-done.1
  26.5 4.1 %collective-permute-done.6 = bf16[96,1024]{1,0:T(8,128)(2,1)S(1)} collective-permute-done((bf16[96,1024]{1,0:T(8,128)(2,1)S(1)}, bf16[96,1024]{1,0:T(8,128)(2,1)S(1)}, u32[]{:S(2)}, u32[]{:S(2)}) %collective-permute-start.6) | collective-permute-done | bytes 196640 | tf_op jit(solution)/shard_map/ppermute | solution.py:70
  30.7 0.8 collective-permute-start.7
  31.5 0.8 multiply_reduce_fusion.5
  33.7 0.8 multiply_reduce_fusion.4
  34.7 5.7 %collective-permute-done.7 = bf16[96,2048]{1,0:T(8,128)(2,1)S(1)} collective-permute-done((bf16[96,2048]{1,0:T(8,128)(2,1)S(1)}, bf16[96,2048]{1,0:T(8,128)(2,1)S(1)}, u32[]{:S(2)}, u32[]{:S(2)}) %collective-permute-start.7) | collective-permute-done | bytes 393248 | tf_op jit(solution)/shard_map/ppermute | solution.py:70
  41.2 60.4 %while.11 = (s32[]{:T(128)}, f32[4096,16]{0,1:T(8,128)S(1)}, f32[]{:T(128)}, f32[4096]{0:T(1024)S(1)}, f32[16,256]{1,0:T(8,128)S(1)}, /*index=5*/bf16[16,32,256]...) while((s32[]{:T(128)}, f32[4096,16]{0,1:T(8,128)S(1)}, ...), condition=%wide.region_4.5_spmd.clone, body=%wide.region_3.4_spmd.clone.sunk | while | flops 112328704 | bytes 832126 | solution.py:51
  41.2 3.7 %convolution_add_fusion.3 = f32[4096,16]{0,1:T(8,128)S(1)} fusion(bf16[32,4096]{1,0:T(8,128)(2,1)S(1)} %get-tuple-element.195, f32[256]{0:T(256)S(1)} %bitcast.72, f32[4096]{0:T(1024)S(1)} %get-tuple-element.192, f32[]{:T(128)} %get-tuple-element.191, f32[4096,16]{0,1:T(8,128)S(1)} %get-tuple-element.180, pred[]{:T(512)S(6)} %compare.3, ...), kind=kOutput, calls=%fused_computation.3.clone.1 | convolution fusion | flops 112328704 | bytes 829956 | tf_op jit(solution)/shard_map/while/body/eval_jaxpr/dot_general | solution.py:44
  45.0 3.7 %convolution_add_fusion.3 = f32[4096,16]{0,1:T(8,128)S(1)} fusion(bf16[32,4096]{1,0:T(8,128)(2,1)S(1)} %get-tuple-element.195, f32[256]{0:T(256)S(1)} %bitcast.72, f32[4096]{0:T(1024)S(1)} %get-tuple-element.192, f32[]{:T(128)} %get-tuple-element.191, f32[4096,16]{0,1:T(8,128)S(1)} %get-tuple-element.180, pred[]{:T(512)S(6)} %compare.3, ...), kind=kOutput, calls=%fused_computation.3.clone.1 | convolution fusion | flops 112328704 | bytes 829956 | tf_op jit(solution)/shard_map/while/body/eval_jaxpr/dot_general | solution.py:44
  48.7 3.7 %convolution_add_fusion.3 = f32[4096,16]{0,1:T(8,128)S(1)} fusion(bf16[32,4096]{1,0:T(8,128)(2,1)S(1)} %get-tuple-element.195, f32[256]{0:T(256)S(1)} %bitcast.72, f32[4096]{0:T(1024)S(1)} %get-tuple-element.192, f32[]{:T(128)} %get-tuple-element.191, f32[4096,16]{0,1:T(8,128)S(1)} %get-tuple-element.180, pred[]{:T(512)S(6)} %compare.3, ...), kind=kOutput, calls=%fused_computation.3.clone.1 | convolution fusion | flops 112328704 | bytes 829956 | tf_op jit(solution)/shard_map/while/body/eval_jaxpr/dot_general | solution.py:44
  52.5 3.7 %convolution_add_fusion.3 = f32[4096,16]{0,1:T(8,128)S(1)} fusion(bf16[32,4096]{1,0:T(8,128)(2,1)S(1)} %get-tuple-element.195, f32[256]{0:T(256)S(1)} %bitcast.72, f32[4096]{0:T(1024)S(1)} %get-tuple-element.192, f32[]{:T(128)} %get-tuple-element.191, f32[4096,16]{0,1:T(8,128)S(1)} %get-tuple-element.180, pred[]{:T(512)S(6)} %compare.3, ...), kind=kOutput, calls=%fused_computation.3.clone.1 | convolution fusion | flops 112328704 | bytes 829956 | tf_op jit(solution)/shard_map/while/body/eval_jaxpr/dot_general | solution.py:44
  56.3 3.7 %convolution_add_fusion.3 = f32[4096,16]{0,1:T(8,128)S(1)} fusion(bf16[32,4096]{1,0:T(8,128)(2,1)S(1)} %get-tuple-element.195, f32[256]{0:T(256)S(1)} %bitcast.72, f32[4096]{0:T(1024)S(1)} %get-tuple-element.192, f32[]{:T(128)} %get-tuple-element.191, f32[4096,16]{0,1:T(8,128)S(1)} %get-tuple-element.180, pred[]{:T(512)S(6)} %compare.3, ...), kind=kOutput, calls=%fused_computation.3.clone.1 | convolution fusion | flops 112328704 | bytes 829956 | tf_op jit(solution)/shard_map/while/body/eval_jaxpr/dot_general | solution.py:44
  60.0 3.7 %convolution_add_fusion.3 = f32[4096,16]{0,1:T(8,128)S(1)} fusion(bf16[32,4096]{1,0:T(8,128)(2,1)S(1)} %get-tuple-element.195, f32[256]{0:T(256)S(1)} %bitcast.72, f32[4096]{0:T(1024)S(1)} %get-tuple-element.192, f32[]{:T(128)} %get-tuple-element.191, f32[4096,16]{0,1:T(8,128)S(1)} %get-tuple-element.180, pred[]{:T(512)S(6)} %compare.3, ...), kind=kOutput, calls=%fused_computation.3.clone.1 | convolution fusion | flops 112328704 | bytes 829956 | tf_op jit(solution)/shard_map/while/body/eval_jaxpr/dot_general | solution.py:44
  63.8 3.7 %convolution_add_fusion.3 = f32[4096,16]{0,1:T(8,128)S(1)} fusion(bf16[32,4096]{1,0:T(8,128)(2,1)S(1)} %get-tuple-element.195, f32[256]{0:T(256)S(1)} %bitcast.72, f32[4096]{0:T(1024)S(1)} %get-tuple-element.192, f32[]{:T(128)} %get-tuple-element.191, f32[4096,16]{0,1:T(8,128)S(1)} %get-tuple-element.180, pred[]{:T(512)S(6)} %compare.3, ...), kind=kOutput, calls=%fused_computation.3.clone.1 | convolution fusion | flops 112328704 | bytes 829956 | tf_op jit(solution)/shard_map/while/body/eval_jaxpr/dot_general | solution.py:44
  67.6 3.7 %convolution_add_fusion.3 = f32[4096,16]{0,1:T(8,128)S(1)} fusion(bf16[32,4096]{1,0:T(8,128)(2,1)S(1)} %get-tuple-element.195, f32[256]{0:T(256)S(1)} %bitcast.72, f32[4096]{0:T(1024)S(1)} %get-tuple-element.192, f32[]{:T(128)} %get-tuple-element.191, f32[4096,16]{0,1:T(8,128)S(1)} %get-tuple-element.180, pred[]{:T(512)S(6)} %compare.3, ...), kind=kOutput, calls=%fused_computation.3.clone.1 | convolution fusion | flops 112328704 | bytes 829956 | tf_op jit(solution)/shard_map/while/body/eval_jaxpr/dot_general | solution.py:44
  71.4 3.7 %convolution_add_fusion.3 = f32[4096,16]{0,1:T(8,128)S(1)} fusion(bf16[32,4096]{1,0:T(8,128)(2,1)S(1)} %get-tuple-element.195, f32[256]{0:T(256)S(1)} %bitcast.72, f32[4096]{0:T(1024)S(1)} %get-tuple-element.192, f32[]{:T(128)} %get-tuple-element.191, f32[4096,16]{0,1:T(8,128)S(1)} %get-tuple-element.180, pred[]{:T(512)S(6)} %compare.3, ...), kind=kOutput, calls=%fused_computation.3.clone.1 | convolution fusion | flops 112328704 | bytes 829956 | tf_op jit(solution)/shard_map/while/body/eval_jaxpr/dot_general | solution.py:44
  75.1 3.7 %convolution_add_fusion.3 = f32[4096,16]{0,1:T(8,128)S(1)} fusion(bf16[32,4096]{1,0:T(8,128)(2,1)S(1)} %get-tuple-element.195, f32[256]{0:T(256)S(1)} %bitcast.72, f32[4096]{0:T(1024)S(1)} %get-tuple-element.192, f32[]{:T(128)} %get-tuple-element.191, f32[4096,16]{0,1:T(8,128)S(1)} %get-tuple-element.180, pred[]{:T(512)S(6)} %compare.3, ...), kind=kOutput, calls=%fused_computation.3.clone.1 | convolution fusion | flops 112328704 | bytes 829956 | tf_op jit(solution)/shard_map/while/body/eval_jaxpr/dot_general | solution.py:44
  78.9 3.7 %convolution_add_fusion.3 = f32[4096,16]{0,1:T(8,128)S(1)} fusion(bf16[32,4096]{1,0:T(8,128)(2,1)S(1)} %get-tuple-element.195, f32[256]{0:T(256)S(1)} %bitcast.72, f32[4096]{0:T(1024)S(1)} %get-tuple-element.192, f32[]{:T(128)} %get-tuple-element.191, f32[4096,16]{0,1:T(8,128)S(1)} %get-tuple-element.180, pred[]{:T(512)S(6)} %compare.3, ...), kind=kOutput, calls=%fused_computation.3.clone.1 | convolution fusion | flops 112328704 | bytes 829956 | tf_op jit(solution)/shard_map/while/body/eval_jaxpr/dot_general | solution.py:44
  82.7 3.7 %convolution_add_fusion.3 = f32[4096,16]{0,1:T(8,128)S(1)} fusion(bf16[32,4096]{1,0:T(8,128)(2,1)S(1)} %get-tuple-element.195, f32[256]{0:T(256)S(1)} %bitcast.72, f32[4096]{0:T(1024)S(1)} %get-tuple-element.192, f32[]{:T(128)} %get-tuple-element.191, f32[4096,16]{0,1:T(8,128)S(1)} %get-tuple-element.180, pred[]{:T(512)S(6)} %compare.3, ...), kind=kOutput, calls=%fused_computation.3.clone.1 | convolution fusion | flops 112328704 | bytes 829956 | tf_op jit(solution)/shard_map/while/body/eval_jaxpr/dot_general | solution.py:44
  86.5 3.7 %convolution_add_fusion.3 = f32[4096,16]{0,1:T(8,128)S(1)} fusion(bf16[32,4096]{1,0:T(8,128)(2,1)S(1)} %get-tuple-element.195, f32[256]{0:T(256)S(1)} %bitcast.72, f32[4096]{0:T(1024)S(1)} %get-tuple-element.192, f32[]{:T(128)} %get-tuple-element.191, f32[4096,16]{0,1:T(8,128)S(1)} %get-tuple-element.180, pred[]{:T(512)S(6)} %compare.3, ...), kind=kOutput, calls=%fused_computation.3.clone.1 | convolution fusion | flops 112328704 | bytes 829956 | tf_op jit(solution)/shard_map/while/body/eval_jaxpr/dot_general | solution.py:44
  90.2 3.7 %convolution_add_fusion.3 = f32[4096,16]{0,1:T(8,128)S(1)} fusion(bf16[32,4096]{1,0:T(8,128)(2,1)S(1)} %get-tuple-element.195, f32[256]{0:T(256)S(1)} %bitcast.72, f32[4096]{0:T(1024)S(1)} %get-tuple-element.192, f32[]{:T(128)} %get-tuple-element.191, f32[4096,16]{0,1:T(8,128)S(1)} %get-tuple-element.180, pred[]{:T(512)S(6)} %compare.3, ...), kind=kOutput, calls=%fused_computation.3.clone.1 | convolution fusion | flops 112328704 | bytes 829956 | tf_op jit(solution)/shard_map/while/body/eval_jaxpr/dot_general | solution.py:44
  94.0 3.7 %convolution_add_fusion.3 = f32[4096,16]{0,1:T(8,128)S(1)} fusion(bf16[32,4096]{1,0:T(8,128)(2,1)S(1)} %get-tuple-element.195, f32[256]{0:T(256)S(1)} %bitcast.72, f32[4096]{0:T(1024)S(1)} %get-tuple-element.192, f32[]{:T(128)} %get-tuple-element.191, f32[4096,16]{0,1:T(8,128)S(1)} %get-tuple-element.180, pred[]{:T(512)S(6)} %compare.3, ...), kind=kOutput, calls=%fused_computation.3.clone.1 | convolution fusion | flops 112328704 | bytes 829956 | tf_op jit(solution)/shard_map/while/body/eval_jaxpr/dot_general | solution.py:44
  97.8 3.7 %convolution_add_fusion.3 = f32[4096,16]{0,1:T(8,128)S(1)} fusion(bf16[32,4096]{1,0:T(8,128)(2,1)S(1)} %get-tuple-element.195, f32[256]{0:T(256)S(1)} %bitcast.72, f32[4096]{0:T(1024)S(1)} %get-tuple-element.192, f32[]{:T(128)} %get-tuple-element.191, f32[4096,16]{0,1:T(8,128)S(1)} %get-tuple-element.180, pred[]{:T(512)S(6)} %compare.3, ...), kind=kOutput, calls=%fused_computation.3.clone.1 | convolution fusion | flops 112328704 | bytes 829956 | tf_op jit(solution)/shard_map/while/body/eval_jaxpr/dot_general | solution.py:44
  102.0 0.7 collective-permute-start.9
  102.7 1.2 collective-permute-start.10
  104.0 1.6 collective-permute-done.9
  107.8 2.5 %collective-permute-start.13 = (f32[32]{0:T(128)S(1)}, f32[32]{0:T(128)S(1)}, u32[]{:S(2)}, u32[]{:S(2)}) collective-permute-start(f32[32]{0:T(128)S(1)} %add_add_fusion.4), channel_id=1, source_target_pairs={{0,34},{1,35},{2,32},{3,33},{4,38},{5,39},{6,36},{7,37},{8,42},{9,... | collective-permute-start | bytes 392 | tf_op jit(solution)/shard_map/ppermute | solution.py:91
  110.3 4.4 %collective-permute-done.11 = f32[16,4098]{1,0:T(8,128)S(1)} collective-permute-done((f32[16,4098]{1,0:T(8,128)S(1)}, f32[16,4098]{1,0:T(8,128)S(1)}, u32[]{:S(2)}, u32[]{:S(2)}) %collective-permute-start.11) | collective-permute-done | bytes 262304 | tf_op jit(solution)/shard_map/ppermute | solution.py:83
  114.9 2.2 %collective-permute-start.14 = (f32[16,4098]{1,0:T(8,128)S(1)}, f32[16,4098]{1,0:T(8,128)S(1)}, u32[]{:S(2)}, u32[]{:S(2)}) collective-permute-start(f32[16,4098]{1,0:T(8,128)S(1)} %pad_maximum_fusion.1), channel_id=1, source_target_pairs={{0,4},{1,5},{2,6},{3,7},{4,0},{5,1},{6,2},{7,3},{8,12},{9,13},{10,... | collective-permute-start | bytes 786824 | tf_op jit(solution)/shard_map/ppermute | solution.py:83
  117.1 7.1 %multiply_convert_fusion.2 = bf16[1024,2048]{1,0:T(8,128)(2,1)} fusion(bf16[32,1024]{1,0:T(8,128)(2,1)S(1)} %mul.165, f32[2048]{0:T(1024)S(1)} %get-tuple-element.114, f32[1024]{0:T(1024)S(1)} %add.219, f32[]{:T(128)} %bitcast.59, bf16[96,4096]{1,0:T(8,128)(2,1)S(1)} %maximum_select_fusion.1), kind=kOutput, calls=%fused_computation.17 | convolution fusion | flops 157286400 | bytes 4403204 | tf_op jit(solution)/shard_map/dot_general | solution.py:19
  124.2 1.0 collective-permute-start.15
  125.3 2.7 %collective-permute-start.16 = (f32[32]{0:T(128)S(1)}, f32[32]{0:T(128)S(1)}, u32[]{:S(2)}, u32[]{:S(2)}) collective-permute-start(f32[32]{0:T(128)S(1)} %add_add_fusion.3), channel_id=1, source_target_pairs={{0,68},{1,69},{2,70},{3,71},{4,64},{5,65},{6,66},{7,67},{8,76},{9,... | collective-permute-start | bytes 392 | tf_op jit(solution)/shard_map/ppermute | solution.py:91
  128.7 3.4 %collective-permute-done.16 = f32[32]{0:T(128)S(1)} collective-permute-done((f32[32]{0:T(128)S(1)}, f32[32]{0:T(128)S(1)}, u32[]{:S(2)}, u32[]{:S(2)}) %collective-permute-start.16) | collective-permute-done | bytes 160 | tf_op jit(solution)/shard_map/ppermute | solution.py:91
  132.3 0.9 collective-permute-start.17
  133.2 7.2 %multiply_convert_fusion.1 = bf16[1024,2048]{1,0:T(8,128)(2,1)} fusion(bf16[32,1024]{1,0:T(8,128)(2,1)S(1)} %mul.165, f32[2048]{0:T(1024)S(1)} %get-tuple-element.113, f32[1024]{0:T(1024)S(1)} %add.219, f32[]{:T(128)} %bitcast.60, bf16[96,4096]{1,0:T(8,128)(2,1)S(1)} %maximum_select_fusion.1), kind=kOutput, calls=%fused_computation.16 | convolution fusion | flops 157286400 | bytes 4403204 | tf_op jit(solution)/shard_map/dot_general | solution.py:19
  140.3 3.4 %collective-permute-start.18 = (f32[32]{0:T(128)S(1)}, f32[32]{0:T(128)S(1)}, u32[]{:S(2)}, u32[]{:S(2)}) collective-permute-start(f32[32]{0:T(128)S(1)} %add_add_fusion.2), channel_id=1, source_target_pairs={{0,128},{16,144},{32,160},{48,176},{64,192},{80,208},{96,224},{112... | collective-permute-start | bytes 392 | tf_op jit(solution)/shard_map/ppermute | solution.py:90
  143.7 4.7 %collective-permute-start.19 = (f32[32]{0:T(128)S(1)}, f32[32]{0:T(128)S(1)}, u32[]{:S(2)}, u32[]{:S(2)}) collective-permute-start(f32[32]{0:T(128)S(1)} %add_add_fusion.2), channel_id=1, source_target_pairs={{0,136},{1,137},{2,138},{3,139},{4,140},{5,141},{6,142},{7,143},{8... | collective-permute-start | bytes 392 | tf_op jit(solution)/shard_map/ppermute | solution.py:91
  148.5 5.1 %collective-permute-done.19 = f32[32]{0:T(128)S(1)} collective-permute-done((f32[32]{0:T(128)S(1)}, f32[32]{0:T(128)S(1)}, u32[]{:S(2)}, u32[]{:S(2)}) %collective-permute-start.19) | collective-permute-done | bytes 160 | tf_op jit(solution)/shard_map/ppermute | solution.py:91
  154.0 3.4 %fusion.18 = f32[16,1024]{1,0:T(8,128)S(1)} fusion(bf16[1024,2048]{1,0:T(8,128)(2,1)} %multiply_convert_fusion.2, bf16[16,4096]{1,0:T(8,128)(2,1)S(1)} %get-tuple-element.119), kind=kOutput, calls=%fused_computation.48 | convolution fusion | flops 67108864 | bytes 4325376 | tf_op jit(solution)/shard_map/dot_general | solution.py:220
  157.4 1.2 convolution_add_fusion.1
  159.2 3.4 %collective-permute-done.21 = f32[16]{0:T(128)S(1)} collective-permute-done((f32[16]{0:T(128)S(1)}, f32[16]{0:T(128)S(1)}, u32[]{:S(2)}, u32[]{:S(2)}) %collective-permute-start.21) | collective-permute-done | bytes 96 | tf_op jit(solution)/shard_map/ppermute | solution.py:109
  162.6 1.5 collective-permute-start.22
  164.2 2.0 %collective-permute-start.23 = (f32[16]{0:T(128)S(1)}, f32[16]{0:T(128)S(1)}, u32[]{:S(2)}, u32[]{:S(2)}) collective-permute-start(f32[16]{0:T(128)S(1)} %add.235), channel_id=1, source_target_pairs={{0,32},{16,48},{32,0},{48,16},{64,96},{80,112},{96,64},{112,80},{1... | collective-permute-start | bytes 200 | tf_op jit(solution)/shard_map/ppermute | solution.py:109
  166.2 1.5 collective-permute-done.23
  168.0 1.9 %collective-permute-start.25 = (f32[16]{0:T(128)S(1)}, f32[16]{0:T(128)S(1)}, u32[]{:S(2)}, u32[]{:S(2)}) collective-permute-start(f32[16]{0:T(128)S(1)} %add.237), channel_id=1, source_target_pairs={{0,64},{16,80},{32,96},{48,112},{64,0},{80,16},{96,32},{112,48},{1... | collective-permute-start | bytes 200 | tf_op jit(solution)/shard_map/ppermute | solution.py:109
  169.9 2.6 %collective-permute-done.25 = f32[16]{0:T(128)S(1)} collective-permute-done((f32[16]{0:T(128)S(1)}, f32[16]{0:T(128)S(1)}, u32[]{:S(2)}, u32[]{:S(2)}) %collective-permute-start.25) | collective-permute-done | bytes 96 | tf_op jit(solution)/shard_map/ppermute | solution.py:109
  173.1 2.5 %collective-permute-start.26 = (f32[16]{0:T(128)S(1)}, f32[16]{0:T(128)S(1)}, u32[]{:S(2)}, u32[]{:S(2)}) collective-permute-start(f32[16]{0:T(128)S(1)} %add.239), channel_id=1, source_target_pairs={{0,128},{16,144},{32,160},{48,176},{64,192},{80,208},{96,224},{112... | collective-permute-start | bytes 200 | tf_op jit(solution)/shard_map/ppermute | solution.py:109
  175.6 2.7 %collective-permute-start.27 = (f32[16,64]{1,0:T(8,128)S(1)}, f32[16,64]{1,0:T(8,128)S(1)}, u32[]{:S(2)}, u32[]{:S(2)}) collective-permute-start(f32[16,64]{1,0:T(8,128)S(1)} %slice_select_fusion.2), channel_id=1, source_target_pairs={{0,8},{1,9},{2,10},{3,11},{4,12},{5,13},{6,14},{7,15},{8,0},{9,1},... | collective-permute-start | bytes 12296 | tf_op jit(solution)/shard_map/ppermute | solution.py:108
  178.3 2.2 %collective-permute-done.26 = f32[16]{0:T(128)S(1)} collective-permute-done((f32[16]{0:T(128)S(1)}, f32[16]{0:T(128)S(1)}, u32[]{:S(2)}, u32[]{:S(2)}) %collective-permute-start.26) | collective-permute-done | bytes 96 | tf_op jit(solution)/shard_map/ppermute | solution.py:109
  180.6 0.7 multiply_add_fusion
  (119 shorter events, 8.5 us)
Async XLA Ops:
  5.3 11.8 %collective-permute-start.4 = (bf16[96,256]{1,0:T(8,128)(2,1)S(1)}, bf16[96,256]{1,0:T(8,128)(2,1)S(1)}, u32[]{:S(2)}, u32[]{:S(2)}) collective-permute-start(bf16[96,256]{1,0:T(8,128)(2,1)S(1)} %constant_dynamic-update-slice_fusion.6), channel_id=1, source_target_pairs={{0,128},{16,144},{32,160},{48,176},{64,192},{80,208},{96,224},{112... | collective-permute-start | bytes 147464 | tf_op jit(solution)/shard_map/ppermute | solution.py:70
  13.9 5.6 %collective-permute-start = (bf16[104,256]{1,0:T(8,128)(2,1)S(1)}, bf16[104,256]{1,0:T(8,128)(2,1)S(1)}, u32[]{:S(2)}, u32[]{:S(2)}) collective-permute-start(bf16[104,256]{1,0:T(8,128)(2,1)S(1)} %constant_dynamic-update-slice_fusion), channel_id=1, source_target_pairs={{0,8},{1,9},{2,10},{3,11},{4,12},{5,13},{6,14},{7,15},{8,0},{9,1},... | collective-permute-start | bytes 159752 | tf_op jit(solution)/shard_map/ppermute | solution.py:70
  17.1 7.1 %collective-permute-start.5 = (bf16[96,512]{1,0:T(8,128)(2,1)S(1)}, bf16[96,512]{1,0:T(8,128)(2,1)S(1)}, u32[]{:S(2)}, u32[]{:S(2)}) collective-permute-start(bf16[96,512]{1,0:T(8,128)(2,1)S(1)} %maximum_select_fusion.7), channel_id=1, source_target_pairs={{0,64},{16,80},{32,96},{48,112},{64,0},{80,16},{96,32},{112,48},{1... | collective-permute-start | bytes 294920 | tf_op jit(solution)/shard_map/ppermute | solution.py:70
  19.5 6.3 %collective-permute-start.1 = (bf16[104,512]{1,0:T(8,128)(2,1)S(1)}, bf16[104,512]{1,0:T(8,128)(2,1)S(1)}, u32[]{:S(2)}, u32[]{:S(2)}) collective-permute-start(bf16[104,512]{1,0:T(8,128)(2,1)S(1)} %maximum_select_fusion.6), channel_id=1, source_target_pairs={{0,4},{1,5},{2,6},{3,7},{4,0},{5,1},{6,2},{7,3},{8,12},{9,13},{10,... | collective-permute-start | bytes 319496 | tf_op jit(solution)/shard_map/ppermute | solution.py:70
  24.2 6.4 %collective-permute-start.6 = (bf16[96,1024]{1,0:T(8,128)(2,1)S(1)}, bf16[96,1024]{1,0:T(8,128)(2,1)S(1)}, u32[]{:S(2)}, u32[]{:S(2)}) collective-permute-start(bf16[96,1024]{1,0:T(8,128)(2,1)S(1)} %maximum_select_fusion.5), channel_id=1, source_target_pairs={{0,32},{16,48},{32,0},{48,16},{64,96},{80,112},{96,64},{112,80},{1... | collective-permute-start | bytes 589832 | tf_op jit(solution)/shard_map/ppermute | solution.py:70
  25.9 8.6 %collective-permute-start.2 = (bf16[104,1024]{1,0:T(8,128)(2,1)S(1)}, bf16[104,1024]{1,0:T(8,128)(2,1)S(1)}, u32[]{:S(2)}, u32[]{:S(2)}) collective-permute-start(bf16[104,1024]{1,0:T(8,128)(2,1)S(1)} %maximum_select_fusion.4), channel_id=1, source_target_pairs={{0,2},{1,3},{2,0},{3,1},{4,6},{5,7},{6,4},{7,5},{8,10},{9,11},{10,... | collective-permute-start | bytes 638984 | tf_op jit(solution)/shard_map/ppermute | solution.py:70
  30.7 9.7 %collective-permute-start.7 = (bf16[96,2048]{1,0:T(8,128)(2,1)S(1)}, bf16[96,2048]{1,0:T(8,128)(2,1)S(1)}, u32[]{:S(2)}, u32[]{:S(2)}) collective-permute-start(bf16[96,2048]{1,0:T(8,128)(2,1)S(1)} %maximum_select_fusion.3), channel_id=1, source_target_pairs={{0,16},{16,0},{32,48},{48,32},{64,80},{80,64},{96,112},{112,96},{1... | collective-permute-start | bytes 1179656 | tf_op jit(solution)/shard_map/ppermute | solution.py:70
  34.6 6.2 %collective-permute-start.3 = (bf16[104,2048]{1,0:T(8,128)(2,1)S(1)}, bf16[104,2048]{1,0:T(8,128)(2,1)S(1)}, u32[]{:S(2)}, u32[]{:S(2)}) collective-permute-start(bf16[104,2048]{1,0:T(8,128)(2,1)S(1)} %maximum_select_fusion.2), channel_id=1, source_target_pairs={{0,1},{1,0},{2,3},{3,2},{4,5},{5,4},{6,7},{7,6},{8,9},{9,8},{10,11... | collective-permute-start | bytes 1277960 | tf_op jit(solution)/shard_map/ppermute | solution.py:70
  101.8 2.1 %collective-permute-start.8 = (f32[16,4098]{1,0:T(8,128)S(1)}, f32[16,4098]{1,0:T(8,128)S(1)}, u32[]{:S(2)}, u32[]{:S(2)}) collective-permute-start(f32[16,4098]{1,0:T(8,128)S(1)} %maximum_maximum_fusion), channel_id=1, source_target_pairs={{0,1},{1,0},{2,3},{3,2},{4,5},{5,4},{6,7},{7,6},{8,9},{9,8},{10,11... | collective-permute-start | bytes 786824 | tf_op jit(solution)/shard_map/ppermute | solution.py:83
  102.0 3.6 %collective-permute-start.9 = (f32[32]{0:T(128)S(1)}, f32[32]{0:T(128)S(1)}, u32[]{:S(2)}, u32[]{:S(2)}) collective-permute-start(f32[32]{0:T(128)S(1)} %pad_maximum_fusion.3), channel_id=1, source_target_pairs={{0,16},{16,0},{32,48},{48,32},{64,80},{80,64},{96,112},{112,96},{1... | collective-permute-start | bytes 392 | tf_op jit(solution)/shard_map/ppermute | solution.py:90
  102.7 3.0 %collective-permute-start.10 = (f32[32]{0:T(128)S(1)}, f32[32]{0:T(128)S(1)}, u32[]{:S(2)}, u32[]{:S(2)}) collective-permute-start(f32[32]{0:T(128)S(1)} %pad_maximum_fusion.3), channel_id=1, source_target_pairs={{0,17},{1,16},{2,19},{3,18},{4,21},{5,20},{6,23},{7,22},{8,25},{9,... | collective-permute-start | bytes 392 | tf_op jit(solution)/shard_map/ppermute | solution.py:91
  105.9 8.7 %collective-permute-start.11 = (f32[16,4098]{1,0:T(8,128)S(1)}, f32[16,4098]{1,0:T(8,128)S(1)}, u32[]{:S(2)}, u32[]{:S(2)}) collective-permute-start(f32[16,4098]{1,0:T(8,128)S(1)} %pad_maximum_fusion), channel_id=1, source_target_pairs={{0,2},{1,3},{2,0},{3,1},{4,6},{5,7},{6,4},{7,5},{8,10},{9,11},{10,... | collective-permute-start | bytes 786824 | tf_op jit(solution)/shard_map/ppermute | solution.py:83
  107.1 7.6 %collective-permute-start.12 = (f32[32]{0:T(128)S(1)}, f32[32]{0:T(128)S(1)}, u32[]{:S(2)}, u32[]{:S(2)}) collective-permute-start(f32[32]{0:T(128)S(1)} %add_add_fusion.4), channel_id=1, source_target_pairs={{0,32},{16,48},{32,0},{48,16},{64,96},{80,112},{96,64},{112,80},{1... | collective-permute-start | bytes 392 | tf_op jit(solution)/shard_map/ppermute | solution.py:90
  107.8 7.0 %collective-permute-start.13 = (f32[32]{0:T(128)S(1)}, f32[32]{0:T(128)S(1)}, u32[]{:S(2)}, u32[]{:S(2)}) collective-permute-start(f32[32]{0:T(128)S(1)} %add_add_fusion.4), channel_id=1, source_target_pairs={{0,34},{1,35},{2,32},{3,33},{4,38},{5,39},{6,36},{7,37},{8,42},{9,... | collective-permute-start | bytes 392 | tf_op jit(solution)/shard_map/ppermute | solution.py:91
  114.9 13.1 %collective-permute-start.14 = (f32[16,4098]{1,0:T(8,128)S(1)}, f32[16,4098]{1,0:T(8,128)S(1)}, u32[]{:S(2)}, u32[]{:S(2)}) collective-permute-start(f32[16,4098]{1,0:T(8,128)S(1)} %pad_maximum_fusion.1), channel_id=1, source_target_pairs={{0,4},{1,5},{2,6},{3,7},{4,0},{5,1},{6,2},{7,3},{8,12},{9,13},{10,... | collective-permute-start | bytes 786824 | tf_op jit(solution)/shard_map/ppermute | solution.py:83
  124.2 4.5 %collective-permute-start.15 = (f32[32]{0:T(128)S(1)}, f32[32]{0:T(128)S(1)}, u32[]{:S(2)}, u32[]{:S(2)}) collective-permute-start(f32[32]{0:T(128)S(1)} %add_add_fusion.3), channel_id=1, source_target_pairs={{0,64},{16,80},{32,96},{48,112},{64,0},{80,16},{96,32},{112,48},{1... | collective-permute-start | bytes 392 | tf_op jit(solution)/shard_map/ppermute | solution.py:90
  125.3 6.9 %collective-permute-start.16 = (f32[32]{0:T(128)S(1)}, f32[32]{0:T(128)S(1)}, u32[]{:S(2)}, u32[]{:S(2)}) collective-permute-start(f32[32]{0:T(128)S(1)} %add_add_fusion.3), channel_id=1, source_target_pairs={{0,68},{1,69},{2,70},{3,71},{4,64},{5,65},{6,66},{7,67},{8,76},{9,... | collective-permute-start | bytes 392 | tf_op jit(solution)/shard_map/ppermute | solution.py:91
  132.3 16.1 %collective-permute-start.17 = (f32[16,4098]{1,0:T(8,128)S(1)}, f32[16,4098]{1,0:T(8,128)S(1)}, u32[]{:S(2)}, u32[]{:S(2)}) collective-permute-start(f32[16,4098]{1,0:T(8,128)S(1)} %pad_maximum_fusion.2), channel_id=1, source_target_pairs={{0,8},{1,9},{2,10},{3,11},{4,12},{5,13},{6,14},{7,15},{8,0},{9,1},... | collective-permute-start | bytes 786824 | tf_op jit(solution)/shard_map/ppermute | solution.py:83
  140.3 8.2 %collective-permute-start.18 = (f32[32]{0:T(128)S(1)}, f32[32]{0:T(128)S(1)}, u32[]{:S(2)}, u32[]{:S(2)}) collective-permute-start(f32[32]{0:T(128)S(1)} %add_add_fusion.2), channel_id=1, source_target_pairs={{0,128},{16,144},{32,160},{48,176},{64,192},{80,208},{96,224},{112... | collective-permute-start | bytes 392 | tf_op jit(solution)/shard_map/ppermute | solution.py:90
  143.7 9.9 %collective-permute-start.19 = (f32[32]{0:T(128)S(1)}, f32[32]{0:T(128)S(1)}, u32[]{:S(2)}, u32[]{:S(2)}) collective-permute-start(f32[32]{0:T(128)S(1)} %add_add_fusion.2), channel_id=1, source_target_pairs={{0,136},{1,137},{2,138},{3,139},{4,140},{5,141},{6,142},{7,143},{8... | collective-permute-start | bytes 392 | tf_op jit(solution)/shard_map/ppermute | solution.py:91
  148.5 8.9 %copy-start = (bf16[1024,2048]{1,0:T(8,128)(2,1)S(1)}, bf16[1024,2048]{1,0:T(8,128)(2,1)}, u32[]{:S(2)}) copy-start(bf16[1024,2048]{1,0:T(8,128)(2,1)} %multiply_convert_fusion.1) | copy-start | bytes 12582916
  153.9 26.6 %copy-start.1 = (f32[16,256]{1,0:T(8,128)S(1)}, f32[16,256]{1,0:T(8,128)}, u32[]{:S(2)}) copy-start(f32[16,256]{1,0:T(8,128)} %param.19) | copy-start | bytes 49156
  153.9 26.6 %copy-start.2 = (f32[16,256]{1,0:T(8,128)S(1)}, f32[16,256]{1,0:T(8,128)}, u32[]{:S(2)}) copy-start(f32[16,256]{1,0:T(8,128)} %param.18) | copy-start | bytes 49156
  153.9 26.6 %copy-start.3 = (f32[16,256]{1,0:T(8,128)S(1)}, f32[16,256]{1,0:T(8,128)}, u32[]{:S(2)}) copy-start(f32[16,256]{1,0:T(8,128)} %param.17) | copy-start | bytes 49156
  154.0 27.3 %copy-start.4 = (f32[64]{0:T(128)S(1)}, f32[64]{0:T(128)}, u32[]{:S(2)}) copy-start(f32[64]{0:T(128)} %param.16) | copy-start | bytes 772
  158.6 4.0 %collective-permute-start.20 = (f32[16,512]{1,0:T(8,128)S(1)}, f32[16,512]{1,0:T(8,128)S(1)}, u32[]{:S(2)}, u32[]{:S(2)}) collective-permute-start(f32[16,512]{1,0:T(8,128)S(1)} %slice_select_fusion), channel_id=1, source_target_pairs={{0,1},{1,0},{2,3},{3,2},{4,5},{5,4},{6,7},{7,6},{8,9},{9,8},{10,11... | collective-permute-start | bytes 98312 | tf_op jit(solution)/shard_map/ppermute | solution.py:108
  158.9 3.7 %collective-permute-start.21 = (f32[16]{0:T(128)S(1)}, f32[16]{0:T(128)S(1)}, u32[]{:S(2)}, u32[]{:S(2)}) collective-permute-start(f32[16]{0:T(128)S(1)} %get-tuple-element.56), channel_id=1, source_target_pairs={{0,16},{16,0},{32,48},{48,32},{64,80},{80,64},{96,112},{112,96},{1... | collective-permute-start | bytes 200 | tf_op jit(solution)/shard_map/ppermute | solution.py:109
  162.6 5.1 %collective-permute-start.22 = (f32[16,256]{1,0:T(8,128)S(1)}, f32[16,256]{1,0:T(8,128)S(1)}, u32[]{:S(2)}, u32[]{:S(2)}) collective-permute-start(f32[16,256]{1,0:T(8,128)S(1)} %slice_select_fusion.1), channel_id=1, source_target_pairs={{0,2},{1,3},{2,0},{3,1},{4,6},{5,7},{6,4},{7,5},{8,10},{9,11},{10,... | collective-permute-start | bytes 49160 | tf_op jit(solution)/shard_map/ppermute | solution.py:108
  164.2 3.6 %collective-permute-start.23 = (f32[16]{0:T(128)S(1)}, f32[16]{0:T(128)S(1)}, u32[]{:S(2)}, u32[]{:S(2)}) collective-permute-start(f32[16]{0:T(128)S(1)} %add.235), channel_id=1, source_target_pairs={{0,32},{16,48},{32,0},{48,16},{64,96},{80,112},{96,64},{112,80},{1... | collective-permute-start | bytes 200 | tf_op jit(solution)/shard_map/ppermute | solution.py:109
  167.7 5.2 %collective-permute-start.24 = (f32[16,128]{1,0:T(8,128)S(1)}, f32[16,128]{1,0:T(8,128)S(1)}, u32[]{:S(2)}, u32[]{:S(2)}) collective-permute-start(f32[16,128]{1,0:T(8,128)S(1)} %slice_select_fusion.3), channel_id=1, source_target_pairs={{0,4},{1,5},{2,6},{3,7},{4,0},{5,1},{6,2},{7,3},{8,12},{9,13},{10,... | collective-permute-start | bytes 24584 | tf_op jit(solution)/shard_map/ppermute | solution.py:108
  168.0 4.5 %collective-permute-start.25 = (f32[16]{0:T(128)S(1)}, f32[16]{0:T(128)S(1)}, u32[]{:S(2)}, u32[]{:S(2)}) collective-permute-start(f32[16]{0:T(128)S(1)} %add.237), channel_id=1, source_target_pairs={{0,64},{16,80},{32,96},{48,112},{64,0},{80,16},{96,32},{112,48},{1... | collective-permute-start | bytes 200 | tf_op jit(solution)/shard_map/ppermute | solution.py:109
  173.1 7.5 %collective-permute-start.26 = (f32[16]{0:T(128)S(1)}, f32[16]{0:T(128)S(1)}, u32[]{:S(2)}, u32[]{:S(2)}) collective-permute-start(f32[16]{0:T(128)S(1)} %add.239), channel_id=1, source_target_pairs={{0,128},{16,144},{32,160},{48,176},{64,192},{80,208},{96,224},{112... | collective-permute-start | bytes 200 | tf_op jit(solution)/shard_map/ppermute | solution.py:109
  175.6 5.7 %collective-permute-start.27 = (f32[16,64]{1,0:T(8,128)S(1)}, f32[16,64]{1,0:T(8,128)S(1)}, u32[]{:S(2)}, u32[]{:S(2)}) collective-permute-start(f32[16,64]{1,0:T(8,128)S(1)} %slice_select_fusion.2), channel_id=1, source_target_pairs={{0,8},{1,9},{2,10},{3,11},{4,12},{5,13},{6,14},{7,15},{8,0},{9,1},... | collective-permute-start | bytes 12296 | tf_op jit(solution)/shard_map/ppermute | solution.py:108

commit v10 on v9

--- a/solution.py
+++ b/solution.py
@@ -179,8 +179,9 @@
         row_pts * jnp.asarray(-2.0, jnp.bfloat16), row_sq, col_pts, col_sq, col_dir, signal_scalar, 256
     )
     cand_blocks = []
-    width = col_pts.shape[1] // 2
-    for k in range(2):
+    pieces = 4
+    width = col_pts.shape[1] // pieces
+    for k in range(pieces):
         lo, hi = k * width, (k + 1) * width
         cand_blocks.append(
             lax.optimization_barrier(
@@ -215,7 +216,7 @@
 
     w_low_col = (w_col + step_len[:, None] * d_col).astype(jnp.bfloat16)
     partial_fit = None
-    for k in range(2):
+    for k in range(pieces):
         lo, hi = k * width, (k + 1) * width
         part = lax.dot_general(
             w_low_col[:, lo:hi], cand_blocks[k], contract_last,

time: 185 us -> 184 us (level)
  starting transfers between devices: 47.9 us -> 45.9 us
    ppermute x4, waiting for transfers between devices: 4.37 us -> 0.93 us  [col_sum_with_grid(): got = lax.ppermute(packed, 'col', xor_perm(n_col, bit))]
    ppermute x4, starting transfers between devices: 6.68 us -> 3.63 us  [tail_sums(): x = x + lax.ppermute(x, axis_ar, xor_perm(size_ar, bit))]
    ppermute x4, starting transfers between devices: 11.1 us -> 8.65 us  [col_sum_with_grid(): from_diag = lax.ppermute(sums, ('row', 'col'), diag)]
    ppermute x4, waiting for transfers between devices: 9.77 us -> 12.1 us  [tail_sums(): x = x + lax.ppermute(x, axis_ar, xor_perm(size_ar, bit))]
    dot_general x2 -> x4, matrix products: 14.3 us -> 16.2 us  [matern_block(): lax.dot_general(row_pts_m2, col_pts, contract_first, preferred_element_ty...]
    dot_general x2 -> x4, matrix products: 4.59 us -> 4.34 us  [per_device(): lax.dot_general(w_low_col[:, lo:hi], cand_blocks[k], contract_last, prefe...]
  transfers between devices with their start and end apart: 28 -> 28, of which waited for: 16 -> 15; matrix products, arithmetic and copies ran while one was open for 11% -> 11% of each run, Pallas kernels for 0% -> 0%
where the time goes in v10:
time: 184 us; the launch traced here: 181 us
  matrix products  80.1 us (44%)
  starting transfers between devices  45.9 us (25%)
  waiting for transfers between devices  40.9 us (22%)
  other arithmetic  9.53 us (5%)
  between operations  2.43 us (1%)
  local copies, waits for them, and re-layouts  1.85 us (1%)
    dot_general x16, matrix products, one_block(): lax.dot_general(kern_vals, vec_blk, contract_last, preferred_element_type...  59.6 us
    dot_general x4, matrix products, matern_block(): lax.dot_general(row_pts_m2, col_pts, contract_first, preferred_element_ty...  16.2 us
    ppermute x8, waiting for transfers between devices, gather_last(): recv = lax.ppermute(buf, axis_name, xor_perm(size, bit))  15.9 us
    ppermute x8, starting transfers between devices, gather_last(): recv = lax.ppermute(buf, axis_name, xor_perm(size, bit))  15.7 us
    ppermute x4, waiting for transfers between devices, tail_sums(): x = x + lax.ppermute(x, axis_ar, xor_perm(size_ar, bit))  12.1 us
    ppermute x4, waiting for transfers between devices, col_sum_with_grid(): from_diag = lax.ppermute(sums, ('row', 'col'), diag)  10.4 us
    ppermute x4, starting transfers between devices, col_sum_with_grid(): from_diag = lax.ppermute(sums, ('row', 'col'), diag)  8.65 us
    ppermute x4, starting transfers between devices, col_sum_with_grid(): from_row = lax.ppermute(sums, 'row', xor_perm(n_row, bit))  7.34 us
  transfers between devices with their start and end apart: 28, of which 15 were waited for; matrix products, arithmetic and copies ran while one was open for 11% of the time, Pallas kernels for 0%

profile of v10, /device:TPU:2, one launch (start us, length us, event | category | flops | bytes accessed | tf_op | source)
XLA Modules:
  0.0 181.2 jit_solution(670074332757901622)
XLA Ops:
  0.7 0.8 constant_dynamic-update-slice_fusion.10
  1.5 0.8 divide_convert_fusion.1
  2.4 0.7 constant_dynamic-update-slice_fusion.9
  3.1 0.7 constant_dynamic-update-slice_fusion.8
  3.8 0.7 constant_dynamic-update-slice_fusion.7
  4.6 0.7 constant_dynamic-update-slice_fusion.6
  5.3 7.2 %collective-permute-start.4 = (bf16[96,256]{1,0:T(8,128)(2,1)S(1)}, bf16[96,256]{1,0:T(8,128)(2,1)S(1)}, u32[]{:S(2)}, u32[]{:S(2)}) collective-permute-start(bf16[96,256]{1,0:T(8,128)(2,1)S(1)} %constant_dynamic-update-slice_fusion.6), channel_id=1, source_target_pairs={{0,128},{16,144},{32,160},{48,176},{64,192},{80,208},{96,224},{112... | collective-permute-start | bytes 147464 | tf_op jit(solution)/shard_map/ppermute | solution.py:70
  12.5 0.7 constant_dynamic-update-slice_fusion.1
  13.2 0.7 constant_dynamic-update-slice_fusion
  13.9 3.2 %collective-permute-start = (bf16[104,256]{1,0:T(8,128)(2,1)S(1)}, bf16[104,256]{1,0:T(8,128)(2,1)S(1)}, u32[]{:S(2)}, u32[]{:S(2)}) collective-permute-start(bf16[104,256]{1,0:T(8,128)(2,1)S(1)} %constant_dynamic-update-slice_fusion), channel_id=1, source_target_pairs={{0,8},{1,9},{2,10},{3,11},{4,12},{5,13},{6,14},{7,15},{8,0},{9,1},... | collective-permute-start | bytes 159752 | tf_op jit(solution)/shard_map/ppermute | solution.py:70
  17.1 1.6 collective-permute-start.5
  18.7 0.9 collective-permute-done
  19.6 2.2 %collective-permute-start.1 = (bf16[104,512]{1,0:T(8,128)(2,1)S(1)}, bf16[104,512]{1,0:T(8,128)(2,1)S(1)}, u32[]{:S(2)}, u32[]{:S(2)}) collective-permute-start(bf16[104,512]{1,0:T(8,128)(2,1)S(1)} %maximum_select_fusion.6), channel_id=1, source_target_pairs={{0,4},{1,5},{2,6},{3,7},{4,0},{5,1},{6,2},{7,3},{8,12},{9,13},{10,... | collective-permute-start | bytes 319496 | tf_op jit(solution)/shard_map/ppermute | solution.py:70
  21.8 2.4 %collective-permute-done.5 = bf16[96,512]{1,0:T(8,128)(2,1)S(1)} collective-permute-done((bf16[96,512]{1,0:T(8,128)(2,1)S(1)}, bf16[96,512]{1,0:T(8,128)(2,1)S(1)}, u32[]{:S(2)}, u32[]{:S(2)}) %collective-permute-start.5) | collective-permute-done | bytes 98336 | tf_op jit(solution)/shard_map/ppermute | solution.py:70
  24.4 1.5 collective-permute-done.1
  26.6 4.1 %collective-permute-done.6 = bf16[96,1024]{1,0:T(8,128)(2,1)S(1)} collective-permute-done((bf16[96,1024]{1,0:T(8,128)(2,1)S(1)}, bf16[96,1024]{1,0:T(8,128)(2,1)S(1)}, u32[]{:S(2)}, u32[]{:S(2)}) %collective-permute-start.6) | collective-permute-done | bytes 196640 | tf_op jit(solution)/shard_map/ppermute | solution.py:70
  30.7 0.8 collective-permute-start.7
  33.3 7.1 %collective-permute-done.7 = bf16[96,2048]{1,0:T(8,128)(2,1)S(1)} collective-permute-done((bf16[96,2048]{1,0:T(8,128)(2,1)S(1)}, bf16[96,2048]{1,0:T(8,128)(2,1)S(1)}, u32[]{:S(2)}, u32[]{:S(2)}) %collective-permute-start.7) | collective-permute-done | bytes 393248 | tf_op jit(solution)/shard_map/ppermute | solution.py:70
  41.2 60.3 %while.11 = (s32[]{:T(128)}, f32[4096,16]{0,1:T(8,128)S(1)}, f32[]{:T(128)}, f32[4096]{0:T(1024)S(1)}, f32[16,256]{1,0:T(8,128)S(1)}, /*index=5*/bf16[16,32,256]...) while((s32[]{:T(128)}, f32[4096,16]{0,1:T(8,128)S(1)}, ...), condition=%wide.region_4.5_spmd.clone, body=%wide.region_3.4_spmd.clone.sunk | while | flops 112328704 | bytes 832126 | solution.py:51
  41.3 3.7 %convolution_add_fusion.5 = f32[4096,16]{0,1:T(8,128)S(1)} fusion(bf16[32,4096]{1,0:T(8,128)(2,1)S(1)} %get-tuple-element.197, f32[256]{0:T(256)S(1)} %bitcast.78, f32[4096]{0:T(1024)S(1)} %get-tuple-element.194, f32[]{:T(128)} %get-tuple-element.193, f32[4096,16]{0,1:T(8,128)S(1)} %get-tuple-element.182, pred[]{:T(512)S(6)} %compare.3, ...), kind=kOutput, calls=%fused_computation.3.clone.1 | convolution fusion | flops 112328704 | bytes 829956 | tf_op jit(solution)/shard_map/while/body/eval_jaxpr/dot_general | solution.py:44
  45.0 3.7 %convolution_add_fusion.5 = f32[4096,16]{0,1:T(8,128)S(1)} fusion(bf16[32,4096]{1,0:T(8,128)(2,1)S(1)} %get-tuple-element.197, f32[256]{0:T(256)S(1)} %bitcast.78, f32[4096]{0:T(1024)S(1)} %get-tuple-element.194, f32[]{:T(128)} %get-tuple-element.193, f32[4096,16]{0,1:T(8,128)S(1)} %get-tuple-element.182, pred[]{:T(512)S(6)} %compare.3, ...), kind=kOutput, calls=%fused_computation.3.clone.1 | convolution fusion | flops 112328704 | bytes 829956 | tf_op jit(solution)/shard_map/while/body/eval_jaxpr/dot_general | solution.py:44
  48.8 3.7 %convolution_add_fusion.5 = f32[4096,16]{0,1:T(8,128)S(1)} fusion(bf16[32,4096]{1,0:T(8,128)(2,1)S(1)} %get-tuple-element.197, f32[256]{0:T(256)S(1)} %bitcast.78, f32[4096]{0:T(1024)S(1)} %get-tuple-element.194, f32[]{:T(128)} %get-tuple-element.193, f32[4096,16]{0,1:T(8,128)S(1)} %get-tuple-element.182, pred[]{:T(512)S(6)} %compare.3, ...), kind=kOutput, calls=%fused_computation.3.clone.1 | convolution fusion | flops 112328704 | bytes 829956 | tf_op jit(solution)/shard_map/while/body/eval_jaxpr/dot_general | solution.py:44
  52.6 3.7 %convolution_add_fusion.5 = f32[4096,16]{0,1:T(8,128)S(1)} fusion(bf16[32,4096]{1,0:T(8,128)(2,1)S(1)} %get-tuple-element.197, f32[256]{0:T(256)S(1)} %bitcast.78, f32[4096]{0:T(1024)S(1)} %get-tuple-element.194, f32[]{:T(128)} %get-tuple-element.193, f32[4096,16]{0,1:T(8,128)S(1)} %get-tuple-element.182, pred[]{:T(512)S(6)} %compare.3, ...), kind=kOutput, calls=%fused_computation.3.clone.1 | convolution fusion | flops 112328704 | bytes 829956 | tf_op jit(solution)/shard_map/while/body/eval_jaxpr/dot_general | solution.py:44
  56.3 3.7 %convolution_add_fusion.5 = f32[4096,16]{0,1:T(8,128)S(1)} fusion(bf16[32,4096]{1,0:T(8,128)(2,1)S(1)} %get-tuple-element.197, f32[256]{0:T(256)S(1)} %bitcast.78, f32[4096]{0:T(1024)S(1)} %get-tuple-element.194, f32[]{:T(128)} %get-tuple-element.193, f32[4096,16]{0,1:T(8,128)S(1)} %get-tuple-element.182, pred[]{:T(512)S(6)} %compare.3, ...), kind=kOutput, calls=%fused_computation.3.clone.1 | convolution fusion | flops 112328704 | bytes 829956 | tf_op jit(solution)/shard_map/while/body/eval_jaxpr/dot_general | solution.py:44
  60.1 3.7 %convolution_add_fusion.5 = f32[4096,16]{0,1:T(8,128)S(1)} fusion(bf16[32,4096]{1,0:T(8,128)(2,1)S(1)} %get-tuple-element.197, f32[256]{0:T(256)S(1)} %bitcast.78, f32[4096]{0:T(1024)S(1)} %get-tuple-element.194, f32[]{:T(128)} %get-tuple-element.193, f32[4096,16]{0,1:T(8,128)S(1)} %get-tuple-element.182, pred[]{:T(512)S(6)} %compare.3, ...), kind=kOutput, calls=%fused_computation.3.clone.1 | convolution fusion | flops 112328704 | bytes 829956 | tf_op jit(solution)/shard_map/while/body/eval_jaxpr/dot_general | solution.py:44
  63.9 3.7 %convolution_add_fusion.5 = f32[4096,16]{0,1:T(8,128)S(1)} fusion(bf16[32,4096]{1,0:T(8,128)(2,1)S(1)} %get-tuple-element.197, f32[256]{0:T(256)S(1)} %bitcast.78, f32[4096]{0:T(1024)S(1)} %get-tuple-element.194, f32[]{:T(128)} %get-tuple-element.193, f32[4096,16]{0,1:T(8,128)S(1)} %get-tuple-element.182, pred[]{:T(512)S(6)} %compare.3, ...), kind=kOutput, calls=%fused_computation.3.clone.1 | convolution fusion | flops 112328704 | bytes 829956 | tf_op jit(solution)/shard_map/while/body/eval_jaxpr/dot_general | solution.py:44
  67.6 3.7 %convolution_add_fusion.5 = f32[4096,16]{0,1:T(8,128)S(1)} fusion(bf16[32,4096]{1,0:T(8,128)(2,1)S(1)} %get-tuple-element.197, f32[256]{0:T(256)S(1)} %bitcast.78, f32[4096]{0:T(1024)S(1)} %get-tuple-element.194, f32[]{:T(128)} %get-tuple-element.193, f32[4096,16]{0,1:T(8,128)S(1)} %get-tuple-element.182, pred[]{:T(512)S(6)} %compare.3, ...), kind=kOutput, calls=%fused_computation.3.clone.1 | convolution fusion | flops 112328704 | bytes 829956 | tf_op jit(solution)/shard_map/while/body/eval_jaxpr/dot_general | solution.py:44
  71.4 3.7 %convolution_add_fusion.5 = f32[4096,16]{0,1:T(8,128)S(1)} fusion(bf16[32,4096]{1,0:T(8,128)(2,1)S(1)} %get-tuple-element.197, f32[256]{0:T(256)S(1)} %bitcast.78, f32[4096]{0:T(1024)S(1)} %get-tuple-element.194, f32[]{:T(128)} %get-tuple-element.193, f32[4096,16]{0,1:T(8,128)S(1)} %get-tuple-element.182, pred[]{:T(512)S(6)} %compare.3, ...), kind=kOutput, calls=%fused_computation.3.clone.1 | convolution fusion | flops 112328704 | bytes 829956 | tf_op jit(solution)/shard_map/while/body/eval_jaxpr/dot_general | solution.py:44
  75.2 3.7 %convolution_add_fusion.5 = f32[4096,16]{0,1:T(8,128)S(1)} fusion(bf16[32,4096]{1,0:T(8,128)(2,1)S(1)} %get-tuple-element.197, f32[256]{0:T(256)S(1)} %bitcast.78, f32[4096]{0:T(1024)S(1)} %get-tuple-element.194, f32[]{:T(128)} %get-tuple-element.193, f32[4096,16]{0,1:T(8,128)S(1)} %get-tuple-element.182, pred[]{:T(512)S(6)} %compare.3, ...), kind=kOutput, calls=%fused_computation.3.clone.1 | convolution fusion | flops 112328704 | bytes 829956 | tf_op jit(solution)/shard_map/while/body/eval_jaxpr/dot_general | solution.py:44
  78.9 3.7 %convolution_add_fusion.5 = f32[4096,16]{0,1:T(8,128)S(1)} fusion(bf16[32,4096]{1,0:T(8,128)(2,1)S(1)} %get-tuple-element.197, f32[256]{0:T(256)S(1)} %bitcast.78, f32[4096]{0:T(1024)S(1)} %get-tuple-element.194, f32[]{:T(128)} %get-tuple-element.193, f32[4096,16]{0,1:T(8,128)S(1)} %get-tuple-element.182, pred[]{:T(512)S(6)} %compare.3, ...), kind=kOutput, calls=%fused_computation.3.clone.1 | convolution fusion | flops 112328704 | bytes 829956 | tf_op jit(solution)/shard_map/while/body/eval_jaxpr/dot_general | solution.py:44
  82.7 3.7 %convolution_add_fusion.5 = f32[4096,16]{0,1:T(8,128)S(1)} fusion(bf16[32,4096]{1,0:T(8,128)(2,1)S(1)} %get-tuple-element.197, f32[256]{0:T(256)S(1)} %bitcast.78, f32[4096]{0:T(1024)S(1)} %get-tuple-element.194, f32[]{:T(128)} %get-tuple-element.193, f32[4096,16]{0,1:T(8,128)S(1)} %get-tuple-element.182, pred[]{:T(512)S(6)} %compare.3, ...), kind=kOutput, calls=%fused_computation.3.clone.1 | convolution fusion | flops 112328704 | bytes 829956 | tf_op jit(solution)/shard_map/while/body/eval_jaxpr/dot_general | solution.py:44
  86.5 3.7 %convolution_add_fusion.5 = f32[4096,16]{0,1:T(8,128)S(1)} fusion(bf16[32,4096]{1,0:T(8,128)(2,1)S(1)} %get-tuple-element.197, f32[256]{0:T(256)S(1)} %bitcast.78, f32[4096]{0:T(1024)S(1)} %get-tuple-element.194, f32[]{:T(128)} %get-tuple-element.193, f32[4096,16]{0,1:T(8,128)S(1)} %get-tuple-element.182, pred[]{:T(512)S(6)} %compare.3, ...), kind=kOutput, calls=%fused_computation.3.clone.1 | convolution fusion | flops 112328704 | bytes 829956 | tf_op jit(solution)/shard_map/while/body/eval_jaxpr/dot_general | solution.py:44
  90.2 3.7 %convolution_add_fusion.5 = f32[4096,16]{0,1:T(8,128)S(1)} fusion(bf16[32,4096]{1,0:T(8,128)(2,1)S(1)} %get-tuple-element.197, f32[256]{0:T(256)S(1)} %bitcast.78, f32[4096]{0:T(1024)S(1)} %get-tuple-element.194, f32[]{:T(128)} %get-tuple-element.193, f32[4096,16]{0,1:T(8,128)S(1)} %get-tuple-element.182, pred[]{:T(512)S(6)} %compare.3, ...), kind=kOutput, calls=%fused_computation.3.clone.1 | convolution fusion | flops 112328704 | bytes 829956 | tf_op jit(solution)/shard_map/while/body/eval_jaxpr/dot_general | solution.py:44
  94.0 3.7 %convolution_add_fusion.5 = f32[4096,16]{0,1:T(8,128)S(1)} fusion(bf16[32,4096]{1,0:T(8,128)(2,1)S(1)} %get-tuple-element.197, f32[256]{0:T(256)S(1)} %bitcast.78, f32[4096]{0:T(1024)S(1)} %get-tuple-element.194, f32[]{:T(128)} %get-tuple-element.193, f32[4096,16]{0,1:T(8,128)S(1)} %get-tuple-element.182, pred[]{:T(512)S(6)} %compare.3, ...), kind=kOutput, calls=%fused_computation.3.clone.1 | convolution fusion | flops 112328704 | bytes 829956 | tf_op jit(solution)/shard_map/while/body/eval_jaxpr/dot_general | solution.py:44
  97.7 3.7 %convolution_add_fusion.5 = f32[4096,16]{0,1:T(8,128)S(1)} fusion(bf16[32,4096]{1,0:T(8,128)(2,1)S(1)} %get-tuple-element.197, f32[256]{0:T(256)S(1)} %bitcast.78, f32[4096]{0:T(1024)S(1)} %get-tuple-element.194, f32[]{:T(128)} %get-tuple-element.193, f32[4096,16]{0,1:T(8,128)S(1)} %get-tuple-element.182, pred[]{:T(512)S(6)} %compare.3, ...), kind=kOutput, calls=%fused_computation.3.clone.1 | convolution fusion | flops 112328704 | bytes 829956 | tf_op jit(solution)/shard_map/while/body/eval_jaxpr/dot_general | solution.py:44
  101.7 0.7 collective-permute-start.9
  103.1 1.7 collective-permute-start.8
  104.8 4.0 %multiply_convert_fusion.4 = bf16[1024,1024]{1,0:T(8,128)(2,1)} fusion(bf16[32,1024]{1,0:T(8,128)(2,1)S(1)} %mul.199, f32[1024]{0:T(1024)S(1)} %get-tuple-element.116, f32[1024]{0:T(1024)S(1)} %add.265, f32[]{:T(128)} %bitcast.63, bf16[96,4096]{1,0:T(8,128)(2,1)S(1)} %maximum_select_fusion.1), kind=kOutput, calls=%fused_computation.19 | convolution fusion | flops 78643200 | bytes 2236420 | tf_op jit(solution)/shard_map/dot_general | solution.py:19
  109.8 4.0 %multiply_convert_fusion.3 = bf16[1024,1024]{1,0:T(8,128)(2,1)} fusion(bf16[32,1024]{1,0:T(8,128)(2,1)S(1)} %mul.199, f32[1024]{0:T(1024)S(1)} %get-tuple-element.115, f32[1024]{0:T(1024)S(1)} %add.265, f32[]{:T(128)} %bitcast.66, bf16[96,4096]{1,0:T(8,128)(2,1)S(1)} %maximum_select_fusion.1), kind=kOutput, calls=%fused_computation.18 | convolution fusion | flops 78643200 | bytes 2236420 | tf_op jit(solution)/shard_map/dot_general | solution.py:19
  114.4 2.4 %collective-permute-start.13 = (f32[32]{0:T(128)S(1)}, f32[32]{0:T(128)S(1)}, u32[]{:S(2)}, u32[]{:S(2)}) collective-permute-start(f32[32]{0:T(128)S(1)} %add_add_fusion.4), channel_id=1, source_target_pairs={{0,34},{1,35},{2,32},{3,33},{4,38},{5,39},{6,36},{7,37},{8,42},{9,... | collective-permute-start | bytes 392 | tf_op jit(solution)/shard_map/ppermute | solution.py:91
  116.8 0.9 collective-permute-done.11
  117.8 1.1 collective-permute-done.13
  119.0 2.5 %collective-permute-start.14 = (f32[16,4098]{1,0:T(8,128)S(1)}, f32[16,4098]{1,0:T(8,128)S(1)}, u32[]{:S(2)}, u32[]{:S(2)}) collective-permute-start(f32[16,4098]{1,0:T(8,128)S(1)} %pad_maximum_fusion.1), channel_id=1, source_target_pairs={{0,4},{1,5},{2,6},{3,7},{4,0},{5,1},{6,2},{7,3},{8,12},{9,13},{10,... | collective-permute-start | bytes 786824 | tf_op jit(solution)/shard_map/ppermute | solution.py:83
  121.5 4.0 %multiply_convert_fusion.2 = bf16[1024,1024]{1,0:T(8,128)(2,1)} fusion(bf16[32,1024]{1,0:T(8,128)(2,1)S(1)} %mul.199, f32[1024]{0:T(1024)S(1)} %get-tuple-element.114, f32[1024]{0:T(1024)S(1)} %add.265, f32[]{:T(128)} %bitcast.65, bf16[96,4096]{1,0:T(8,128)(2,1)S(1)} %maximum_select_fusion.1), kind=kOutput, calls=%fused_computation.17 | convolution fusion | flops 78643200 | bytes 2236420 | tf_op jit(solution)/shard_map/dot_general | solution.py:19
  125.5 1.9 %collective-permute-start.15 = (f32[32]{0:T(128)S(1)}, f32[32]{0:T(128)S(1)}, u32[]{:S(2)}, u32[]{:S(2)}) collective-permute-start(f32[32]{0:T(128)S(1)} %add_add_fusion.3), channel_id=1, source_target_pairs={{0,64},{16,80},{32,96},{48,112},{64,0},{80,16},{96,32},{112,48},{1... | collective-permute-start | bytes 392 | tf_op jit(solution)/shard_map/ppermute | solution.py:90
  127.5 1.5 collective-permute-start.16
  129.1 0.9 collective-permute-done.15
  130.0 4.3 %collective-permute-done.16 = f32[32]{0:T(128)S(1)} collective-permute-done((f32[32]{0:T(128)S(1)}, f32[32]{0:T(128)S(1)}, u32[]{:S(2)}, u32[]{:S(2)}) %collective-permute-start.16) | collective-permute-done | bytes 160 | tf_op jit(solution)/shard_map/ppermute | solution.py:91
  134.6 4.1 %multiply_convert_fusion.1 = bf16[1024,1024]{1,0:T(8,128)(2,1)} fusion(bf16[32,1024]{1,0:T(8,128)(2,1)S(1)} %mul.199, f32[1024]{0:T(1024)S(1)} %get-tuple-element.113, f32[1024]{0:T(1024)S(1)} %add.265, f32[]{:T(128)} %bitcast.64, bf16[96,4096]{1,0:T(8,128)(2,1)S(1)} %maximum_select_fusion.1), kind=kOutput, calls=%fused_computation.16 | convolution fusion | flops 78643200 | bytes 2236420 | tf_op jit(solution)/shard_map/dot_general | solution.py:19
  138.7 4.2 %collective-permute-start.18 = (f32[32]{0:T(128)S(1)}, f32[32]{0:T(128)S(1)}, u32[]{:S(2)}, u32[]{:S(2)}) collective-permute-start(f32[32]{0:T(128)S(1)} %add_add_fusion.2), channel_id=1, source_target_pairs={{0,128},{16,144},{32,160},{48,176},{64,192},{80,208},{96,224},{112... | collective-permute-start | bytes 392 | tf_op jit(solution)/shard_map/ppermute | solution.py:90
  142.9 4.7 %collective-permute-start.19 = (f32[32]{0:T(128)S(1)}, f32[32]{0:T(128)S(1)}, u32[]{:S(2)}, u32[]{:S(2)}) collective-permute-start(f32[32]{0:T(128)S(1)} %add_add_fusion.2), channel_id=1, source_target_pairs={{0,136},{1,137},{2,138},{3,139},{4,140},{5,141},{6,142},{7,143},{8... | collective-permute-start | bytes 392 | tf_op jit(solution)/shard_map/ppermute | solution.py:91
  147.7 5.0 %collective-permute-done.19 = f32[32]{0:T(128)S(1)} collective-permute-done((f32[32]{0:T(128)S(1)}, f32[32]{0:T(128)S(1)}, u32[]{:S(2)}, u32[]{:S(2)}) %collective-permute-start.19) | collective-permute-done | bytes 160 | tf_op jit(solution)/shard_map/ppermute | solution.py:91
  153.1 2.4 %fusion.22 = f32[16,1024]{1,0:T(8,128)S(1)} fusion(bf16[1024,1024]{1,0:T(8,128)(2,1)} %multiply_convert_fusion.4, bf16[16,4096]{1,0:T(8,128)(2,1)S(1)} %get-tuple-element.121), kind=kOutput, calls=%fused_computation.57 | convolution fusion | flops 33554432 | bytes 2195456 | tf_op jit(solution)/shard_map/dot_general | solution.py:221
  157.8 0.8 collective-permute-start.21
  158.6 2.9 %collective-permute-done.21 = f32[16]{0:T(128)S(1)} collective-permute-done((f32[16]{0:T(128)S(1)}, f32[16]{0:T(128)S(1)}, u32[]{:S(2)}, u32[]{:S(2)}) %collective-permute-start.21) | collective-permute-done | bytes 96 | tf_op jit(solution)/shard_map/ppermute | solution.py:109
  161.5 1.9 %collective-permute-start.22 = (f32[16,256]{1,0:T(8,128)S(1)}, f32[16,256]{1,0:T(8,128)S(1)}, u32[]{:S(2)}, u32[]{:S(2)}) collective-permute-start(f32[16,256]{1,0:T(8,128)S(1)} %slice_select_fusion.1), channel_id=1, source_target_pairs={{0,2},{1,3},{2,0},{3,1},{4,6},{5,7},{6,4},{7,5},{8,10},{9,11},{10,... | collective-permute-start | bytes 49160 | tf_op jit(solution)/shard_map/ppermute | solution.py:108
  163.4 3.6 %collective-permute-done.23 = f32[16]{0:T(128)S(1)} collective-permute-done((f32[16]{0:T(128)S(1)}, f32[16]{0:T(128)S(1)}, u32[]{:S(2)}, u32[]{:S(2)}) %collective-permute-start.23) | collective-permute-done | bytes 96 | tf_op jit(solution)/shard_map/ppermute | solution.py:109
  167.1 1.1 collective-permute-start.25
  168.2 3.5 %collective-permute-done.25 = f32[16]{0:T(128)S(1)} collective-permute-done((f32[16]{0:T(128)S(1)}, f32[16]{0:T(128)S(1)}, u32[]{:S(2)}, u32[]{:S(2)}) %collective-permute-start.25) | collective-permute-done | bytes 96 | tf_op jit(solution)/shard_map/ppermute | solution.py:109
  172.3 1.8 collective-permute-start.26
  174.1 3.5 %collective-permute-start.27 = (f32[16,64]{1,0:T(8,128)S(1)}, f32[16,64]{1,0:T(8,128)S(1)}, u32[]{:S(2)}, u32[]{:S(2)}) collective-permute-start(f32[16,64]{1,0:T(8,128)S(1)} %slice_select_fusion.2), channel_id=1, source_target_pairs={{0,8},{1,9},{2,10},{3,11},{4,12},{5,13},{6,14},{7,15},{8,0},{9,1},... | collective-permute-start | bytes 12296 | tf_op jit(solution)/shard_map/ppermute | solution.py:108
  177.6 2.2 %collective-permute-done.26 = f32[16]{0:T(128)S(1)} collective-permute-done((f32[16]{0:T(128)S(1)}, f32[16]{0:T(128)S(1)}, u32[]{:S(2)}, u32[]{:S(2)}) %collective-permute-start.26) | collective-permute-done | bytes 96 | tf_op jit(solution)/shard_map/ppermute | solution.py:109
  179.8 0.7 multiply_add_fusion
  180.5 0.7 add_add_fusion
  (127 shorter events, 8.9 us)
Async XLA Ops:
  0.6 32.4 %copy-start.3 = (f32[16,256]{1,0:T(8,128)S(1)}, f32[16,256]{1,0:T(8,128)}, u32[]{:S(2)}) copy-start(f32[16,256]{1,0:T(8,128)} %param.19) | copy-start | bytes 49156
  0.6 30.9 %copy-start.4 = (f32[16,256]{1,0:T(8,128)S(1)}, f32[16,256]{1,0:T(8,128)}, u32[]{:S(2)}) copy-start(f32[16,256]{1,0:T(8,128)} %param.18) | copy-start | bytes 49156
  5.3 11.8 %collective-permute-start.4 = (bf16[96,256]{1,0:T(8,128)(2,1)S(1)}, bf16[96,256]{1,0:T(8,128)(2,1)S(1)}, u32[]{:S(2)}, u32[]{:S(2)}) collective-permute-start(bf16[96,256]{1,0:T(8,128)(2,1)S(1)} %constant_dynamic-update-slice_fusion.6), channel_id=1, source_target_pairs={{0,128},{16,144},{32,160},{48,176},{64,192},{80,208},{96,224},{112... | collective-permute-start | bytes 147464 | tf_op jit(solution)/shard_map/ppermute | solution.py:70
  13.9 5.6 %collective-permute-start = (bf16[104,256]{1,0:T(8,128)(2,1)S(1)}, bf16[104,256]{1,0:T(8,128)(2,1)S(1)}, u32[]{:S(2)}, u32[]{:S(2)}) collective-permute-start(bf16[104,256]{1,0:T(8,128)(2,1)S(1)} %constant_dynamic-update-slice_fusion), channel_id=1, source_target_pairs={{0,8},{1,9},{2,10},{3,11},{4,12},{5,13},{6,14},{7,15},{8,0},{9,1},... | collective-permute-start | bytes 159752 | tf_op jit(solution)/shard_map/ppermute | solution.py:70
  17.1 7.1 %collective-permute-start.5 = (bf16[96,512]{1,0:T(8,128)(2,1)S(1)}, bf16[96,512]{1,0:T(8,128)(2,1)S(1)}, u32[]{:S(2)}, u32[]{:S(2)}) collective-permute-start(bf16[96,512]{1,0:T(8,128)(2,1)S(1)} %maximum_select_fusion.7), channel_id=1, source_target_pairs={{0,64},{16,80},{32,96},{48,112},{64,0},{80,16},{96,32},{112,48},{1... | collective-permute-start | bytes 294920 | tf_op jit(solution)/shard_map/ppermute | solution.py:70
  19.6 6.3 %collective-permute-start.1 = (bf16[104,512]{1,0:T(8,128)(2,1)S(1)}, bf16[104,512]{1,0:T(8,128)(2,1)S(1)}, u32[]{:S(2)}, u32[]{:S(2)}) collective-permute-start(bf16[104,512]{1,0:T(8,128)(2,1)S(1)} %maximum_select_fusion.6), channel_id=1, source_target_pairs={{0,4},{1,5},{2,6},{3,7},{4,0},{5,1},{6,2},{7,3},{8,12},{9,13},{10,... | collective-permute-start | bytes 319496 | tf_op jit(solution)/shard_map/ppermute | solution.py:70
  24.3 6.4 %collective-permute-start.6 = (bf16[96,1024]{1,0:T(8,128)(2,1)S(1)}, bf16[96,1024]{1,0:T(8,128)(2,1)S(1)}, u32[]{:S(2)}, u32[]{:S(2)}) collective-permute-start(bf16[96,1024]{1,0:T(8,128)(2,1)S(1)} %maximum_select_fusion.5), channel_id=1, source_target_pairs={{0,32},{16,48},{32,0},{48,16},{64,96},{80,112},{96,64},{112,80},{1... | collective-permute-start | bytes 589832 | tf_op jit(solution)/shard_map/ppermute | solution.py:70
  25.9 7.2 %collective-permute-start.2 = (bf16[104,1024]{1,0:T(8,128)(2,1)S(1)}, bf16[104,1024]{1,0:T(8,128)(2,1)S(1)}, u32[]{:S(2)}, u32[]{:S(2)}) collective-permute-start(bf16[104,1024]{1,0:T(8,128)(2,1)S(1)} %maximum_select_fusion.4), channel_id=1, source_target_pairs={{0,2},{1,3},{2,0},{3,1},{4,6},{5,7},{6,4},{7,5},{8,10},{9,11},{10,... | collective-permute-start | bytes 638984 | tf_op jit(solution)/shard_map/ppermute | solution.py:70
  30.7 9.7 %collective-permute-start.7 = (bf16[96,2048]{1,0:T(8,128)(2,1)S(1)}, bf16[96,2048]{1,0:T(8,128)(2,1)S(1)}, u32[]{:S(2)}, u32[]{:S(2)}) collective-permute-start(bf16[96,2048]{1,0:T(8,128)(2,1)S(1)} %maximum_select_fusion.3), channel_id=1, source_target_pairs={{0,16},{16,0},{32,48},{48,32},{64,80},{80,64},{96,112},{112,96},{1... | collective-permute-start | bytes 1179656 | tf_op jit(solution)/shard_map/ppermute | solution.py:70
  33.2 7.6 %collective-permute-start.3 = (bf16[104,2048]{1,0:T(8,128)(2,1)S(1)}, bf16[104,2048]{1,0:T(8,128)(2,1)S(1)}, u32[]{:S(2)}, u32[]{:S(2)}) collective-permute-start(bf16[104,2048]{1,0:T(8,128)(2,1)S(1)} %maximum_select_fusion.2), channel_id=1, source_target_pairs={{0,1},{1,0},{2,3},{3,2},{4,5},{5,4},{6,7},{7,6},{8,9},{9,8},{10,11... | collective-permute-start | bytes 1277960 | tf_op jit(solution)/shard_map/ppermute | solution.py:70
  101.7 7.2 %collective-permute-start.9 = (f32[32]{0:T(128)S(1)}, f32[32]{0:T(128)S(1)}, u32[]{:S(2)}, u32[]{:S(2)}) collective-permute-start(f32[32]{0:T(128)S(1)} %pad_maximum_fusion.3), channel_id=1, source_target_pairs={{0,16},{16,0},{32,48},{48,32},{64,80},{80,64},{96,112},{112,96},{1... | collective-permute-start | bytes 392 | tf_op jit(solution)/shard_map/ppermute | solution.py:90
  102.4 6.5 %collective-permute-start.10 = (f32[32]{0:T(128)S(1)}, f32[32]{0:T(128)S(1)}, u32[]{:S(2)}, u32[]{:S(2)}) collective-permute-start(f32[32]{0:T(128)S(1)} %pad_maximum_fusion.3), channel_id=1, source_target_pairs={{0,17},{1,16},{2,19},{3,18},{4,21},{5,20},{6,23},{7,22},{8,25},{9,... | collective-permute-start | bytes 392 | tf_op jit(solution)/shard_map/ppermute | solution.py:91
  103.1 5.7 %collective-permute-start.8 = (f32[16,4098]{1,0:T(8,128)S(1)}, f32[16,4098]{1,0:T(8,128)S(1)}, u32[]{:S(2)}, u32[]{:S(2)}) collective-permute-start(f32[16,4098]{1,0:T(8,128)S(1)} %maximum_maximum_fusion), channel_id=1, source_target_pairs={{0,1},{1,0},{2,3},{3,2},{4,5},{5,4},{6,7},{7,6},{8,9},{9,8},{10,11... | collective-permute-start | bytes 786824 | tf_op jit(solution)/shard_map/ppermute | solution.py:83
  109.2 8.5 %collective-permute-start.11 = (f32[16,4098]{1,0:T(8,128)S(1)}, f32[16,4098]{1,0:T(8,128)S(1)}, u32[]{:S(2)}, u32[]{:S(2)}) collective-permute-start(f32[16,4098]{1,0:T(8,128)S(1)} %pad_maximum_fusion), channel_id=1, source_target_pairs={{0,2},{1,3},{2,0},{3,1},{4,6},{5,7},{6,4},{7,5},{8,10},{9,11},{10,... | collective-permute-start | bytes 786824 | tf_op jit(solution)/shard_map/ppermute | solution.py:83
  113.8 4.0 %collective-permute-start.12 = (f32[32]{0:T(128)S(1)}, f32[32]{0:T(128)S(1)}, u32[]{:S(2)}, u32[]{:S(2)}) collective-permute-start(f32[32]{0:T(128)S(1)} %add_add_fusion.4), channel_id=1, source_target_pairs={{0,32},{16,48},{32,0},{48,16},{64,96},{80,112},{96,64},{112,80},{1... | collective-permute-start | bytes 392 | tf_op jit(solution)/shard_map/ppermute | solution.py:90
  114.4 4.5 %collective-permute-start.13 = (f32[32]{0:T(128)S(1)}, f32[32]{0:T(128)S(1)}, u32[]{:S(2)}, u32[]{:S(2)}) collective-permute-start(f32[32]{0:T(128)S(1)} %add_add_fusion.4), channel_id=1, source_target_pairs={{0,34},{1,35},{2,32},{3,33},{4,38},{5,39},{6,36},{7,37},{8,42},{9,... | collective-permute-start | bytes 392 | tf_op jit(solution)/shard_map/ppermute | solution.py:91
  119.0 10.0 %collective-permute-start.14 = (f32[16,4098]{1,0:T(8,128)S(1)}, f32[16,4098]{1,0:T(8,128)S(1)}, u32[]{:S(2)}, u32[]{:S(2)}) collective-permute-start(f32[16,4098]{1,0:T(8,128)S(1)} %pad_maximum_fusion.1), channel_id=1, source_target_pairs={{0,4},{1,5},{2,6},{3,7},{4,0},{5,1},{6,2},{7,3},{8,12},{9,13},{10,... | collective-permute-start | bytes 786824 | tf_op jit(solution)/shard_map/ppermute | solution.py:83
  125.5 4.5 %collective-permute-start.15 = (f32[32]{0:T(128)S(1)}, f32[32]{0:T(128)S(1)}, u32[]{:S(2)}, u32[]{:S(2)}) collective-permute-start(f32[32]{0:T(128)S(1)} %add_add_fusion.3), channel_id=1, source_target_pairs={{0,64},{16,80},{32,96},{48,112},{64,0},{80,16},{96,32},{112,48},{1... | collective-permute-start | bytes 392 | tf_op jit(solution)/shard_map/ppermute | solution.py:90
  127.5 6.9 %collective-permute-start.16 = (f32[32]{0:T(128)S(1)}, f32[32]{0:T(128)S(1)}, u32[]{:S(2)}, u32[]{:S(2)}) collective-permute-start(f32[32]{0:T(128)S(1)} %add_add_fusion.3), channel_id=1, source_target_pairs={{0,68},{1,69},{2,70},{3,71},{4,64},{5,65},{6,66},{7,67},{8,76},{9,... | collective-permute-start | bytes 392 | tf_op jit(solution)/shard_map/ppermute | solution.py:91
  134.5 13.1 %collective-permute-start.17 = (f32[16,4098]{1,0:T(8,128)S(1)}, f32[16,4098]{1,0:T(8,128)S(1)}, u32[]{:S(2)}, u32[]{:S(2)}) collective-permute-start(f32[16,4098]{1,0:T(8,128)S(1)} %pad_maximum_fusion.2), channel_id=1, source_target_pairs={{0,8},{1,9},{2,10},{3,11},{4,12},{5,13},{6,14},{7,15},{8,0},{9,1},... | collective-permute-start | bytes 786824 | tf_op jit(solution)/shard_map/ppermute | solution.py:83
  138.7 9.0 %collective-permute-start.18 = (f32[32]{0:T(128)S(1)}, f32[32]{0:T(128)S(1)}, u32[]{:S(2)}, u32[]{:S(2)}) collective-permute-start(f32[32]{0:T(128)S(1)} %add_add_fusion.2), channel_id=1, source_target_pairs={{0,128},{16,144},{32,160},{48,176},{64,192},{80,208},{96,224},{112... | collective-permute-start | bytes 392 | tf_op jit(solution)/shard_map/ppermute | solution.py:90
  142.9 9.9 %collective-permute-start.19 = (f32[32]{0:T(128)S(1)}, f32[32]{0:T(128)S(1)}, u32[]{:S(2)}, u32[]{:S(2)}) collective-permute-start(f32[32]{0:T(128)S(1)} %add_add_fusion.2), channel_id=1, source_target_pairs={{0,136},{1,137},{2,138},{3,139},{4,140},{5,141},{6,142},{7,143},{8... | collective-permute-start | bytes 392 | tf_op jit(solution)/shard_map/ppermute | solution.py:91
  147.7 7.8 %copy-start = (bf16[1024,1024]{1,0:T(8,128)(2,1)S(1)}, bf16[1024,1024]{1,0:T(8,128)(2,1)}, u32[]{:S(2)}) copy-start(bf16[1024,1024]{1,0:T(8,128)(2,1)} %multiply_convert_fusion.3) | copy-start | bytes 6291460
  153.1 3.1 %copy-start.1 = (bf16[1024,1024]{1,0:T(8,128)(2,1)S(1)}, bf16[1024,1024]{1,0:T(8,128)(2,1)}, u32[]{:S(2)}) copy-start(bf16[1024,1024]{1,0:T(8,128)(2,1)} %multiply_convert_fusion.2) | copy-start | bytes 6291460
  155.5 1.6 copy-start.2
  156.1 23.7 %copy-start.5 = (f32[16,256]{1,0:T(8,128)S(1)}, f32[16,256]{1,0:T(8,128)}, u32[]{:S(2)}) copy-start(f32[16,256]{1,0:T(8,128)} %param.17) | copy-start | bytes 49156
  156.1 24.4 %copy-start.6 = (f32[64]{0:T(128)S(1)}, f32[64]{0:T(128)}, u32[]{:S(2)}) copy-start(f32[64]{0:T(128)} %param.16) | copy-start | bytes 772
  157.7 3.8 %collective-permute-start.20 = (f32[16,512]{1,0:T(8,128)S(1)}, f32[16,512]{1,0:T(8,128)S(1)}, u32[]{:S(2)}, u32[]{:S(2)}) collective-permute-start(f32[16,512]{1,0:T(8,128)S(1)} %slice_select_fusion), channel_id=1, source_target_pairs={{0,1},{1,0},{2,3},{3,2},{4,5},{5,4},{6,7},{7,6},{8,9},{9,8},{10,11... | collective-permute-start | bytes 98312 | tf_op jit(solution)/shard_map/ppermute | solution.py:108
  157.8 3.7 %collective-permute-start.21 = (f32[16]{0:T(128)S(1)}, f32[16]{0:T(128)S(1)}, u32[]{:S(2)}, u32[]{:S(2)}) collective-permute-start(f32[16]{0:T(128)S(1)} %get-tuple-element.56), channel_id=1, source_target_pairs={{0,16},{16,0},{32,48},{48,32},{64,80},{80,64},{96,112},{112,96},{1... | collective-permute-start | bytes 200 | tf_op jit(solution)/shard_map/ppermute | solution.py:109
  161.5 5.5 %collective-permute-start.22 = (f32[16,256]{1,0:T(8,128)S(1)}, f32[16,256]{1,0:T(8,128)S(1)}, u32[]{:S(2)}, u32[]{:S(2)}) collective-permute-start(f32[16,256]{1,0:T(8,128)S(1)} %slice_select_fusion.1), channel_id=1, source_target_pairs={{0,2},{1,3},{2,0},{3,1},{4,6},{5,7},{6,4},{7,5},{8,10},{9,11},{10,... | collective-permute-start | bytes 49160 | tf_op jit(solution)/shard_map/ppermute | solution.py:108
  163.4 3.6 %collective-permute-start.23 = (f32[16]{0:T(128)S(1)}, f32[16]{0:T(128)S(1)}, u32[]{:S(2)}, u32[]{:S(2)}) collective-permute-start(f32[16]{0:T(128)S(1)} %add.293), channel_id=1, source_target_pairs={{0,32},{16,48},{32,0},{48,16},{64,96},{80,112},{96,64},{112,80},{1... | collective-permute-start | bytes 200 | tf_op jit(solution)/shard_map/ppermute | solution.py:109
  167.0 5.2 %collective-permute-start.24 = (f32[16,128]{1,0:T(8,128)S(1)}, f32[16,128]{1,0:T(8,128)S(1)}, u32[]{:S(2)}, u32[]{:S(2)}) collective-permute-start(f32[16,128]{1,0:T(8,128)S(1)} %slice_select_fusion.3), channel_id=1, source_target_pairs={{0,4},{1,5},{2,6},{3,7},{4,0},{5,1},{6,2},{7,3},{8,12},{9,13},{10,... | collective-permute-start | bytes 24584 | tf_op jit(solution)/shard_map/ppermute | solution.py:108
  167.1 4.6 %collective-permute-start.25 = (f32[16]{0:T(128)S(1)}, f32[16]{0:T(128)S(1)}, u32[]{:S(2)}, u32[]{:S(2)}) collective-permute-start(f32[16]{0:T(128)S(1)} %add.295), channel_id=1, source_target_pairs={{0,64},{16,80},{32,96},{48,112},{64,0},{80,16},{96,32},{112,48},{1... | collective-permute-start | bytes 200 | tf_op jit(solution)/shard_map/ppermute | solution.py:109
  172.3 7.5 %collective-permute-start.26 = (f32[16]{0:T(128)S(1)}, f32[16]{0:T(128)S(1)}, u32[]{:S(2)}, u32[]{:S(2)}) collective-permute-start(f32[16]{0:T(128)S(1)} %add.297), channel_id=1, source_target_pairs={{0,128},{16,144},{32,160},{48,176},{64,192},{80,208},{96,224},{112... | collective-permute-start | bytes 200 | tf_op jit(solution)/shard_map/ppermute | solution.py:109
  174.1 6.4 %collective-permute-start.27 = (f32[16,64]{1,0:T(8,128)S(1)}, f32[16,64]{1,0:T(8,128)S(1)}, u32[]{:S(2)}, u32[]{:S(2)}) collective-permute-start(f32[16,64]{1,0:T(8,128)S(1)} %slice_select_fusion.2), channel_id=1, source_target_pairs={{0,8},{1,9},{2,10},{3,11},{4,12},{5,13},{6,14},{7,15},{8,0},{9,1},... | collective-permute-start | bytes 12296 | tf_op jit(solution)/shard_map/ppermute | solution.py:108
